TPU v7x, 32 devices: a whole 2x2x4 slice. The times are simulated.
32 devices in a mesh: groups: 2 (over x), heads: 8 (over z, y), tp: 2 (over core).
Axes of the slice: x: 2, y: 2, z: 4, core: 2. Of those that a mesh axis runs over, the one named last changes fastest.
Arguments:
- query_span: bfloat16 [32, 128, 16, 256], P(('groups', 'heads'), None, 'tp'), parts along dimension 0, may hold values from -6 to 6
- key_span: bfloat16 [32, 128, 16, 256], P(('groups', 'heads'), None, 'tp'), parts along dimension 0, may hold values from -6 to 6
- value_span: bfloat16 [32, 128, 16, 512], P(('groups', 'heads'), None, 'tp'), parts along dimension 0, may hold values from -6 to 6
- prior_state: bfloat16 [32, 16, 256, 512], P(('groups', 'heads'), 'tp'), parts along dimension 0, may hold values from -0.59765625 to 0.59765625
- decay_rates: float32 [16], replicated, may hold values from 0.001 to 0.05
- prompt_lengths: int32 [32], P('groups'), parts along dimension 0, may hold values from 1024 to 4095
- decode_inputs: bfloat16 [4, 32, 4096], P(None, 'groups'), parts along dimension 1, may hold values from -6 to 6
- w_query: bfloat16 [4096, 2, 8, 256], P(None, 'tp', 'heads'), may hold values from -0.09375 to 0.09375
- w_key: bfloat16 [4096, 2, 8, 256], P(None, 'tp', 'heads'), may hold values from -0.09375 to 0.09375
- w_value: bfloat16 [4096, 2, 8, 8, 64], P(None, 'tp', None, 'heads'), may hold values from -0.09375 to 0.09375
- w_gate: bfloat16 [4096, 2, 8, 8, 64], P(None, 'tp', None, 'heads'), may hold values from -0.09375 to 0.09375
- w_out: bfloat16 [2, 8, 8, 64, 4096], P('tp', None, 'heads'), may hold values from -0.09375 to 0.09375
Outputs:
- prefill_out: bfloat16 [32, 128, 16, 512], P(('groups', 'heads'), None, 'tp'), parts along dimension 0
- decode_out: bfloat16 [4, 32, 4096], P(None, 'groups', ('heads', 'tp')), parts along dimension 1
There are 2 independent parts, one for each index of `groups`. A program takes and returns all parts, laid end to end along the dimension named above; an argument that names none is the same for every part. Nothing has to cross between parts.
All inputs are finite; a program needn't handle non-finite values.
Results may differ from a plain program's by a relative error of at most 0.0083.
Values may be sent and summed in bfloat16 or wider, within the bound.
No kernel may reach another device: no remote copies, remote signals or barrier semaphores. Data moves between devices by JAX's collectives and lax.ppermute only.
A program may use at most 128 MiB of HBM per device.

v0:
```python
import jax
import jax.numpy as jnp
from jax import lax
from jax.sharding import PartitionSpec as P

EPSILON = 1e-05


def rotate(values, positions):
    halfway = values.shape[-1] // 2
    frequency = 10000.0 ** (-jnp.arange(halfway).astype(jnp.float32) / halfway)
    angles = positions[..., None] * frequency
    cosine = jnp.cos(angles)
    sine_part = jnp.sin(angles)
    paired = values.reshape(values.shape[:-1] + (halfway, 2))
    even_part = paired[..., 0]
    odd_part = paired[..., 1]
    turned = jnp.stack(
        [even_part * cosine - odd_part * sine_part, odd_part * cosine + even_part * sine_part], -1
    )
    return turned.reshape(values.shape)


def norm_with(output, mean_value, mean_square):
    return (output - mean_value) * lax.rsqrt(mean_square - mean_value * mean_value + EPSILON)


def per_device(
    query_span,
    key_span,
    value_span,
    prior_state,
    decay_rates,
    prompt_lengths,
    decode_inputs,
    w_query,
    w_key,
    w_value,
    w_gate,
    w_out,
):
    prompts_here, span_len, heads_here, key_width = query_span.shape
    value_width = value_span.shape[3]
    model_width = decode_inputs.shape[2]
    step_total = decode_inputs.shape[0]
    head_slots = lax.axis_size("heads")
    total_prompts = prompts_here * head_slots
    key_piece = w_query.shape[3]
    value_slice = w_value.shape[4]
    tp_index = lax.axis_index("tp")
    slot_index = lax.axis_index("heads")
    local_rates = lax.dynamic_slice_in_dim(decay_rates, tp_index * heads_here, heads_here)
    local_lengths = lax.dynamic_slice_in_dim(
        prompt_lengths, slot_index * prompts_here, prompts_here
    )
    span_start = span_len * ((local_lengths - 1) // span_len)
    live_count = local_lengths - span_start
    offsets = jnp.arange(span_len)
    positions = (span_start[:, None] + offsets[None, :]).astype(jnp.float32)
    queries = rotate(query_span.astype(jnp.float32), positions[:, :, None]).astype(jnp.bfloat16)
    keys = (
        rotate(key_span.astype(jnp.float32), positions[:, :, None]) * key_width ** (-0.5)
    ).astype(jnp.bfloat16)
    valid_rows = offsets[None, :] < live_count[:, None]
    distance = (offsets[:, None] - offsets[None, :]).astype(jnp.float32)
    decay_table = jnp.where(
        distance[None] >= 0,
        jnp.exp(-local_rates[:, None, None] * jnp.maximum(distance, 0.0)[None]),
        0.0,
    )
    scores = jnp.einsum("bihk,bjhk->bhij", queries, keys, preferred_element_type=jnp.float32)
    weights = jnp.where(valid_rows[:, None, None, :], scores * decay_table[None], 0.0).astype(
        jnp.bfloat16
    )
    inner_sum = jnp.einsum(
        "bhij,bjhv->bihv", weights, value_span, preferred_element_type=jnp.float32
    )
    carried = jnp.einsum(
        "bihk,bhkv->bihv", queries, prior_state, preferred_element_type=jnp.float32
    )
    lead_decay = jnp.exp(-local_rates[None, :] * (offsets[:, None] + 1).astype(jnp.float32))
    mixed = inner_sum + lead_decay[None, :, :, None] * carried
    mean_value = jnp.mean(mixed, -1, keepdims=True)
    mean_square = jnp.mean(mixed * mixed, -1, keepdims=True)
    prefill_out = jnp.where(
        valid_rows[:, :, None, None], norm_with(mixed, mean_value, mean_square), 0.0
    ).astype(jnp.bfloat16)
    remaining = (live_count[:, None] - 1 - offsets[None, :]).astype(jnp.float32)
    key_weight = jnp.where(
        valid_rows[:, :, None],
        jnp.exp(-local_rates[None, None, :] * jnp.maximum(remaining, 0.0)[:, :, None]),
        0.0,
    )
    weighted = (keys.astype(jnp.float32) * key_weight[..., None]).astype(jnp.bfloat16)
    update = jnp.einsum("bjhk,bjhv->bhkv", weighted, value_span, preferred_element_type=jnp.float32)
    kept_share = jnp.exp(-local_rates[None, :] * live_count[:, None].astype(jnp.float32))
    state_new = (kept_share[:, :, None, None] * prior_state.astype(jnp.float32) + update).astype(
        jnp.bfloat16
    )
    outgoing = state_new.reshape(prompts_here, heads_here, key_width, head_slots, value_slice)
    outgoing = outgoing.transpose(3, 0, 1, 4, 2)
    received = lax.all_to_all(outgoing, "heads", split_axis=0, concat_axis=1, tiled=True)
    state_now = received[0].astype(jnp.float32)
    flat_inputs = decode_inputs.reshape(step_total * total_prompts, model_width)
    query_part = jnp.dot(
        flat_inputs, w_query.reshape(model_width, key_piece), preferred_element_type=jnp.float32
    ).astype(jnp.bfloat16)
    key_part = jnp.dot(
        flat_inputs, w_key.reshape(model_width, key_piece), preferred_element_type=jnp.float32
    ).astype(jnp.bfloat16)
    query_all, key_all = (
        lax.all_gather(query_part[:, None, :], "heads", axis=1, tiled=True),
        lax.all_gather(key_part[:, None, :], "heads", axis=1, tiled=True),
    )
    query_heads = query_all.reshape(-1, heads_here, key_width)
    key_heads = key_all.reshape(-1, heads_here, key_width)
    value_dec = jnp.dot(
        flat_inputs,
        w_value.reshape(model_width, heads_here * value_slice),
        preferred_element_type=jnp.float32,
    ).astype(jnp.bfloat16)
    gate_values = jnp.dot(
        flat_inputs,
        w_gate.reshape(model_width, heads_here * value_slice),
        preferred_element_type=jnp.float32,
    )
    dec_positions = (
        (prompt_lengths[None, :] + jnp.arange(step_total)[:, None])
        .astype(jnp.float32)
        .reshape(-1, 1)
    )
    query_rot = (
        rotate(query_heads.astype(jnp.float32), dec_positions)
        .astype(jnp.bfloat16)
        .reshape(step_total, total_prompts, heads_here, key_width)
    )
    key_rot = (
        (rotate(key_heads.astype(jnp.float32), dec_positions) * key_width ** (-0.5))
        .astype(jnp.bfloat16)
        .reshape(step_total, total_prompts, heads_here, key_width)
    )
    value_steps = value_dec.reshape(step_total, total_prompts, heads_here, value_slice)
    retain = jnp.exp(-local_rates)[None, :, None, None]
    outputs = []
    for step_index in range(step_total):
        state_now = (
            retain * state_now
            + value_steps[step_index].astype(jnp.float32)[:, :, :, None]
            * key_rot[step_index].astype(jnp.float32)[:, :, None, :]
        )
        outputs.append(
            jnp.einsum(
                "bhk,bhvk->bhv",
                query_rot[step_index].astype(jnp.float32),
                state_now,
                precision=lax.Precision.HIGHEST,
            )
        )
    readout = jnp.stack(outputs)
    piece_sums = jnp.sum(readout, -1)
    piece_squares = jnp.sum(readout * readout, -1)
    total_sums, total_squares = lax.psum((piece_sums, piece_squares), "heads")
    head_mean = total_sums[..., None] / value_width
    head_square = total_squares[..., None] / value_width
    normed = norm_with(readout, head_mean, head_square)
    gates_steps = gate_values.reshape(step_total, total_prompts, heads_here, value_slice)
    activated = (
        (jax.nn.silu(gates_steps) * normed)
        .astype(jnp.bfloat16)
        .reshape(-1, heads_here * value_slice)
    )
    partial_out = jnp.dot(
        activated,
        w_out.reshape(heads_here * value_slice, model_width),
        preferred_element_type=jnp.float32,
    )
    partial_out = partial_out.reshape(step_total, total_prompts, model_width)
    summed = lax.psum_scatter(partial_out, ("heads", "tp"), scatter_dimension=2, tiled=True)
    decode_out = summed.astype(jnp.bfloat16)
    return (prefill_out, decode_out)


def solution(mesh):
    placed = (
        P(("groups", "heads"), None, "tp", None),
        P(("groups", "heads"), None, "tp", None),
        P(("groups", "heads"), None, "tp", None),
        P(("groups", "heads"), "tp", None, None),
        P(),
        P("groups"),
        P(None, "groups", None),
        P(None, "tp", "heads", None),
        P(None, "tp", "heads", None),
        P(None, "tp", None, "heads", None),
        P(None, "tp", None, "heads", None),
        P("tp", None, "heads", None, None),
    )
    return jax.shard_map(
        per_device,
        mesh=mesh,
        in_specs=placed,
        out_specs=(P(("groups", "heads"), None, "tp", None), P(None, "groups", ("heads", "tp"))),
        check_vma=False,
    )
```

profile of v0, /device:TPU:1, one launch (start us, length us, event | category | flops | bytes accessed | tf_op | source)
XLA Modules:
  0.0 396.2 jit_solution(17549836702236685842)
XLA Ops:
  18.1 6.2 %add_convert_fusion = bf16[2,8,256,512]{3,2,1,0:T(8,128)(2,1)} fusion(bf16[2,8,256,512]{3,2,1,0:T(8,128)(2,1)} %param.15, f32[2,8]{1,0:T(2,128)S(1)} %multiply_exponential_fusion.1, bf16[2,128,8,512]{3,2,1,0:T(8,128)(2,1)S(1)} %copy-done, bf16[2,128,8,256]{1,2,3,0:T(8,128)(2,1)S(1)} %multiply_convert_fusion), kind=kOutput, calls=%fused_computation.9 | convolution fusion | flops 545259520 | bytes 11534400 | tf_op jit(solution)/shard_map/bjhk,bjhv->bhkv/dot_general | solution.py:95
  24.3 6.2 %copy.110 = bf16[2,8,256,512]{2,3,1,0:T(8,128)(2,1)} copy(bf16[2,8,256,512]{3,2,1,0:T(8,128)(2,1)} %add_convert_fusion) | data formatting | bytes 8388608 | tf_op jit(solution)/shard_map/convert_element_type | solution.py:97
  30.5 4.8 %copy.111 = bf16[8,2,8,64,256]{4,3,2,1,0:T(8,128)(2,1)} copy(bf16[8,2,8,64,256]{4,3,0,2,1:T(8,128)(2,1)} %bitcast.95) | data formatting | bytes 8388608 | tf_op jit(solution)/shard_map/transpose | solution.py:101
  35.3 6.4 %all-to-all-start = ((bf16[8,2,8,64,256]{4,3,2,1,0:T(8,128)(2,1)}), bf16[8,2,8,64,256]{4,3,2,1,0:T(8,128)(2,1)}, u32[]{:S(2)}, u32[]{:S(2)}) async-start(bf16[8,2,8,64,256]{4,3,2,1,0:T(8,128)(2,1)} %copy.111), calls=%async_computation | async-start | bytes 8388608 | tf_op jit(solution)/shard_map/all_to_all | solution.py:102
  44.0 106.6 %all-gather = bf16[64,2048]{1,0:T(8,128)(2,1)S(1)} all-gather(bf16[64,256]{1,0:T(8,128)(2,1)S(1)} %fusion.45), channel_id=2, replica_groups=mesh['groups'=2,'heads'=8,'tp'=2] {'heads'}, dimensions={1}, use_global_device_ids=true | all-gather | bytes 294912 | tf_op jit(solution)/shard_map/all_gather | solution.py:112
  151.8 3.6 fusion.73
  161.5 25.0 %all-gather.1 = bf16[64,2048]{1,0:T(8,128)(2,1)S(1)} all-gather(bf16[64,256]{1,0:T(8,128)(2,1)S(1)} %fusion.48), channel_id=3, replica_groups=mesh['groups'=2,'heads'=8,'tp'=2] {'heads'}, dimensions={1}, use_global_device_ids=true | all-gather | bytes 294912 | tf_op jit(solution)/shard_map/all_gather | solution.py:113
  187.6 3.6 fusion.72
  208.0 3.7 convolution_convert_fusion
  219.6 2.4 copy.131
  228.3 2.4 copy.133
  242.5 2.4 copy.100
  246.1 7.2 %fusion.5 = f32[16,8,1,64]{3,2,1,0:T(1,128)S(1)} fusion(bf16[16,8,256,1]{2,3,1,0:T(2,128)(2,1)S(1)} %copy-done.6, bf16[16,8,64,256]{3,2,1,0:T(8,128)(2,1)} %bitcast.51, f32[16,8,256]{2,1,0:T(8,128)S(1)} %copy-done.4, f32[16,8,64]{2,1,0:T(8,128)} %reshape.508, f32[8]{0:T(128)S(1)} %get-tuple-element.18), kind=kOutput, calls=%fused_computation.8 | convolution fusion | flops 33554432 | bytes 4456480 | tf_op jit(solution)/shard_map/bhk,bhvk->bhv/dot_general | solution.py:152
  253.3 7.7 %fusion.7 = f32[16,8,1,64]{3,2,1,0:T(1,128)S(1)} fusion(bf16[16,8,256,1]{2,3,1,0:T(2,128)(2,1)S(1)} %copy-done.8, bf16[16,8,64,256]{3,2,1,0:T(8,128)(2,1)} %bitcast.51, f32[16,8,256]{2,1,0:T(8,128)S(1)} %copy-done.5, f32[16,8,64]{2,1,0:T(8,128)S(1)} %copy-done.12, f32[16,8,256]{2,1,0:T(8,128)S(1)} %copy-done.4, f32[16,8,64]{2,1,0:T(8,128)S(1)} %copy-done.11, ...), kind=kOutput, calls=%fused_computation.10 | convolution fusion | flops 39845888 | bytes 4620320 | tf_op jit(solution)/shard_map/bhk,bhvk->bhv/dot_general | solution.py:152
  261.1 8.5 %fusion.8 = f32[16,8,1,64]{3,2,1,0:T(1,128)S(1)} fusion(bf16[16,8,256,1]{2,3,1,0:T(2,128)(2,1)S(1)} %copy-done.10, bf16[16,8,64,256]{3,2,1,0:T(8,128)(2,1)} %bitcast.51, f32[16,8,256]{2,1,0:T(8,128)S(1)} %copy-done.7, f32[16,8,64]{2,1,0:T(8,128)S(1)} %copy-done.13, f32[16,8,256]{2,1,0:T(8,128)S(1)} %copy-done.5, f32[16,8,64]{2,1,0:T(8,128)S(1)} %copy-done.12, ...), kind=kOutput, calls=%fused_computation.11 | convolution fusion | flops 46137344 | bytes 4784160 | tf_op jit(solution)/shard_map/bhk,bhvk->bhv/dot_general | solution.py:152
  269.6 9.9 %fusion.1 = f32[16,8,1,64]{3,2,1,0:T(1,128)S(1)} fusion(bf16[16,8,256,1]{2,3,1,0:T(2,128)(2,1)S(1)} %copy.135, bf16[16,8,64,256]{3,2,1,0:T(8,128)(2,1)} %bitcast.51, f32[16,8,256]{2,1,0:T(8,128)S(1)} %copy-done.9, f32[16,8,64]{2,1,0:T(8,128)S(1)} %copy-done.14, f32[16,8,256]{2,1,0:T(8,128)S(1)} %copy-done.7, f32[16,8,64]{2,1,0:T(8,128)S(1)} %copy-done.13, ...), kind=kOutput, calls=%fused_computation.2 | convolution fusion | flops 52428800 | bytes 4948000 | tf_op jit(solution)/shard_map/bhk,bhvk->bhv/dot_general | solution.py:152
  279.8 26.4 %all-reduce = (f32[4,16,8]{1,2,0:T(8,128)S(1)}, f32[4,16,8]{1,2,0:T(8,128)S(1)}) all-reduce(f32[4,16,8]{1,2,0:T(8,128)S(1)} %get-tuple-element.15, f32[4,16,8]{1,2,0:T(8,128)S(1)} %get-tuple-element.14), channel_id=1, replica_groups=mesh['groups'=2,'heads'=8,'tp'=2] {'heads'}, use_global_device_ids=true, to_apply=%region_5.6 | all-reduce | flops 1024 | bytes 8192 | tf_op jit(solution)/shard_map/psum | solution.py:162
  306.1 4.5 %multiply_convert_fusion.1 = bf16[4,16,8,64]{3,1,2,0:T(8,128)(2,1)S(1)} fusion(bf16[4096,1,8,1,64]{0,4,3,2,1:T(8,128)(2,1)} %param.22, bf16[4,16,4096]{2,1,0:T(8,128)(2,1)} %param.18, f32[4,16,8]{1,2,0:T(8,128)S(1)} %get-tuple-element.52, f32[4,16,8]{1,2,0:T(8,128)S(1)} %get-tuple-element.51, f32[1,16,8,64]{3,1,2,0:T(8,128)S(1)} %get-tuple-element.60, ...), kind=kOutput, calls=%fused_computation.78 | convolution fusion | flops 268795904 | bytes 4919296 | tf_op jit(solution)/shard_map/dot_general | solution.py:122
  310.8 4.0 %fusion.77 = f32[4,16,4096]{2,1,0:T(8,128)} fusion(bf16[4,16,512]{2,1,0:T(8,128)(2,1)S(1)} %dot_general.59, bf16[512,4096,1]{1,0,2:T(8,128)(2,1)} %bitcast.110), kind=kOutput, calls=%fused_computation.135 | convolution fusion | flops 268435456 | bytes 5308416 | tf_op jit(solution)/shard_map/dot_general | solution.py:172
  314.9 5.2 %fusion.76 = f32[2,8,128,512]{3,2,1,0:T(8,128)} fusion(bf16[2,128,8,256]{3,1,2,0:T(8,128)(2,1)} %copy.100, bf16[2,8,256,512]{3,2,1,0:T(8,128)(2,1)} %param.15), kind=kOutput, calls=%fused_computation.134 | convolution fusion | flops 536870912 | bytes 9437184 | tf_op jit(solution)/shard_map/bihk,bhkv->bihv/dot_general | solution.py:78
  320.1 7.0 %fusion.69 = (f32[2,128,8]{1,2,0:T(8,128)S(1)}, f32[2,128,8]{1,2,0:T(8,128)S(1)}, f32[2,128,8,512]{3,1,2,0:T(8,128)}) fusion(f32[2,8,128,512]{3,2,1,0:T(8,128)} %fusion.76, f32[128,8]{0,1:T(8,128)S(1)} %multiply_exponential_fusion, bf16[2,128,8,512]{3,2,1,0:T(8,128)(2,1)S(1)} %copy-done, bf16[2,128,8,256]{3,1,2,0:T(8,128)(2,1)} %copy.100, ...), kind=kOutput, calls=%fused_computation.130 | convolution fusion | flops 408678400 | bytes 13127936 | tf_op jit(solution)/shard_map/bhij,bjhv->bihv/dot_general | solution.py:75
  327.1 2.6 select_convert_fusion
  329.7 2.5 copy.127
  332.2 55.7 %reduce-scatter.2.cloned.1.call-done = f32[4,16,256]{2,1,0:T(8,128)} async-done(((f32[4,16,4096]{2,1,0:T(8,128)}), f32[4,16,256]{2,1,0:T(8,128)}) %reduce-scatter.2.cloned.1.call-update) | async-done | bytes 65552 | tf_op jit(solution)/shard_map/reduce_scatter | solution.py:178
  (102 shorter events, 67.3 us)
Async XLA Ops:
  7.2 10.9 %copy-start = (bf16[2,128,8,512]{3,2,1,0:T(8,128)(2,1)S(1)}, bf16[2,128,8,512]{3,2,1,0:T(8,128)(2,1)}, u32[]{:S(2)}) copy-start(bf16[2,128,8,512]{3,2,1,0:T(8,128)(2,1)} %param.14) | copy-start | bytes 6291460
  14.2 1.6 copy-start.1
  15.8 1.8 copy-start.16
  35.3 210.7 %all-to-all-start = ((bf16[8,2,8,64,256]{4,3,2,1,0:T(8,128)(2,1)}), bf16[8,2,8,64,256]{4,3,2,1,0:T(8,128)(2,1)}, u32[]{:S(2)}, u32[]{:S(2)}) async-start(bf16[8,2,8,64,256]{4,3,2,1,0:T(8,128)(2,1)} %copy.111), calls=%async_computation | async-start | bytes 8388608 | tf_op jit(solution)/shard_map/all_to_all | solution.py:102
  41.7 346.2 %reduce-scatter.2.cloned.1.call-start = ((), (), s32[]{:S(2)}) async-start(), calls=%async_computation.2 | async-start | bytes 1114112 | tf_op jit(solution)/shard_map/reduce_scatter | solution.py:178
  157.3 37.1 %copy-start.15 = (s32[16]{0:T(128)S(1)}, s32[16]{0:T(128)}, u32[]{:S(2)}) copy-start(s32[16]{0:T(128)} %param.17) | copy-start | bytes 196
  215.3 11.8 %copy-start.3 = (bf16[16,8,128,2]{2,1,3,0:T(8,128)(2,1)S(1)}, bf16[16,8,128,2]{2,1,3,0:T(8,128)(2,1)}, u32[]{:S(2)}) copy-start(bf16[16,8,128,2]{2,1,3,0:T(8,128)(2,1)} %get-tuple-element.38) | copy-start | bytes 196612
  215.3 20.5 %copy-start.2 = (bf16[16,8,128,2]{2,1,3,0:T(8,128)(2,1)S(1)}, bf16[16,8,128,2]{2,1,3,0:T(8,128)(2,1)}, u32[]{:S(2)}) copy-start(bf16[16,8,128,2]{2,1,3,0:T(8,128)(2,1)} %get-tuple-element.37) | copy-start | bytes 196612
  232.1 13.9 %copy-start.4 = (f32[16,8,256]{2,1,0:T(8,128)S(1)}, f32[16,8,256]{2,1,0:T(8,128)}, u32[]{:S(2)}) copy-start(f32[16,8,256]{2,1,0:T(8,128)} %copy.116) | copy-start | bytes 393220
  233.5 12.5 %copy-start.6 = (bf16[16,8,256,1]{2,3,1,0:T(2,128)(2,1)S(1)}, bf16[16,8,256,1]{2,3,1,0:T(2,128)(2,1)}, u32[]{:S(2)}) copy-start(bf16[16,8,256,1]{2,3,1,0:T(2,128)(2,1)} %copy.129) | copy-start | bytes 196612
  246.0 7.2 %copy-start.5 = (f32[16,8,256]{2,1,0:T(8,128)S(1)}, f32[16,8,256]{2,1,0:T(8,128)}, u32[]{:S(2)}) copy-start(f32[16,8,256]{2,1,0:T(8,128)} %copy.119) | copy-start | bytes 393220
  246.0 7.2 %copy-start.8 = (bf16[16,8,256,1]{2,3,1,0:T(2,128)(2,1)S(1)}, bf16[16,8,256,1]{2,3,1,0:T(2,128)(2,1)}, u32[]{:S(2)}) copy-start(bf16[16,8,256,1]{2,3,1,0:T(2,128)(2,1)} %copy.131) | copy-start | bytes 196612
  246.0 7.2 %copy-start.11 = (f32[16,8,64]{2,1,0:T(8,128)S(1)}, f32[16,8,64]{2,1,0:T(8,128)}, u32[]{:S(2)}) copy-start(f32[16,8,64]{2,1,0:T(8,128)} %reshape.508) | copy-start | bytes 98308
  246.1 7.2 %copy-start.12 = (f32[16,8,64]{2,1,0:T(8,128)S(1)}, f32[16,8,64]{2,1,0:T(8,128)}, u32[]{:S(2)}) copy-start(f32[16,8,64]{2,1,0:T(8,128)} %reshape.512) | copy-start | bytes 98308
  253.3 7.7 %copy-start.7 = (f32[16,8,256]{2,1,0:T(8,128)S(1)}, f32[16,8,256]{2,1,0:T(8,128)}, u32[]{:S(2)}) copy-start(f32[16,8,256]{2,1,0:T(8,128)} %copy.122) | copy-start | bytes 393220
  253.3 7.7 %copy-start.10 = (bf16[16,8,256,1]{2,3,1,0:T(2,128)(2,1)S(1)}, bf16[16,8,256,1]{2,3,1,0:T(2,128)(2,1)}, u32[]{:S(2)}) copy-start(bf16[16,8,256,1]{2,3,1,0:T(2,128)(2,1)} %copy.133) | copy-start | bytes 196612
  253.3 7.7 %copy-start.13 = (f32[16,8,64]{2,1,0:T(8,128)S(1)}, f32[16,8,64]{2,1,0:T(8,128)}, u32[]{:S(2)}) copy-start(f32[16,8,64]{2,1,0:T(8,128)} %reshape.514) | copy-start | bytes 98308
  261.1 8.5 %copy-start.9 = (f32[16,8,256]{2,1,0:T(8,128)S(1)}, f32[16,8,256]{2,1,0:T(8,128)}, u32[]{:S(2)}) copy-start(f32[16,8,256]{2,1,0:T(8,128)} %copy.125) | copy-start | bytes 393220
  261.1 8.5 %copy-start.14 = (f32[16,8,64]{2,1,0:T(8,128)S(1)}, f32[16,8,64]{2,1,0:T(8,128)}, u32[]{:S(2)}) copy-start(f32[16,8,64]{2,1,0:T(8,128)} %reshape.516) | copy-start | bytes 98308
Sparse Core Ops, SparseCore 0:
  315.0 72.7 reduce-scatter.1
where the time goes:
time: 401 us; the launch traced here: 396 us
  blocking collectives  158 us (39%)
  local copies, waits for them, and re-layouts  74.9 us (19%)
  matrix products  68.4 us (17%)
  waiting for transfers between devices  55.7 us (14%)
  other arithmetic  18.4 us (5%)
  between operations  14.4 us (4%)
  starting transfers between devices  6.42 us (2%)
    all_gather x1, blocking collectives, per_device(): lax.all_gather(query_part[:, None, :], 'heads', axis=1, tiled=True)  107 us
    reduce_scatter x1, waiting for transfers between devices, per_device(): lax.psum_scatter(partial_out, ('heads', 'tp'), scatter_dimension=2, tiled...  55.7 us
    dot_general x4, matrix products, per_device(): jnp.einsum('bhk,bhvk->bhv', query_rot[step_index].astype(jnp.float32), st...  33.2 us
    psum x1, blocking collectives, per_device(): total_sums, total_squares = lax.psum((piece_sums, piece_squares), 'heads')  26.4 us
    all_gather x1, blocking collectives, per_device(): lax.all_gather(key_part[:, None, :], 'heads', axis=1, tiled=True)  25 us
    slice x8, local copies, waits for them, and re-layouts, per_device(): query_rot[step_index].astype(jnp.float32)  15.6 us
    convert_element_type x8, local copies, waits for them, and re-layouts, per_device(): key_rot[step_index].astype(jnp.float32)[:, :, None, :]  15.3 us
    unnamed x41, local copies, waits for them, and re-layouts  14.9 us
  transfers between devices with their start and end apart: 2, of which 1 were waited for; matrix products, arithmetic and copies ran while one was open for 23% of the time, Pallas kernels for 0%

commit v1 on v0

--- a/solution.py
+++ b/solution.py
@@ -97,10 +97,7 @@
     state_new = (kept_share[:, :, None, None] * prior_state.astype(jnp.float32) + update).astype(
         jnp.bfloat16
     )
-    outgoing = state_new.reshape(prompts_here, heads_here, key_width, head_slots, value_slice)
-    outgoing = outgoing.transpose(3, 0, 1, 4, 2)
-    received = lax.all_to_all(outgoing, "heads", split_axis=0, concat_axis=1, tiled=True)
-    state_now = received[0].astype(jnp.float32)
+    slots = head_slots
     flat_inputs = decode_inputs.reshape(step_total * total_prompts, model_width)
     query_part = jnp.dot(
         flat_inputs, w_query.reshape(model_width, key_piece), preferred_element_type=jnp.float32
@@ -108,12 +105,6 @@
     key_part = jnp.dot(
         flat_inputs, w_key.reshape(model_width, key_piece), preferred_element_type=jnp.float32
     ).astype(jnp.bfloat16)
-    query_all, key_all = (
-        lax.all_gather(query_part[:, None, :], "heads", axis=1, tiled=True),
-        lax.all_gather(key_part[:, None, :], "heads", axis=1, tiled=True),
-    )
-    query_heads = query_all.reshape(-1, heads_here, key_width)
-    key_heads = key_all.reshape(-1, heads_here, key_width)
     value_dec = jnp.dot(
         flat_inputs,
         w_value.reshape(model_width, heads_here * value_slice),
@@ -124,45 +115,62 @@
         w_gate.reshape(model_width, heads_here * value_slice),
         preferred_element_type=jnp.float32,
     )
-    dec_positions = (
-        (prompt_lengths[None, :] + jnp.arange(step_total)[:, None])
-        .astype(jnp.float32)
-        .reshape(-1, 1)
-    )
-    query_rot = (
-        rotate(query_heads.astype(jnp.float32), dec_positions)
-        .astype(jnp.bfloat16)
-        .reshape(step_total, total_prompts, heads_here, key_width)
+    packed = jnp.concatenate([query_part, key_part, value_dec], -1)
+    packed = packed.reshape(step_total, slots, prompts_here, -1).transpose(1, 0, 2, 3)
+    arrived = lax.all_to_all(packed, "heads", 0, 0, tiled=True)
+    query_own = (
+        arrived[..., :key_piece]
+        .transpose(1, 2, 0, 3)
+        .reshape(step_total, prompts_here, heads_here, key_width)
+    )
+    key_own = (
+        arrived[..., key_piece : 2 * key_piece]
+        .transpose(1, 2, 0, 3)
+        .reshape(step_total, prompts_here, heads_here, key_width)
+    )
+    value_own = (
+        arrived[..., 2 * key_piece :]
+        .reshape(slots, step_total, prompts_here, heads_here, value_slice)
+        .transpose(1, 2, 3, 0, 4)
+        .reshape(step_total, prompts_here, heads_here, value_width)
+    )
+    steps = jnp.arange(step_total)
+    dec_positions = (local_lengths[None, :] + steps[:, None]).astype(jnp.float32)
+    query_rot = rotate(query_own.astype(jnp.float32), dec_positions[:, :, None]).astype(
+        jnp.bfloat16
     )
     key_rot = (
-        (rotate(key_heads.astype(jnp.float32), dec_positions) * key_width ** (-0.5))
-        .astype(jnp.bfloat16)
-        .reshape(step_total, total_prompts, heads_here, key_width)
-    )
-    value_steps = value_dec.reshape(step_total, total_prompts, heads_here, value_slice)
-    retain = jnp.exp(-local_rates)[None, :, None, None]
-    outputs = []
-    for step_index in range(step_total):
-        state_now = (
-            retain * state_now
-            + value_steps[step_index].astype(jnp.float32)[:, :, :, None]
-            * key_rot[step_index].astype(jnp.float32)[:, :, None, :]
-        )
-        outputs.append(
-            jnp.einsum(
-                "bhk,bhvk->bhv",
-                query_rot[step_index].astype(jnp.float32),
-                state_now,
-                precision=lax.Precision.HIGHEST,
-            )
-        )
-    readout = jnp.stack(outputs)
-    piece_sums = jnp.sum(readout, -1)
-    piece_squares = jnp.sum(readout * readout, -1)
-    total_sums, total_squares = lax.psum((piece_sums, piece_squares), "heads")
-    head_mean = total_sums[..., None] / value_width
-    head_square = total_squares[..., None] / value_width
-    normed = norm_with(readout, head_mean, head_square)
+        rotate(key_own.astype(jnp.float32), dec_positions[:, :, None]) * key_width ** (-0.5)
+    ).astype(jnp.bfloat16)
+    from_state = jnp.einsum(
+        "tbhk,bhkv->tbhv", query_rot, state_new, preferred_element_type=jnp.float32
+    )
+    step_gap = (steps[:, None] - steps[None, :]).astype(jnp.float32)
+    step_decay = jnp.where(
+        step_gap[None] >= 0,
+        jnp.exp(-local_rates[:, None, None] * jnp.maximum(step_gap, 0.0)[None]),
+        0.0,
+    )
+    step_scores = jnp.einsum(
+        "tbhk,ubhk->bhtu", query_rot, key_rot, preferred_element_type=jnp.float32
+    )
+    from_steps = jnp.einsum(
+        "bhtu,ubhv->tbhv",
+        step_scores * step_decay[None],
+        value_own.astype(jnp.float32),
+        precision=lax.Precision.HIGHEST,
+    )
+    state_decay = jnp.exp(-local_rates[None, :] * (steps[:, None] + 1).astype(jnp.float32))
+    readout = state_decay[:, None, :, None] * from_state + from_steps
+    read_mean = jnp.mean(readout, -1, keepdims=True)
+    read_square = jnp.mean(readout * readout, -1, keepdims=True)
+    normed = norm_with(readout, read_mean, read_square)
+    normed = normed.reshape(step_total, prompts_here, heads_here, slots, value_slice)
+    normed = normed.transpose(3, 0, 1, 2, 4)
+    normed = lax.all_to_all(normed, "heads", 0, 0, tiled=True)
+    normed = normed.transpose(1, 0, 2, 3, 4).reshape(
+        step_total, total_prompts, heads_here, value_slice
+    )
     gates_steps = gate_values.reshape(step_total, total_prompts, heads_here, value_slice)
     activated = (
         (jax.nn.silu(gates_steps) * normed)

time: 401 us -> 166 us (0.41)
  the two profiles are of different devices: /device:TPU:1 before, /device:TPU:0 now
where the time goes in v1:
time: 166 us; the launch traced here: 165 us
  waiting for transfers between devices  42.4 us (26%)
  other arithmetic  31.7 us (19%)
  matrix products  31.4 us (19%)
  local copies, waits for them, and re-layouts  31.1 us (19%)
  between operations  14.5 us (9%)
  starting transfers between devices  13.5 us (8%)
    reduce_scatter x1, waiting for transfers between devices, per_device(): lax.psum_scatter(partial_out, ('heads', 'tp'), scatter_dimension=2, tiled...  37.8 us
    unnamed x37, local copies, waits for them, and re-layouts  9.16 us
    mul x1, other arithmetic, rotate(): odd_part * sine_part  7.32 us
    all_to_all x1, starting transfers between devices, per_device(): arrived = lax.all_to_all(packed, 'heads', 0, 0, tiled=True)  7.28 us
    dot_general x1, matrix products, per_device(): jnp.einsum('bhij,bjhv->bihv', weights, value_span, preferred_element_type...  7.11 us
    all_to_all x1, starting transfers between devices, per_device(): normed = lax.all_to_all(normed, 'heads', 0, 0, tiled=True)  6 us
    dot_general x1, matrix products, per_device(): jnp.einsum('tbhk,bhkv->tbhv', query_rot, state_new, preferred_element_typ...  5.24 us
    dot_general x1, matrix products, per_device(): jnp.einsum('bihk,bhkv->bihv', queries, prior_state, preferred_element_typ...  5.2 us
  transfers between devices with their start and end apart: 3, of which 2 were waited for; matrix products, arithmetic and copies ran while one was open for 26% of the time, Pallas kernels for 0%

profile of v1, /device:TPU:0, one launch (start us, length us, event | category | flops | bytes accessed | tf_op | source)
XLA Modules:
  0.0 164.7 jit_solution(11623395224212586450)
XLA Ops:
  7.2 3.9 %convolution_convert_fusion = bf16[64,512]{1,0:T(8,128)(2,1)S(1)} fusion(bf16[64,4096]{1,0:T(8,128)(2,1)} %bitcast.106, bf16[4096,512]{0,1:T(8,128)(2,1)} %bitcast.111), kind=kOutput, calls=%fused_computation.26 | convolution fusion | flops 268468224 | bytes 4784128 | tf_op jit(solution)/shard_map/dot_general | solution.py:108
  12.9 7.3 %all-to-all-start = ((bf16[8,4,2,1024]{3,1,2,0:T(4,128)(2,1)}), bf16[8,4,2,1024]{3,1,2,0:T(4,128)(2,1)S(1)}, u32[]{:S(2)}, u32[]{:S(2)}) async-start(bf16[8,4,2,1024]{3,1,2,0:T(4,128)(2,1)} %bitcast.101), calls=%async_computation | async-start | bytes 262144 | tf_op jit(solution)/shard_map/all_to_all | solution.py:120
  25.2 2.3 %copy.36 = bf16[2,128,8,256]{1,2,3,0:T(8,128)(2,1)S(1)} copy(bf16[2,128,8,256]{3,2,1,0:T(8,128)(2,1)} %param.12) | data formatting | bytes 2097152 | tf_op args[0]
  27.5 1.5 convert.22
  29.0 2.2 %copy.37 = bf16[2,128,8,256]{1,2,3,0:T(8,128)(2,1)S(1)} copy(bf16[2,128,8,256]{3,2,1,0:T(8,128)(2,1)} %param.13) | data formatting | bytes 2097152 | tf_op args[1]
  31.2 1.5 convert.23
  34.7 1.3 multiply_exponential_fusion.2
  36.1 1.4 multiply_exponential_fusion
  37.4 2.7 %multiply_subtract_fusion = (f32[2,128,8,128,1]{1,2,4,3,0:T(8,128)S(1)}, f32[2,128,8,128,1]{1,2,4,3,0:T(8,128)S(1)}, bf16[2,128,8,128,1]{1,2,4,3,0:T(8,128)(2,1)S(1)}, bf16[2,128,8,128,1]{1,2,4,3,0:T(8,128)(2,1)S(1)}) fusion(f32[2,128,8,128,2]{1,2,4,3,0:T(8,128)} %convert.23, f32[2,128,128]{1,2,0:T(8,128)S(1)} %get-tuple-element.47, ...), kind=kLoop, calls=%fused_computation.34 | loop fusion | flops 3670016 | bytes 7602176 | tf_op jit(solution)/shard_map/sub | solution.py:19
  43.9 1.3 copy.45
  46.6 7.3 %slice_multiply_fusion.5 = (f32[4,2,8,128,1]{2,4,3,1,0:T(1,128)}, f32[4,2,8,128,1]{2,4,3,1,0:T(1,128)}, f32[4,2,8,128,1]{2,4,3,1,0:T(1,128)}, f32[4,2,8,128,1]{2...) fusion(f32[4,2,8,128,2]{2,4,3,1,0:T(2,128)} %bitcast.114, ...), kind=kLoop, calls=%fused_computation.47 | loop fusion | flops 65536 | bytes 401408 | tf_op jit(solution)/shard_map/mul | solution.py:19
  68.4 5.2 %fusion.21 = f32[4,2,8,512]{3,0,2,1:T(4,128)S(1)} fusion(bf16[4,2,8,256]{3,0,2,1:T(4,128)(2,1)S(1)} %copy.51, bf16[2,8,256,512]{3,2,1,0:T(8,128)(2,1)} %param.15, f32[2,8]{1,0:T(2,128)S(1)} %copy-done.14, bf16[2,128,8,512]{3,2,1,0:T(8,128)(2,1)S(1)} %copy-done, bf16[2,128,8,256]{1,2,3,0:T(8,128)(2,1)} %multiply_convert_fusion, f32[4,8]{0,1:T(8,128)S(1)} %copy-done.12), kind=kOutput, calls=%fused_computation.25 | convolution fusion | flops 562069504 | bytes 7504064 | tf_op jit(solution)/shard_map/tbhk,bhkv->tbhv/dot_general | solution.py:145
  75.2 1.9 %reshape.459 = f32[8,1,4096]{2,1,0:T(1,128)} reshape(f32[8,4,8,2,64]{4,3,2,1,0:T(2,128)} %bitcast.118) | data formatting | bytes 262144
  77.1 6.0 %all-to-all-start.1 = ((f32[8,1,4096]{2,1,0:T(1,128)}), f32[8,1,4096]{2,1,0:T(1,128)S(1)}, u32[]{:S(2)}, u32[]{:S(2)}) async-start(f32[8,1,4096]{2,1,0:T(1,128)} %reshape.459), calls=%async_computation.1 | async-start | bytes 262144 | tf_op jit(solution)/shard_map/all_to_all | solution.py:170
  83.3 2.4 %copy.38 = bf16[2,128,8,256]{3,1,2,0:T(8,128)(2,1)} copy(bf16[2,128,8,256]{1,2,3,0:T(8,128)(2,1)} %bitcast.113) | data formatting | bytes 2097152 | tf_op jit(solution)/shard_map/convert_element_type | solution.py:60
  85.8 4.6 %all-to-all-done.1 = f32[8,1,4096]{2,1,0:T(1,128)S(1)} async-done(((f32[8,1,4096]{2,1,0:T(1,128)}), f32[8,1,4096]{2,1,0:T(1,128)S(1)}, u32[]{:S(2)}, u32[]{:S(2)}) %all-to-all-start.1) | async-done | bytes 131104 | tf_op jit(solution)/shard_map/all_to_all | solution.py:170
  92.2 4.5 %multiply_convert_fusion.1 = bf16[4,16,8,64]{3,1,2,0:T(8,128)(2,1)S(1)} fusion(f32[4,16,8,64]{3,1,2,0:T(8,128)S(1)} %bitcast.120, bf16[4096,1,8,1,64]{0,4,3,2,1:T(8,128)(2,1)} %param.22, bf16[4,16,4096]{2,1,0:T(8,128)(2,1)} %param.18), kind=kOutput, calls=%fused_computation.51 | convolution fusion | flops 268632064 | bytes 4915200 | tf_op jit(solution)/shard_map/dot_general | solution.py:113
  97.0 4.0 %fusion.52 = f32[4,16,4096]{2,1,0:T(8,128)} fusion(bf16[4,16,512]{2,1,0:T(8,128)(2,1)S(1)} %dot_general.55, bf16[512,4096,1]{1,0,2:T(8,128)(2,1)} %bitcast.112), kind=kOutput, calls=%fused_computation.103 | convolution fusion | flops 268435456 | bytes 5308416 | tf_op jit(solution)/shard_map/dot_general | solution.py:180
  101.0 5.2 %fusion.51 = f32[2,8,128,512]{3,2,1,0:T(8,128)} fusion(bf16[2,128,8,256]{3,1,2,0:T(8,128)(2,1)} %copy.38, bf16[2,8,256,512]{3,2,1,0:T(8,128)(2,1)} %param.15), kind=kOutput, calls=%fused_computation.102 | convolution fusion | flops 536870912 | bytes 9437184 | tf_op jit(solution)/shard_map/bihk,bhkv->bihv/dot_general | solution.py:78
  106.2 7.1 %fusion.45 = (f32[2,128,8]{1,2,0:T(8,128)S(1)}, f32[2,128,8]{1,2,0:T(8,128)S(1)}, f32[2,128,8,512]{3,1,2,0:T(8,128)}) fusion(f32[2,8,128,512]{3,2,1,0:T(8,128)} %fusion.51, f32[128,8]{0,1:T(8,128)S(1)} %multiply_exponential_fusion.1, bf16[2,128,8,512]{3,2,1,0:T(8,128)(2,1)S(1)} %copy-done, bf16[2,128,8,256]{3,1,2,0:T(8,128)(2,1)} %copy.38, ...), kind=kOutput, calls=%fused_computation.98 | convolution fusion | flops 408678400 | bytes 13127936 | tf_op jit(solution)/shard_map/bhij,bjhv->bihv/dot_general | solution.py:75
  113.4 2.7 %select_convert_fusion = bf16[2,128,8,512]{3,1,2,0:T(8,128)(2,1)S(1)} fusion(f32[2,128,8,512]{3,1,2,0:T(8,128)} %get-tuple-element.48, f32[2,128,8]{1,2,0:T(8,128)S(1)} %get-tuple-element.43, f32[2,128,8]{1,2,0:T(8,128)S(1)} %get-tuple-element.42, pred[2,128]{1,0:T(4,128)(4,1)S(1)} %copy-done.11), kind=kLoop, calls=%fused_computation.7 | loop fusion | flops 4194304 | bytes 6308096 | tf_op jit(solution)/shard_map/convert_element_type | solution.py:87
  116.1 2.5 %copy.64 = bf16[2,128,8,512]{3,2,1,0:T(8,128)(2,1)} copy(bf16[2,128,8,512]{3,1,2,0:T(8,128)(2,1)S(1)} %select_convert_fusion) | data formatting | bytes 4194304
  118.5 37.8 %reduce-scatter.2.cloned.1.call-done = f32[4,16,256]{2,1,0:T(8,128)} async-done(((f32[4,16,4096]{2,1,0:T(8,128)}), f32[4,16,256]{2,1,0:T(8,128)}) %reduce-scatter.2.cloned.1.call-update) | async-done | bytes 65552 | tf_op jit(solution)/shard_map/reduce_scatter | solution.py:186
  156.3 1.5 convert_element_type.168
  (100 shorter events, 32.0 us)
Async XLA Ops:
  7.2 61.2 %copy-start = (bf16[2,128,8,512]{3,2,1,0:T(8,128)(2,1)S(1)}, bf16[2,128,8,512]{3,2,1,0:T(8,128)(2,1)}, u32[]{:S(2)}) copy-start(bf16[2,128,8,512]{3,2,1,0:T(8,128)(2,1)} %param.14) | copy-start | bytes 6291460
  7.2 3.9 %copy-start.1 = (bf16[4,16,4096]{2,1,0:T(8,128)(2,1)S(1)}, bf16[4,16,4096]{2,1,0:T(8,128)(2,1)}, u32[]{:S(2)}) copy-start(bf16[4,16,4096]{2,1,0:T(8,128)(2,1)} %param.18) | copy-start | bytes 1572868
  7.2 3.9 %copy-start.2 = (bf16[4096,1,1,256]{3,0,2,1:T(8,128)(2,1)S(1)}, bf16[4096,1,1,256]{3,0,2,1:T(8,128)(2,1)}, u32[]{:S(2)}) copy-start(bf16[4096,1,1,256]{3,0,2,1:T(8,128)(2,1)} %param.19) | copy-start | bytes 6291460
  7.2 4.4 %copy-start.3 = (bf16[4096,1,1,256]{3,0,2,1:T(8,128)(2,1)S(1)}, bf16[4096,1,1,256]{3,0,2,1:T(8,128)(2,1)}, u32[]{:S(2)}) copy-start(bf16[4096,1,1,256]{3,0,2,1:T(8,128)(2,1)} %param.20) | copy-start | bytes 6291460
  11.1 9.7 %copy-start.15 = (s32[16]{0:T(128)S(1)}, s32[16]{0:T(128)}, u32[]{:S(2)}) copy-start(s32[16]{0:T(128)} %param.17) | copy-start | bytes 196
  12.9 31.0 %all-to-all-start = ((bf16[8,4,2,1024]{3,1,2,0:T(4,128)(2,1)}), bf16[8,4,2,1024]{3,1,2,0:T(4,128)(2,1)S(1)}, u32[]{:S(2)}, u32[]{:S(2)}) async-start(bf16[8,4,2,1024]{3,1,2,0:T(4,128)(2,1)} %bitcast.101), calls=%async_computation | async-start | bytes 262144 | tf_op jit(solution)/shard_map/all_to_all | solution.py:120
  34.7 9.0 %copy-start.5 = (f32[8]{0:T(128)}, f32[8]{0:T(128)S(1)}, u32[]{:S(2)}) copy-start(f32[8]{0:T(128)S(1)} %dynamic-slice_negate_fusion) | copy-start | bytes 100
  37.4 2.9 %copy-start.10 = (pred[2,128]{1,0:T(4,128)(4,1)S(1)}, pred[2,128]{1,0:T(4,128)(4,1)}, u32[]{:S(2)}) copy-start(pred[2,128]{1,0:T(4,128)(4,1)} %iota_compare_fusion) | copy-start | bytes 772
  37.4 2.9 %copy-start.13 = (f32[2,128]{1,0:T(2,128)S(1)}, f32[2,128]{1,0:T(2,128)}, u32[]{:S(2)}) copy-start(f32[2,128]{1,0:T(2,128)} %convert_maximum_fusion.2) | copy-start | bytes 3076
  40.1 2.7 %copy-start.4 = (f32[128,128]{1,0:T(8,128)S(1)}, f32[128,128]{1,0:T(8,128)}, u32[]{:S(2)}) copy-start(f32[128,128]{1,0:T(8,128)} %convert_maximum_fusion) | copy-start | bytes 196612
  40.2 3.6 %copy-start.9 = (f32[4,4]{1,0:T(4,128)S(1)}, f32[4,4]{1,0:T(4,128)}, u32[]{:S(2)}) copy-start(f32[4,4]{1,0:T(4,128)} %convert_maximum_fusion.1) | copy-start | bytes 196
  40.4 6.2 %copy-start.7 = (f32[4,2,128]{2,1,0:T(2,128)S(1)}, f32[4,2,128]{2,1,0:T(2,128)}, u32[]{:S(2)}) copy-start(f32[4,2,128]{2,1,0:T(2,128)} %get-tuple-element.44) | copy-start | bytes 12292
  40.4 6.2 %copy-start.8 = (f32[4,2,128]{2,1,0:T(2,128)S(1)}, f32[4,2,128]{2,1,0:T(2,128)}, u32[]{:S(2)}) copy-start(f32[4,2,128]{2,1,0:T(2,128)} %get-tuple-element.45) | copy-start | bytes 12292
  53.9 14.5 %copy-start.12 = (f32[4,8]{0,1:T(8,128)S(1)}, f32[4,8]{0,1:T(8,128)}, u32[]{:S(2)}) copy-start(f32[4,8]{0,1:T(8,128)} %multiply_exponential_fusion) | copy-start | bytes 388
  53.9 14.5 %copy-start.14 = (f32[2,8]{1,0:T(2,128)S(1)}, f32[2,8]{1,0:T(2,128)}, u32[]{:S(2)}) copy-start(f32[2,8]{1,0:T(2,128)} %multiply_exponential_fusion.2) | copy-start | bytes 196
  73.7 12.1 %copy-start.6 = (f32[8]{0:T(128)S(1)}, f32[8]{0:T(128)}, u32[]{:S(2)}) copy-start(f32[8]{0:T(128)} %copy-done.5) | copy-start | bytes 100
  77.1 13.3 %all-to-all-start.1 = ((f32[8,1,4096]{2,1,0:T(1,128)}), f32[8,1,4096]{2,1,0:T(1,128)S(1)}, u32[]{:S(2)}, u32[]{:S(2)}) async-start(f32[8,1,4096]{2,1,0:T(1,128)} %reshape.459), calls=%async_computation.1 | async-start | bytes 262144 | tf_op jit(solution)/shard_map/all_to_all | solution.py:170
  83.1 73.2 %reduce-scatter.2.cloned.1.call-start = ((), (), s32[]{:S(2)}) async-start(), calls=%async_computation.3 | async-start | bytes 1114112 | tf_op jit(solution)/shard_map/reduce_scatter | solution.py:186
  101.0 5.2 %copy-start.11 = (pred[2,128]{1,0:T(4,128)(4,1)S(1)}, pred[2,128]{1,0:T(4,128)(4,1)}, u32[]{:S(2)}) copy-start(pred[2,128]{1,0:T(4,128)(4,1)} %iota_compare_fusion) | copy-start | bytes 772
Sparse Core Ops, SparseCore 0:
  101.1 55.1 reduce-scatter.1

commit v2 on v1

--- a/solution.py
+++ b/solution.py
@@ -68,23 +68,6 @@
         jnp.exp(-local_rates[:, None, None] * jnp.maximum(distance, 0.0)[None]),
         0.0,
     )
-    scores = jnp.einsum("bihk,bjhk->bhij", queries, keys, preferred_element_type=jnp.float32)
-    weights = jnp.where(valid_rows[:, None, None, :], scores * decay_table[None], 0.0).astype(
-        jnp.bfloat16
-    )
-    inner_sum = jnp.einsum(
-        "bhij,bjhv->bihv", weights, value_span, preferred_element_type=jnp.float32
-    )
-    carried = jnp.einsum(
-        "bihk,bhkv->bihv", queries, prior_state, preferred_element_type=jnp.float32
-    )
-    lead_decay = jnp.exp(-local_rates[None, :] * (offsets[:, None] + 1).astype(jnp.float32))
-    mixed = inner_sum + lead_decay[None, :, :, None] * carried
-    mean_value = jnp.mean(mixed, -1, keepdims=True)
-    mean_square = jnp.mean(mixed * mixed, -1, keepdims=True)
-    prefill_out = jnp.where(
-        valid_rows[:, :, None, None], norm_with(mixed, mean_value, mean_square), 0.0
-    ).astype(jnp.bfloat16)
     remaining = (live_count[:, None] - 1 - offsets[None, :]).astype(jnp.float32)
     key_weight = jnp.where(
         valid_rows[:, :, None],
@@ -183,8 +166,31 @@
         preferred_element_type=jnp.float32,
     )
     partial_out = partial_out.reshape(step_total, total_prompts, model_width)
-    summed = lax.psum_scatter(partial_out, ("heads", "tp"), scatter_dimension=2, tiled=True)
-    decode_out = summed.astype(jnp.bfloat16)
+    queries, keys, value_span, prior_state, _ = lax.optimization_barrier(
+        (queries, keys, value_span, prior_state, partial_out)
+    )
+    scores = jnp.einsum("bihk,bjhk->bhij", queries, keys, preferred_element_type=jnp.float32)
+    weights = jnp.where(valid_rows[:, None, None, :], scores * decay_table[None], 0.0).astype(
+        jnp.bfloat16
+    )
+    inner_sum = jnp.einsum(
+        "bhij,bjhv->bihv", weights, value_span, preferred_element_type=jnp.float32
+    )
+    carried = jnp.einsum(
+        "bihk,bhkv->bihv", queries, prior_state, preferred_element_type=jnp.float32
+    )
+    lead_decay = jnp.exp(-local_rates[None, :] * (offsets[:, None] + 1).astype(jnp.float32))
+    mixed = inner_sum + lead_decay[None, :, :, None] * carried
+    mean_value = jnp.mean(mixed, -1, keepdims=True)
+    mean_square = jnp.mean(mixed * mixed, -1, keepdims=True)
+    prefill_out = jnp.where(
+        valid_rows[:, :, None, None], norm_with(mixed, mean_value, mean_square), 0.0
+    ).astype(jnp.bfloat16)
+    out_slots = head_slots * lax.axis_size("tp")
+    column_block = model_width // out_slots
+    pieces = partial_out.reshape(step_total, total_prompts, out_slots, column_block)
+    pieces = lax.all_to_all(pieces.transpose(2, 0, 1, 3), ("heads", "tp"), 0, 0, tiled=True)
+    decode_out = jnp.sum(pieces, 0).astype(jnp.bfloat16)
     return (prefill_out, decode_out)
 
 

time: 166 us -> 113 us (0.68)
  the two profiles are of different devices: /device:TPU:0 before, /device:TPU:1 now
where the time goes in v2:
time: 113 us; the launch traced here: 111 us
  local copies, waits for them, and re-layouts  32.4 us (29%)
  matrix products  31.4 us (28%)
  other arithmetic  25.2 us (22%)
  starting transfers between devices  19.3 us (17%)
  waiting for transfers between devices  1.31 us (1%)
    unnamed x25, local copies, waits for them, and re-layouts  10.6 us
    all_to_all x1, starting transfers between devices, per_device(): lax.all_to_all(pieces.transpose(2, 0, 1, 3), ('heads', 'tp'), 0, 0, tiled...  7.51 us
    mul x1, other arithmetic, rotate(): odd_part * sine_part  7.51 us
    dot_general x1, matrix products, per_device(): jnp.einsum('bhij,bjhv->bihv', weights, value_span, preferred_element_type...  6.77 us
    dot_general x2, local copies, waits for them, and re-layouts, per_device(): jnp.dot(activated, w_out.reshape(heads_here * value_slice, model_width),...  6.6 us
    all_to_all x1, starting transfers between devices, per_device(): arrived = lax.all_to_all(packed, 'heads', 0, 0, tiled=True)  6.39 us
    dot_general x1, matrix products, per_device(): jnp.einsum('tbhk,bhkv->tbhv', query_rot, state_new, preferred_element_typ...  5.85 us
    dot_general x1, matrix products, per_device(): jnp.einsum('bihk,bhkv->bihv', queries, prior_state, preferred_element_typ...  5.51 us
  transfers between devices with their start and end apart: 3, of which 1 were waited for; matrix products, arithmetic and copies ran while one was open for 39% of the time, Pallas kernels for 0%

profile of v2, /device:TPU:1, one launch (start us, length us, event | category | flops | bytes accessed | tf_op | source)
XLA Modules:
  0.0 110.7 jit_solution(2232787593109850897)
XLA Ops:
  0.7 3.9 %convolution_convert_fusion = bf16[64,512]{1,0:T(8,128)(2,1)S(1)} fusion(bf16[64,4096]{1,0:T(8,128)(2,1)} %bitcast.113, bf16[4096,512]{0,1:T(8,128)(2,1)} %bitcast.118), kind=kOutput, calls=%fused_computation.27 | convolution fusion | flops 268468224 | bytes 4784128 | tf_op jit(solution)/shard_map/dot_general | solution.py:91
  6.4 6.4 %all-to-all-start = ((bf16[8,4,2,1024]{3,1,2,0:T(4,128)(2,1)}), bf16[8,4,2,1024]{3,1,2,0:T(4,128)(2,1)S(1)}, u32[]{:S(2)}, u32[]{:S(2)}) async-start(bf16[8,4,2,1024]{3,1,2,0:T(4,128)(2,1)} %bitcast.108), calls=%async_computation | async-start | bytes 262144 | tf_op jit(solution)/shard_map/all_to_all | solution.py:103
  13.8 2.0 %copy.37 = bf16[2,128,8,256]{1,2,3,0:T(8,128)(2,1)} copy(bf16[2,128,8,256]{3,2,1,0:T(8,128)(2,1)S(1)} %copy-done.7) | data formatting | bytes 2097152 | tf_op args[0]
  15.8 1.4 %convert.22 = f32[2,128,8,128,2]{1,2,4,3,0:T(8,128)S(1)} convert(bf16[2,128,8,128,2]{1,2,4,3,0:T(8,128)(2,1)} %bitcast.116) | non-fusion elementwise | flops 524288 | bytes 3145728 | tf_op jit(solution)/shard_map/reshape | solution.py:15
  17.2 3.0 %copy.38 = bf16[2,128,8,256]{1,2,3,0:T(8,128)(2,1)} copy(bf16[2,128,8,256]{3,2,1,0:T(8,128)(2,1)} %param.13) | data formatting | bytes 2097152 | tf_op args[1]
  20.1 2.7 %convert.23 = f32[2,128,8,128,2]{1,2,4,3,0:T(8,128)} convert(bf16[2,128,8,128,2]{1,2,4,3,0:T(8,128)(2,1)} %bitcast.117) | non-fusion elementwise | flops 524288 | bytes 3145728 | tf_op jit(solution)/shard_map/reshape | solution.py:15
  23.1 2.1 %multiply_subtract_fusion = (f32[2,128,8,128,1]{1,2,4,3,0:T(8,128)S(1)}, f32[2,128,8,128,1]{1,2,4,3,0:T(8,128)S(1)}, bf16[2,128,8,128,1]{1,2,4,3,0:T(8,128)(2,1)S(1)}, bf16[2,128,8,128,1]{1,2,4,3,0:T(8,128)(2,1)S(1)}) fusion(f32[2,128,8,128,2]{1,2,4,3,0:T(8,128)} %convert.23, f32[2,128,128]{1,2,0:T(8,128)S(1)} %get-tuple-element.55, ...), kind=kLoop, calls=%fused_computation.35 | loop fusion | flops 3670016 | bytes 7602176 | tf_op jit(solution)/shard_map/sub | solution.py:19
  25.5 1.2 %multiply_convert_fusion = bf16[2,128,8,256]{1,2,3,0:T(8,128)(2,1)} fusion(bf16[2,128,8,256]{1,2,3,0:T(8,128)(2,1)S(1)} %bitcast.111, f32[2,128,8]{1,2,0:T(8,128)S(1)} %exponential_select_fusion.2), kind=kLoop, calls=%fused_computation.18 | loop fusion | flops 1572864 | bytes 2105344 | tf_op jit(solution)/shard_map/convert_element_type | solution.py:77
  28.3 1.4 %copy.55 = f32[4,2,8,256]{2,3,1,0:T(8,128)} copy(f32[4,2,8,256]{3,0,1,2:T(4,128)S(1)} %get-tuple-element.42) | data formatting | bytes 131072 | tf_op jit(solution)/shard_map/reshape | solution.py:15
  29.7 7.5 %slice_multiply_fusion.5 = (f32[4,2,8,128,1]{2,4,3,1,0:T(1,128)}, f32[4,2,8,128,1]{2,4,3,1,0:T(1,128)}, f32[4,2,8,128,1]{2,4,3,1,0:T(1,128)}, f32[4,2,8,128,1]{2...) fusion(f32[4,2,8,128,2]{2,4,3,1,0:T(2,128)S(1)} %bitcast.122, ...), kind=kLoop, calls=%fused_computation.48 | loop fusion | flops 65536 | bytes 401408 | tf_op jit(solution)/shard_map/mul | solution.py:19
  37.2 1.2 %copy.48 = f32[4,2,8,128,1]{3,2,4,1,0:T(8,128)S(1)} copy(f32[4,2,8,128,1]{2,4,3,1,0:T(1,128)} %get-tuple-element.39) | data formatting | bytes 65536 | tf_op jit(solution)/shard_map/mul | solution.py:19
  43.0 1.2 %copy.53 = bf16[4,2,8,256]{3,0,2,1:T(4,128)(2,1)S(1)} copy(bf16[4,2,8,256]{2,3,1,0:T(8,128)(2,1)} %bitcast.124) | data formatting | bytes 65536 | tf_op jit(solution)/shard_map/convert_element_type | solution.py:122
  47.3 5.8 %fusion.21 = f32[4,2,8,512]{3,0,2,1:T(4,128)S(1)} fusion(bf16[4,2,8,256]{3,0,2,1:T(4,128)(2,1)S(1)} %copy.53, bf16[2,8,256,512]{3,2,1,0:T(8,128)(2,1)} %param.15, f32[2,8]{1,0:T(2,128)S(1)} %multiply_exponential_fusion.2, bf16[2,128,8,512]{3,2,1,0:T(8,128)(2,1)} %param.14, bf16[2,128,8,256]{1,2,3,0:T(8,128)(2,1)} %multiply_convert_fusion, ...), kind=kOutput, calls=%fused_computation.26 | convolution fusion | flops 562069504 | bytes 7504064 | tf_op jit(solution)/shard_map/tbhk,bhkv->tbhv/dot_general | solution.py:128
  54.9 5.4 %all-to-all-start.1 = ((f32[8,1,4096]{2,1,0:T(1,128)}), f32[8,1,4096]{2,1,0:T(1,128)S(1)}, u32[]{:S(2)}, u32[]{:S(2)}) async-start(f32[8,1,4096]{2,1,0:T(1,128)} %reshape.462), calls=%async_computation.1 | async-start | bytes 262144 | tf_op jit(solution)/shard_map/all_to_all | solution.py:153
  60.4 6.5 %copy.66 = bf16[4096,512]{1,0:T(8,128)(2,1)} copy(bf16[4096,512]{0,1:T(8,128)(2,1)} %bitcast.119) | data formatting | bytes 8388608 | tf_op jit(solution)/shard_map/dot_general | solution.py:163
  68.7 4.3 %multiply_convert_fusion.1 = bf16[4,16,8,64]{3,1,2,0:T(8,128)(2,1)S(1)} fusion(f32[4,16,8,64]{3,1,2,0:T(8,128)S(1)} %bitcast.128, bf16[4096,1,8,1,64]{0,4,3,2,1:T(8,128)(2,1)} %param.22, bf16[4,16,4096]{2,1,0:T(8,128)(2,1)S(1)} %copy-done.2), kind=kOutput, calls=%fused_computation.52 | convolution fusion | flops 268632064 | bytes 4915200 | tf_op jit(solution)/shard_map/dot_general | solution.py:96
  73.2 3.6 %convolution_bitcast_fusion = f32[16,4,16,256]{3,2,0,1:T(8,128)S(1)} fusion(bf16[16,256,512,1]{2,1,0,3:T(8,128)(2,1)} %bitcast.120, bf16[4,16,512,1]{2,1,0,3:T(8,128)(2,1)S(1)} %reshape.457), kind=kOutput, calls=%fused_computation.19 | convolution fusion | flops 268435456 | bytes 5308416 | tf_op jit(solution)/shard_map/dot_general | solution.py:163
  78.0 7.5 %all-to-all-start.2 = ((f32[16,4,16,256]{3,2,1,0:T(8,128)}), f32[16,4,16,256]{3,2,1,0:T(8,128)}, u32[]{:S(2)}, u32[]{:S(2)}) async-start(f32[16,4,16,256]{3,2,1,0:T(8,128)} %copy.67), calls=%async_computation.2 | async-start | bytes 2097152 | tf_op jit(solution)/shard_map/all_to_all | solution.py:192
  86.4 5.5 %fusion.52 = f32[2,8,512,128]{3,2,1,0:T(8,128)} fusion(bf16[2,8,256,512]{3,2,1,0:T(8,128)(2,1)} %param.15, bf16[2,128,8,256]{3,1,2,0:T(8,128)(2,1)S(1)} %copy.39), kind=kOutput, calls=%fused_computation.104 | convolution fusion | flops 536870912 | bytes 9437184 | tf_op jit(solution)/shard_map/bihk,bhkv->bihv/dot_general | solution.py:179
  91.9 6.8 %fusion.46 = (f32[2,128,8]{1,2,0:T(8,128)S(1)}, f32[2,128,8]{1,2,0:T(8,128)S(1)}, f32[2,128,8,512]{1,3,2,0:T(8,128)}) fusion(f32[2,8,512,128]{3,2,1,0:T(8,128)} %fusion.52, f32[128,8]{0,1:T(8,128)S(1)} %multiply_exponential_fusion.1, bf16[2,128,8,256]{3,1,2,0:T(8,128)(2,1)S(1)} %copy.39, bf16[2,128,8,256]{1,2,3,0:T(8,128)(2,1)S(1)} %bitcast.112, ...), kind=kOutput, calls=%fused_computation.100 | convolution fusion | flops 408678400 | bytes 13127936 | tf_op jit(solution)/shard_map/bhij,bjhv->bihv/dot_general | solution.py:176
  98.7 4.3 %select_convert_fusion = bf16[2,128,8,512]{1,3,2,0:T(8,128)(2,1)} fusion(f32[2,128,8,512]{1,3,2,0:T(8,128)} %get-tuple-element.56, f32[2,128,8]{1,2,0:T(8,128)S(1)} %get-tuple-element.51, f32[2,128,8]{1,2,0:T(8,128)S(1)} %get-tuple-element.50, pred[2,128]{1,0:T(4,128)(4,1)S(1)} %iota_compare_fusion), kind=kLoop, calls=%fused_computation.7 | loop fusion | flops 4194304 | bytes 6308096 | tf_op jit(solution)/shard_map/convert_element_type | solution.py:188
  103.0 4.5 %copy.68 = bf16[2,128,8,512]{3,2,1,0:T(8,128)(2,1)} copy(bf16[2,128,8,512]{1,3,2,0:T(8,128)(2,1)} %select_convert_fusion) | data formatting | bytes 4194304
  107.5 1.3 %all-to-all-done.2 = f32[16,4,16,256]{3,2,1,0:T(8,128)} async-done(((f32[16,4,16,256]{3,2,1,0:T(8,128)}), f32[16,4,16,256]{3,2,1,0:T(8,128)}, u32[]{:S(2)}, u32[]{:S(2)}) %all-to-all-start.2) | async-done | bytes 1048608 | tf_op jit(solution)/shard_map/all_to_all | solution.py:192
  108.8 1.9 %reduce_sum.49 = bf16[4,16,256]{2,1,0:T(8,128)(2,1)} reduce(f32[16,4,16,256]{3,2,1,0:T(8,128)} %all-to-all-done.2, f32[]{:T(128)} %constant.62.clone.1), dimensions={0}, to_apply=%region_4.5 | reduce | flops 245760 | bytes 1081348 | tf_op jit(solution)/shard_map/reduce_sum | solution.py:193
  (89 shorter events, 18.2 us)
Async XLA Ops:
  0.6 3.9 %copy-start = (bf16[4096,1,1,256]{3,0,2,1:T(8,128)(2,1)S(1)}, bf16[4096,1,1,256]{3,0,2,1:T(8,128)(2,1)}, u32[]{:S(2)}) copy-start(bf16[4096,1,1,256]{3,0,2,1:T(8,128)(2,1)} %param.19) | copy-start | bytes 6291460
  0.6 3.9 %copy-start.2 = (bf16[4,16,4096]{2,1,0:T(8,128)(2,1)S(1)}, bf16[4,16,4096]{2,1,0:T(8,128)(2,1)}, u32[]{:S(2)}) copy-start(bf16[4,16,4096]{2,1,0:T(8,128)(2,1)} %param.18) | copy-start | bytes 1572868
  0.7 4.4 %copy-start.6 = (bf16[4096,1,1,256]{3,0,2,1:T(8,128)(2,1)S(1)}, bf16[4096,1,1,256]{3,0,2,1:T(8,128)(2,1)}, u32[]{:S(2)}) copy-start(bf16[4096,1,1,256]{3,0,2,1:T(8,128)(2,1)} %param.20) | copy-start | bytes 6291460
  4.6 8.2 %copy-start.8 = (s32[16]{0:T(128)S(1)}, s32[16]{0:T(128)}, u32[]{:S(2)}) copy-start(s32[16]{0:T(128)} %param.17) | copy-start | bytes 196
  5.1 8.7 %copy-start.7 = (bf16[2,128,8,256]{3,2,1,0:T(8,128)(2,1)S(1)}, bf16[2,128,8,256]{3,2,1,0:T(8,128)(2,1)}, u32[]{:S(2)}) copy-start(bf16[2,128,8,256]{3,2,1,0:T(8,128)(2,1)} %param.12) | copy-start | bytes 3145732
  6.4 21.5 %all-to-all-start = ((bf16[8,4,2,1024]{3,1,2,0:T(4,128)(2,1)}), bf16[8,4,2,1024]{3,1,2,0:T(4,128)(2,1)S(1)}, u32[]{:S(2)}, u32[]{:S(2)}) async-start(bf16[8,4,2,1024]{3,1,2,0:T(4,128)(2,1)} %bitcast.108), calls=%async_computation | async-start | bytes 262144 | tf_op jit(solution)/shard_map/all_to_all | solution.py:103
  15.8 7.1 %copy-start.9 = (f32[16]{0:T(128)S(1)}, f32[16]{0:T(128)}, u32[]{:S(2)}) copy-start(f32[16]{0:T(128)} %param.16) | copy-start | bytes 196
  37.2 8.2 %copy-start.5 = (f32[4,2,8,128,1]{2,4,3,1,0:T(1,128)S(1)}, f32[4,2,8,128,1]{2,4,3,1,0:T(1,128)}, u32[]{:S(2)}) copy-start(f32[4,2,8,128,1]{2,4,3,1,0:T(1,128)} %get-tuple-element.46) | copy-start | bytes 98308
  37.2 8.5 %copy-start.4 = (f32[4,2,8,128,1]{2,4,3,1,0:T(1,128)S(1)}, f32[4,2,8,128,1]{2,4,3,1,0:T(1,128)}, u32[]{:S(2)}) copy-start(f32[4,2,8,128,1]{2,4,3,1,0:T(1,128)} %get-tuple-element.44) | copy-start | bytes 98308
  54.9 12.0 %all-to-all-start.1 = ((f32[8,1,4096]{2,1,0:T(1,128)}), f32[8,1,4096]{2,1,0:T(1,128)S(1)}, u32[]{:S(2)}, u32[]{:S(2)}) async-start(f32[8,1,4096]{2,1,0:T(1,128)} %reshape.462), calls=%async_computation.1 | async-start | bytes 262144 | tf_op jit(solution)/shard_map/all_to_all | solution.py:153
  73.2 12.3 %copy-start.3 = (bf16[2,128,8,128,2]{1,2,4,3,0:T(8,128)(2,1)S(1)}, bf16[2,128,8,128,2]{1,2,4,3,0:T(8,128)(2,1)}, u32[]{:S(2)}) copy-start(bf16[2,128,8,128,2]{1,2,4,3,0:T(8,128)(2,1)} %pad_maximum_fusion) | copy-start | bytes 3145732
  78.0 30.8 %all-to-all-start.2 = ((f32[16,4,16,256]{3,2,1,0:T(8,128)}), f32[16,4,16,256]{3,2,1,0:T(8,128)}, u32[]{:S(2)}, u32[]{:S(2)}) async-start(f32[16,4,16,256]{3,2,1,0:T(8,128)} %copy.67), calls=%async_computation.2 | async-start | bytes 2097152 | tf_op jit(solution)/shard_map/all_to_all | solution.py:192
  98.7 12.0 %copy-start.1 = (bf16[4096,1,1,256]{3,0,2,1:T(8,128)(2,1)S(1)}, bf16[4096,1,1,256]{3,0,2,1:T(8,128)(2,1)}, u32[]{:S(2)}) copy-start(bf16[4096,1,1,256]{3,0,2,1:T(8,128)(2,1)} %param.19) | copy-start | bytes 6291460

commit v3 on v2

--- a/solution.py
+++ b/solution.py
@@ -1,6 +1,8 @@
 import jax
 import jax.numpy as jnp
 from jax import lax
+from jax.experimental import pallas as pl
+from jax.experimental.pallas import tpu as pltpu
 from jax.sharding import PartitionSpec as P
 
 EPSILON = 1e-05
@@ -23,6 +25,124 @@
 
 def norm_with(output, mean_value, mean_square):
     return (output - mean_value) * lax.rsqrt(mean_square - mean_value * mean_value + EPSILON)
+
+
+def prefill_kernel(
+    q_ref, k_ref, v_ref, prior_ref, cos_ref, sin_ref, swap_ref, table_ref, rows_ref,
+    out_ref, state_ref,
+):
+    swap = swap_ref[...]
+    cosine = cos_ref[...]
+    sine_part = sin_ref[...]
+    q_raw = q_ref[...]
+    k_raw = k_ref[...]
+    q_partner = jnp.dot(q_raw, swap, preferred_element_type=jnp.float32)
+    k_partner = jnp.dot(k_raw, swap, preferred_element_type=jnp.float32)
+    queries = (q_raw.astype(jnp.float32) * cosine + q_partner * sine_part).astype(jnp.bfloat16)
+    keys_wide = (k_raw.astype(jnp.float32) * cosine + k_partner * sine_part) * (
+        q_raw.shape[-1] ** (-0.5)
+    )
+    keys = keys_wide.astype(jnp.bfloat16)
+    values = v_ref[...]
+    prior = prior_ref[...]
+    rows = rows_ref[...]
+    lead = rows[:, 0:1]
+    valid = rows[:, 1:2]
+    key_weight = rows[:, 2:3]
+    kept = rows[0:1, 3:4]
+    scores = lax.dot_general(
+        queries, keys, (((1,), (1,)), ((), ())), preferred_element_type=jnp.float32
+    )
+    weights = (scores * table_ref[...]).astype(jnp.bfloat16)
+    inner = jnp.dot(weights, values, preferred_element_type=jnp.float32)
+    carried = jnp.dot(queries, prior, preferred_element_type=jnp.float32)
+    mixed = inner + lead * carried
+    mean_value = jnp.mean(mixed, -1, keepdims=True)
+    mean_square = jnp.mean(mixed * mixed, -1, keepdims=True)
+    normed = norm_with(mixed, mean_value, mean_square)
+    out_ref[...] = jnp.where(valid > 0.5, normed, 0.0).astype(out_ref.dtype)
+    weighted = (keys.astype(jnp.float32) * key_weight).astype(jnp.bfloat16)
+    update = lax.dot_general(
+        weighted, values, (((0,), (0,)), ((), ())), preferred_element_type=jnp.float32
+    )
+    state_ref[...] = (kept * prior.astype(jnp.float32) + update).astype(state_ref.dtype)
+
+
+def prefill(query_span, key_span, value_span, prior_state, local_rates, span_start, live_count):
+    prompts_here, span_len, heads_here, key_width = query_span.shape
+    value_width = value_span.shape[3]
+    halfway = key_width // 2
+    offsets = jnp.arange(span_len)
+    positions = (span_start[:, None] + offsets[None, :]).astype(jnp.float32)
+    frequency = 10000.0 ** (-jnp.arange(halfway).astype(jnp.float32) / halfway)
+    angles = positions[..., None] * frequency
+    cosine = jnp.repeat(jnp.cos(angles), 2, axis=-1)
+    sine_part = jnp.sin(angles)
+    sine_part = jnp.stack([-sine_part, sine_part], -1).reshape(cosine.shape)
+    lane = jnp.arange(key_width)
+    swap = (lane[:, None] == (lane[None, :] ^ 1)).astype(jnp.bfloat16)
+    valid_rows = offsets[None, :] < live_count[:, None]
+    distance = (offsets[:, None] - offsets[None, :]).astype(jnp.float32)
+    decay_table = jnp.where(
+        distance[None] >= 0,
+        jnp.exp(-local_rates[:, None, None] * jnp.maximum(distance, 0.0)[None]),
+        0.0,
+    )
+    table = jnp.where(valid_rows[:, None, None, :], decay_table[None], 0.0)
+    lead_decay = jnp.exp(-local_rates[:, None] * (offsets[None, :] + 1).astype(jnp.float32))
+    remaining = (live_count[:, None] - 1 - offsets[None, :]).astype(jnp.float32)
+    key_weight = jnp.where(
+        valid_rows[:, None, :],
+        jnp.exp(-local_rates[None, :, None] * jnp.maximum(remaining, 0.0)[:, None, :]),
+        0.0,
+    )
+    kept_share = jnp.exp(-local_rates[None, :] * live_count[:, None].astype(jnp.float32))
+    shape_rows = (prompts_here, heads_here, span_len)
+    rows = jnp.stack(
+        [
+            jnp.broadcast_to(lead_decay[None], shape_rows),
+            jnp.broadcast_to(valid_rows[:, None, :].astype(jnp.float32), shape_rows),
+            key_weight,
+            jnp.broadcast_to(kept_share[:, :, None], shape_rows),
+        ]
+        + [jnp.zeros(shape_rows, jnp.float32)] * 4,
+        -1,
+    )
+    grid = (prompts_here, heads_here)
+    out, state = pl.pallas_call(
+        prefill_kernel,
+        grid=grid,
+        in_specs=[
+            pl.BlockSpec((None, span_len, key_width), lambda b, h: (b, 0, h)),
+            pl.BlockSpec((None, span_len, key_width), lambda b, h: (b, 0, h)),
+            pl.BlockSpec((None, span_len, value_width), lambda b, h: (b, 0, h)),
+            pl.BlockSpec((None, None, key_width, value_width), lambda b, h: (b, h, 0, 0)),
+            pl.BlockSpec((None, span_len, key_width), lambda b, h: (b, 0, 0)),
+            pl.BlockSpec((None, span_len, key_width), lambda b, h: (b, 0, 0)),
+            pl.BlockSpec((key_width, key_width), lambda b, h: (0, 0)),
+            pl.BlockSpec((None, None, span_len, span_len), lambda b, h: (b, h, 0, 0)),
+            pl.BlockSpec((None, None, span_len, 8), lambda b, h: (b, h, 0, 0)),
+        ],
+        out_specs=[
+            pl.BlockSpec((None, span_len, value_width), lambda b, h: (b, 0, h)),
+            pl.BlockSpec((None, None, key_width, value_width), lambda b, h: (b, h, 0, 0)),
+        ],
+        out_shape=[
+            jax.ShapeDtypeStruct((prompts_here, span_len, heads_here * value_width), jnp.bfloat16),
+            jax.ShapeDtypeStruct(prior_state.shape, jnp.bfloat16),
+        ],
+    )(
+        query_span.reshape(prompts_here, span_len, heads_here * key_width),
+        key_span.reshape(prompts_here, span_len, heads_here * key_width),
+        value_span.reshape(prompts_here, span_len, heads_here * value_width),
+        prior_state,
+        cosine,
+        sine_part,
+        swap,
+        table,
+        rows,
+    )
+    return out.reshape(value_span.shape), state
 
 
 def per_device(
@@ -55,30 +175,8 @@
     )
     span_start = span_len * ((local_lengths - 1) // span_len)
     live_count = local_lengths - span_start
-    offsets = jnp.arange(span_len)
-    positions = (span_start[:, None] + offsets[None, :]).astype(jnp.float32)
-    queries = rotate(query_span.astype(jnp.float32), positions[:, :, None]).astype(jnp.bfloat16)
-    keys = (
-        rotate(key_span.astype(jnp.float32), positions[:, :, None]) * key_width ** (-0.5)
-    ).astype(jnp.bfloat16)
-    valid_rows = offsets[None, :] < live_count[:, None]
-    distance = (offsets[:, None] - offsets[None, :]).astype(jnp.float32)
-    decay_table = jnp.where(
-        distance[None] >= 0,
-        jnp.exp(-local_rates[:, None, None] * jnp.maximum(distance, 0.0)[None]),
-        0.0,
-    )
-    remaining = (live_count[:, None] - 1 - offsets[None, :]).astype(jnp.float32)
-    key_weight = jnp.where(
-        valid_rows[:, :, None],
-        jnp.exp(-local_rates[None, None, :] * jnp.maximum(remaining, 0.0)[:, :, None]),
-        0.0,
-    )
-    weighted = (keys.astype(jnp.float32) * key_weight[..., None]).astype(jnp.bfloat16)
-    update = jnp.einsum("bjhk,bjhv->bhkv", weighted, value_span, preferred_element_type=jnp.float32)
-    kept_share = jnp.exp(-local_rates[None, :] * live_count[:, None].astype(jnp.float32))
-    state_new = (kept_share[:, :, None, None] * prior_state.astype(jnp.float32) + update).astype(
-        jnp.bfloat16
+    prefill_out, state_new = prefill(
+        query_span, key_span, value_span, prior_state, local_rates, span_start, live_count
     )
     slots = head_slots
     flat_inputs = decode_inputs.reshape(step_total * total_prompts, model_width)
@@ -166,26 +264,6 @@
         preferred_element_type=jnp.float32,
     )
     partial_out = partial_out.reshape(step_total, total_prompts, model_width)
-    queries, keys, value_span, prior_state, _ = lax.optimization_barrier(
-        (queries, keys, value_span, prior_state, partial_out)
-    )
-    scores = jnp.einsum("bihk,bjhk->bhij", queries, keys, preferred_element_type=jnp.float32)
-    weights = jnp.where(valid_rows[:, None, None, :], scores * decay_table[None], 0.0).astype(
-        jnp.bfloat16
-    )
-    inner_sum = jnp.einsum(
-        "bhij,bjhv->bihv", weights, value_span, preferred_element_type=jnp.float32
-    )
-    carried = jnp.einsum(
-        "bihk,bhkv->bihv", queries, prior_state, preferred_element_type=jnp.float32
-    )
-    lead_decay = jnp.exp(-local_rates[None, :] * (offsets[:, None] + 1).astype(jnp.float32))
-    mixed = inner_sum + lead_decay[None, :, :, None] * carried
-    mean_value = jnp.mean(mixed, -1, keepdims=True)
-    mean_square = jnp.mean(mixed * mixed, -1, keepdims=True)
-    prefill_out = jnp.where(
-        valid_rows[:, :, None, None], norm_with(mixed, mean_value, mean_square), 0.0
-    ).astype(jnp.bfloat16)
     out_slots = head_slots * lax.axis_size("tp")
     column_block = model_width // out_slots
     pieces = partial_out.reshape(step_total, total_prompts, out_slots, column_block)

time: 113 us -> 130 us (1.15)
  waiting for transfers between devices: 1.31 us -> 19.4 us
  Pallas kernels: 0 us -> 16 us
  matrix products: 31.4 us -> 16.8 us
  other arithmetic: 25.2 us -> 14.2 us
  local copies, waits for them, and re-layouts: 32.4 us -> 40.8 us
    all_to_all x1, waiting for transfers between devices: 1.3 us -> 19.4 us  [per_device(): lax.all_to_all(pieces.transpose(2, 0, 1, 3), ('heads', 'tp'), 0, 0, tiled...]
    pallas_call x0 -> x1, Pallas kernels: none -> 16 us  [prefill(): pl.pallas_call(prefill_kernel, grid=grid, in_specs=[pl.BlockSpec((None, s...]
    dot_general x2 -> x0, matrix products: 12.3 us -> none  [the longest x1 6.77 us: per_device(): jnp.einsum('bhij,bjhv->bihv', weights, value_span, preferred_element_type...]
    reshape x0 -> x5, local copies, waits for them, and re-layouts: none -> 10.6 us  [the longest x1 4.19 us: prefill(): value_span.reshape(prompts_here, span_len, heads_here * value_width)]
    convert_element_type x6 -> x5, other arithmetic: 5.72 us -> 0.92 us  [the longest x1 0.68 us: prefill(): swap = (lane[:, None] == lane[None, :] ^ 1).astype(jnp.bfloat16)]
    reshape x3 -> x1, other arithmetic: 4.11 us -> 0.01 us  [rotate(): paired = values.reshape(values.shape[:-1] + (halfway, 2))]
    unnamed x25 -> x13, local copies, waits for them, and re-layouts: 10.6 us -> 6.51 us
    dot_general x1, matrix products: 5.85 us -> 2.84 us  [per_device(): jnp.einsum('tbhk,bhkv->tbhv', query_rot, state_new, preferred_element_typ...]
  transfers between devices with their start and end apart: 3 -> 3, of which waited for: 1 -> 1; matrix products, arithmetic and copies ran while one was open for 39% -> 21% of each run, Pallas kernels for 0% -> 13%
where the time goes in v3:
time: 130 us; the launch traced here: 128 us
  local copies, waits for them, and re-layouts  40.8 us (31%)
  waiting for transfers between devices  19.4 us (15%)
  starting transfers between devices  19.3 us (15%)
  matrix products  16.8 us (13%)
  Pallas kernels  16 us (12%)
  other arithmetic  14.2 us (11%)
    all_to_all x1, waiting for transfers between devices, per_device(): lax.all_to_all(pieces.transpose(2, 0, 1, 3), ('heads', 'tp'), 0, 0, tiled...  19.4 us
    pallas_call x1, Pallas kernels, prefill(): pl.pallas_call(prefill_kernel, grid=grid, in_specs=[pl.BlockSpec((None, s...  16 us
    all_to_all x1, starting transfers between devices, per_device(): lax.all_to_all(pieces.transpose(2, 0, 1, 3), ('heads', 'tp'), 0, 0, tiled...  7.51 us
    mul x1, other arithmetic, rotate(): odd_part * sine_part  7.16 us
    dot_general x2, local copies, waits for them, and re-layouts, per_device(): jnp.dot(activated, w_out.reshape(heads_here * value_slice, model_width),...  6.6 us
    unnamed x13, local copies, waits for them, and re-layouts  6.51 us
    all_to_all x1, starting transfers between devices, per_device(): arrived = lax.all_to_all(packed, 'heads', 0, 0, tiled=True)  6.39 us
    all_to_all x1, starting transfers between devices, per_device(): normed = lax.all_to_all(normed, 'heads', 0, 0, tiled=True)  5.44 us
  transfers between devices with their start and end apart: 3, of which 1 were waited for; matrix products, arithmetic and copies ran while one was open for 21% of the time, Pallas kernels for 13%

profile of v3, /device:TPU:1, one launch (start us, length us, event | category | flops | bytes accessed | tf_op | source)
XLA Modules:
  0.0 127.6 jit_solution(671512860304332889)
XLA Ops:
  0.7 1.6 %copy-done = bf16[4096,1,1,256]{3,0,2,1:T(8,128)(2,1)S(1)} copy-done((bf16[4096,1,1,256]{3,0,2,1:T(8,128)(2,1)S(1)}, bf16[4096,1,1,256]{3,0,2,1:T(8,128)(2,1)}, u32[]{:S(2)}) %copy-start) | copy-done | bytes 2097176
  2.2 1.9 %fusion.8 = bf16[64,256]{1,0:T(8,128)(2,1)S(1)} fusion(bf16[64,4096]{1,0:T(8,128)(2,1)} %bitcast.109, bf16[4096,1,1,256]{3,0,2,1:T(8,128)(2,1)S(1)} %copy-done), kind=kOutput, calls=%fused_computation.12 | convolution fusion | flops 134234112 | bytes 2654208 | tf_op jit(solution)/shard_map/dot_general | solution.py:183
  4.1 2.2 %fusion.11 = bf16[64,256]{1,0:T(8,128)(2,1)S(1)} fusion(bf16[64,4096]{1,0:T(8,128)(2,1)} %bitcast.110, bf16[4096,1,1,256]{3,0,2,1:T(8,128)(2,1)} %param.20), kind=kOutput, calls=%fused_computation.13 | convolution fusion | flops 134234112 | bytes 2654208 | tf_op jit(solution)/shard_map/dot_general | solution.py:186
  6.4 1.4 %convolution_convert_fusion = bf16[64,512]{1,0:T(8,128)(2,1)S(1)} fusion(bf16[64,4096]{1,0:T(8,128)(2,1)S(1)} %bitcast.111, bf16[4096,512]{0,1:T(8,128)(2,1)S(1)} %bitcast.112), kind=kOutput, calls=%fused_computation.11 | convolution fusion | flops 268468224 | bytes 4784128 | tf_op jit(solution)/shard_map/dot_general | solution.py:189
  8.6 6.4 %all-to-all-start = ((bf16[8,4,2,1024]{3,1,2,0:T(4,128)(2,1)}), bf16[8,4,2,1024]{3,1,2,0:T(4,128)(2,1)S(1)}, u32[]{:S(2)}, u32[]{:S(2)}) async-start(bf16[8,4,2,1024]{3,1,2,0:T(4,128)(2,1)} %bitcast.106), calls=%async_computation | async-start | bytes 262144 | tf_op jit(solution)/shard_map/all_to_all | solution.py:201
  17.8 1.2 broadcast_select_fusion.table_ref
  21.2 1.3 %copy.57.rows_ref = f32[2,8,128,8]{3,2,1,0:T(8,128)} copy(f32[2,8,128,8]{2,3,1,0:T(8,128)S(1)} %stack.25) | data formatting | bytes 131072 | tf_op jit(solution)/shard_map/stack | solution.py:101
  22.5 2.3 %reshape.359.q_ref = bf16[2,128,2048]{2,1,0:T(8,128)(2,1)} reshape(bf16[2,128,8,256]{3,2,1,0:T(8,128)(2,1)} %param.12) | data formatting | bytes 2097152 | tf_op jit(solution)/shard_map/reshape | solution.py:135
  24.8 2.4 %reshape.360.k_ref = bf16[2,128,2048]{2,1,0:T(8,128)(2,1)} reshape(bf16[2,128,8,256]{3,2,1,0:T(8,128)(2,1)} %param.13) | data formatting | bytes 2097152 | tf_op jit(solution)/shard_map/reshape | solution.py:136
  27.2 4.2 %reshape.361.v_ref = bf16[2,128,4096]{2,1,0:T(8,128)(2,1)} reshape(bf16[2,128,8,512]{3,2,1,0:T(8,128)(2,1)} %param.14) | data formatting | bytes 4194304 | tf_op jit(solution)/shard_map/reshape | solution.py:137
  31.4 16.0 %shard_map.131 = (bf16[2,128,4096]{2,1,0:T(8,128)(2,1)}, bf16[2,8,256,512]{3,2,1,0:T(8,128)(2,1)}) custom-call(bf16[2,128,2048]{2,1,0:T(8,128)(2,1)} %reshape.359.q_ref, bf16[2,128,2048]{2,1,0:T(8,128)(2,1)} %reshape.360.k_ref, bf16[2,128,4096]{2,1,0:T(8,128)(2,1)} %reshape.361.v_ref, bf16[2,8,256,512]{3,2,1,0:T(8,128)(2,1)} %prior_ref.1, ...), custom_call_target="tpu_custom_call" | custom-call | tf_op jit(solution)/shard_map/pallas_call | solution.py:112
  47.9 1.3 %copy.67 = f32[4,2,8,256]{2,3,1,0:T(8,128)} copy(f32[4,2,8,256]{3,0,1,2:T(4,128)S(1)} %get-tuple-element.24) | data formatting | bytes 131072 | tf_op jit(solution)/shard_map/reshape | solution.py:17
  49.2 1.3 %copy.59 = f32[4,2,8,256]{2,3,1,0:T(8,128)} copy(f32[4,2,8,256]{3,0,1,2:T(4,128)S(1)} %get-tuple-element.25) | data formatting | bytes 131072 | tf_op jit(solution)/shard_map/reshape | solution.py:17
  50.6 7.2 %slice_multiply_fusion.5 = (f32[4,2,8,128,1]{2,4,3,1,0:T(1,128)}, f32[4,2,8,128,1]{2,4,3,1,0:T(1,128)}, f32[4,2,8,128,1]{2,4,3,1,0:T(1,128)}, f32[4,2,8,128,1]{2...) fusion(f32[4,2,8,128,2]{2,4,3,1,0:T(2,128)} %bitcast.116, ...), kind=kLoop, calls=%fused_computation.23 | loop fusion | flops 65536 | bytes 401408 | tf_op jit(solution)/shard_map/mul | solution.py:21
  63.5 1.2 copy.70
  67.5 2.8 %fusion.7 = f32[4,2,8,512]{3,0,2,1:T(4,128)S(1)} fusion(bf16[2,8,256,512]{3,2,1,0:T(8,128)(2,1)} %get-tuple-element.5, bf16[4,2,8,256]{3,0,2,1:T(4,128)(2,1)S(1)} %copy.65, f32[4,8]{0,1:T(8,128)S(1)} %multiply_exponential_fusion), kind=kOutput, calls=%fused_computation.10 | convolution fusion | flops 16809984 | bytes 4358272 | tf_op jit(solution)/shard_map/tbhk,bhkv->tbhv/dot_general | solution.py:226
  72.1 5.4 %all-to-all-start.1 = ((f32[8,1,4096]{2,1,0:T(1,128)}), f32[8,1,4096]{2,1,0:T(1,128)S(1)}, u32[]{:S(2)}, u32[]{:S(2)}) async-start(f32[8,1,4096]{2,1,0:T(1,128)} %reshape.393), calls=%async_computation.1 | async-start | bytes 262144 | tf_op jit(solution)/shard_map/all_to_all | solution.py:251
  77.5 6.5 %copy.78 = bf16[4096,512]{1,0:T(8,128)(2,1)} copy(bf16[4096,512]{0,1:T(8,128)(2,1)} %bitcast.113) | data formatting | bytes 8388608 | tf_op jit(solution)/shard_map/dot_general | solution.py:261
  85.8 4.3 %multiply_convert_fusion = bf16[4,16,8,64]{3,1,2,0:T(8,128)(2,1)S(1)} fusion(f32[4,16,8,64]{3,1,2,0:T(8,128)S(1)} %bitcast.125, bf16[4096,1,8,1,64]{0,4,3,2,1:T(8,128)(2,1)} %param.22, bf16[4,16,4096]{2,1,0:T(8,128)(2,1)S(1)} %copy-done.1), kind=kOutput, calls=%fused_computation.28 | convolution fusion | flops 268632064 | bytes 4915200 | tf_op jit(solution)/shard_map/dot_general | solution.py:194
  90.3 3.6 %convolution_bitcast_fusion = f32[16,4,16,256]{3,2,0,1:T(8,128)S(1)} fusion(bf16[16,256,512,1]{2,1,0,3:T(8,128)(2,1)} %bitcast.114, bf16[4,16,512,1]{2,1,0,3:T(8,128)(2,1)S(1)} %reshape.388), kind=kOutput, calls=%fused_computation.6 | convolution fusion | flops 268435456 | bytes 5308416 | tf_op jit(solution)/shard_map/dot_general | solution.py:261
  95.0 7.5 %all-to-all-start.2 = ((f32[16,4,16,256]{3,2,1,0:T(8,128)}), f32[16,4,16,256]{3,2,1,0:T(8,128)}, u32[]{:S(2)}, u32[]{:S(2)}) async-start(f32[16,4,16,256]{3,2,1,0:T(8,128)} %copy.79), calls=%async_computation.2 | async-start | bytes 2097152 | tf_op jit(solution)/shard_map/all_to_all | solution.py:270
  102.5 3.8 %copy.82 = bf16[32,8,8,512]{3,2,1,0:T(8,128)(2,1)} copy(bf16[32,8,8,512]{3,1,2,0:T(8,128)(2,1)} %bitcast.117) | data formatting | bytes 4194304
  106.3 19.4 %all-to-all-done.2 = f32[16,4,16,256]{3,2,1,0:T(8,128)} async-done(((f32[16,4,16,256]{3,2,1,0:T(8,128)}), f32[16,4,16,256]{3,2,1,0:T(8,128)}, u32[]{:S(2)}, u32[]{:S(2)}) %all-to-all-start.2) | async-done | bytes 1048608 | tf_op jit(solution)/shard_map/all_to_all | solution.py:270
  125.7 1.9 %reduce_sum.29 = bf16[4,16,256]{2,1,0:T(8,128)(2,1)} reduce(f32[16,4,16,256]{3,2,1,0:T(8,128)} %all-to-all-done.2, f32[]{:T(128)} %constant.58.clone.1), dimensions={0}, to_apply=%region_2.3 | reduce | flops 245760 | bytes 1081348 | tf_op jit(solution)/shard_map/reduce_sum | solution.py:271
  (85 shorter events, 19.5 us)
Async XLA Ops:
  0.6 1.6 %copy-start = (bf16[4096,1,1,256]{3,0,2,1:T(8,128)(2,1)S(1)}, bf16[4096,1,1,256]{3,0,2,1:T(8,128)(2,1)}, u32[]{:S(2)}) copy-start(bf16[4096,1,1,256]{3,0,2,1:T(8,128)(2,1)} %param.19) | copy-start | bytes 6291460
  0.6 5.7 %copy-start.1 = (bf16[4,16,4096]{2,1,0:T(8,128)(2,1)S(1)}, bf16[4,16,4096]{2,1,0:T(8,128)(2,1)}, u32[]{:S(2)}) copy-start(bf16[4,16,4096]{2,1,0:T(8,128)(2,1)} %param.18) | copy-start | bytes 1572868
  0.7 5.7 %copy-start.2 = (bf16[4096,1,8,1,64]{0,4,3,2,1:T(8,128)(2,1)S(1)}, bf16[4096,1,8,1,64]{0,4,3,2,1:T(8,128)(2,1)}, u32[]{:S(2)}) copy-start(bf16[4096,1,8,1,64]{0,4,3,2,1:T(8,128)(2,1)} %param.21) | copy-start | bytes 12582916
  4.1 10.9 %copy-start.3 = (s32[16]{0:T(128)S(1)}, s32[16]{0:T(128)}, u32[]{:S(2)}) copy-start(s32[16]{0:T(128)} %param.17) | copy-start | bytes 196
  4.1 12.3 %copy-start.4 = (f32[16]{0:T(128)S(1)}, f32[16]{0:T(128)}, u32[]{:S(2)}) copy-start(f32[16]{0:T(128)} %param.16) | copy-start | bytes 196
  8.6 38.8 %all-to-all-start = ((bf16[8,4,2,1024]{3,1,2,0:T(4,128)(2,1)}), bf16[8,4,2,1024]{3,1,2,0:T(4,128)(2,1)S(1)}, u32[]{:S(2)}, u32[]{:S(2)}) async-start(bf16[8,4,2,1024]{3,1,2,0:T(4,128)(2,1)} %bitcast.106), calls=%async_computation | async-start | bytes 262144 | tf_op jit(solution)/shard_map/all_to_all | solution.py:201
  72.1 11.9 %all-to-all-start.1 = ((f32[8,1,4096]{2,1,0:T(1,128)}), f32[8,1,4096]{2,1,0:T(1,128)S(1)}, u32[]{:S(2)}, u32[]{:S(2)}) async-start(f32[8,1,4096]{2,1,0:T(1,128)} %reshape.393), calls=%async_computation.1 | async-start | bytes 262144 | tf_op jit(solution)/shard_map/all_to_all | solution.py:251
  95.0 30.7 %all-to-all-start.2 = ((f32[16,4,16,256]{3,2,1,0:T(8,128)}), f32[16,4,16,256]{3,2,1,0:T(8,128)}, u32[]{:S(2)}, u32[]{:S(2)}) async-start(f32[16,4,16,256]{3,2,1,0:T(8,128)} %copy.79), calls=%async_computation.2 | async-start | bytes 2097152 | tf_op jit(solution)/shard_map/all_to_all | solution.py:270

commit v4 on v3

--- a/solution.py
+++ b/solution.py
@@ -34,38 +34,41 @@
     swap = swap_ref[...]
     cosine = cos_ref[...]
     sine_part = sin_ref[...]
-    q_raw = q_ref[...]
-    k_raw = k_ref[...]
-    q_partner = jnp.dot(q_raw, swap, preferred_element_type=jnp.float32)
-    k_partner = jnp.dot(k_raw, swap, preferred_element_type=jnp.float32)
-    queries = (q_raw.astype(jnp.float32) * cosine + q_partner * sine_part).astype(jnp.bfloat16)
-    keys_wide = (k_raw.astype(jnp.float32) * cosine + k_partner * sine_part) * (
-        q_raw.shape[-1] ** (-0.5)
-    )
-    keys = keys_wide.astype(jnp.bfloat16)
-    values = v_ref[...]
-    prior = prior_ref[...]
-    rows = rows_ref[...]
-    lead = rows[:, 0:1]
-    valid = rows[:, 1:2]
-    key_weight = rows[:, 2:3]
-    kept = rows[0:1, 3:4]
-    scores = lax.dot_general(
-        queries, keys, (((1,), (1,)), ((), ())), preferred_element_type=jnp.float32
-    )
-    weights = (scores * table_ref[...]).astype(jnp.bfloat16)
-    inner = jnp.dot(weights, values, preferred_element_type=jnp.float32)
-    carried = jnp.dot(queries, prior, preferred_element_type=jnp.float32)
-    mixed = inner + lead * carried
-    mean_value = jnp.mean(mixed, -1, keepdims=True)
-    mean_square = jnp.mean(mixed * mixed, -1, keepdims=True)
-    normed = norm_with(mixed, mean_value, mean_square)
-    out_ref[...] = jnp.where(valid > 0.5, normed, 0.0).astype(out_ref.dtype)
-    weighted = (keys.astype(jnp.float32) * key_weight).astype(jnp.bfloat16)
-    update = lax.dot_general(
-        weighted, values, (((0,), (0,)), ((), ())), preferred_element_type=jnp.float32
-    )
-    state_ref[...] = (kept * prior.astype(jnp.float32) + update).astype(state_ref.dtype)
+    for head in range(q_ref.shape[1]):
+        q_raw = q_ref[:, head, :]
+        k_raw = k_ref[:, head, :]
+        q_partner = jnp.dot(q_raw, swap, preferred_element_type=jnp.float32)
+        k_partner = jnp.dot(k_raw, swap, preferred_element_type=jnp.float32)
+        queries = (q_raw.astype(jnp.float32) * cosine + q_partner * sine_part).astype(
+            jnp.bfloat16
+        )
+        keys_wide = (k_raw.astype(jnp.float32) * cosine + k_partner * sine_part) * (
+            q_raw.shape[-1] ** (-0.5)
+        )
+        keys = keys_wide.astype(jnp.bfloat16)
+        values = v_ref[:, head, :]
+        prior = prior_ref[head]
+        rows = rows_ref[head]
+        lead = rows[:, 0:1]
+        valid = rows[:, 1:2]
+        key_weight = rows[:, 2:3]
+        kept = rows[0:1, 3:4]
+        scores = lax.dot_general(
+            queries, keys, (((1,), (1,)), ((), ())), preferred_element_type=jnp.float32
+        )
+        weights = (scores * table_ref[head]).astype(jnp.bfloat16)
+        inner = jnp.dot(weights, values, preferred_element_type=jnp.float32)
+        carried = jnp.dot(queries, prior, preferred_element_type=jnp.float32)
+        mixed = inner + lead * carried
+        mean_value = jnp.mean(mixed, -1, keepdims=True)
+        mean_square = jnp.mean(mixed * mixed, -1, keepdims=True)
+        normed = norm_with(mixed, mean_value, mean_square)
+        out_ref[:, head, :] = jnp.where(valid > 0.5, normed, 0.0).astype(out_ref.dtype)
+        weighted = (keys.astype(jnp.float32) * key_weight).astype(jnp.bfloat16)
+        update = lax.dot_general(
+            weighted, values, (((0,), (0,)), ((), ())), preferred_element_type=jnp.float32
+        )
+        state_ref[head] = (kept * prior.astype(jnp.float32) + update).astype(state_ref.dtype)
 
 
 def prefill(query_span, key_span, value_span, prior_state, local_rates, span_start, live_count):
@@ -108,33 +111,33 @@
         + [jnp.zeros(shape_rows, jnp.float32)] * 4,
         -1,
     )
-    grid = (prompts_here, heads_here)
+    grid = (prompts_here,)
     out, state = pl.pallas_call(
         prefill_kernel,
         grid=grid,
         in_specs=[
-            pl.BlockSpec((None, span_len, key_width), lambda b, h: (b, 0, h)),
-            pl.BlockSpec((None, span_len, key_width), lambda b, h: (b, 0, h)),
-            pl.BlockSpec((None, span_len, value_width), lambda b, h: (b, 0, h)),
-            pl.BlockSpec((None, None, key_width, value_width), lambda b, h: (b, h, 0, 0)),
-            pl.BlockSpec((None, span_len, key_width), lambda b, h: (b, 0, 0)),
-            pl.BlockSpec((None, span_len, key_width), lambda b, h: (b, 0, 0)),
-            pl.BlockSpec((key_width, key_width), lambda b, h: (0, 0)),
-            pl.BlockSpec((None, None, span_len, span_len), lambda b, h: (b, h, 0, 0)),
-            pl.BlockSpec((None, None, span_len, 8), lambda b, h: (b, h, 0, 0)),
+            pl.BlockSpec((None, span_len, heads_here, key_width), lambda b: (b, 0, 0, 0)),
+            pl.BlockSpec((None, span_len, heads_here, key_width), lambda b: (b, 0, 0, 0)),
+            pl.BlockSpec((None, span_len, heads_here, value_width), lambda b: (b, 0, 0, 0)),
+            pl.BlockSpec((None, heads_here, key_width, value_width), lambda b: (b, 0, 0, 0)),
+            pl.BlockSpec((None, span_len, key_width), lambda b: (b, 0, 0)),
+            pl.BlockSpec((None, span_len, key_width), lambda b: (b, 0, 0)),
+            pl.BlockSpec((key_width, key_width), lambda b: (0, 0)),
+            pl.BlockSpec((None, heads_here, span_len, span_len), lambda b: (b, 0, 0, 0)),
+            pl.BlockSpec((None, heads_here, span_len, 8), lambda b: (b, 0, 0, 0)),
         ],
         out_specs=[
-            pl.BlockSpec((None, span_len, value_width), lambda b, h: (b, 0, h)),
-            pl.BlockSpec((None, None, key_width, value_width), lambda b, h: (b, h, 0, 0)),
+            pl.BlockSpec((None, span_len, heads_here, value_width), lambda b: (b, 0, 0, 0)),
+            pl.BlockSpec((None, heads_here, key_width, value_width), lambda b: (b, 0, 0, 0)),
         ],
         out_shape=[
-            jax.ShapeDtypeStruct((prompts_here, span_len, heads_here * value_width), jnp.bfloat16),
+            jax.ShapeDtypeStruct(value_span.shape, jnp.bfloat16),
             jax.ShapeDtypeStruct(prior_state.shape, jnp.bfloat16),
         ],
     )(
-        query_span.reshape(prompts_here, span_len, heads_here * key_width),
-        key_span.reshape(prompts_here, span_len, heads_here * key_width),
-        value_span.reshape(prompts_here, span_len, heads_here * value_width),
+        query_span,
+        key_span,
+        value_span,
         prior_state,
         cosine,
         sine_part,
@@ -142,7 +145,7 @@
         table,
         rows,
     )
-    return out.reshape(value_span.shape), state
+    return out, state
 
 
 def per_device(
@@ -196,15 +199,36 @@
         w_gate.reshape(model_width, heads_here * value_slice),
         preferred_element_type=jnp.float32,
     )
-    packed = jnp.concatenate([query_part, key_part, value_dec], -1)
+    steps = jnp.arange(step_total)
+    halfway = key_width // 2
+    head_column = (slot_index * key_piece + jnp.arange(key_piece)) % key_width
+    column_frequency = 10000.0 ** (-(head_column // 2).astype(jnp.float32) / halfway)
+    dec_positions = (
+        (prompt_lengths[None, :] + steps[:, None]).astype(jnp.float32).reshape(-1, 1)
+    )
+    dec_angles = dec_positions * column_frequency[None, :]
+    dec_cosine = jnp.cos(dec_angles)
+    dec_sine = jnp.where(head_column % 2 == 0, -1.0, 1.0)[None, :] * jnp.sin(dec_angles)
+    lane = jnp.arange(key_piece)
+    swap = (lane[:, None] == (lane[None, :] ^ 1)).astype(jnp.bfloat16)
+    query_partner = jnp.dot(query_part, swap, preferred_element_type=jnp.float32)
+    key_partner = jnp.dot(key_part, swap, preferred_element_type=jnp.float32)
+    query_turned = (
+        query_part.astype(jnp.float32) * dec_cosine + query_partner * dec_sine
+    ).astype(jnp.bfloat16)
+    key_turned = (
+        (key_part.astype(jnp.float32) * dec_cosine + key_partner * dec_sine)
+        * key_width ** (-0.5)
+    ).astype(jnp.bfloat16)
+    packed = jnp.concatenate([query_turned, key_turned, value_dec], -1)
     packed = packed.reshape(step_total, slots, prompts_here, -1).transpose(1, 0, 2, 3)
     arrived = lax.all_to_all(packed, "heads", 0, 0, tiled=True)
-    query_own = (
+    query_rot = (
         arrived[..., :key_piece]
         .transpose(1, 2, 0, 3)
         .reshape(step_total, prompts_here, heads_here, key_width)
     )
-    key_own = (
+    key_rot = (
         arrived[..., key_piece : 2 * key_piece]
         .transpose(1, 2, 0, 3)
         .reshape(step_total, prompts_here, heads_here, key_width)
@@ -215,14 +239,6 @@
         .transpose(1, 2, 3, 0, 4)
         .reshape(step_total, prompts_here, heads_here, value_width)
     )
-    steps = jnp.arange(step_total)
-    dec_positions = (local_lengths[None, :] + steps[:, None]).astype(jnp.float32)
-    query_rot = rotate(query_own.astype(jnp.float32), dec_positions[:, :, None]).astype(
-        jnp.bfloat16
-    )
-    key_rot = (
-        rotate(key_own.astype(jnp.float32), dec_positions[:, :, None]) * key_width ** (-0.5)
-    ).astype(jnp.bfloat16)
     from_state = jnp.einsum(
         "tbhk,bhkv->tbhv", query_rot, state_new, preferred_element_type=jnp.float32
     )

time: 130 us -> 107 us (0.82); the launches traced: 128 us -> 106 us
  blocking collectives: 0 us -> 32.6 us
  local copies, waits for them, and re-layouts: 40.8 us -> 14.2 us
  waiting for transfers between devices: 19.4 us -> 0.01 us
  starting transfers between devices: 19.3 us -> 11.8 us
  other arithmetic: 14.2 us -> 7.59 us
  Pallas kernels: 16 us -> 21.5 us
    all_to_all x0 -> x1, blocking collectives: none -> 32.6 us  [per_device(): lax.all_to_all(pieces.transpose(2, 0, 1, 3), ('heads', 'tp'), 0, 0, tiled...]
    all_to_all x1 -> x0, waiting for transfers between devices: 19.4 us -> none  [per_device(): lax.all_to_all(pieces.transpose(2, 0, 1, 3), ('heads', 'tp'), 0, 0, tiled...]
    reshape x5 -> x0, local copies, waits for them, and re-layouts: 11.6 us -> none  [the longest x1 4.19 us: prefill(): value_span.reshape(prompts_here, span_len, heads_here * value_width)]
    mul x8 -> x0, local copies, waits for them, and re-layouts: 8.34 us -> none  [the longest x2 2.31 us: rotate(): odd_part * cosine + even_part * sine_part]
    all_to_all x1 -> x0, starting transfers between devices: 7.51 us -> none  [per_device(): lax.all_to_all(pieces.transpose(2, 0, 1, 3), ('heads', 'tp'), 0, 0, tiled...]
    mul x1 -> x0, other arithmetic: 7.16 us -> none  [rotate(): odd_part * sine_part]
    pallas_call x1, Pallas kernels: 16 us -> 21.5 us  [prefill(): pl.pallas_call(prefill_kernel, grid=grid, in_specs=[pl.BlockSpec((None, s...]
    unnamed x13 -> x12, local copies, waits for them, and re-layouts: 6.51 us -> 1.76 us
  transfers between devices with their start and end apart: 3 -> 2, of which waited for: 1 -> 0; matrix products, arithmetic and copies ran while one was open for 21% -> 13% of each run, Pallas kernels for 13% -> 20%
where the time goes in v4:
time: 107 us; the launch traced here: 106 us
  blocking collectives  32.6 us (30%)
  Pallas kernels  21.5 us (20%)
  matrix products  17.3 us (16%)
  local copies, waits for them, and re-layouts  14.2 us (13%)
  starting transfers between devices  11.8 us (11%)
  other arithmetic  7.59 us (7%)
    all_to_all x1, blocking collectives, per_device(): lax.all_to_all(pieces.transpose(2, 0, 1, 3), ('heads', 'tp'), 0, 0, tiled...  32.6 us
    pallas_call x1, Pallas kernels, prefill(): pl.pallas_call(prefill_kernel, grid=grid, in_specs=[pl.BlockSpec((None, s...  21.5 us
    dot_general x2, local copies, waits for them, and re-layouts, per_device(): jnp.dot(activated, w_out.reshape(heads_here * value_slice, model_width),...  6.61 us
    all_to_all x1, starting transfers between devices, per_device(): arrived = lax.all_to_all(packed, 'heads', 0, 0, tiled=True)  6.38 us
    all_to_all x1, starting transfers between devices, per_device(): normed = lax.all_to_all(normed, 'heads', 0, 0, tiled=True)  5.45 us
    dot_general x1, matrix products, per_device(): jnp.dot(flat_inputs, w_gate.reshape(model_width, heads_here * value_slice...  4.33 us
    dot_general x1, matrix products, per_device(): jnp.dot(activated, w_out.reshape(heads_here * value_slice, model_width),...  3.56 us
    dot_general x1, matrix products, per_device(): jnp.einsum('tbhk,bhkv->tbhv', query_rot, state_new, preferred_element_typ...  2.83 us
  transfers between devices with their start and end apart: 2, of which 0 were waited for; matrix products, arithmetic and copies ran while one was open for 13% of the time, Pallas kernels for 20%

profile of v4, /device:TPU:1, one launch (start us, length us, event | category | flops | bytes accessed | tf_op | source)
XLA Modules:
  0.0 106.0 jit_solution(9693900330811160939)
XLA Ops:
  0.7 0.8 add_convert_fusion
  1.6 0.6 copy-done
  2.2 1.8 %fusion.13 = bf16[64,256]{1,0:T(8,128)(2,1)S(1)} fusion(bf16[64,4096]{1,0:T(8,128)(2,1)} %bitcast.97, bf16[4096,1,1,256]{3,0,2,1:T(8,128)(2,1)S(1)} %copy-done), kind=kOutput, calls=%fused_computation.19 | convolution fusion | flops 134234112 | bytes 2654208 | tf_op jit(solution)/shard_map/dot_general | solution.py:186
  4.0 2.2 %fusion.16 = bf16[64,256]{1,0:T(8,128)(2,1)S(1)} fusion(bf16[64,4096]{1,0:T(8,128)(2,1)} %bitcast.98, bf16[4096,1,1,256]{3,0,2,1:T(8,128)(2,1)} %param.20), kind=kOutput, calls=%fused_computation.20 | convolution fusion | flops 134234112 | bytes 2654208 | tf_op jit(solution)/shard_map/dot_general | solution.py:189
  7.0 1.4 %convolution_convert_fusion = bf16[64,512]{1,0:T(8,128)(2,1)S(1)} fusion(bf16[64,4096]{1,0:T(8,128)(2,1)S(1)} %bitcast.99, bf16[4096,512]{0,1:T(8,128)(2,1)S(1)} %bitcast.100), kind=kOutput, calls=%fused_computation.11 | convolution fusion | flops 268468224 | bytes 4784128 | tf_op jit(solution)/shard_map/dot_general | solution.py:192
  8.4 0.8 copy.65
  9.2 6.4 %all-to-all-start = ((bf16[8,4,2,1024]{3,1,2,0:T(4,128)(2,1)}), bf16[8,4,2,1024]{3,1,2,0:T(4,128)(2,1)S(1)}, u32[]{:S(2)}, u32[]{:S(2)}) async-start(bf16[8,4,2,1024]{3,1,2,0:T(4,128)(2,1)} %bitcast.94), calls=%async_computation | async-start | bytes 262144 | tf_op jit(solution)/shard_map/all_to_all | solution.py:225
  15.9 0.5 fusion.31
  16.9 0.7 fusion.24.swap_ref
  18.1 1.1 %broadcast_select_fusion.table_ref = f32[2,8,128,128]{3,2,1,0:T(8,128)} fusion(f32[8,128,128]{2,1,0:T(8,128)S(1)} %exponential_select_fusion, pred[2,128]{1,0:T(4,128)(4,1)S(1)} %get-tuple-element.18), kind=kLoop, calls=%fused_computation.23 | loop fusion | flops 262144 | bytes 1573120 | tf_op jit(solution)/shard_map/jit(_where)/select_n | solution.py:94
  19.5 1.3 %copy.40.rows_ref = f32[2,8,128,8]{3,2,1,0:T(8,128)} copy(f32[2,8,128,8]{2,3,1,0:T(8,128)S(1)} %stack.14) | data formatting | bytes 131072 | tf_op jit(solution)/shard_map/stack | solution.py:104
  21.0 0.8 copy.39.sin_ref
  22.0 0.8 copy.38.cos_ref
  22.8 21.5 %shard_map.131 = (bf16[2,128,8,512]{3,2,1,0:T(8,128)(2,1)}, bf16[2,8,256,512]{3,2,1,0:T(8,128)(2,1)}) custom-call(bf16[2,128,8,256]{3,2,1,0:T(8,128)(2,1)} %q_ref.1, bf16[2,128,8,256]{3,2,1,0:T(8,128)(2,1)} %k_ref.1, bf16[2,128,8,512]{3,2,1,0:T(8,128)(2,1)} %v_ref.1, bf16[2,8,256,512]{3,2,1,0:T(8,128)(2,1)} %prior_ref.1, f32[2,128,256]{2,1,0:T(8,128)} %copy.38.cos_ref, ...), custom_call_target="tpu_custom_call" | custom-call | tf_op jit(solution)/shard_map/pallas_call | solution.py:115
  44.9 2.8 %fusion.7 = f32[4,2,8,512]{3,0,2,1:T(4,128)S(1)} fusion(bf16[2,8,256,512]{3,2,1,0:T(8,128)(2,1)} %get-tuple-element.5, f32[4,8]{0,1:T(8,128)S(1)} %multiply_exponential_fusion, bf16[8,4,2,256]{3,1,2,0:T(4,128)(2,1)S(1)} %get-tuple-element.12), kind=kOutput, calls=%fused_computation.10 | convolution fusion | flops 16809984 | bytes 4358272 | tf_op jit(solution)/shard_map/tbhk,bhkv->tbhv/dot_general | solution.py:242
  48.7 0.9 reshape.378
  49.6 5.4 %all-to-all-start.1 = ((f32[8,1,4096]{2,1,0:T(1,128)}), f32[8,1,4096]{2,1,0:T(1,128)S(1)}, u32[]{:S(2)}, u32[]{:S(2)}) async-start(f32[8,1,4096]{2,1,0:T(1,128)} %reshape.378), calls=%async_computation.1 | async-start | bytes 262144 | tf_op jit(solution)/shard_map/all_to_all | solution.py:267
  55.0 6.5 %copy.48 = bf16[4096,512]{1,0:T(8,128)(2,1)} copy(bf16[4096,512]{0,1:T(8,128)(2,1)} %bitcast.101) | data formatting | bytes 8388608 | tf_op jit(solution)/shard_map/dot_general | solution.py:277
  61.5 0.5 broadcast.459
  62.0 1.0 reduce
  63.3 4.3 %multiply_convert_fusion = bf16[4,16,8,64]{3,1,2,0:T(8,128)(2,1)S(1)} fusion(f32[4,16,8,64]{3,1,2,0:T(8,128)S(1)} %bitcast.107, bf16[4096,1,8,1,64]{0,4,3,2,1:T(8,128)(2,1)} %param.22, bf16[4,16,4096]{2,1,0:T(8,128)(2,1)S(1)} %copy-done.1), kind=kOutput, calls=%fused_computation.27 | convolution fusion | flops 268632064 | bytes 4915200 | tf_op jit(solution)/shard_map/dot_general | solution.py:197
  67.8 3.6 %convolution_bitcast_fusion = f32[16,4,16,256]{3,2,0,1:T(8,128)S(1)} fusion(bf16[16,256,512,1]{2,1,0,3:T(8,128)(2,1)} %bitcast.102, bf16[4,16,512,1]{2,1,0,3:T(8,128)(2,1)S(1)} %reshape.375), kind=kOutput, calls=%fused_computation.6 | convolution fusion | flops 268435456 | bytes 5308416 | tf_op jit(solution)/shard_map/dot_general | solution.py:277
  71.5 32.6 %all_to_all.15 = f32[16,4,16,256]{3,2,1,0:T(8,128)} all-to-all(f32[16,4,16,256]{3,2,1,0:T(8,128)S(1)} %copy.49), channel_id=1, replica_groups=mesh['groups'=2,'heads'=8,'tp'=2] {'heads','tp'}, dimensions={0} | all-to-all | bytes 2097152 | tf_op jit(solution)/shard_map/all_to_all | solution.py:286
  104.1 1.9 %reduce_sum.29 = bf16[4,16,256]{2,1,0:T(8,128)(2,1)} reduce(f32[16,4,16,256]{3,2,1,0:T(8,128)} %all_to_all.15, f32[]{:T(128)} %constant.94.clone.1), dimensions={0}, to_apply=%region_2.3 | reduce | flops 245760 | bytes 1081348 | tf_op jit(solution)/shard_map/reduce_sum | solution.py:287
  (63 shorter events, 4.7 us)
Async XLA Ops:
  0.6 1.6 %copy-start = (bf16[4096,1,1,256]{3,0,2,1:T(8,128)(2,1)S(1)}, bf16[4096,1,1,256]{3,0,2,1:T(8,128)(2,1)}, u32[]{:S(2)}) copy-start(bf16[4096,1,1,256]{3,0,2,1:T(8,128)(2,1)} %param.19) | copy-start | bytes 6291460
  0.6 6.3 %copy-start.1 = (bf16[4,16,4096]{2,1,0:T(8,128)(2,1)S(1)}, bf16[4,16,4096]{2,1,0:T(8,128)(2,1)}, u32[]{:S(2)}) copy-start(bf16[4,16,4096]{2,1,0:T(8,128)(2,1)} %param.18) | copy-start | bytes 1572868
  1.6 5.4 %copy-start.2 = (bf16[4096,1,8,1,64]{0,4,3,2,1:T(8,128)(2,1)S(1)}, bf16[4096,1,8,1,64]{0,4,3,2,1:T(8,128)(2,1)}, u32[]{:S(2)}) copy-start(bf16[4096,1,8,1,64]{0,4,3,2,1:T(8,128)(2,1)} %param.21) | copy-start | bytes 12582916
  4.0 11.6 %copy-start.3 = (s32[16]{0:T(128)S(1)}, s32[16]{0:T(128)}, u32[]{:S(2)}) copy-start(s32[16]{0:T(128)} %param.17) | copy-start | bytes 196
  4.0 13.6 %copy-start.4 = (f32[16]{0:T(128)S(1)}, f32[16]{0:T(128)}, u32[]{:S(2)}) copy-start(f32[16]{0:T(128)} %param.16) | copy-start | bytes 196
  9.2 35.2 %all-to-all-start = ((bf16[8,4,2,1024]{3,1,2,0:T(4,128)(2,1)}), bf16[8,4,2,1024]{3,1,2,0:T(4,128)(2,1)S(1)}, u32[]{:S(2)}, u32[]{:S(2)}) async-start(bf16[8,4,2,1024]{3,1,2,0:T(4,128)(2,1)} %bitcast.94), calls=%async_computation | async-start | bytes 262144 | tf_op jit(solution)/shard_map/all_to_all | solution.py:225
  49.6 11.9 %all-to-all-start.1 = ((f32[8,1,4096]{2,1,0:T(1,128)}), f32[8,1,4096]{2,1,0:T(1,128)S(1)}, u32[]{:S(2)}, u32[]{:S(2)}) async-start(f32[8,1,4096]{2,1,0:T(1,128)} %reshape.378), calls=%async_computation.1 | async-start | bytes 262144 | tf_op jit(solution)/shard_map/all_to_all | solution.py:267

commit v5 on v4

--- a/solution.py
+++ b/solution.py
@@ -27,9 +27,34 @@
     return (output - mean_value) * lax.rsqrt(mean_square - mean_value * mean_value + EPSILON)
 
 
-def prefill_kernel(
-    q_ref, k_ref, v_ref, prior_ref, cos_ref, sin_ref, swap_ref, table_ref, rows_ref,
-    out_ref, state_ref,
+def turn_lanes(raw, swap, cosine, sine_part):
+    partner = jnp.dot(raw, swap, preferred_element_type=jnp.float32)
+    return raw.astype(jnp.float32) * cosine + partner * sine_part
+
+
+def state_kernel(k_ref, v_ref, prior_ref, cos_ref, sin_ref, swap_ref, rows_ref, state_ref):
+    swap = swap_ref[...]
+    cosine = cos_ref[...]
+    sine_part = sin_ref[...]
+    for head in range(k_ref.shape[1]):
+        k_raw = k_ref[:, head, :]
+        keys = (turn_lanes(k_raw, swap, cosine, sine_part) * (k_raw.shape[-1] ** (-0.5))).astype(
+            jnp.bfloat16
+        )
+        rows = rows_ref[head]
+        weighted = (keys.astype(jnp.float32) * rows[:, 2:3]).astype(jnp.bfloat16)
+        update = lax.dot_general(
+            weighted, v_ref[:, head, :], (((0,), (0,)), ((), ())),
+            preferred_element_type=jnp.float32,
+        )
+        kept = rows[0:1, 3:4]
+        state_ref[head] = (kept * prior_ref[head].astype(jnp.float32) + update).astype(
+            state_ref.dtype
+        )
+
+
+def output_kernel(
+    q_ref, k_ref, v_ref, prior_ref, cos_ref, sin_ref, swap_ref, table_ref, rows_ref, out_ref
 ):
     swap = swap_ref[...]
     cosine = cos_ref[...]
@@ -37,43 +62,25 @@
     for head in range(q_ref.shape[1]):
         q_raw = q_ref[:, head, :]
         k_raw = k_ref[:, head, :]
-        q_partner = jnp.dot(q_raw, swap, preferred_element_type=jnp.float32)
-        k_partner = jnp.dot(k_raw, swap, preferred_element_type=jnp.float32)
-        queries = (q_raw.astype(jnp.float32) * cosine + q_partner * sine_part).astype(
+        queries = turn_lanes(q_raw, swap, cosine, sine_part).astype(jnp.bfloat16)
+        keys = (turn_lanes(k_raw, swap, cosine, sine_part) * (k_raw.shape[-1] ** (-0.5))).astype(
             jnp.bfloat16
         )
-        keys_wide = (k_raw.astype(jnp.float32) * cosine + k_partner * sine_part) * (
-            q_raw.shape[-1] ** (-0.5)
-        )
-        keys = keys_wide.astype(jnp.bfloat16)
-        values = v_ref[:, head, :]
-        prior = prior_ref[head]
         rows = rows_ref[head]
-        lead = rows[:, 0:1]
-        valid = rows[:, 1:2]
-        key_weight = rows[:, 2:3]
-        kept = rows[0:1, 3:4]
         scores = lax.dot_general(
             queries, keys, (((1,), (1,)), ((), ())), preferred_element_type=jnp.float32
         )
         weights = (scores * table_ref[head]).astype(jnp.bfloat16)
-        inner = jnp.dot(weights, values, preferred_element_type=jnp.float32)
-        carried = jnp.dot(queries, prior, preferred_element_type=jnp.float32)
-        mixed = inner + lead * carried
+        inner = jnp.dot(weights, v_ref[:, head, :], preferred_element_type=jnp.float32)
+        carried = jnp.dot(queries, prior_ref[head], preferred_element_type=jnp.float32)
+        mixed = inner + rows[:, 0:1] * carried
         mean_value = jnp.mean(mixed, -1, keepdims=True)
         mean_square = jnp.mean(mixed * mixed, -1, keepdims=True)
         normed = norm_with(mixed, mean_value, mean_square)
-        out_ref[:, head, :] = jnp.where(valid > 0.5, normed, 0.0).astype(out_ref.dtype)
-        weighted = (keys.astype(jnp.float32) * key_weight).astype(jnp.bfloat16)
-        update = lax.dot_general(
-            weighted, values, (((0,), (0,)), ((), ())), preferred_element_type=jnp.float32
-        )
-        state_ref[head] = (kept * prior.astype(jnp.float32) + update).astype(state_ref.dtype)
-
-
-def prefill(query_span, key_span, value_span, prior_state, local_rates, span_start, live_count):
-    prompts_here, span_len, heads_here, key_width = query_span.shape
-    value_width = value_span.shape[3]
+        out_ref[:, head, :] = jnp.where(rows[:, 1:2] > 0.5, normed, 0.0).astype(out_ref.dtype)
+
+
+def prefill_tables(key_width, span_len, local_rates, span_start, live_count):
     halfway = key_width // 2
     offsets = jnp.arange(span_len)
     positions = (span_start[:, None] + offsets[None, :]).astype(jnp.float32)
@@ -85,13 +92,6 @@
     lane = jnp.arange(key_width)
     swap = (lane[:, None] == (lane[None, :] ^ 1)).astype(jnp.bfloat16)
     valid_rows = offsets[None, :] < live_count[:, None]
-    distance = (offsets[:, None] - offsets[None, :]).astype(jnp.float32)
-    decay_table = jnp.where(
-        distance[None] >= 0,
-        jnp.exp(-local_rates[:, None, None] * jnp.maximum(distance, 0.0)[None]),
-        0.0,
-    )
-    table = jnp.where(valid_rows[:, None, None, :], decay_table[None], 0.0)
     lead_decay = jnp.exp(-local_rates[:, None] * (offsets[None, :] + 1).astype(jnp.float32))
     remaining = (live_count[:, None] - 1 - offsets[None, :]).astype(jnp.float32)
     key_weight = jnp.where(
@@ -100,7 +100,7 @@
         0.0,
     )
     kept_share = jnp.exp(-local_rates[None, :] * live_count[:, None].astype(jnp.float32))
-    shape_rows = (prompts_here, heads_here, span_len)
+    shape_rows = key_weight.shape
     rows = jnp.stack(
         [
             jnp.broadcast_to(lead_decay[None], shape_rows),
@@ -111,10 +111,47 @@
         + [jnp.zeros(shape_rows, jnp.float32)] * 4,
         -1,
     )
-    grid = (prompts_here,)
-    out, state = pl.pallas_call(
-        prefill_kernel,
-        grid=grid,
+    return cosine, sine_part, swap, rows, valid_rows
+
+
+def new_state(key_span, value_span, prior_state, tables):
+    prompts_here, span_len, heads_here, key_width = key_span.shape
+    cosine, sine_part, swap, rows, _ = tables
+    column_block = 128
+    return pl.pallas_call(
+        state_kernel,
+        grid=(prompts_here, value_span.shape[3] // column_block),
+        in_specs=[
+            pl.BlockSpec((None, span_len, heads_here, key_width), lambda b, c: (b, 0, 0, 0)),
+            pl.BlockSpec((None, span_len, heads_here, column_block), lambda b, c: (b, 0, 0, c)),
+            pl.BlockSpec((None, heads_here, key_width, column_block), lambda b, c: (b, 0, 0, c)),
+            pl.BlockSpec((None, span_len, key_width), lambda b, c: (b, 0, 0)),
+            pl.BlockSpec((None, span_len, key_width), lambda b, c: (b, 0, 0)),
+            pl.BlockSpec((key_width, key_width), lambda b, c: (0, 0)),
+            pl.BlockSpec((None, heads_here, span_len, 8), lambda b, c: (b, 0, 0, 0)),
+        ],
+        out_specs=pl.BlockSpec(
+            (None, heads_here, key_width, column_block), lambda b, c: (b, 0, 0, c)
+        ),
+        out_shape=jax.ShapeDtypeStruct(prior_state.shape, jnp.bfloat16),
+    )(key_span, value_span, prior_state, cosine, sine_part, swap, rows)
+
+
+def prefill_output(query_span, key_span, value_span, prior_state, local_rates, tables):
+    prompts_here, span_len, heads_here, key_width = query_span.shape
+    value_width = value_span.shape[3]
+    cosine, sine_part, swap, rows, valid_rows = tables
+    offsets = jnp.arange(span_len)
+    distance = (offsets[:, None] - offsets[None, :]).astype(jnp.float32)
+    decay_table = jnp.where(
+        distance[None] >= 0,
+        jnp.exp(-local_rates[:, None, None] * jnp.maximum(distance, 0.0)[None]),
+        0.0,
+    )
+    table = jnp.where(valid_rows[:, None, None, :], decay_table[None], 0.0)
+    return pl.pallas_call(
+        output_kernel,
+        grid=(prompts_here,),
         in_specs=[
             pl.BlockSpec((None, span_len, heads_here, key_width), lambda b: (b, 0, 0, 0)),
             pl.BlockSpec((None, span_len, heads_here, key_width), lambda b: (b, 0, 0, 0)),
@@ -126,26 +163,11 @@
             pl.BlockSpec((None, heads_here, span_len, span_len), lambda b: (b, 0, 0, 0)),
             pl.BlockSpec((None, heads_here, span_len, 8), lambda b: (b, 0, 0, 0)),
         ],
-        out_specs=[
-            pl.BlockSpec((None, span_len, heads_here, value_width), lambda b: (b, 0, 0, 0)),
-            pl.BlockSpec((None, heads_here, key_width, value_width), lambda b: (b, 0, 0, 0)),
-        ],
-        out_shape=[
-            jax.ShapeDtypeStruct(value_span.shape, jnp.bfloat16),
-            jax.ShapeDtypeStruct(prior_state.shape, jnp.bfloat16),
-        ],
-    )(
-        query_span,
-        key_span,
-        value_span,
-        prior_state,
-        cosine,
-        sine_part,
-        swap,
-        table,
-        rows,
-    )
-    return out, state
+        out_specs=pl.BlockSpec(
+            (None, span_len, heads_here, value_width), lambda b: (b, 0, 0, 0)
+        ),
+        out_shape=jax.ShapeDtypeStruct(value_span.shape, jnp.bfloat16),
+    )(query_span, key_span, value_span, prior_state, cosine, sine_part, swap, table, rows)
 
 
 def per_device(
@@ -178,9 +200,8 @@
     )
     span_start = span_len * ((local_lengths - 1) // span_len)
     live_count = local_lengths - span_start
-    prefill_out, state_new = prefill(
-        query_span, key_span, value_span, prior_state, local_rates, span_start, live_count
-    )
+    tables = prefill_tables(key_width, span_len, local_rates, span_start, live_count)
+    state_new = new_state(key_span, value_span, prior_state, tables)
     slots = head_slots
     flat_inputs = decode_inputs.reshape(step_total * total_prompts, model_width)
     query_part = jnp.dot(
@@ -280,6 +301,12 @@
         preferred_element_type=jnp.float32,
     )
     partial_out = partial_out.reshape(step_total, total_prompts, model_width)
+    query_span, key_span, value_span, prior_state, _ = lax.optimization_barrier(
+        (query_span, key_span, value_span, prior_state, partial_out)
+    )
+    prefill_out = prefill_output(
+        query_span, key_span, value_span, prior_state, local_rates, tables
+    )
     out_slots = head_slots * lax.axis_size("tp")
     column_block = model_width // out_slots
     pieces = partial_out.reshape(step_total, total_prompts, out_slots, column_block)

time: 107 us -> 106 us (level)
  blocking collectives: 32.6 us -> 0 us
  Pallas kernels: 21.5 us -> 39.9 us
  starting transfers between devices: 11.8 us -> 19.3 us
  waiting for transfers between devices: 0.01 us -> 3.64 us
    all_to_all x1 -> x0, blocking collectives: 32.6 us -> none  [per_device(): lax.all_to_all(pieces.transpose(2, 0, 1, 3), ('heads', 'tp'), 0, 0, tiled...]
    pallas_call x1 -> x2, Pallas kernels: 21.5 us -> 39.9 us  [the longest x1 21.6 us: new_state(): pl.pallas_call(state_kernel, grid=(prompts_here, value_span.shape[3] // c...]
    all_to_all x0 -> x1, starting transfers between devices: none -> 7.52 us  [per_device(): lax.all_to_all(pieces.transpose(2, 0, 1, 3), ('heads', 'tp'), 0, 0, tiled...]
    all_to_all x0 -> x1, waiting for transfers between devices: none -> 3.64 us  [per_device(): lax.all_to_all(pieces.transpose(2, 0, 1, 3), ('heads', 'tp'), 0, 0, tiled...]
  transfers between devices with their start and end apart: 2 -> 3, of which waited for: 0 -> 1; matrix products, arithmetic and copies ran while one was open for 13% -> 13% of each run, Pallas kernels for 20% -> 38%
where the time goes in v5:
time: 106 us; the launch traced here: 104 us
  Pallas kernels  39.9 us (38%)
  starting transfers between devices  19.3 us (18%)
  matrix products  17.3 us (16%)
  local copies, waits for them, and re-layouts  15.2 us (14%)
  other arithmetic  7.65 us (7%)
  waiting for transfers between devices  3.64 us (3%)
    pallas_call x1, Pallas kernels, new_state(): pl.pallas_call(state_kernel, grid=(prompts_here, value_span.shape[3] // c...  21.6 us
    pallas_call x1, Pallas kernels, prefill_output(): pl.pallas_call(output_kernel, grid=(prompts_here,), in_specs=[pl.BlockSpe...  18.3 us
    all_to_all x1, starting transfers between devices, per_device(): lax.all_to_all(pieces.transpose(2, 0, 1, 3), ('heads', 'tp'), 0, 0, tiled...  7.52 us
    dot_general x2, local copies, waits for them, and re-layouts, per_device(): jnp.dot(activated, w_out.reshape(heads_here * value_slice, model_width),...  6.61 us
    all_to_all x1, starting transfers between devices, per_device(): arrived = lax.all_to_all(packed, 'heads', 0, 0, tiled=True)  6.38 us
    all_to_all x1, starting transfers between devices, per_device(): normed = lax.all_to_all(normed, 'heads', 0, 0, tiled=True)  5.43 us
    dot_general x1, matrix products, per_device(): jnp.dot(flat_inputs, w_gate.reshape(model_width, heads_here * value_slice...  4.33 us
    all_to_all x1, waiting for transfers between devices, per_device(): lax.all_to_all(pieces.transpose(2, 0, 1, 3), ('heads', 'tp'), 0, 0, tiled...  3.64 us
  transfers between devices with their start and end apart: 3, of which 1 were waited for; matrix products, arithmetic and copies ran while one was open for 13% of the time, Pallas kernels for 38%

profile of v5, /device:TPU:1, one launch (start us, length us, event | category | flops | bytes accessed | tf_op | source)
XLA Modules:
  0.0 103.9 jit_solution(5414814839189105910)
XLA Ops:
  0.7 0.8 add_convert_fusion
  2.2 1.8 %fusion.13 = bf16[64,256]{1,0:T(8,128)(2,1)S(1)} fusion(bf16[64,4096]{1,0:T(8,128)(2,1)} %bitcast.97, bf16[4096,1,1,256]{3,0,2,1:T(8,128)(2,1)S(1)} %copy-done), kind=kOutput, calls=%fused_computation.19 | convolution fusion | flops 134234112 | bytes 2654208 | tf_op jit(solution)/shard_map/dot_general | solution.py:207
  4.0 2.2 %fusion.16 = bf16[64,256]{1,0:T(8,128)(2,1)S(1)} fusion(bf16[64,4096]{1,0:T(8,128)(2,1)} %bitcast.98, bf16[4096,1,1,256]{3,0,2,1:T(8,128)(2,1)} %param.20), kind=kOutput, calls=%fused_computation.20 | convolution fusion | flops 134234112 | bytes 2654208 | tf_op jit(solution)/shard_map/dot_general | solution.py:210
  7.0 1.4 %convolution_convert_fusion = bf16[64,512]{1,0:T(8,128)(2,1)S(1)} fusion(bf16[64,4096]{1,0:T(8,128)(2,1)S(1)} %bitcast.99, bf16[4096,512]{0,1:T(8,128)(2,1)S(1)} %bitcast.100), kind=kOutput, calls=%fused_computation.11 | convolution fusion | flops 268468224 | bytes 4784128 | tf_op jit(solution)/shard_map/dot_general | solution.py:213
  8.4 0.8 copy.73
  9.2 6.4 %all-to-all-start = ((bf16[8,4,2,1024]{3,1,2,0:T(4,128)(2,1)}), bf16[8,4,2,1024]{3,1,2,0:T(4,128)(2,1)S(1)}, u32[]{:S(2)}, u32[]{:S(2)}) async-start(bf16[8,4,2,1024]{3,1,2,0:T(4,128)(2,1)} %bitcast.94), calls=%async_computation | async-start | bytes 262144 | tf_op jit(solution)/shard_map/all_to_all | solution.py:246
  16.8 0.7 fusion.24.swap_ref
  18.3 1.3 %copy.45.rows_ref = f32[2,8,128,8]{3,2,1,0:T(8,128)} copy(f32[2,8,128,8]{2,3,1,0:T(8,128)S(1)} %stack.14) | data formatting | bytes 131072 | tf_op jit(solution)/shard_map/stack | solution.py:104
  19.7 0.8 copy.44.sin_ref
  20.7 0.8 copy.43.cos_ref
  21.5 21.6 %shard_map.132 = bf16[2,8,256,512]{3,2,1,0:T(8,128)(2,1)} custom-call(bf16[2,128,8,256]{3,2,1,0:T(8,128)(2,1)} %k_ref.2, bf16[2,128,8,512]{3,2,1,0:T(8,128)(2,1)} %v_ref.2, bf16[2,8,256,512]{3,2,1,0:T(8,128)(2,1)} %prior_ref.2, f32[2,128,256]{2,1,0:T(8,128)} %copy.43.cos_ref, f32[2,128,256]{2,1,0:T(8,128)} %copy.44.sin_ref, ...), custom_call_target="tpu_custom_call" | custom-call | tf_op jit(solution)/shard_map/pallas_call | solution.py:121
  43.6 2.8 %fusion.7 = f32[4,2,8,512]{3,0,2,1:T(4,128)S(1)} fusion(bf16[2,8,256,512]{3,2,1,0:T(8,128)(2,1)} %shard_map.132, f32[4,8]{0,1:T(8,128)S(1)} %multiply_exponential_fusion, bf16[8,4,2,256]{3,1,2,0:T(4,128)(2,1)S(1)} %get-tuple-element.16), kind=kOutput, calls=%fused_computation.10 | convolution fusion | flops 16809984 | bytes 4358272 | tf_op jit(solution)/shard_map/tbhk,bhkv->tbhv/dot_general | solution.py:263
  47.4 0.9 reshape.379
  48.4 5.4 %all-to-all-start.1 = ((f32[8,1,4096]{2,1,0:T(1,128)}), f32[8,1,4096]{2,1,0:T(1,128)S(1)}, u32[]{:S(2)}, u32[]{:S(2)}) async-start(f32[8,1,4096]{2,1,0:T(1,128)} %reshape.379), calls=%async_computation.1 | async-start | bytes 262144 | tf_op jit(solution)/shard_map/all_to_all | solution.py:288
  53.8 6.5 %copy.56 = bf16[4096,512]{1,0:T(8,128)(2,1)} copy(bf16[4096,512]{0,1:T(8,128)(2,1)} %bitcast.101) | data formatting | bytes 8388608 | tf_op jit(solution)/shard_map/dot_general | solution.py:298
  60.8 1.0 reduce
  62.1 4.3 %multiply_convert_fusion = bf16[4,16,8,64]{3,1,2,0:T(8,128)(2,1)S(1)} fusion(f32[4,16,8,64]{3,1,2,0:T(8,128)S(1)} %bitcast.107, bf16[4096,1,8,1,64]{0,4,3,2,1:T(8,128)(2,1)} %param.22, bf16[4,16,4096]{2,1,0:T(8,128)(2,1)S(1)} %copy-done.1), kind=kOutput, calls=%fused_computation.27 | convolution fusion | flops 268632064 | bytes 4915200 | tf_op jit(solution)/shard_map/dot_general | solution.py:218
  66.6 3.6 %convolution_bitcast_fusion = f32[16,4,16,256]{3,2,0,1:T(8,128)S(1)} fusion(bf16[16,256,512,1]{2,1,0,3:T(8,128)(2,1)} %bitcast.102, bf16[4,16,512,1]{2,1,0,3:T(8,128)(2,1)S(1)} %reshape.376), kind=kOutput, calls=%fused_computation.6 | convolution fusion | flops 268435456 | bytes 5308416 | tf_op jit(solution)/shard_map/dot_general | solution.py:298
  70.1 1.1 %copy.57 = f32[16,4,16,256]{3,2,1,0:T(8,128)} copy(f32[16,4,16,256]{3,2,0,1:T(8,128)S(1)} %convolution_bitcast_fusion) | data formatting | bytes 2097152 | tf_op jit(solution)/shard_map/transpose | solution.py:313
  71.3 7.5 %all-to-all-start.2 = ((f32[16,4,16,256]{3,2,1,0:T(8,128)}), f32[16,4,16,256]{3,2,1,0:T(8,128)}, u32[]{:S(2)}, u32[]{:S(2)}) async-start(f32[16,4,16,256]{3,2,1,0:T(8,128)} %copy.57), calls=%async_computation.2 | async-start | bytes 2097152 | tf_op jit(solution)/shard_map/all_to_all | solution.py:313
  79.0 1.1 %broadcast_select_fusion.table_ref = f32[2,8,128,128]{3,2,1,0:T(8,128)} fusion(f32[8,128,128]{2,1,0:T(8,128)S(1)} %exponential_select_fusion, pred[2,128]{1,0:T(4,128)(4,1)S(1)} %get-tuple-element.22), kind=kLoop, calls=%fused_computation.23 | loop fusion | flops 262144 | bytes 1573120 | tf_op jit(solution)/shard_map/jit(_where)/select_n | solution.py:151
  80.1 18.3 %shard_map.131 = bf16[2,128,8,512]{3,2,1,0:T(8,128)(2,1)} custom-call(bf16[2,128,8,256]{3,2,1,0:T(8,128)(2,1)} %q_ref, bf16[2,128,8,256]{3,2,1,0:T(8,128)(2,1)} %k_ref.2, bf16[2,128,8,512]{3,2,1,0:T(8,128)(2,1)} %v_ref.2, bf16[2,8,256,512]{3,2,1,0:T(8,128)(2,1)} %prior_ref.2, f32[2,128,256]{2,1,0:T(8,128)} %copy.43.cos_ref, f32[2,128,256]{2,1,0:T(8,128)} %copy.44.sin_ref, ...), custom_call_target="tpu_custom_call" | custom-call | tf_op jit(solution)/shard_map/pallas_call | solution.py:152
  98.4 3.6 %all-to-all-done.2 = f32[16,4,16,256]{3,2,1,0:T(8,128)} async-done(((f32[16,4,16,256]{3,2,1,0:T(8,128)}), f32[16,4,16,256]{3,2,1,0:T(8,128)}, u32[]{:S(2)}, u32[]{:S(2)}) %all-to-all-start.2) | async-done | bytes 1048608 | tf_op jit(solution)/shard_map/all_to_all | solution.py:313
  102.0 1.9 %reduce_sum.29 = bf16[4,16,256]{2,1,0:T(8,128)(2,1)} reduce(f32[16,4,16,256]{3,2,1,0:T(8,128)} %all-to-all-done.2, f32[]{:T(128)} %constant.94.clone.1), dimensions={0}, to_apply=%region_2.3 | reduce | flops 245760 | bytes 1081348 | tf_op jit(solution)/shard_map/reduce_sum | solution.py:314
  (65 shorter events, 6.3 us)
Async XLA Ops:
  0.6 1.6 %copy-start = (bf16[4096,1,1,256]{3,0,2,1:T(8,128)(2,1)S(1)}, bf16[4096,1,1,256]{3,0,2,1:T(8,128)(2,1)}, u32[]{:S(2)}) copy-start(bf16[4096,1,1,256]{3,0,2,1:T(8,128)(2,1)} %param.19) | copy-start | bytes 6291460
  0.6 6.3 %copy-start.1 = (bf16[4,16,4096]{2,1,0:T(8,128)(2,1)S(1)}, bf16[4,16,4096]{2,1,0:T(8,128)(2,1)}, u32[]{:S(2)}) copy-start(bf16[4,16,4096]{2,1,0:T(8,128)(2,1)} %param.18) | copy-start | bytes 1572868
  1.6 5.4 %copy-start.2 = (bf16[4096,1,8,1,64]{0,4,3,2,1:T(8,128)(2,1)S(1)}, bf16[4096,1,8,1,64]{0,4,3,2,1:T(8,128)(2,1)}, u32[]{:S(2)}) copy-start(bf16[4096,1,8,1,64]{0,4,3,2,1:T(8,128)(2,1)} %param.21) | copy-start | bytes 12582916
  4.0 11.6 %copy-start.3 = (s32[16]{0:T(128)S(1)}, s32[16]{0:T(128)}, u32[]{:S(2)}) copy-start(s32[16]{0:T(128)} %param.17) | copy-start | bytes 196
  4.0 13.6 %copy-start.4 = (f32[16]{0:T(128)S(1)}, f32[16]{0:T(128)}, u32[]{:S(2)}) copy-start(f32[16]{0:T(128)} %param.16) | copy-start | bytes 196
  9.2 34.0 %all-to-all-start = ((bf16[8,4,2,1024]{3,1,2,0:T(4,128)(2,1)}), bf16[8,4,2,1024]{3,1,2,0:T(4,128)(2,1)S(1)}, u32[]{:S(2)}, u32[]{:S(2)}) async-start(bf16[8,4,2,1024]{3,1,2,0:T(4,128)(2,1)} %bitcast.94), calls=%async_computation | async-start | bytes 262144 | tf_op jit(solution)/shard_map/all_to_all | solution.py:246
  48.4 11.9 %all-to-all-start.1 = ((f32[8,1,4096]{2,1,0:T(1,128)}), f32[8,1,4096]{2,1,0:T(1,128)S(1)}, u32[]{:S(2)}, u32[]{:S(2)}) async-start(f32[8,1,4096]{2,1,0:T(1,128)} %reshape.379), calls=%async_computation.1 | async-start | bytes 262144 | tf_op jit(solution)/shard_map/all_to_all | solution.py:288
  71.3 30.8 %all-to-all-start.2 = ((f32[16,4,16,256]{3,2,1,0:T(8,128)}), f32[16,4,16,256]{3,2,1,0:T(8,128)}, u32[]{:S(2)}, u32[]{:S(2)}) async-start(f32[16,4,16,256]{3,2,1,0:T(8,128)} %copy.57), calls=%async_computation.2 | async-start | bytes 2097152 | tf_op jit(solution)/shard_map/all_to_all | solution.py:313

commit v6 on v5

--- a/solution.py
+++ b/solution.py
@@ -30,27 +30,6 @@
 def turn_lanes(raw, swap, cosine, sine_part):
     partner = jnp.dot(raw, swap, preferred_element_type=jnp.float32)
     return raw.astype(jnp.float32) * cosine + partner * sine_part
-
-
-def state_kernel(k_ref, v_ref, prior_ref, cos_ref, sin_ref, swap_ref, rows_ref, state_ref):
-    swap = swap_ref[...]
-    cosine = cos_ref[...]
-    sine_part = sin_ref[...]
-    for head in range(k_ref.shape[1]):
-        k_raw = k_ref[:, head, :]
-        keys = (turn_lanes(k_raw, swap, cosine, sine_part) * (k_raw.shape[-1] ** (-0.5))).astype(
-            jnp.bfloat16
-        )
-        rows = rows_ref[head]
-        weighted = (keys.astype(jnp.float32) * rows[:, 2:3]).astype(jnp.bfloat16)
-        update = lax.dot_general(
-            weighted, v_ref[:, head, :], (((0,), (0,)), ((), ())),
-            preferred_element_type=jnp.float32,
-        )
-        kept = rows[0:1, 3:4]
-        state_ref[head] = (kept * prior_ref[head].astype(jnp.float32) + update).astype(
-            state_ref.dtype
-        )
 
 
 def output_kernel(
@@ -112,29 +91,6 @@
         -1,
     )
     return cosine, sine_part, swap, rows, valid_rows
-
-
-def new_state(key_span, value_span, prior_state, tables):
-    prompts_here, span_len, heads_here, key_width = key_span.shape
-    cosine, sine_part, swap, rows, _ = tables
-    column_block = 128
-    return pl.pallas_call(
-        state_kernel,
-        grid=(prompts_here, value_span.shape[3] // column_block),
-        in_specs=[
-            pl.BlockSpec((None, span_len, heads_here, key_width), lambda b, c: (b, 0, 0, 0)),
-            pl.BlockSpec((None, span_len, heads_here, column_block), lambda b, c: (b, 0, 0, c)),
-            pl.BlockSpec((None, heads_here, key_width, column_block), lambda b, c: (b, 0, 0, c)),
-            pl.BlockSpec((None, span_len, key_width), lambda b, c: (b, 0, 0)),
-            pl.BlockSpec((None, span_len, key_width), lambda b, c: (b, 0, 0)),
-            pl.BlockSpec((key_width, key_width), lambda b, c: (0, 0)),
-            pl.BlockSpec((None, heads_here, span_len, 8), lambda b, c: (b, 0, 0, 0)),
-        ],
-        out_specs=pl.BlockSpec(
-            (None, heads_here, key_width, column_block), lambda b, c: (b, 0, 0, c)
-        ),
-        out_shape=jax.ShapeDtypeStruct(prior_state.shape, jnp.bfloat16),
-    )(key_span, value_span, prior_state, cosine, sine_part, swap, rows)
 
 
 def prefill_output(query_span, key_span, value_span, prior_state, local_rates, tables):
@@ -201,7 +157,24 @@
     span_start = span_len * ((local_lengths - 1) // span_len)
     live_count = local_lengths - span_start
     tables = prefill_tables(key_width, span_len, local_rates, span_start, live_count)
-    state_new = new_state(key_span, value_span, prior_state, tables)
+    offsets = jnp.arange(span_len)
+    positions = (span_start[:, None] + offsets[None, :]).astype(jnp.float32)
+    keys = (
+        rotate(key_span.astype(jnp.float32), positions[:, :, None]) * key_width ** (-0.5)
+    ).astype(jnp.bfloat16)
+    valid_rows = offsets[None, :] < live_count[:, None]
+    remaining = (live_count[:, None] - 1 - offsets[None, :]).astype(jnp.float32)
+    key_weight = jnp.where(
+        valid_rows[:, :, None],
+        jnp.exp(-local_rates[None, None, :] * jnp.maximum(remaining, 0.0)[:, :, None]),
+        0.0,
+    )
+    weighted = (keys.astype(jnp.float32) * key_weight[..., None]).astype(jnp.bfloat16)
+    update = jnp.einsum("bjhk,bjhv->bhkv", weighted, value_span, preferred_element_type=jnp.float32)
+    kept_share = jnp.exp(-local_rates[None, :] * live_count[:, None].astype(jnp.float32))
+    state_new = (kept_share[:, :, None, None] * prior_state.astype(jnp.float32) + update).astype(
+        jnp.bfloat16
+    )
     slots = head_slots
     flat_inputs = decode_inputs.reshape(step_total * total_prompts, model_width)
     query_part = jnp.dot(

time: 106 us -> 91.5 us (0.86); the launches traced: 104 us -> 90.7 us
  Pallas kernels: 39.9 us -> 18.3 us
  other arithmetic: 7.65 us -> 12.4 us
  local copies, waits for them, and re-layouts: 15.2 us -> 19.7 us
  waiting for transfers between devices: 3.64 us -> 0.01 us
  matrix products: 17.3 us -> 20 us
    pallas_call x1 -> x0, Pallas kernels: 21.6 us -> none  [new_state(): pl.pallas_call(state_kernel, grid=(prompts_here, value_span.shape[3] // c...]
    all_to_all x1, waiting for transfers between devices: 3.64 us -> 0.01 us  [per_device(): lax.all_to_all(pieces.transpose(2, 0, 1, 3), ('heads', 'tp'), 0, 0, tiled...]
    dot_general x1, matrix products: 2.83 us -> 5.85 us  [per_device(): jnp.einsum('tbhk,bhkv->tbhv', query_rot, state_new, preferred_element_typ...]
    unnamed x12 -> x13, local copies, waits for them, and re-layouts: 1.78 us -> 4.74 us
    reshape x0 -> x1, other arithmetic: none -> 2.72 us  [rotate(): paired = values.reshape(values.shape[:-1] + (halfway, 2))]
    sub x1 -> x2, other arithmetic: 0.01 us -> 1.77 us  [the longest x1 1.76 us: rotate(): even_part * cosine - odd_part * sine_part]
    convert_element_type x3 -> x5, other arithmetic: 0.86 us -> 2.2 us  [the longest x1 1.18 us: per_device(): (keys.astype(jnp.float32) * key_weight[..., None]).astype(jnp.bfloat16)]
    reduce_sum x1, other arithmetic: 1.92 us -> 0.68 us  [per_device(): decode_out = jnp.sum(pieces, 0).astype(jnp.bfloat16)]
  transfers between devices with their start and end apart: 3 -> 3, of which waited for: 1 -> 0; matrix products, arithmetic and copies ran while one was open for 13% -> 27% of each run, Pallas kernels for 38% -> 20%
where the time goes in v6:
time: 91.5 us; the launch traced here: 90.7 us
  matrix products  20 us (22%)
  local copies, waits for them, and re-layouts  19.7 us (22%)
  starting transfers between devices  19.3 us (21%)
  Pallas kernels  18.3 us (20%)
  other arithmetic  12.4 us (14%)
  between operations  0.97 us (1%)
    pallas_call x1, Pallas kernels, prefill_output(): pl.pallas_call(output_kernel, grid=(prompts_here,), in_specs=[pl.BlockSpe...  18.3 us
    all_to_all x1, starting transfers between devices, per_device(): lax.all_to_all(pieces.transpose(2, 0, 1, 3), ('heads', 'tp'), 0, 0, tiled...  7.52 us
    dot_general x2, local copies, waits for them, and re-layouts, per_device(): jnp.dot(activated, w_out.reshape(heads_here * value_slice, model_width),...  6.6 us
    all_to_all x1, starting transfers between devices, per_device(): arrived = lax.all_to_all(packed, 'heads', 0, 0, tiled=True)  6.38 us
    dot_general x1, matrix products, per_device(): jnp.einsum('tbhk,bhkv->tbhv', query_rot, state_new, preferred_element_typ...  5.85 us
    all_to_all x1, starting transfers between devices, per_device(): normed = lax.all_to_all(normed, 'heads', 0, 0, tiled=True)  5.44 us
    unnamed x13, local copies, waits for them, and re-layouts  4.74 us
    dot_general x1, matrix products, per_device(): jnp.dot(flat_inputs, w_gate.reshape(model_width, heads_here * value_slice...  4.33 us
  transfers between devices with their start and end apart: 3, of which 0 were waited for; matrix products, arithmetic and copies ran while one was open for 27% of the time, Pallas kernels for 20%

profile of v6, /device:TPU:1, one launch (start us, length us, event | category | flops | bytes accessed | tf_op | source)
XLA Modules:
  0.0 90.7 jit_solution(2746652314028877085)
XLA Ops:
  0.7 0.8 add_convert_fusion.6
  2.2 1.6 %fusion.26 = bf16[64,256]{1,0:T(8,128)(2,1)S(1)} fusion(bf16[64,4096]{1,0:T(8,128)(2,1)} %bitcast.100, bf16[4096,1,1,256]{3,0,2,1:T(8,128)(2,1)S(1)} %copy-done), kind=kOutput, calls=%fused_computation.28 | convolution fusion | flops 134234112 | bytes 2654208 | tf_op jit(solution)/shard_map/dot_general | solution.py:180
  3.9 2.1 %fusion.29 = bf16[64,256]{1,0:T(8,128)(2,1)S(1)} fusion(bf16[64,4096]{1,0:T(8,128)(2,1)S(1)} %bitcast.101, bf16[4096,1,1,256]{3,0,2,1:T(8,128)(2,1)} %param.20), kind=kOutput, calls=%fused_computation.29 | convolution fusion | flops 134234112 | bytes 2654208 | tf_op jit(solution)/shard_map/dot_general | solution.py:183
  6.6 1.4 %convolution_convert_fusion = bf16[64,512]{1,0:T(8,128)(2,1)S(1)} fusion(bf16[64,4096]{1,0:T(8,128)(2,1)S(1)} %bitcast.102, bf16[4096,512]{0,1:T(8,128)(2,1)S(1)} %bitcast.105), kind=kOutput, calls=%fused_computation.20 | convolution fusion | flops 268468224 | bytes 4784128 | tf_op jit(solution)/shard_map/dot_general | solution.py:186
  8.9 6.4 %all-to-all-start = ((bf16[8,4,2,1024]{3,1,2,0:T(4,128)(2,1)}), bf16[8,4,2,1024]{3,1,2,0:T(4,128)(2,1)S(1)}, u32[]{:S(2)}, u32[]{:S(2)}) async-start(bf16[8,4,2,1024]{3,1,2,0:T(4,128)(2,1)} %bitcast.97), calls=%async_computation | async-start | bytes 262144 | tf_op jit(solution)/shard_map/all_to_all | solution.py:219
  15.5 3.0 %copy.45 = bf16[2,128,8,256]{1,2,3,0:T(8,128)(2,1)} copy(bf16[2,128,8,256]{3,2,1,0:T(8,128)(2,1)} %k_ref) | data formatting | bytes 2097152 | tf_op args[1]
  18.5 2.7 %convert.2 = f32[2,128,8,128,2]{1,2,4,3,0:T(8,128)} convert(bf16[2,128,8,128,2]{1,2,4,3,0:T(8,128)(2,1)} %bitcast.104) | non-fusion elementwise | flops 524288 | bytes 3145728 | tf_op jit(solution)/shard_map/reshape | solution.py:17
  22.1 1.8 %multiply_subtract_fusion = (f32[2,128,8,128,1]{1,2,4,3,0:T(8,128)S(1)}, f32[2,128,8,128,1]{1,2,4,3,0:T(8,128)S(1)}) fusion(f32[2,128,8,128,2]{1,2,4,3,0:T(8,128)} %convert.2, f32[2,128,128]{1,2,0:T(8,128)S(1)} %get-tuple-element.21, f32[2,128,128]{1,2,0:T(8,128)S(1)} %get-tuple-element.22), kind=kLoop, calls=%fused_computation.33 | loop fusion | flops 1572864 | bytes 4456448 | tf_op jit(solution)/shard_map/sub | solution.py:21
  24.1 1.2 %fusion.7 = bf16[2,128,8,256]{1,2,3,0:T(8,128)(2,1)} fusion(bf16[2,128,8,256]{1,2,3,0:T(8,128)(2,1)S(1)} %bitcast.103, f32[2,128,8]{1,2,0:T(8,128)S(1)} %exponential_select_fusion.2), kind=kLoop, calls=%fused_computation.9 | loop fusion | flops 1572864 | bytes 2105344 | tf_op jit(solution)/shard_map/convert_element_type | solution.py:172
  25.9 5.8 %fusion.18 = f32[4,2,8,512]{3,0,2,1:T(4,128)S(1)} fusion(bf16[2,8,256,512]{3,2,1,0:T(8,128)(2,1)} %prior_ref, f32[2,8]{1,0:T(2,128)S(1)} %multiply_exponential_fusion.2, bf16[2,128,8,512]{3,2,1,0:T(8,128)(2,1)} %v_ref, bf16[2,128,8,256]{1,2,3,0:T(8,128)(2,1)} %fusion.7, f32[4,8]{0,1:T(8,128)S(1)} %multiply_exponential_fusion, ...), kind=kOutput, calls=%fused_computation.19 | convolution fusion | flops 562069504 | bytes 7504064 | tf_op jit(solution)/shard_map/tbhk,bhkv->tbhv/dot_general | solution.py:236
  32.6 0.9 %reshape.502 = f32[8,1,4096]{2,1,0:T(1,128)} reshape(f32[8,4,8,2,64]{4,3,2,1,0:T(2,128)S(1)} %bitcast.108) | data formatting | bytes 262144
  33.6 5.4 %all-to-all-start.1 = ((f32[8,1,4096]{2,1,0:T(1,128)}), f32[8,1,4096]{2,1,0:T(1,128)S(1)}, u32[]{:S(2)}, u32[]{:S(2)}) async-start(f32[8,1,4096]{2,1,0:T(1,128)} %reshape.502), calls=%async_computation.1 | async-start | bytes 262144 | tf_op jit(solution)/shard_map/all_to_all | solution.py:261
  39.0 6.5 %copy.55 = bf16[4096,512]{1,0:T(8,128)(2,1)} copy(bf16[4096,512]{0,1:T(8,128)(2,1)} %bitcast.106) | data formatting | bytes 8388608 | tf_op jit(solution)/shard_map/dot_general | solution.py:271
  46.0 1.0 %reduce = f32[8,4096]{1,0:T(8,128)S(1)} reduce(f32[8,1,4096]{2,1,0:T(1,128)S(1)} %all-to-all-done.1, f32[]{:T(128)} %broadcast.588), dimensions={1}, to_apply=%all_to_all.10.reduce_sub_computation | reduce | bytes 262148 | tf_op jit(solution)/shard_map/all_to_all | solution.py:261
  47.3 4.3 %multiply_convert_fusion = bf16[4,16,8,64]{3,1,2,0:T(8,128)(2,1)S(1)} fusion(f32[4,16,8,64]{3,1,2,0:T(8,128)S(1)} %bitcast.112, bf16[4096,1,8,1,64]{0,4,3,2,1:T(8,128)(2,1)} %param.22, bf16[4,16,4096]{2,1,0:T(8,128)(2,1)S(1)} %copy-done.1), kind=kOutput, calls=%fused_computation.39 | convolution fusion | flops 268632064 | bytes 4915200 | tf_op jit(solution)/shard_map/dot_general | solution.py:191
  51.8 3.6 %convolution_bitcast_fusion = f32[16,4,16,256]{3,2,0,1:T(8,128)S(1)} fusion(bf16[16,256,512,1]{2,1,0,3:T(8,128)(2,1)} %bitcast.107, bf16[4,16,512,1]{2,1,0,3:T(8,128)(2,1)S(1)} %reshape.499), kind=kOutput, calls=%fused_computation.15 | convolution fusion | flops 268435456 | bytes 5308416 | tf_op jit(solution)/shard_map/dot_general | solution.py:271
  55.3 1.0 %copy.56 = f32[16,4,16,256]{3,2,1,0:T(8,128)} copy(f32[16,4,16,256]{3,2,0,1:T(8,128)S(1)} %convolution_bitcast_fusion) | data formatting | bytes 2097152 | tf_op jit(solution)/shard_map/transpose | solution.py:286
  56.4 7.5 %all-to-all-start.2 = ((f32[16,4,16,256]{3,2,1,0:T(8,128)}), f32[16,4,16,256]{3,2,1,0:T(8,128)S(1)}, u32[]{:S(2)}, u32[]{:S(2)}) async-start(f32[16,4,16,256]{3,2,1,0:T(8,128)} %copy.56), calls=%async_computation.2 | async-start | bytes 2097152 | tf_op jit(solution)/shard_map/all_to_all | solution.py:286
  64.3 1.3 %copy.44.rows_ref = f32[2,8,128,8]{3,2,1,0:T(8,128)} copy(f32[2,8,128,8]{2,3,1,0:T(8,128)S(1)} %stack.19) | data formatting | bytes 131072 | tf_op jit(solution)/shard_map/stack | solution.py:83
  66.1 0.8 copy.41
  67.0 1.8 %copy.43.sin_ref = f32[2,128,256]{2,1,0:T(8,128)} copy(f32[2,128,256]{1,2,0:T(8,128)} %bitcast.109) | data formatting | bytes 524288 | tf_op jit(solution)/shard_map/reshape | solution.py:70
  68.9 0.8 copy.42.cos_ref
  70.6 1.1 %broadcast_select_fusion.table_ref = f32[2,8,128,128]{3,2,1,0:T(8,128)} fusion(f32[8,128,128]{2,1,0:T(8,128)S(1)} %exponential_select_fusion, pred[2,128]{1,0:T(4,128)(4,1)S(1)} %get-tuple-element.26), kind=kLoop, calls=%fused_computation.35 | loop fusion | flops 262144 | bytes 1573120 | tf_op jit(solution)/shard_map/jit(_where)/select_n | solution.py:107
  71.7 18.3 %shard_map.131 = bf16[2,128,8,512]{3,2,1,0:T(8,128)(2,1)} custom-call(bf16[2,128,8,256]{3,2,1,0:T(8,128)(2,1)} %q_ref, bf16[2,128,8,256]{3,2,1,0:T(8,128)(2,1)} %k_ref, bf16[2,128,8,512]{3,2,1,0:T(8,128)(2,1)} %v_ref, bf16[2,8,256,512]{3,2,1,0:T(8,128)(2,1)} %prior_ref, f32[2,128,256]{2,1,0:T(8,128)} %copy.42.cos_ref, f32[2,128,256]{2,1,0:T(8,128)} %copy.43.sin_ref, ...), custom_call_target="tpu_custom_call" | custom-call | tf_op jit(solution)/shard_map/pallas_call | solution.py:108
  (70 shorter events, 8.5 us)
Async XLA Ops:
  0.6 1.6 %copy-start = (bf16[4096,1,1,256]{3,0,2,1:T(8,128)(2,1)S(1)}, bf16[4096,1,1,256]{3,0,2,1:T(8,128)(2,1)}, u32[]{:S(2)}) copy-start(bf16[4096,1,1,256]{3,0,2,1:T(8,128)(2,1)} %param.19) | copy-start | bytes 6291460
  0.6 3.3 %copy-start.1 = (bf16[4,16,4096]{2,1,0:T(8,128)(2,1)S(1)}, bf16[4,16,4096]{2,1,0:T(8,128)(2,1)}, u32[]{:S(2)}) copy-start(bf16[4,16,4096]{2,1,0:T(8,128)(2,1)} %param.18) | copy-start | bytes 1572868
  2.2 4.4 %copy-start.2 = (bf16[4096,1,8,1,64]{0,4,3,2,1:T(8,128)(2,1)S(1)}, bf16[4096,1,8,1,64]{0,4,3,2,1:T(8,128)(2,1)}, u32[]{:S(2)}) copy-start(bf16[4096,1,8,1,64]{0,4,3,2,1:T(8,128)(2,1)} %param.21) | copy-start | bytes 12582916
  6.6 8.6 %copy-start.3 = (s32[16]{0:T(128)S(1)}, s32[16]{0:T(128)}, u32[]{:S(2)}) copy-start(s32[16]{0:T(128)} %param.17) | copy-start | bytes 196
  8.9 16.5 %all-to-all-start = ((bf16[8,4,2,1024]{3,1,2,0:T(4,128)(2,1)}), bf16[8,4,2,1024]{3,1,2,0:T(4,128)(2,1)S(1)}, u32[]{:S(2)}, u32[]{:S(2)}) async-start(bf16[8,4,2,1024]{3,1,2,0:T(4,128)(2,1)} %bitcast.97), calls=%async_computation | async-start | bytes 262144 | tf_op jit(solution)/shard_map/all_to_all | solution.py:219
  18.5 2.8 %copy-start.4 = (f32[16]{0:T(128)S(1)}, f32[16]{0:T(128)}, u32[]{:S(2)}) copy-start(f32[16]{0:T(128)} %param.16) | copy-start | bytes 196
  33.6 11.9 %all-to-all-start.1 = ((f32[8,1,4096]{2,1,0:T(1,128)}), f32[8,1,4096]{2,1,0:T(1,128)S(1)}, u32[]{:S(2)}, u32[]{:S(2)}) async-start(f32[8,1,4096]{2,1,0:T(1,128)} %reshape.502), calls=%async_computation.1 | async-start | bytes 262144 | tf_op jit(solution)/shard_map/all_to_all | solution.py:261
  56.4 33.6 %all-to-all-start.2 = ((f32[16,4,16,256]{3,2,1,0:T(8,128)}), f32[16,4,16,256]{3,2,1,0:T(8,128)S(1)}, u32[]{:S(2)}, u32[]{:S(2)}) async-start(f32[16,4,16,256]{3,2,1,0:T(8,128)} %copy.56), calls=%async_computation.2 | async-start | bytes 2097152 | tf_op jit(solution)/shard_map/all_to_all | solution.py:286

commit v7 on v6

--- a/solution.py
+++ b/solution.py
@@ -274,7 +274,7 @@
         preferred_element_type=jnp.float32,
     )
     partial_out = partial_out.reshape(step_total, total_prompts, model_width)
-    query_span, key_span, value_span, prior_state, _ = lax.optimization_barrier(
+    query_span, key_span, value_span, prior_state, partial_out = lax.optimization_barrier(
         (query_span, key_span, value_span, prior_state, partial_out)
     )
     prefill_out = prefill_output(
@@ -283,8 +283,8 @@
     out_slots = head_slots * lax.axis_size("tp")
     column_block = model_width // out_slots
     pieces = partial_out.reshape(step_total, total_prompts, out_slots, column_block)
-    pieces = lax.all_to_all(pieces.transpose(2, 0, 1, 3), ("heads", "tp"), 0, 0, tiled=True)
-    decode_out = jnp.sum(pieces, 0).astype(jnp.bfloat16)
+    pieces = lax.all_to_all(pieces, ("heads", "tp"), 2, 2, tiled=True)
+    decode_out = jnp.sum(pieces, 2).astype(jnp.bfloat16)
     return (prefill_out, decode_out)
 
 

time: 91.5 us -> 88.6 us (0.968)
  blocking collectives: 0 us -> 11.4 us
  local copies, waits for them, and re-layouts: 19.7 us -> 12.7 us
  starting transfers between devices: 19.3 us -> 12.7 us
    all_to_all x0 -> x1, blocking collectives: none -> 11.4 us  [per_device(): normed = lax.all_to_all(normed, 'heads', 0, 0, tiled=True)]
    all_to_all x2 -> x1, starting transfers between devices: 13 us -> 6.29 us  [per_device(): pieces = lax.all_to_all(pieces, ('heads', 'tp'), 2, 2, tiled=True)]
    dot_general x2 -> x1, local copies, waits for them, and re-layouts: 6.6 us -> 0.14 us  [per_device(): jnp.dot(activated, w_out.reshape(heads_here * value_slice, model_width),...]
    reshape x0 -> x1, local copies, waits for them, and re-layouts: none -> 1.1 us  [per_device(): partial_out.reshape(step_total, total_prompts, out_slots, column_block)]
    transpose x1 -> x0, local copies, waits for them, and re-layouts: 1.05 us -> none  [per_device(): pieces.transpose(2, 0, 1, 3)]
  transfers between devices with their start and end apart: 3 -> 2, of which waited for: 0 -> 0; matrix products, arithmetic and copies ran while one was open for 27% -> 20% of each run, Pallas kernels for 20% -> 21%
where the time goes in v7:
time: 88.6 us; the launch traced here: 87.9 us
  matrix products  19.4 us (22%)
  Pallas kernels  18.3 us (21%)
  local copies, waits for them, and re-layouts  12.7 us (14%)
  starting transfers between devices  12.7 us (14%)
  other arithmetic  12.4 us (14%)
  blocking collectives  11.4 us (13%)
  between operations  0.99 us (1%)
    pallas_call x1, Pallas kernels, prefill_output(): pl.pallas_call(output_kernel, grid=(prompts_here,), in_specs=[pl.BlockSpe...  18.3 us
    all_to_all x1, blocking collectives, per_device(): normed = lax.all_to_all(normed, 'heads', 0, 0, tiled=True)  11.4 us
    all_to_all x1, starting transfers between devices, per_device(): arrived = lax.all_to_all(packed, 'heads', 0, 0, tiled=True)  6.38 us
    all_to_all x1, starting transfers between devices, per_device(): pieces = lax.all_to_all(pieces, ('heads', 'tp'), 2, 2, tiled=True)  6.29 us
    dot_general x1, matrix products, per_device(): jnp.einsum('tbhk,bhkv->tbhv', query_rot, state_new, preferred_element_typ...  5.85 us
    dot_general x1, matrix products, per_device(): jnp.dot(flat_inputs, w_gate.reshape(model_width, heads_here * value_slice...  4.33 us
    unnamed x13, local copies, waits for them, and re-layouts  4.08 us
    dot_general x1, matrix products, per_device(): jnp.dot(activated, w_out.reshape(heads_here * value_slice, model_width),...  3.03 us
  transfers between devices with their start and end apart: 2, of which 0 were waited for; matrix products, arithmetic and copies ran while one was open for 20% of the time, Pallas kernels for 21%

profile of v7, /device:TPU:1, one launch (start us, length us, event | category | flops | bytes accessed | tf_op | source)
XLA Modules:
  0.0 87.9 jit_solution(16274795351156090460)
XLA Ops:
  0.7 0.8 add_convert_fusion.6
  2.2 1.6 %fusion.26 = bf16[64,256]{1,0:T(8,128)(2,1)S(1)} fusion(bf16[64,4096]{1,0:T(8,128)(2,1)} %bitcast.97, bf16[4096,1,1,256]{3,0,2,1:T(8,128)(2,1)S(1)} %copy-done), kind=kOutput, calls=%fused_computation.27 | convolution fusion | flops 134234112 | bytes 2654208 | tf_op jit(solution)/shard_map/dot_general | solution.py:180
  3.9 2.1 %fusion.29 = bf16[64,256]{1,0:T(8,128)(2,1)S(1)} fusion(bf16[64,4096]{1,0:T(8,128)(2,1)S(1)} %bitcast.98, bf16[4096,1,1,256]{3,0,2,1:T(8,128)(2,1)} %param.20), kind=kOutput, calls=%fused_computation.28 | convolution fusion | flops 134234112 | bytes 2654208 | tf_op jit(solution)/shard_map/dot_general | solution.py:183
  6.6 1.4 %convolution_convert_fusion = bf16[64,512]{1,0:T(8,128)(2,1)S(1)} fusion(bf16[64,4096]{1,0:T(8,128)(2,1)S(1)} %bitcast.99, bf16[4096,512]{0,1:T(8,128)(2,1)S(1)} %bitcast.102), kind=kOutput, calls=%fused_computation.19 | convolution fusion | flops 268468224 | bytes 4784128 | tf_op jit(solution)/shard_map/dot_general | solution.py:186
  8.1 0.8 copy.80
  8.9 6.4 %all-to-all-start = ((bf16[8,4,2,1024]{3,1,2,0:T(4,128)(2,1)}), bf16[8,4,2,1024]{3,1,2,0:T(4,128)(2,1)S(1)}, u32[]{:S(2)}, u32[]{:S(2)}) async-start(bf16[8,4,2,1024]{3,1,2,0:T(4,128)(2,1)} %bitcast.94), calls=%async_computation | async-start | bytes 262144 | tf_op jit(solution)/shard_map/all_to_all | solution.py:219
  15.5 3.0 %copy.38 = bf16[2,128,8,256]{1,2,3,0:T(8,128)(2,1)} copy(bf16[2,128,8,256]{3,2,1,0:T(8,128)(2,1)} %k_ref) | data formatting | bytes 2097152 | tf_op args[1]
  18.5 2.7 %convert.2 = f32[2,128,8,128,2]{1,2,4,3,0:T(8,128)} convert(bf16[2,128,8,128,2]{1,2,4,3,0:T(8,128)(2,1)} %bitcast.101) | non-fusion elementwise | flops 524288 | bytes 3145728 | tf_op jit(solution)/shard_map/reshape | solution.py:17
  22.1 1.8 %multiply_subtract_fusion = (f32[2,128,8,128,1]{1,2,4,3,0:T(8,128)S(1)}, f32[2,128,8,128,1]{1,2,4,3,0:T(8,128)S(1)}) fusion(f32[2,128,8,128,2]{1,2,4,3,0:T(8,128)} %convert.2, f32[2,128,128]{1,2,0:T(8,128)S(1)} %get-tuple-element.26, f32[2,128,128]{1,2,0:T(8,128)S(1)} %get-tuple-element.25), kind=kLoop, calls=%fused_computation.33 | loop fusion | flops 1572864 | bytes 4456448 | tf_op jit(solution)/shard_map/sub | solution.py:21
  24.1 1.2 %fusion.7 = bf16[2,128,8,256]{1,2,3,0:T(8,128)(2,1)} fusion(bf16[2,128,8,256]{1,2,3,0:T(8,128)(2,1)S(1)} %bitcast.100, f32[2,128,8]{1,2,0:T(8,128)S(1)} %exponential_select_fusion.2), kind=kLoop, calls=%fused_computation.9 | loop fusion | flops 1572864 | bytes 2105344 | tf_op jit(solution)/shard_map/convert_element_type | solution.py:172
  25.9 5.8 %fusion.18 = f32[4,2,8,512]{3,0,2,1:T(4,128)S(1)} fusion(bf16[2,8,256,512]{3,2,1,0:T(8,128)(2,1)} %prior_ref, f32[2,8]{1,0:T(2,128)S(1)} %multiply_exponential_fusion.2, bf16[2,128,8,512]{3,2,1,0:T(8,128)(2,1)} %v_ref, bf16[2,128,8,256]{1,2,3,0:T(8,128)(2,1)} %fusion.7, f32[4,8]{0,1:T(8,128)S(1)} %multiply_exponential_fusion.1, ...), kind=kOutput, calls=%fused_computation.18 | convolution fusion | flops 562069504 | bytes 7504064 | tf_op jit(solution)/shard_map/tbhk,bhkv->tbhv/dot_general | solution.py:236
  32.9 11.4 %all_to_all.15 = f32[8,1,4096]{2,1,0:T(1,128)S(1)} all-to-all(f32[8,1,4096]{2,1,0:T(1,128)S(1)} %reshape.505), channel_id=1, replica_groups=mesh['groups'=2,'heads'=8,'tp'=2] {'heads'}, dimensions={0} | all-to-all | bytes 262144 | tf_op jit(solution)/shard_map/all_to_all | solution.py:261
  44.8 1.0 %reduce = f32[8,4096]{1,0:T(8,128)S(1)} reduce(f32[8,1,4096]{2,1,0:T(1,128)S(1)} %all_to_all.15, f32[]{:T(128)} %broadcast.576), dimensions={1}, to_apply=%all_to_all.10.reduce_sub_computation | reduce | bytes 262148 | tf_op jit(solution)/shard_map/all_to_all | solution.py:261
  46.1 4.3 %multiply_convert_fusion = bf16[4,16,8,64]{3,1,2,0:T(8,128)(2,1)S(1)} fusion(f32[4,16,8,64]{3,1,2,0:T(8,128)S(1)} %bitcast.110, bf16[4096,1,8,1,64]{0,4,3,2,1:T(8,128)(2,1)} %param.22, bf16[4,16,4096]{2,1,0:T(8,128)(2,1)S(1)} %copy-done.1), kind=kOutput, calls=%fused_computation.39 | convolution fusion | flops 268632064 | bytes 4915200 | tf_op jit(solution)/shard_map/dot_general | solution.py:191
  50.7 3.0 %fusion.53 = f32[4,16,4096]{2,1,0:T(8,128)S(1)} fusion(bf16[4,16,512]{2,1,0:T(8,128)(2,1)S(1)} %dot_general.51, bf16[512,4096,1]{1,0,2:T(8,128)(2,1)} %bitcast.103), kind=kOutput, calls=%fused_computation.108 | convolution fusion | flops 268435456 | bytes 5308416 | tf_op jit(solution)/shard_map/dot_general | solution.py:271
  53.7 1.1 %copy.78 = f32[4,2,16,8,256]{4,3,1,0,2:T(8,128)} copy(f32[4,2,16,8,256]{4,3,2,1,0:T(8,128)S(1)} %bitcast.105) | data formatting | bytes 2097152 | tf_op jit(solution)/shard_map/reshape | solution.py:285
  54.8 6.3 %all-to-all-start.2 = ((f32[4,16,16,256]{3,1,0,2:T(8,128)}), f32[4,16,16,256]{3,1,0,2:T(8,128)S(1)}, u32[]{:S(2)}, u32[]{:S(2)}) async-start(f32[4,16,16,256]{3,1,0,2:T(8,128)} %bitcast.104), calls=%async_computation.2 | async-start | bytes 2097152 | tf_op jit(solution)/shard_map/all_to_all | solution.py:286
  61.5 1.3 %copy.51.rows_ref = f32[2,8,128,8]{3,2,1,0:T(8,128)} copy(f32[2,8,128,8]{2,3,1,0:T(8,128)S(1)} %stack.20) | data formatting | bytes 131072 | tf_op jit(solution)/shard_map/stack | solution.py:83
  63.3 0.8 copy.48
  64.2 1.8 %copy.50.sin_ref = f32[2,128,256]{2,1,0:T(8,128)} copy(f32[2,128,256]{1,2,0:T(8,128)} %bitcast.107) | data formatting | bytes 524288 | tf_op jit(solution)/shard_map/reshape | solution.py:70
  66.0 0.8 copy.49.cos_ref
  67.7 1.1 %broadcast_select_fusion.table_ref = f32[2,8,128,128]{3,2,1,0:T(8,128)} fusion(f32[8,128,128]{2,1,0:T(8,128)S(1)} %exponential_select_fusion, pred[2,128]{1,0:T(4,128)(4,1)S(1)} %get-tuple-element.28), kind=kLoop, calls=%fused_computation.35 | loop fusion | flops 262144 | bytes 1573120 | tf_op jit(solution)/shard_map/jit(_where)/select_n | solution.py:107
  68.9 18.3 %shard_map.131 = bf16[2,128,8,512]{3,2,1,0:T(8,128)(2,1)} custom-call(bf16[2,128,8,256]{3,2,1,0:T(8,128)(2,1)} %q_ref, bf16[2,128,8,256]{3,2,1,0:T(8,128)(2,1)} %k_ref, bf16[2,128,8,512]{3,2,1,0:T(8,128)(2,1)} %v_ref, bf16[2,8,256,512]{3,2,1,0:T(8,128)(2,1)} %prior_ref, f32[2,128,256]{2,1,0:T(8,128)} %copy.49.cos_ref, f32[2,128,256]{2,1,0:T(8,128)} %copy.50.sin_ref, ...), custom_call_target="tpu_custom_call" | custom-call | tf_op jit(solution)/shard_map/pallas_call | solution.py:108
  87.2 0.7 reduce_sum.29
  (68 shorter events, 7.3 us)
Async XLA Ops:
  0.6 1.6 %copy-start = (bf16[4096,1,1,256]{3,0,2,1:T(8,128)(2,1)S(1)}, bf16[4096,1,1,256]{3,0,2,1:T(8,128)(2,1)}, u32[]{:S(2)}) copy-start(bf16[4096,1,1,256]{3,0,2,1:T(8,128)(2,1)} %param.19) | copy-start | bytes 6291460
  0.6 3.3 %copy-start.1 = (bf16[4,16,4096]{2,1,0:T(8,128)(2,1)S(1)}, bf16[4,16,4096]{2,1,0:T(8,128)(2,1)}, u32[]{:S(2)}) copy-start(bf16[4,16,4096]{2,1,0:T(8,128)(2,1)} %param.18) | copy-start | bytes 1572868
  2.2 4.4 %copy-start.2 = (bf16[4096,1,8,1,64]{0,4,3,2,1:T(8,128)(2,1)S(1)}, bf16[4096,1,8,1,64]{0,4,3,2,1:T(8,128)(2,1)}, u32[]{:S(2)}) copy-start(bf16[4096,1,8,1,64]{0,4,3,2,1:T(8,128)(2,1)} %param.21) | copy-start | bytes 12582916
  6.6 8.6 %copy-start.3 = (s32[16]{0:T(128)S(1)}, s32[16]{0:T(128)}, u32[]{:S(2)}) copy-start(s32[16]{0:T(128)} %param.17) | copy-start | bytes 196
  8.9 16.5 %all-to-all-start = ((bf16[8,4,2,1024]{3,1,2,0:T(4,128)(2,1)}), bf16[8,4,2,1024]{3,1,2,0:T(4,128)(2,1)S(1)}, u32[]{:S(2)}, u32[]{:S(2)}) async-start(bf16[8,4,2,1024]{3,1,2,0:T(4,128)(2,1)} %bitcast.94), calls=%async_computation | async-start | bytes 262144 | tf_op jit(solution)/shard_map/all_to_all | solution.py:219
  18.5 2.8 %copy-start.4 = (f32[16]{0:T(128)S(1)}, f32[16]{0:T(128)}, u32[]{:S(2)}) copy-start(f32[16]{0:T(128)} %param.16) | copy-start | bytes 196
  54.8 32.4 %all-to-all-start.2 = ((f32[4,16,16,256]{3,1,0,2:T(8,128)}), f32[4,16,16,256]{3,1,0,2:T(8,128)S(1)}, u32[]{:S(2)}, u32[]{:S(2)}) async-start(f32[4,16,16,256]{3,1,0,2:T(8,128)} %bitcast.104), calls=%async_computation.2 | async-start | bytes 2097152 | tf_op jit(solution)/shard_map/all_to_all | solution.py:286

commit v8 on v7

--- a/solution.py
+++ b/solution.py
@@ -93,7 +93,9 @@
     return cosine, sine_part, swap, rows, valid_rows
 
 
-def prefill_output(query_span, key_span, value_span, prior_state, local_rates, tables):
+def prefill_output(
+    query_span, key_span, value_span, prior_state, local_rates, tables, first, count, earlier
+):
     prompts_here, span_len, heads_here, key_width = query_span.shape
     value_width = value_span.shape[3]
     cosine, sine_part, swap, rows, valid_rows = tables
@@ -105,25 +107,39 @@
         0.0,
     )
     table = jnp.where(valid_rows[:, None, None, :], decay_table[None], 0.0)
+    def pick(*shape_tail):
+        return lambda i: (first + i,) + (0,) * len(shape_tail)
+
+    in_specs = [
+        pl.BlockSpec((None, span_len, heads_here, key_width), pick(0, 0, 0)),
+        pl.BlockSpec((None, span_len, heads_here, key_width), pick(0, 0, 0)),
+        pl.BlockSpec((None, span_len, heads_here, value_width), pick(0, 0, 0)),
+        pl.BlockSpec((None, heads_here, key_width, value_width), pick(0, 0, 0)),
+        pl.BlockSpec((None, span_len, key_width), pick(0, 0)),
+        pl.BlockSpec((None, span_len, key_width), pick(0, 0)),
+        pl.BlockSpec((key_width, key_width), lambda i: (0, 0)),
+        pl.BlockSpec((None, heads_here, span_len, span_len), pick(0, 0, 0)),
+        pl.BlockSpec((None, heads_here, span_len, 8), pick(0, 0, 0)),
+    ]
+    operands = [query_span, key_span, value_span, prior_state, cosine, sine_part, swap, table, rows]
+    kernel = output_kernel
+    aliases = {}
+    if earlier is not None:
+        in_specs.append(pl.BlockSpec(memory_space=pl.ANY))
+        operands.append(earlier)
+        aliases = {len(operands) - 1: 0}
+
+        def kernel(*refs):
+            output_kernel(*refs[:9], refs[10])
+
     return pl.pallas_call(
-        output_kernel,
-        grid=(prompts_here,),
-        in_specs=[
-            pl.BlockSpec((None, span_len, heads_here, key_width), lambda b: (b, 0, 0, 0)),
-            pl.BlockSpec((None, span_len, heads_here, key_width), lambda b: (b, 0, 0, 0)),
-            pl.BlockSpec((None, span_len, heads_here, value_width), lambda b: (b, 0, 0, 0)),
-            pl.BlockSpec((None, heads_here, key_width, value_width), lambda b: (b, 0, 0, 0)),
-            pl.BlockSpec((None, span_len, key_width), lambda b: (b, 0, 0)),
-            pl.BlockSpec((None, span_len, key_width), lambda b: (b, 0, 0)),
-            pl.BlockSpec((key_width, key_width), lambda b: (0, 0)),
-            pl.BlockSpec((None, heads_here, span_len, span_len), lambda b: (b, 0, 0, 0)),
-            pl.BlockSpec((None, heads_here, span_len, 8), lambda b: (b, 0, 0, 0)),
-        ],
-        out_specs=pl.BlockSpec(
-            (None, span_len, heads_here, value_width), lambda b: (b, 0, 0, 0)
-        ),
+        kernel,
+        grid=(count,),
+        in_specs=in_specs,
+        out_specs=pl.BlockSpec((None, span_len, heads_here, value_width), pick(0, 0, 0)),
         out_shape=jax.ShapeDtypeStruct(value_span.shape, jnp.bfloat16),
-    )(query_span, key_span, value_span, prior_state, cosine, sine_part, swap, table, rows)
+        input_output_aliases=aliases,
+    )(*operands)
 
 
 def per_device(
@@ -258,7 +274,15 @@
     normed = norm_with(readout, read_mean, read_square)
     normed = normed.reshape(step_total, prompts_here, heads_here, slots, value_slice)
     normed = normed.transpose(3, 0, 1, 2, 4)
+    first_half = prompts_here // 2
+    q_early, k_early, v_early, prior_early, normed = lax.optimization_barrier(
+        (query_span, key_span, value_span, prior_state, normed)
+    )
+    prefill_early = prefill_output(
+        q_early, k_early, v_early, prior_early, local_rates, tables, 0, first_half, None
+    )
     normed = lax.all_to_all(normed, "heads", 0, 0, tiled=True)
+    normed, prefill_early = lax.optimization_barrier((normed, prefill_early))
     normed = normed.transpose(1, 0, 2, 3, 4).reshape(
         step_total, total_prompts, heads_here, value_slice
     )
@@ -278,7 +302,8 @@
         (query_span, key_span, value_span, prior_state, partial_out)
     )
     prefill_out = prefill_output(
-        query_span, key_span, value_span, prior_state, local_rates, tables
+        query_span, key_span, value_span, prior_state, local_rates, tables,
+        first_half, prompts_here - first_half, prefill_early,
     )
     out_slots = head_slots * lax.axis_size("tp")
     column_block = model_width // out_slots

time: 88.6 us -> 100 us (1.13)
  waiting for transfers between devices: 0.01 us -> 12.7 us
  blocking collectives: 11.4 us -> 0 us
  starting transfers between devices: 12.7 us -> 19.5 us
  Pallas kernels: 18.3 us -> 20.9 us
  other arithmetic: 12.4 us -> 10.9 us
  local copies, waits for them, and re-layouts: 12.7 us -> 13.8 us
    all_to_all x1, waiting for transfers between devices: 0.01 us -> 12.7 us  [per_device(): pieces = lax.all_to_all(pieces, ('heads', 'tp'), 2, 2, tiled=True)]
    all_to_all x1 -> x0, blocking collectives: 11.4 us -> none  [per_device(): normed = lax.all_to_all(normed, 'heads', 0, 0, tiled=True)]
    all_to_all x0 -> x1, starting transfers between devices: none -> 5.57 us  [per_device(): normed = lax.all_to_all(normed, 'heads', 0, 0, tiled=True)]
    pallas_call x1 -> x2, Pallas kernels: 18.3 us -> 20.9 us  [prefill_output(): pl.pallas_call(kernel, grid=(count,), in_specs=in_specs, out_specs=pl.Blo...]
    reshape x3, local copies, waits for them, and re-layouts: 0.34 us -> 2.77 us  [per_device(): value_own = arrived[..., 2 * key_piece:].reshape(slots, step_total, promp...]
    sub x1, other arithmetic: 1.76 us -> 0.25 us  [rotate(): even_part * cosine - odd_part * sine_part]
    reshape x1, other arithmetic: 2.72 us -> 1.38 us  [rotate(): paired = values.reshape(values.shape[:-1] + (halfway, 2))]
    all_to_all x1, starting transfers between devices: 6.29 us -> 7.52 us  [per_device(): pieces = lax.all_to_all(pieces, ('heads', 'tp'), 2, 2, tiled=True)]
  transfers between devices with their start and end apart: 2 -> 3, of which waited for: 0 -> 1; matrix products, arithmetic and copies ran while one was open for 20% -> 14% of each run, Pallas kernels for 21% -> 21%
where the time goes in v8:
time: 100 us; the launch traced here: 98.8 us
  Pallas kernels  20.9 us (21%)
  matrix products  19.9 us (20%)
  starting transfers between devices  19.5 us (20%)
  local copies, waits for them, and re-layouts  13.8 us (14%)
  waiting for transfers between devices  12.7 us (13%)
  other arithmetic  10.9 us (11%)
  between operations  1.05 us (1%)
    pallas_call x2, Pallas kernels, prefill_output(): pl.pallas_call(kernel, grid=(count,), in_specs=in_specs, out_specs=pl.Blo...  20.9 us
    all_to_all x1, waiting for transfers between devices, per_device(): pieces = lax.all_to_all(pieces, ('heads', 'tp'), 2, 2, tiled=True)  12.7 us
    all_to_all x1, starting transfers between devices, per_device(): pieces = lax.all_to_all(pieces, ('heads', 'tp'), 2, 2, tiled=True)  7.52 us
    all_to_all x1, starting transfers between devices, per_device(): arrived = lax.all_to_all(packed, 'heads', 0, 0, tiled=True)  6.38 us
    dot_general x1, matrix products, per_device(): jnp.einsum('tbhk,bhkv->tbhv', query_rot, state_new, preferred_element_typ...  5.6 us
    all_to_all x1, starting transfers between devices, per_device(): normed = lax.all_to_all(normed, 'heads', 0, 0, tiled=True)  5.57 us
    dot_general x1, matrix products, per_device(): jnp.dot(flat_inputs, w_gate.reshape(model_width, heads_here * value_slice...  4.34 us
    unnamed x29, local copies, waits for them, and re-layouts  3.78 us
  transfers between devices with their start and end apart: 3, of which 1 were waited for; matrix products, arithmetic and copies ran while one was open for 14% of the time, Pallas kernels for 21%

profile of v8, /device:TPU:1, one launch (start us, length us, event | category | flops | bytes accessed | tf_op | source)
XLA Modules:
  0.0 98.8 jit_solution(17587770964857999832)
XLA Ops:
  2.2 1.6 %fusion.26 = bf16[64,256]{1,0:T(8,128)(2,1)S(1)} fusion(bf16[64,4096]{1,0:T(8,128)(2,1)} %bitcast.91, bf16[4096,1,1,256]{3,0,2,1:T(8,128)(2,1)S(1)} %copy-done), kind=kOutput, calls=%fused_computation.27 | convolution fusion | flops 134234112 | bytes 2654208 | tf_op jit(solution)/shard_map/dot_general | solution.py:196
  3.9 2.1 %fusion.29 = bf16[64,256]{1,0:T(8,128)(2,1)S(1)} fusion(bf16[64,4096]{1,0:T(8,128)(2,1)S(1)} %bitcast.92, bf16[4096,1,1,256]{3,0,2,1:T(8,128)(2,1)} %param.20), kind=kOutput, calls=%fused_computation.28 | convolution fusion | flops 134234112 | bytes 2654208 | tf_op jit(solution)/shard_map/dot_general | solution.py:199
  6.7 1.4 %convolution_convert_fusion = bf16[64,512]{1,0:T(8,128)(2,1)S(1)} fusion(bf16[64,4096]{1,0:T(8,128)(2,1)S(1)} %bitcast.93, bf16[4096,512]{0,1:T(8,128)(2,1)S(1)} %bitcast.96), kind=kOutput, calls=%fused_computation.19 | convolution fusion | flops 268468224 | bytes 4784128 | tf_op jit(solution)/shard_map/dot_general | solution.py:202
  8.9 6.4 %all-to-all-start = ((bf16[8,4,2,1024]{3,1,2,0:T(4,128)(2,1)}), bf16[8,4,2,1024]{3,1,2,0:T(4,128)(2,1)S(1)}, u32[]{:S(2)}, u32[]{:S(2)}) async-start(bf16[8,4,2,1024]{3,1,2,0:T(4,128)(2,1)} %bitcast.90), calls=%async_computation | async-start | bytes 262144 | tf_op jit(solution)/shard_map/all_to_all | solution.py:235
  17.5 1.1 %broadcast_select_fusion.table_ref.refs_7_ = f32[2,8,128,128]{3,2,1,0:T(8,128)} fusion(f32[8,128,128]{2,1,0:T(8,128)S(1)} %exponential_select_fusion, pred[2,128]{1,0:T(4,128)(4,1)S(1)} %get-tuple-element.42), kind=kLoop, calls=%fused_computation.35 | loop fusion | flops 262144 | bytes 1573120 | tf_op jit(solution)/shard_map/jit(_where)/select_n | solution.py:109
  18.6 2.0 %copy.44 = bf16[2,128,8,256]{1,2,3,0:T(8,128)(2,1)} copy(bf16[2,128,8,256]{3,2,1,0:T(8,128)(2,1)S(1)} %copy-done.1) | data formatting | bytes 2097152 | tf_op args[1]
  20.5 1.4 %convert.2 = f32[2,128,8,128,2]{1,2,4,3,0:T(8,128)S(1)} convert(bf16[2,128,8,128,2]{1,2,4,3,0:T(8,128)(2,1)} %bitcast.95) | non-fusion elementwise | flops 524288 | bytes 3145728 | tf_op jit(solution)/shard_map/reshape | solution.py:17
  23.8 1.2 %fusion.45 = (f32[2,128,128,1]{2,1,3,0:T(8,128)}, f32[2,128,128,1]{2,1,3,0:T(8,128)}) fusion(f32[128]{0:T(128)S(1)} %multiply_power_fusion.1, f32[2,128]{1,0:T(2,128)S(1)} %add_convert_fusion.7), kind=kLoop, calls=%fused_computation.60 | loop fusion | flops 65536 | bytes 263680 | tf_op jit(solution)/shard_map/neg | solution.py:70
  25.7 1.0 reshape.491
  27.4 1.0 %reshape.492 = bf16[4,2,8,512]{3,0,2,1:T(4,128)(2,1)S(1)} reshape(bf16[4,2,8,8,64]{4,3,0,2,1:T(8,128)(2,1)} %bitcast.104) | data formatting | bytes 131072 | tf_op jit(solution)/shard_map/reshape | solution.py:250
  28.5 0.9 convolution_multiply_fusion.2
  29.3 5.6 %fusion.18 = f32[4,2,8,512]{3,0,2,1:T(4,128)S(1)} fusion(bf16[2,8,256,512]{3,2,1,0:T(8,128)(2,1)} %refs_3_, f32[2,8]{1,0:T(2,128)} %multiply_exponential_fusion.2, bf16[2,128,8,512]{3,2,1,0:T(8,128)(2,1)} %refs_2_, bf16[2,128,8,256]{1,2,3,0:T(8,128)(2,1)S(1)} %fusion.7, f32[4,8]{0,1:T(8,128)S(1)} %multiply_exponential_fusion.1, ...), kind=kOutput, calls=%fused_computation.18 | convolution fusion | flops 562069504 | bytes 7504064 | tf_op jit(solution)/shard_map/tbhk,bhkv->tbhv/dot_general | solution.py:252
  35.8 0.9 reshape.505
  36.7 5.6 %all-to-all-start.1 = ((f32[8,1,4096]{2,1,0:T(1,128)}), f32[8,1,4096]{2,1,0:T(1,128)S(1)}, u32[]{:S(2)}, u32[]{:S(2)}) async-start(f32[8,1,4096]{2,1,0:T(1,128)} %reshape.505), calls=%async_computation.1 | async-start | bytes 262144 | tf_op jit(solution)/shard_map/all_to_all | solution.py:284
  43.4 0.8 copy.53.cos_ref.refs_4_
  44.5 1.3 %copy.55.rows_ref.refs_8_ = f32[2,8,128,8]{3,2,1,0:T(8,128)} copy(f32[2,8,128,8]{2,3,1,0:T(8,128)S(1)} %stack.20) | data formatting | bytes 131072 | tf_op jit(solution)/shard_map/stack | solution.py:83
  46.5 10.5 %shard_map.131.refs_9_ = bf16[2,128,8,512]{3,2,1,0:T(8,128)(2,1)} custom-call(bf16[2,128,8,256]{3,2,1,0:T(8,128)(2,1)} %refs_0_, bf16[2,128,8,256]{3,2,1,0:T(8,128)(2,1)} %refs_1_, bf16[2,128,8,512]{3,2,1,0:T(8,128)(2,1)} %refs_2_, bf16[2,8,256,512]{3,2,1,0:T(8,128)(2,1)} %refs_3_, f32[2,128,256]{2,1,0:T(8,128)} %copy.53.cos_ref.refs_4_, ...), custom_call_target="tpu_custom_call" | custom-call | tf_op jit(solution)/shard_map/pallas_call | solution.py:135
  57.5 1.0 reduce
  58.8 4.3 %multiply_convert_fusion = bf16[4,16,8,64]{3,1,2,0:T(8,128)(2,1)S(1)} fusion(f32[4,16,8,64]{3,1,2,0:T(8,128)S(1)} %bitcast.105, bf16[4096,1,8,1,64]{0,4,3,2,1:T(8,128)(2,1)} %param.22, bf16[4,16,4096]{2,1,0:T(8,128)(2,1)S(1)} %copy-done.3), kind=kOutput, calls=%fused_computation.39 | convolution fusion | flops 268632064 | bytes 4915200 | tf_op jit(solution)/shard_map/dot_general | solution.py:207
  63.3 3.0 %fusion.52 = f32[4,16,4096]{2,1,0:T(8,128)S(1)} fusion(bf16[4,16,512]{2,1,0:T(8,128)(2,1)S(1)} %dot_general.51, bf16[512,4096,1]{1,0,2:T(8,128)(2,1)} %bitcast.97), kind=kOutput, calls=%fused_computation.106 | convolution fusion | flops 268435456 | bytes 5308416 | tf_op jit(solution)/shard_map/dot_general | solution.py:295
  66.3 1.1 %copy.85 = f32[4,2,16,8,256]{4,3,1,0,2:T(8,128)} copy(f32[4,2,16,8,256]{4,3,2,1,0:T(8,128)S(1)} %bitcast.99) | data formatting | bytes 2097152 | tf_op jit(solution)/shard_map/reshape | solution.py:310
  67.4 7.5 %all-to-all-start.2 = ((f32[4,16,16,256]{3,1,0,2:T(8,128)}), f32[4,16,16,256]{3,1,0,2:T(8,128)S(1)}, u32[]{:S(2)}, u32[]{:S(2)}) async-start(f32[4,16,16,256]{3,1,0,2:T(8,128)} %bitcast.98), calls=%async_computation.2 | async-start | bytes 2097152 | tf_op jit(solution)/shard_map/all_to_all | solution.py:311
  75.0 10.4 %shard_map.132 = bf16[2,128,8,512]{3,2,1,0:T(8,128)(2,1)} custom-call(bf16[2,128,8,256]{3,2,1,0:T(8,128)(2,1)} %refs_0_, bf16[2,128,8,256]{3,2,1,0:T(8,128)(2,1)} %refs_1_, bf16[2,128,8,512]{3,2,1,0:T(8,128)(2,1)} %refs_2_, bf16[2,8,256,512]{3,2,1,0:T(8,128)(2,1)} %refs_3_, f32[2,128,256]{2,1,0:T(8,128)} %copy.53.cos_ref.refs_4_, ...), custom_call_target="tpu_custom_call", output_to_operand_aliasing={{}: (9, {})} | custom-call | tf_op jit(solution)/shard_map/pallas_call | solution.py:135
  85.4 12.7 %all-to-all-done.2 = f32[4,16,16,256]{3,1,0,2:T(8,128)S(1)} async-done(((f32[4,16,16,256]{3,1,0,2:T(8,128)}), f32[4,16,16,256]{3,1,0,2:T(8,128)S(1)}, u32[]{:S(2)}, u32[]{:S(2)}) %all-to-all-start.2) | async-done | bytes 1048608 | tf_op jit(solution)/shard_map/all_to_all | solution.py:311
  (85 shorter events, 12.9 us)
Async XLA Ops:
  0.6 1.6 %copy-start = (bf16[4096,1,1,256]{3,0,2,1:T(8,128)(2,1)S(1)}, bf16[4096,1,1,256]{3,0,2,1:T(8,128)(2,1)}, u32[]{:S(2)}) copy-start(bf16[4096,1,1,256]{3,0,2,1:T(8,128)(2,1)} %param.19) | copy-start | bytes 6291460
  0.6 3.3 %copy-start.2 = (bf16[4,16,4096]{2,1,0:T(8,128)(2,1)S(1)}, bf16[4,16,4096]{2,1,0:T(8,128)(2,1)}, u32[]{:S(2)}) copy-start(bf16[4,16,4096]{2,1,0:T(8,128)(2,1)} %param.18) | copy-start | bytes 1572868
  0.7 5.6 %copy-start.10 = (s32[256]{0:T(256)}, s32[256]{0:T(256)S(1)}, u32[]{:S(2)}) copy-start(s32[256]{0:T(256)S(1)} %iota_xor_fusion) | copy-start | bytes 3076
  2.2 4.4 %copy-start.4 = (bf16[4096,1,8,1,64]{0,4,3,2,1:T(8,128)(2,1)S(1)}, bf16[4096,1,8,1,64]{0,4,3,2,1:T(8,128)(2,1)}, u32[]{:S(2)}) copy-start(bf16[4096,1,8,1,64]{0,4,3,2,1:T(8,128)(2,1)} %param.21) | copy-start | bytes 12582916
  6.6 8.7 %copy-start.9 = (s32[16]{0:T(128)S(1)}, s32[16]{0:T(128)}, u32[]{:S(2)}) copy-start(s32[16]{0:T(128)} %param.17) | copy-start | bytes 196
  6.7 9.5 %copy-start.12 = (f32[16]{0:T(128)S(1)}, f32[16]{0:T(128)}, u32[]{:S(2)}) copy-start(f32[16]{0:T(128)} %param.16) | copy-start | bytes 196
  8.1 10.5 %copy-start.1 = (bf16[2,128,8,256]{3,2,1,0:T(8,128)(2,1)S(1)}, bf16[2,128,8,256]{3,2,1,0:T(8,128)(2,1)}, u32[]{:S(2)}) copy-start(bf16[2,128,8,256]{3,2,1,0:T(8,128)(2,1)} %refs_1_) | copy-start | bytes 3145732
  8.9 16.1 %all-to-all-start = ((bf16[8,4,2,1024]{3,1,2,0:T(4,128)(2,1)}), bf16[8,4,2,1024]{3,1,2,0:T(4,128)(2,1)S(1)}, u32[]{:S(2)}, u32[]{:S(2)}) async-start(bf16[8,4,2,1024]{3,1,2,0:T(4,128)(2,1)} %bitcast.90), calls=%async_computation | async-start | bytes 262144 | tf_op jit(solution)/shard_map/all_to_all | solution.py:235
  34.9 7.4 %copy-start.5 = (f32[2,128,128,1]{2,1,3,0:T(8,128)S(1)}, f32[2,128,128,1]{2,1,3,0:T(8,128)}, u32[]{:S(2)}) copy-start(f32[2,128,128,1]{2,1,3,0:T(8,128)} %get-tuple-element.37) | copy-start | bytes 393220
  34.9 7.4 %copy-start.6 = (f32[2,128,128,1]{2,1,3,0:T(8,128)S(1)}, f32[2,128,128,1]{2,1,3,0:T(8,128)}, u32[]{:S(2)}) copy-start(f32[2,128,128,1]{2,1,3,0:T(8,128)} %get-tuple-element.38) | copy-start | bytes 393220
  35.4 8.8 %copy-start.7 = (f32[2,128]{1,0:T(2,128)S(1)}, f32[2,128]{1,0:T(2,128)}, u32[]{:S(2)}) copy-start(f32[2,128]{1,0:T(2,128)} %get-tuple-element.41) | copy-start | bytes 3076
  35.5 8.8 %copy-start.8 = (f32[2,8]{1,0:T(2,128)S(1)}, f32[2,8]{1,0:T(2,128)}, u32[]{:S(2)}) copy-start(f32[2,8]{1,0:T(2,128)} %multiply_exponential_fusion.2) | copy-start | bytes 196
  36.7 9.1 %copy-start.11 = (s32[256]{0:T(256)S(1)}, s32[256]{0:T(256)}, u32[]{:S(2)}) copy-start(s32[256]{0:T(256)} %copy-done.10) | copy-start | bytes 3076
  36.7 20.3 %all-to-all-start.1 = ((f32[8,1,4096]{2,1,0:T(1,128)}), f32[8,1,4096]{2,1,0:T(1,128)S(1)}, u32[]{:S(2)}, u32[]{:S(2)}) async-start(f32[8,1,4096]{2,1,0:T(1,128)} %reshape.505), calls=%async_computation.1 | async-start | bytes 262144 | tf_op jit(solution)/shard_map/all_to_all | solution.py:284
  46.5 12.3 %copy-start.3 = (bf16[4,16,4096]{2,1,0:T(8,128)(2,1)S(1)}, bf16[4,16,4096]{2,1,0:T(8,128)(2,1)}, u32[]{:S(2)}) copy-start(bf16[4,16,4096]{2,1,0:T(8,128)(2,1)} %param.18) | copy-start | bytes 1572868
  67.4 30.7 %all-to-all-start.2 = ((f32[4,16,16,256]{3,1,0,2:T(8,128)}), f32[4,16,16,256]{3,1,0,2:T(8,128)S(1)}, u32[]{:S(2)}, u32[]{:S(2)}) async-start(f32[4,16,16,256]{3,1,0,2:T(8,128)} %bitcast.98), calls=%async_computation.2 | async-start | bytes 2097152 | tf_op jit(solution)/shard_map/all_to_all | solution.py:311

commit v9 on v7

--- a/solution.py
+++ b/solution.py
@@ -33,30 +33,40 @@
 
 
 def output_kernel(
-    q_ref, k_ref, v_ref, prior_ref, cos_ref, sin_ref, swap_ref, table_ref, rows_ref, out_ref
+    rates_ref, live_ref, q_ref, k_ref, v_ref, prior_ref, cos_ref, sin_ref, swap_ref, out_ref
 ):
     swap = swap_ref[...]
     cosine = cos_ref[...]
     sine_part = sin_ref[...]
+    span_len = q_ref.shape[0]
+    live = live_ref[pl.program_id(0)]
+    row = lax.broadcasted_iota(jnp.int32, (span_len, span_len), 0)
+    column = lax.broadcasted_iota(jnp.int32, (span_len, span_len), 1)
+    distance = jnp.maximum(row - column, 0).astype(jnp.float32)
+    keep = (row >= column) & (column < live)
+    row_index = lax.broadcasted_iota(jnp.int32, (span_len, 1), 0)
+    valid = row_index < live
     for head in range(q_ref.shape[1]):
+        rate = rates_ref[head]
         q_raw = q_ref[:, head, :]
         k_raw = k_ref[:, head, :]
         queries = turn_lanes(q_raw, swap, cosine, sine_part).astype(jnp.bfloat16)
         keys = (turn_lanes(k_raw, swap, cosine, sine_part) * (k_raw.shape[-1] ** (-0.5))).astype(
             jnp.bfloat16
         )
-        rows = rows_ref[head]
         scores = lax.dot_general(
             queries, keys, (((1,), (1,)), ((), ())), preferred_element_type=jnp.float32
         )
-        weights = (scores * table_ref[head]).astype(jnp.bfloat16)
+        table = jnp.where(keep, jnp.exp(-rate * distance), 0.0)
+        weights = (scores * table).astype(jnp.bfloat16)
         inner = jnp.dot(weights, v_ref[:, head, :], preferred_element_type=jnp.float32)
         carried = jnp.dot(queries, prior_ref[head], preferred_element_type=jnp.float32)
-        mixed = inner + rows[:, 0:1] * carried
+        lead = jnp.exp(-rate * (row_index + 1).astype(jnp.float32))
+        mixed = inner + lead * carried
         mean_value = jnp.mean(mixed, -1, keepdims=True)
         mean_square = jnp.mean(mixed * mixed, -1, keepdims=True)
         normed = norm_with(mixed, mean_value, mean_square)
-        out_ref[:, head, :] = jnp.where(rows[:, 1:2] > 0.5, normed, 0.0).astype(out_ref.dtype)
+        out_ref[:, head, :] = jnp.where(valid, normed, 0.0).astype(out_ref.dtype)
 
 
 def prefill_tables(key_width, span_len, local_rates, span_start, live_count):
@@ -93,22 +103,17 @@
     return cosine, sine_part, swap, rows, valid_rows
 
 
-def prefill_output(query_span, key_span, value_span, prior_state, local_rates, tables):
+def prefill_output(query_span, key_span, value_span, prior_state, local_rates, tables, live_count):
     prompts_here, span_len, heads_here, key_width = query_span.shape
     value_width = value_span.shape[3]
     cosine, sine_part, swap, rows, valid_rows = tables
-    offsets = jnp.arange(span_len)
-    distance = (offsets[:, None] - offsets[None, :]).astype(jnp.float32)
-    decay_table = jnp.where(
-        distance[None] >= 0,
-        jnp.exp(-local_rates[:, None, None] * jnp.maximum(distance, 0.0)[None]),
-        0.0,
-    )
-    table = jnp.where(valid_rows[:, None, None, :], decay_table[None], 0.0)
+    whole = pl.BlockSpec(memory_space=pltpu.SMEM)
     return pl.pallas_call(
         output_kernel,
         grid=(prompts_here,),
         in_specs=[
+            whole,
+            whole,
             pl.BlockSpec((None, span_len, heads_here, key_width), lambda b: (b, 0, 0, 0)),
             pl.BlockSpec((None, span_len, heads_here, key_width), lambda b: (b, 0, 0, 0)),
             pl.BlockSpec((None, span_len, heads_here, value_width), lambda b: (b, 0, 0, 0)),
@@ -116,14 +121,15 @@
             pl.BlockSpec((None, span_len, key_width), lambda b: (b, 0, 0)),
             pl.BlockSpec((None, span_len, key_width), lambda b: (b, 0, 0)),
             pl.BlockSpec((key_width, key_width), lambda b: (0, 0)),
-            pl.BlockSpec((None, heads_here, span_len, span_len), lambda b: (b, 0, 0, 0)),
-            pl.BlockSpec((None, heads_here, span_len, 8), lambda b: (b, 0, 0, 0)),
         ],
         out_specs=pl.BlockSpec(
             (None, span_len, heads_here, value_width), lambda b: (b, 0, 0, 0)
         ),
         out_shape=jax.ShapeDtypeStruct(value_span.shape, jnp.bfloat16),
-    )(query_span, key_span, value_span, prior_state, cosine, sine_part, swap, table, rows)
+    )(
+        local_rates, live_count.astype(jnp.int32), query_span, key_span, value_span,
+        prior_state, cosine, sine_part, swap,
+    )
 
 
 def per_device(
@@ -278,7 +284,7 @@
         (query_span, key_span, value_span, prior_state, partial_out)
     )
     prefill_out = prefill_output(
-        query_span, key_span, value_span, prior_state, local_rates, tables
+        query_span, key_span, value_span, prior_state, local_rates, tables, live_count
     )
     out_slots = head_slots * lax.axis_size("tp")
     column_block = model_width // out_slots

time: 88.6 us -> 89.1 us (level)
  local copies, waits for them, and re-layouts: 12.7 us -> 9.59 us
  waiting for transfers between devices: 0.01 us -> 1.22 us
    another operation x6 -> x0, local copies, waits for them, and re-layouts: 1.51 us -> none  [prefill_tables(): jnp.stack([jnp.broadcast_to(lead_decay[None], shape_rows), jnp.broadcast_...]
    select_n x3 -> x0, other arithmetic: 1.37 us -> none  [the longest x1 1.14 us: prefill_output(): table = jnp.where(valid_rows[:, None, None, :], decay_table[None], 0.0)]
    reduce_sum x1, other arithmetic: 0.68 us -> 1.92 us  [per_device(): decode_out = jnp.sum(pieces, 2).astype(jnp.bfloat16)]
    all_to_all x1, waiting for transfers between devices: 0.01 us -> 1.22 us  [per_device(): pieces = lax.all_to_all(pieces, ('heads', 'tp'), 2, 2, tiled=True)]
    reshape x1, local copies, waits for them, and re-layouts: 1.77 us -> 0.84 us  [prefill_tables(): sine_part = jnp.stack([-sine_part, sine_part], -1).reshape(cosine.shape)]
    unnamed x13 -> x15, local copies, waits for them, and re-layouts: 4.08 us -> 4.08 us
  transfers between devices with their start and end apart: 2 -> 2, of which waited for: 0 -> 1; matrix products, arithmetic and copies ran while one was open for 20% -> 16% of each run, Pallas kernels for 21% -> 22%
where the time goes in v9:
time: 89.1 us; the launch traced here: 87.5 us
  matrix products  19.4 us (22%)
  Pallas kernels  18.9 us (21%)
  starting transfers between devices  13.3 us (15%)
  other arithmetic  12.7 us (14%)
  blocking collectives  11.4 us (13%)
  local copies, waits for them, and re-layouts  9.59 us (11%)
  waiting for transfers between devices  1.22 us (1%)
  between operations  0.94 us (1%)
    pallas_call x1, Pallas kernels, prefill_output(): pl.pallas_call(output_kernel, grid=(prompts_here,), in_specs=[whole, whol...  18.9 us
    all_to_all x1, blocking collectives, per_device(): normed = lax.all_to_all(normed, 'heads', 0, 0, tiled=True)  11.4 us
    all_to_all x1, starting transfers between devices, per_device(): pieces = lax.all_to_all(pieces, ('heads', 'tp'), 2, 2, tiled=True)  6.91 us
    all_to_all x1, starting transfers between devices, per_device(): arrived = lax.all_to_all(packed, 'heads', 0, 0, tiled=True)  6.38 us
    dot_general x1, matrix products, per_device(): jnp.einsum('tbhk,bhkv->tbhv', query_rot, state_new, preferred_element_typ...  5.85 us
    dot_general x1, matrix products, per_device(): jnp.dot(flat_inputs, w_gate.reshape(model_width, heads_here * value_slice...  4.33 us
    unnamed x15, local copies, waits for them, and re-layouts  4.08 us
    dot_general x1, matrix products, per_device(): jnp.dot(activated, w_out.reshape(heads_here * value_slice, model_width),...  3.03 us
  transfers between devices with their start and end apart: 2, of which 1 were waited for; matrix products, arithmetic and copies ran while one was open for 16% of the time, Pallas kernels for 22%

profile of v9, /device:TPU:1, one launch (start us, length us, event | category | flops | bytes accessed | tf_op | source)
XLA Modules:
  0.0 87.5 jit_solution(13769704488147711643)
XLA Ops:
  0.7 0.8 add_convert_fusion.6
  1.6 0.6 copy-done
  2.2 1.6 %fusion.26 = bf16[64,256]{1,0:T(8,128)(2,1)S(1)} fusion(bf16[64,4096]{1,0:T(8,128)(2,1)} %bitcast.97, bf16[4096,1,1,256]{3,0,2,1:T(8,128)(2,1)S(1)} %copy-done), kind=kOutput, calls=%fused_computation.27 | convolution fusion | flops 134234112 | bytes 2654208 | tf_op jit(solution)/shard_map/dot_general | solution.py:186
  3.9 2.1 %fusion.29 = bf16[64,256]{1,0:T(8,128)(2,1)S(1)} fusion(bf16[64,4096]{1,0:T(8,128)(2,1)S(1)} %bitcast.98, bf16[4096,1,1,256]{3,0,2,1:T(8,128)(2,1)} %param.20), kind=kOutput, calls=%fused_computation.28 | convolution fusion | flops 134234112 | bytes 2654208 | tf_op jit(solution)/shard_map/dot_general | solution.py:189
  6.6 1.4 %convolution_convert_fusion = bf16[64,512]{1,0:T(8,128)(2,1)S(1)} fusion(bf16[64,4096]{1,0:T(8,128)(2,1)S(1)} %bitcast.99, bf16[4096,512]{0,1:T(8,128)(2,1)S(1)} %bitcast.102), kind=kOutput, calls=%fused_computation.19 | convolution fusion | flops 268468224 | bytes 4784128 | tf_op jit(solution)/shard_map/dot_general | solution.py:192
  8.1 0.8 copy.78
  8.9 6.4 %all-to-all-start = ((bf16[8,4,2,1024]{3,1,2,0:T(4,128)(2,1)}), bf16[8,4,2,1024]{3,1,2,0:T(4,128)(2,1)S(1)}, u32[]{:S(2)}, u32[]{:S(2)}) async-start(bf16[8,4,2,1024]{3,1,2,0:T(4,128)(2,1)} %bitcast.94), calls=%async_computation | async-start | bytes 262144 | tf_op jit(solution)/shard_map/all_to_all | solution.py:225
  15.5 2.9 %copy.37 = bf16[2,128,8,256]{1,2,3,0:T(8,128)(2,1)} copy(bf16[2,128,8,256]{3,2,1,0:T(8,128)(2,1)} %k_ref) | data formatting | bytes 2097152 | tf_op args[1]
  18.5 2.7 %convert.2 = f32[2,128,8,128,2]{1,2,4,3,0:T(8,128)} convert(bf16[2,128,8,128,2]{1,2,4,3,0:T(8,128)(2,1)} %bitcast.101) | non-fusion elementwise | flops 524288 | bytes 3145728 | tf_op jit(solution)/shard_map/reshape | solution.py:17
  22.6 1.8 %multiply_subtract_fusion = (f32[2,128,8,128,1]{1,2,4,3,0:T(8,128)S(1)}, f32[2,128,8,128,1]{1,2,4,3,0:T(8,128)S(1)}) fusion(f32[2,128,8,128,2]{1,2,4,3,0:T(8,128)} %convert.2, f32[2,128,128]{1,2,0:T(8,128)S(1)} %get-tuple-element.28, f32[2,128,128]{1,2,0:T(8,128)S(1)} %get-tuple-element.27), kind=kLoop, calls=%fused_computation.33 | loop fusion | flops 1572864 | bytes 4456448 | tf_op jit(solution)/shard_map/sub | solution.py:21
  24.6 1.2 %fusion.7 = bf16[2,128,8,256]{1,2,3,0:T(8,128)(2,1)} fusion(bf16[2,128,8,256]{1,2,3,0:T(8,128)(2,1)S(1)} %bitcast.100, f32[2,128,8]{1,2,0:T(8,128)S(1)} %exponential_select_fusion.1), kind=kLoop, calls=%fused_computation.9 | loop fusion | flops 1572864 | bytes 2105344 | tf_op jit(solution)/shard_map/convert_element_type | solution.py:178
  26.5 5.8 %fusion.18 = f32[4,2,8,512]{3,0,2,1:T(4,128)S(1)} fusion(bf16[2,8,256,512]{3,2,1,0:T(8,128)(2,1)} %prior_ref, f32[2,8]{1,0:T(2,128)S(1)} %multiply_exponential_fusion.1, bf16[2,128,8,512]{3,2,1,0:T(8,128)(2,1)} %v_ref, bf16[2,128,8,256]{1,2,3,0:T(8,128)(2,1)} %fusion.7, f32[4,8]{0,1:T(8,128)S(1)} %multiply_exponential_fusion, ...), kind=kOutput, calls=%fused_computation.18 | convolution fusion | flops 562069504 | bytes 7504064 | tf_op jit(solution)/shard_map/tbhk,bhkv->tbhv/dot_general | solution.py:242
  33.4 11.4 %all_to_all.15 = f32[8,1,4096]{2,1,0:T(1,128)S(1)} all-to-all(f32[8,1,4096]{2,1,0:T(1,128)S(1)} %reshape.395), channel_id=1, replica_groups=mesh['groups'=2,'heads'=8,'tp'=2] {'heads'}, dimensions={0} | all-to-all | bytes 262144 | tf_op jit(solution)/shard_map/all_to_all | solution.py:267
  45.4 1.0 %reduce = f32[8,4096]{1,0:T(8,128)S(1)} reduce(f32[8,1,4096]{2,1,0:T(1,128)S(1)} %all_to_all.15, f32[]{:T(128)} %broadcast.458), dimensions={1}, to_apply=%all_to_all.10.reduce_sub_computation | reduce | bytes 262148 | tf_op jit(solution)/shard_map/all_to_all | solution.py:267
  46.7 4.3 %multiply_convert_fusion = bf16[4,16,8,64]{3,1,2,0:T(8,128)(2,1)S(1)} fusion(f32[4,16,8,64]{3,1,2,0:T(8,128)S(1)} %bitcast.110, bf16[4096,1,8,1,64]{0,4,3,2,1:T(8,128)(2,1)} %param.22, bf16[4,16,4096]{2,1,0:T(8,128)(2,1)S(1)} %copy-done.1), kind=kOutput, calls=%fused_computation.37 | convolution fusion | flops 268632064 | bytes 4915200 | tf_op jit(solution)/shard_map/dot_general | solution.py:197
  51.2 3.0 %fusion.53 = f32[4,16,4096]{2,1,0:T(8,128)S(1)} fusion(bf16[4,16,512]{2,1,0:T(8,128)(2,1)S(1)} %dot_general.51, bf16[512,4096,1]{1,0,2:T(8,128)(2,1)} %bitcast.103), kind=kOutput, calls=%fused_computation.99 | convolution fusion | flops 268435456 | bytes 5308416 | tf_op jit(solution)/shard_map/dot_general | solution.py:277
  54.2 1.2 %copy.76 = f32[4,2,16,8,256]{4,3,1,0,2:T(8,128)} copy(f32[4,2,16,8,256]{4,3,2,1,0:T(8,128)S(1)} %bitcast.105) | data formatting | bytes 2097152 | tf_op jit(solution)/shard_map/reshape | solution.py:291
  55.4 6.9 %all-to-all-start.2 = ((f32[4,16,16,256]{3,1,0,2:T(8,128)}), f32[4,16,16,256]{3,1,0,2:T(8,128)}, u32[]{:S(2)}, u32[]{:S(2)}) async-start(f32[4,16,16,256]{3,1,0,2:T(8,128)} %bitcast.104), calls=%async_computation.2 | async-start | bytes 2097152 | tf_op jit(solution)/shard_map/all_to_all | solution.py:292
  63.0 0.8 copy.49.sin_ref
  63.9 0.8 copy.48.cos_ref
  64.8 0.7 fusion.35.swap_ref
  65.5 18.9 %shard_map.131 = bf16[2,128,8,512]{3,2,1,0:T(8,128)(2,1)} custom-call(f32[8]{0:T(128)} %get-tuple-element.18.rates_ref, s32[2]{0:T(128)} %copy-done.3, bf16[2,128,8,256]{3,2,1,0:T(8,128)(2,1)} %q_ref, bf16[2,128,8,256]{3,2,1,0:T(8,128)(2,1)} %k_ref, bf16[2,128,8,512]{3,2,1,0:T(8,128)(2,1)} %v_ref, bf16[2,8,256,512]{3,2,1,0:T(8,128)(2,1)} %prior_ref, ...), custom_call_target="tpu_custom_call" | custom-call | tf_op jit(solution)/shard_map/pallas_call | solution.py:111
  84.4 1.2 %all-to-all-done.2 = f32[4,16,16,256]{3,1,0,2:T(8,128)} async-done(((f32[4,16,16,256]{3,1,0,2:T(8,128)}), f32[4,16,16,256]{3,1,0,2:T(8,128)}, u32[]{:S(2)}, u32[]{:S(2)}) %all-to-all-start.2) | async-done | bytes 1048608 | tf_op jit(solution)/shard_map/all_to_all | solution.py:292
  85.6 1.9 %reduce_sum.29 = bf16[4,16,256]{2,1,0:T(8,128)(2,1)} reduce(f32[4,16,16,256]{3,1,0,2:T(8,128)} %all-to-all-done.2, f32[]{:T(128)} %constant.94.clone.1), dimensions={2}, to_apply=%region_2.3 | reduce | flops 245760 | bytes 1081348 | tf_op jit(solution)/shard_map/reduce_sum | solution.py:293
  (57 shorter events, 6.2 us)
Async XLA Ops:
  0.6 1.6 %copy-start = (bf16[4096,1,1,256]{3,0,2,1:T(8,128)(2,1)S(1)}, bf16[4096,1,1,256]{3,0,2,1:T(8,128)(2,1)}, u32[]{:S(2)}) copy-start(bf16[4096,1,1,256]{3,0,2,1:T(8,128)(2,1)} %param.19) | copy-start | bytes 6291460
  0.6 3.3 %copy-start.1 = (bf16[4,16,4096]{2,1,0:T(8,128)(2,1)S(1)}, bf16[4,16,4096]{2,1,0:T(8,128)(2,1)}, u32[]{:S(2)}) copy-start(bf16[4,16,4096]{2,1,0:T(8,128)(2,1)} %param.18) | copy-start | bytes 1572868
  2.2 4.4 %copy-start.2 = (bf16[4096,1,8,1,64]{0,4,3,2,1:T(8,128)(2,1)S(1)}, bf16[4096,1,8,1,64]{0,4,3,2,1:T(8,128)(2,1)}, u32[]{:S(2)}) copy-start(bf16[4096,1,8,1,64]{0,4,3,2,1:T(8,128)(2,1)} %param.21) | copy-start | bytes 12582916
  6.6 8.6 %copy-start.4 = (s32[16]{0:T(128)S(1)}, s32[16]{0:T(128)}, u32[]{:S(2)}) copy-start(s32[16]{0:T(128)} %param.17) | copy-start | bytes 196
  8.9 17.0 %all-to-all-start = ((bf16[8,4,2,1024]{3,1,2,0:T(4,128)(2,1)}), bf16[8,4,2,1024]{3,1,2,0:T(4,128)(2,1)S(1)}, u32[]{:S(2)}, u32[]{:S(2)}) async-start(bf16[8,4,2,1024]{3,1,2,0:T(4,128)(2,1)} %bitcast.94), calls=%async_computation | async-start | bytes 262144 | tf_op jit(solution)/shard_map/all_to_all | solution.py:225
  15.4 5.8 %copy-start.3 = (s32[2]{0:T(128)}, s32[2]{0:T(128)S(1)}, u32[]{:S(2)}) copy-start(s32[2]{0:T(128)S(1)} %get-tuple-element.15.live_ref) | copy-start | bytes 28
  18.5 2.8 %copy-start.5 = (f32[16]{0:T(128)S(1)}, f32[16]{0:T(128)}, u32[]{:S(2)}) copy-start(f32[16]{0:T(128)} %param.16) | copy-start | bytes 196
  55.4 30.2 %all-to-all-start.2 = ((f32[4,16,16,256]{3,1,0,2:T(8,128)}), f32[4,16,16,256]{3,1,0,2:T(8,128)}, u32[]{:S(2)}, u32[]{:S(2)}) async-start(f32[4,16,16,256]{3,1,0,2:T(8,128)} %bitcast.104), calls=%async_computation.2 | async-start | bytes 2097152 | tf_op jit(solution)/shard_map/all_to_all | solution.py:292

commit v10 on v9

--- a/solution.py
+++ b/solution.py
@@ -194,10 +194,12 @@
         w_value.reshape(model_width, heads_here * value_slice),
         preferred_element_type=jnp.float32,
     ).astype(jnp.bfloat16)
-    gate_values = jnp.dot(
-        flat_inputs,
-        w_gate.reshape(model_width, heads_here * value_slice),
-        preferred_element_type=jnp.float32,
+    gate_values = lax.optimization_barrier(
+        jnp.dot(
+            flat_inputs,
+            w_gate.reshape(model_width, heads_here * value_slice),
+            preferred_element_type=jnp.float32,
+        )
     )
     steps = jnp.arange(step_total)
     halfway = key_width // 2

time: 89.1 us -> 85.1 us (0.955)
  blocking collectives: 11.4 us -> 0 us
  starting transfers between devices: 13.3 us -> 18.5 us
  waiting for transfers between devices: 1.22 us -> 3.84 us
    all_to_all x1 -> x0, blocking collectives: 11.4 us -> none  [per_device(): normed = lax.all_to_all(normed, 'heads', 0, 0, tiled=True)]
    all_to_all x0 -> x1, starting transfers between devices: none -> 5.44 us  [per_device(): normed = lax.all_to_all(normed, 'heads', 0, 0, tiled=True)]
    all_to_all x0 -> x1, waiting for transfers between devices: none -> 2.62 us  [per_device(): normed = lax.all_to_all(normed, 'heads', 0, 0, tiled=True)]
  transfers between devices with their start and end apart: 2 -> 3, of which waited for: 1 -> 2; matrix products, arithmetic and copies ran while one was open for 16% -> 21% of each run, Pallas kernels for 22% -> 23%
where the time goes in v10:
time: 85.1 us; the launch traced here: 83.5 us
  Pallas kernels  18.9 us (22%)
  matrix products  18.7 us (22%)
  starting transfers between devices  18.5 us (22%)
  other arithmetic  12.7 us (15%)
  local copies, waits for them, and re-layouts  9.85 us (12%)
  waiting for transfers between devices  3.84 us (5%)
  between operations  0.91 us (1%)
    pallas_call x1, Pallas kernels, prefill_output(): pl.pallas_call(output_kernel, grid=(prompts_here,), in_specs=[whole, whol...  18.9 us
    all_to_all x1, starting transfers between devices, per_device(): pieces = lax.all_to_all(pieces, ('heads', 'tp'), 2, 2, tiled=True)  6.72 us
    all_to_all x1, starting transfers between devices, per_device(): arrived = lax.all_to_all(packed, 'heads', 0, 0, tiled=True)  6.38 us
    dot_general x1, matrix products, per_device(): jnp.einsum('tbhk,bhkv->tbhv', query_rot, state_new, preferred_element_typ...  5.85 us
    all_to_all x1, starting transfers between devices, per_device(): normed = lax.all_to_all(normed, 'heads', 0, 0, tiled=True)  5.44 us
    unnamed x15, local copies, waits for them, and re-layouts  4.55 us
    dot_general x1, matrix products, per_device(): jnp.dot(flat_inputs, w_gate.reshape(model_width, heads_here * value_slice...  3.58 us
    dot_general x1, matrix products, per_device(): jnp.dot(activated, w_out.reshape(heads_here * value_slice, model_width),...  3.03 us
  transfers between devices with their start and end apart: 3, of which 2 were waited for; matrix products, arithmetic and copies ran while one was open for 21% of the time, Pallas kernels for 23%

profile of v10, /device:TPU:1, one launch (start us, length us, event | category | flops | bytes accessed | tf_op | source)
XLA Modules:
  0.0 83.5 jit_solution(13586223544120976651)
XLA Ops:
  0.7 0.8 add_convert_fusion.6
  2.2 1.6 %fusion.24 = bf16[64,256]{1,0:T(8,128)(2,1)S(1)} fusion(bf16[64,4096]{1,0:T(8,128)(2,1)} %bitcast.74, bf16[4096,1,1,256]{3,0,2,1:T(8,128)(2,1)S(1)} %copy-done), kind=kOutput, calls=%fused_computation.25 | convolution fusion | flops 134234112 | bytes 2654208 | tf_op jit(solution)/shard_map/dot_general | solution.py:186
  3.9 2.1 %fusion.27 = bf16[64,256]{1,0:T(8,128)(2,1)S(1)} fusion(bf16[64,4096]{1,0:T(8,128)(2,1)S(1)} %bitcast.75, bf16[4096,1,1,256]{3,0,2,1:T(8,128)(2,1)} %param.20), kind=kOutput, calls=%fused_computation.26 | convolution fusion | flops 134234112 | bytes 2654208 | tf_op jit(solution)/shard_map/dot_general | solution.py:189
  6.6 1.4 %convolution_convert_fusion = bf16[64,512]{1,0:T(8,128)(2,1)S(1)} fusion(bf16[64,4096]{1,0:T(8,128)(2,1)S(1)} %bitcast.76, bf16[4096,512]{0,1:T(8,128)(2,1)S(1)} %bitcast.80), kind=kOutput, calls=%fused_computation.17 | convolution fusion | flops 268468224 | bytes 4784128 | tf_op jit(solution)/shard_map/dot_general | solution.py:192
  8.1 0.8 copy.73
  8.9 6.4 %all-to-all-start = ((bf16[8,4,2,1024]{3,1,2,0:T(4,128)(2,1)}), bf16[8,4,2,1024]{3,1,2,0:T(4,128)(2,1)S(1)}, u32[]{:S(2)}, u32[]{:S(2)}) async-start(bf16[8,4,2,1024]{3,1,2,0:T(4,128)(2,1)} %bitcast.73), calls=%async_computation | async-start | bytes 262144 | tf_op jit(solution)/shard_map/all_to_all | solution.py:227
  15.5 2.9 %copy.35 = bf16[2,128,8,256]{1,2,3,0:T(8,128)(2,1)} copy(bf16[2,128,8,256]{3,2,1,0:T(8,128)(2,1)} %k_ref) | data formatting | bytes 2097152 | tf_op args[1]
  18.5 2.7 %convert.2 = f32[2,128,8,128,2]{1,2,4,3,0:T(8,128)} convert(bf16[2,128,8,128,2]{1,2,4,3,0:T(8,128)(2,1)} %bitcast.79) | non-fusion elementwise | flops 524288 | bytes 3145728 | tf_op jit(solution)/shard_map/reshape | solution.py:17
  22.6 1.8 %multiply_subtract_fusion = (f32[2,128,8,128,1]{1,2,4,3,0:T(8,128)S(1)}, f32[2,128,8,128,1]{1,2,4,3,0:T(8,128)S(1)}) fusion(f32[2,128,8,128,2]{1,2,4,3,0:T(8,128)} %convert.2, f32[2,128,128]{1,2,0:T(8,128)S(1)} %get-tuple-element.28, f32[2,128,128]{1,2,0:T(8,128)S(1)} %get-tuple-element.27), kind=kLoop, calls=%fused_computation.31 | loop fusion | flops 1572864 | bytes 4456448 | tf_op jit(solution)/shard_map/sub | solution.py:21
  24.6 1.2 %fusion.5 = bf16[2,128,8,256]{1,2,3,0:T(8,128)(2,1)} fusion(bf16[2,128,8,256]{1,2,3,0:T(8,128)(2,1)S(1)} %bitcast.78, f32[2,128,8]{1,2,0:T(8,128)S(1)} %exponential_select_fusion.1), kind=kLoop, calls=%fused_computation.7 | loop fusion | flops 1572864 | bytes 2105344 | tf_op jit(solution)/shard_map/convert_element_type | solution.py:178
  26.5 5.8 %fusion.16 = f32[4,2,8,512]{3,0,2,1:T(4,128)S(1)} fusion(bf16[2,8,256,512]{3,2,1,0:T(8,128)(2,1)} %prior_ref, f32[2,8]{1,0:T(2,128)S(1)} %multiply_exponential_fusion.1, bf16[2,128,8,512]{3,2,1,0:T(8,128)(2,1)} %v_ref, bf16[2,128,8,256]{1,2,3,0:T(8,128)(2,1)} %fusion.5, f32[4,8]{0,1:T(8,128)S(1)} %multiply_exponential_fusion, ...), kind=kOutput, calls=%fused_computation.16 | convolution fusion | flops 562069504 | bytes 7504064 | tf_op jit(solution)/shard_map/tbhk,bhkv->tbhv/dot_general | solution.py:244
  33.1 0.8 %reshape.390 = f32[8,1,4096]{2,1,0:T(1,128)} reshape(f32[8,4,2,8,64]{4,3,2,1,0:T(8,128)S(1)} %bitcast.85) | data formatting | bytes 262144
  34.0 5.4 %all-to-all-start.1 = ((f32[8,1,4096]{2,1,0:T(1,128)}), f32[8,1,4096]{2,1,0:T(1,128)S(1)}, u32[]{:S(2)}, u32[]{:S(2)}) async-start(f32[8,1,4096]{2,1,0:T(1,128)} %reshape.390), calls=%async_computation.1 | async-start | bytes 262144 | tf_op jit(solution)/shard_map/all_to_all | solution.py:269
  39.4 3.6 %fusion.45 = f32[64,512]{1,0:T(8,128)S(1)} fusion(bf16[64,4096]{1,0:T(8,128)(2,1)S(1)} %bitcast.77, bf16[4096,512]{0,1:T(8,128)(2,1)} %bitcast.81), kind=kOutput, calls=%fused_computation.94 | convolution fusion | flops 268435456 | bytes 4849664 | tf_op jit(solution)/shard_map/dot_general | solution.py:198
  43.0 2.6 %all-to-all-done.1 = f32[8,1,4096]{2,1,0:T(1,128)S(1)} async-done(((f32[8,1,4096]{2,1,0:T(1,128)}), f32[8,1,4096]{2,1,0:T(1,128)S(1)}, u32[]{:S(2)}, u32[]{:S(2)}) %all-to-all-start.1) | async-done | bytes 131104 | tf_op jit(solution)/shard_map/all_to_all | solution.py:269
  46.1 1.0 %reduce = f32[8,4096]{1,0:T(8,128)S(1)} reduce(f32[8,1,4096]{2,1,0:T(1,128)S(1)} %all-to-all-done.1, f32[]{:T(128)} %broadcast.460), dimensions={1}, to_apply=%all_to_all.10.reduce_sub_computation | reduce | bytes 262148 | tf_op jit(solution)/shard_map/all_to_all | solution.py:269
  47.4 3.0 %fusion.46 = f32[4,16,4096]{2,1,0:T(8,128)S(1)} fusion(bf16[4,16,512]{2,1,0:T(8,128)(2,1)S(1)} %bitcast.90, bf16[512,4096,1]{1,0,2:T(8,128)(2,1)} %bitcast.82), kind=kOutput, calls=%fused_computation.95 | convolution fusion | flops 268435456 | bytes 5308416 | tf_op jit(solution)/shard_map/dot_general | solution.py:279
  50.4 1.1 %copy.70 = f32[4,2,16,8,256]{4,3,1,0,2:T(8,128)} copy(f32[4,2,16,8,256]{4,3,2,1,0:T(8,128)S(1)} %bitcast.84) | data formatting | bytes 2097152 | tf_op jit(solution)/shard_map/reshape | solution.py:293
  51.5 6.7 %all-to-all-start.2 = ((f32[4,16,16,256]{3,1,0,2:T(8,128)}), f32[4,16,16,256]{3,1,0,2:T(8,128)}, u32[]{:S(2)}, u32[]{:S(2)}) async-start(f32[4,16,16,256]{3,1,0,2:T(8,128)} %bitcast.83), calls=%async_computation.2 | async-start | bytes 2097152 | tf_op jit(solution)/shard_map/all_to_all | solution.py:294
  59.0 0.8 %copy.46.sin_ref = f32[2,128,256]{2,1,0:T(8,128)} copy(f32[2,128,256]{1,2,0:T(8,128)S(1)} %bitcast.87) | data formatting | bytes 524288 | tf_op jit(solution)/shard_map/reshape | solution.py:80
  59.9 0.8 copy.45.cos_ref
  61.4 18.9 %shard_map.131 = bf16[2,128,8,512]{3,2,1,0:T(8,128)(2,1)} custom-call(f32[8]{0:T(128)} %get-tuple-element.18.rates_ref, s32[2]{0:T(128)} %copy-done.3, bf16[2,128,8,256]{3,2,1,0:T(8,128)(2,1)} %q_ref, bf16[2,128,8,256]{3,2,1,0:T(8,128)(2,1)} %k_ref, bf16[2,128,8,512]{3,2,1,0:T(8,128)(2,1)} %v_ref, bf16[2,8,256,512]{3,2,1,0:T(8,128)(2,1)} %prior_ref, ...), custom_call_target="tpu_custom_call" | custom-call | tf_op jit(solution)/shard_map/pallas_call | solution.py:111
  80.3 1.2 %all-to-all-done.2 = f32[4,16,16,256]{3,1,0,2:T(8,128)} async-done(((f32[4,16,16,256]{3,1,0,2:T(8,128)}), f32[4,16,16,256]{3,1,0,2:T(8,128)}, u32[]{:S(2)}, u32[]{:S(2)}) %all-to-all-start.2) | async-done | bytes 1048608 | tf_op jit(solution)/shard_map/all_to_all | solution.py:294
  81.6 1.9 %reduce_sum.29 = bf16[4,16,256]{2,1,0:T(8,128)(2,1)} reduce(f32[4,16,16,256]{3,1,0,2:T(8,128)} %all-to-all-done.2, f32[]{:T(128)} %constant.94.clone.1), dimensions={2}, to_apply=%region_2.3 | reduce | flops 245760 | bytes 1081348 | tf_op jit(solution)/shard_map/reduce_sum | solution.py:295
  (57 shorter events, 7.0 us)
Async XLA Ops:
  0.6 1.6 %copy-start = (bf16[4096,1,1,256]{3,0,2,1:T(8,128)(2,1)S(1)}, bf16[4096,1,1,256]{3,0,2,1:T(8,128)(2,1)}, u32[]{:S(2)}) copy-start(bf16[4096,1,1,256]{3,0,2,1:T(8,128)(2,1)} %param.19) | copy-start | bytes 6291460
  0.6 3.3 %copy-start.1 = (bf16[4,16,4096]{2,1,0:T(8,128)(2,1)S(1)}, bf16[4,16,4096]{2,1,0:T(8,128)(2,1)}, u32[]{:S(2)}) copy-start(bf16[4,16,4096]{2,1,0:T(8,128)(2,1)} %param.18) | copy-start | bytes 1572868
  2.2 4.4 %copy-start.2 = (bf16[4096,1,8,1,64]{0,4,3,2,1:T(8,128)(2,1)S(1)}, bf16[4096,1,8,1,64]{0,4,3,2,1:T(8,128)(2,1)}, u32[]{:S(2)}) copy-start(bf16[4096,1,8,1,64]{0,4,3,2,1:T(8,128)(2,1)} %param.21) | copy-start | bytes 12582916
  6.6 8.7 %copy-start.4 = (s32[16]{0:T(128)S(1)}, s32[16]{0:T(128)}, u32[]{:S(2)}) copy-start(s32[16]{0:T(128)} %param.17) | copy-start | bytes 196
  8.9 17.0 %all-to-all-start = ((bf16[8,4,2,1024]{3,1,2,0:T(4,128)(2,1)}), bf16[8,4,2,1024]{3,1,2,0:T(4,128)(2,1)S(1)}, u32[]{:S(2)}, u32[]{:S(2)}) async-start(bf16[8,4,2,1024]{3,1,2,0:T(4,128)(2,1)} %bitcast.73), calls=%async_computation | async-start | bytes 262144 | tf_op jit(solution)/shard_map/all_to_all | solution.py:227
  15.4 5.8 %copy-start.3 = (s32[2]{0:T(128)}, s32[2]{0:T(128)S(1)}, u32[]{:S(2)}) copy-start(s32[2]{0:T(128)S(1)} %get-tuple-element.15.live_ref) | copy-start | bytes 28
  18.5 2.8 %copy-start.5 = (f32[16]{0:T(128)S(1)}, f32[16]{0:T(128)}, u32[]{:S(2)}) copy-start(f32[16]{0:T(128)} %param.16) | copy-start | bytes 196
  34.0 11.6 %all-to-all-start.1 = ((f32[8,1,4096]{2,1,0:T(1,128)}), f32[8,1,4096]{2,1,0:T(1,128)S(1)}, u32[]{:S(2)}, u32[]{:S(2)}) async-start(f32[8,1,4096]{2,1,0:T(1,128)} %reshape.390), calls=%async_computation.1 | async-start | bytes 262144 | tf_op jit(solution)/shard_map/all_to_all | solution.py:269
  51.5 30.0 %all-to-all-start.2 = ((f32[4,16,16,256]{3,1,0,2:T(8,128)}), f32[4,16,16,256]{3,1,0,2:T(8,128)}, u32[]{:S(2)}, u32[]{:S(2)}) async-start(f32[4,16,16,256]{3,1,0,2:T(8,128)} %bitcast.83), calls=%async_computation.2 | async-start | bytes 2097152 | tf_op jit(solution)/shard_map/all_to_all | solution.py:294

commit v11 on v10

--- a/solution.py
+++ b/solution.py
@@ -73,40 +73,19 @@
     halfway = key_width // 2
     offsets = jnp.arange(span_len)
     positions = (span_start[:, None] + offsets[None, :]).astype(jnp.float32)
-    frequency = 10000.0 ** (-jnp.arange(halfway).astype(jnp.float32) / halfway)
+    lane = jnp.arange(key_width)
+    frequency = 10000.0 ** (-(lane // 2).astype(jnp.float32) / halfway)
     angles = positions[..., None] * frequency
-    cosine = jnp.repeat(jnp.cos(angles), 2, axis=-1)
-    sine_part = jnp.sin(angles)
-    sine_part = jnp.stack([-sine_part, sine_part], -1).reshape(cosine.shape)
-    lane = jnp.arange(key_width)
+    cosine = jnp.cos(angles)
+    sine_part = jnp.where(lane % 2 == 0, -1.0, 1.0) * jnp.sin(angles)
     swap = (lane[:, None] == (lane[None, :] ^ 1)).astype(jnp.bfloat16)
-    valid_rows = offsets[None, :] < live_count[:, None]
-    lead_decay = jnp.exp(-local_rates[:, None] * (offsets[None, :] + 1).astype(jnp.float32))
-    remaining = (live_count[:, None] - 1 - offsets[None, :]).astype(jnp.float32)
-    key_weight = jnp.where(
-        valid_rows[:, None, :],
-        jnp.exp(-local_rates[None, :, None] * jnp.maximum(remaining, 0.0)[:, None, :]),
-        0.0,
-    )
-    kept_share = jnp.exp(-local_rates[None, :] * live_count[:, None].astype(jnp.float32))
-    shape_rows = key_weight.shape
-    rows = jnp.stack(
-        [
-            jnp.broadcast_to(lead_decay[None], shape_rows),
-            jnp.broadcast_to(valid_rows[:, None, :].astype(jnp.float32), shape_rows),
-            key_weight,
-            jnp.broadcast_to(kept_share[:, :, None], shape_rows),
-        ]
-        + [jnp.zeros(shape_rows, jnp.float32)] * 4,
-        -1,
-    )
-    return cosine, sine_part, swap, rows, valid_rows
+    return cosine, sine_part, swap
 
 
 def prefill_output(query_span, key_span, value_span, prior_state, local_rates, tables, live_count):
     prompts_here, span_len, heads_here, key_width = query_span.shape
     value_width = value_span.shape[3]
-    cosine, sine_part, swap, rows, valid_rows = tables
+    cosine, sine_part, swap = tables
     whole = pl.BlockSpec(memory_space=pltpu.SMEM)
     return pl.pallas_call(
         output_kernel,
@@ -162,7 +141,6 @@
     )
     span_start = span_len * ((local_lengths - 1) // span_len)
     live_count = local_lengths - span_start
-    tables = prefill_tables(key_width, span_len, local_rates, span_start, live_count)
     offsets = jnp.arange(span_len)
     positions = (span_start[:, None] + offsets[None, :]).astype(jnp.float32)
     keys = (
@@ -266,7 +244,12 @@
     normed = norm_with(readout, read_mean, read_square)
     normed = normed.reshape(step_total, prompts_here, heads_here, slots, value_slice)
     normed = normed.transpose(3, 0, 1, 2, 4)
+    table_rates, table_start, table_live, normed = lax.optimization_barrier(
+        (local_rates, span_start, live_count, normed)
+    )
+    tables = prefill_tables(key_width, span_len, table_rates, table_start, table_live)
     normed = lax.all_to_all(normed, "heads", 0, 0, tiled=True)
+    normed, tables = lax.optimization_barrier((normed, tables))
     normed = normed.transpose(1, 0, 2, 3, 4).reshape(
         step_total, total_prompts, heads_here, value_slice
     )

time: 85.1 us -> 89.7 us (1.054)
  waiting for transfers between devices: 3.84 us -> 8.54 us
  local copies, waits for them, and re-layouts: 9.85 us -> 11 us
    all_to_all x1, waiting for transfers between devices: 1.22 us -> 4.26 us  [per_device(): pieces = lax.all_to_all(pieces, ('heads', 'tp'), 2, 2, tiled=True)]
    reshape x3, local copies, waits for them, and re-layouts: 0.34 us -> 2.76 us  [per_device(): value_own = arrived[..., 2 * key_piece:].reshape(slots, step_total, promp...]
    mul x0 -> x1, other arithmetic: none -> 1.83 us  [prefill_tables(): sine_part = jnp.where(lane % 2 == 0, -1.0, 1.0) * jnp.sin(angles)]
    reshape x2 -> x0, local copies, waits for them, and re-layouts: 1.67 us -> none  [the longest x1 0.84 us: prefill_tables(): sine_part = jnp.stack([-sine_part, sine_part], -1).reshape(cosine.shape)]
    all_to_all x1, waiting for transfers between devices: 2.62 us -> 4.28 us  [per_device(): normed = lax.all_to_all(normed, 'heads', 0, 0, tiled=True)]
    sub x1, other arithmetic: 1.8 us -> 0.26 us  [rotate(): even_part * cosine - odd_part * sine_part]
    reduce_sum x1, other arithmetic: 1.92 us -> 0.68 us  [per_device(): decode_out = jnp.sum(pieces, 2).astype(jnp.bfloat16)]
    convert_element_type x1, other arithmetic: 1.18 us -> 0.21 us  [per_device(): (keys.astype(jnp.float32) * key_weight[..., None]).astype(jnp.bfloat16)]
  transfers between devices with their start and end apart: 3 -> 3, of which waited for: 2 -> 2; matrix products, arithmetic and copies ran while one was open for 21% -> 18% of each run, Pallas kernels for 23% -> 21%
where the time goes in v11:
time: 89.7 us; the launch traced here: 88.2 us
  Pallas kernels  18.9 us (21%)
  matrix products  18.6 us (21%)
  starting transfers between devices  18.1 us (20%)
  other arithmetic  12.2 us (14%)
  local copies, waits for them, and re-layouts  11 us (12%)
  waiting for transfers between devices  8.54 us (10%)
  between operations  0.91 us (1%)
    pallas_call x1, Pallas kernels, prefill_output(): pl.pallas_call(output_kernel, grid=(prompts_here,), in_specs=[whole, whol...  18.9 us
    all_to_all x1, starting transfers between devices, per_device(): arrived = lax.all_to_all(packed, 'heads', 0, 0, tiled=True)  6.38 us
    all_to_all x1, starting transfers between devices, per_device(): pieces = lax.all_to_all(pieces, ('heads', 'tp'), 2, 2, tiled=True)  6.29 us
    dot_general x1, matrix products, per_device(): jnp.einsum('tbhk,bhkv->tbhv', query_rot, state_new, preferred_element_typ...  5.59 us
    all_to_all x1, starting transfers between devices, per_device(): normed = lax.all_to_all(normed, 'heads', 0, 0, tiled=True)  5.44 us
    unnamed x24, local copies, waits for them, and re-layouts  4.49 us
    all_to_all x1, waiting for transfers between devices, per_device(): normed = lax.all_to_all(normed, 'heads', 0, 0, tiled=True)  4.28 us
    all_to_all x1, waiting for transfers between devices, per_device(): pieces = lax.all_to_all(pieces, ('heads', 'tp'), 2, 2, tiled=True)  4.26 us
  transfers between devices with their start and end apart: 3, of which 2 were waited for; matrix products, arithmetic and copies ran while one was open for 18% of the time, Pallas kernels for 21%

profile of v11, /device:TPU:1, one launch (start us, length us, event | category | flops | bytes accessed | tf_op | source)
XLA Modules:
  0.0 88.2 jit_solution(8531383887314079972)
XLA Ops:
  0.7 0.8 add_convert_fusion.6
  2.2 1.6 %fusion.24 = bf16[64,256]{1,0:T(8,128)(2,1)S(1)} fusion(bf16[64,4096]{1,0:T(8,128)(2,1)} %bitcast.72, bf16[4096,1,1,256]{3,0,2,1:T(8,128)(2,1)S(1)} %copy-done), kind=kOutput, calls=%fused_computation.25 | convolution fusion | flops 134234112 | bytes 2654208 | tf_op jit(solution)/shard_map/dot_general | solution.py:164
  3.9 2.1 %fusion.27 = bf16[64,256]{1,0:T(8,128)(2,1)S(1)} fusion(bf16[64,4096]{1,0:T(8,128)(2,1)S(1)} %bitcast.73, bf16[4096,1,1,256]{3,0,2,1:T(8,128)(2,1)} %param.20), kind=kOutput, calls=%fused_computation.26 | convolution fusion | flops 134234112 | bytes 2654208 | tf_op jit(solution)/shard_map/dot_general | solution.py:167
  6.6 1.4 %convolution_convert_fusion = bf16[64,512]{1,0:T(8,128)(2,1)S(1)} fusion(bf16[64,4096]{1,0:T(8,128)(2,1)S(1)} %bitcast.74, bf16[4096,512]{0,1:T(8,128)(2,1)S(1)} %bitcast.78), kind=kOutput, calls=%fused_computation.17 | convolution fusion | flops 268468224 | bytes 4784128 | tf_op jit(solution)/shard_map/dot_general | solution.py:170
  8.1 0.7 copy.56
  8.9 6.4 %all-to-all-start = ((bf16[8,4,2,1024]{3,1,2,0:T(4,128)(2,1)}), bf16[8,4,2,1024]{3,1,2,0:T(4,128)(2,1)S(1)}, u32[]{:S(2)}, u32[]{:S(2)}) async-start(bf16[8,4,2,1024]{3,1,2,0:T(4,128)(2,1)} %bitcast.71), calls=%async_computation | async-start | bytes 262144 | tf_op jit(solution)/shard_map/all_to_all | solution.py:205
  15.6 3.0 %copy.21 = bf16[2,128,8,256]{1,2,3,0:T(8,128)(2,1)} copy(bf16[2,128,8,256]{3,2,1,0:T(8,128)(2,1)} %k_ref) | data formatting | bytes 2097152 | tf_op args[1]
  18.5 2.7 %convert.2 = f32[2,128,8,128,2]{1,2,4,3,0:T(8,128)} convert(bf16[2,128,8,128,2]{1,2,4,3,0:T(8,128)(2,1)} %bitcast.77) | non-fusion elementwise | flops 524288 | bytes 3145728 | tf_op jit(solution)/shard_map/reshape | solution.py:17
  23.3 3.7 %fusion.51 = f32[64,512]{1,0:T(8,128)S(1)} fusion(bf16[64,4096]{1,0:T(8,128)(2,1)S(1)} %bitcast.75, bf16[4096,512]{0,1:T(8,128)(2,1)} %bitcast.79), kind=kOutput, calls=%fused_computation.107 | convolution fusion | flops 268435456 | bytes 4849664 | tf_op jit(solution)/shard_map/dot_general | solution.py:176
  30.3 1.0 %reshape.386 = bf16[8,4,2,8,64]{4,3,1,2,0:T(8,128)(2,1)S(1)} reshape(bf16[8,4,2,512]{3,1,2,0:T(4,128)(2,1)} %slice.23) | data formatting | bytes 131072 | tf_op jit(solution)/shard_map/reshape | solution.py:218
  31.3 0.7 copy.55
  32.0 1.0 %reshape.387 = bf16[4,2,8,512]{3,0,2,1:T(4,128)(2,1)S(1)} reshape(bf16[4,2,8,8,64]{4,3,0,2,1:T(8,128)(2,1)} %bitcast.85) | data formatting | bytes 131072 | tf_op jit(solution)/shard_map/reshape | solution.py:220
  33.2 5.6 %fusion.16 = f32[4,2,8,512]{3,0,2,1:T(4,128)S(1)} fusion(bf16[2,8,256,512]{3,2,1,0:T(8,128)(2,1)} %prior_ref, f32[2,8]{1,0:T(2,128)} %multiply_exponential_fusion.1, bf16[2,128,8,512]{3,2,1,0:T(8,128)(2,1)} %v_ref, bf16[2,128,8,256]{1,2,3,0:T(8,128)(2,1)S(1)} %fusion.5, f32[4,8]{0,1:T(8,128)} %multiply_exponential_fusion, ...), kind=kOutput, calls=%fused_computation.16 | convolution fusion | flops 562069504 | bytes 7504064 | tf_op jit(solution)/shard_map/tbhk,bhkv->tbhv/dot_general | solution.py:222
  39.6 0.8 reshape.396
  40.5 5.4 %all-to-all-start.1 = ((f32[8,1,4096]{2,1,0:T(1,128)}), f32[8,1,4096]{2,1,0:T(1,128)S(1)}, u32[]{:S(2)}, u32[]{:S(2)}) async-start(f32[8,1,4096]{2,1,0:T(1,128)} %reshape.396), calls=%async_computation.1 | async-start | bytes 262144 | tf_op jit(solution)/shard_map/all_to_all | solution.py:251
  46.0 1.8 %fusion.32 = (f32[2,128,256]{2,1,0:T(8,128)}, f32[2,128,256]{2,1,0:T(8,128)}) fusion(f32[256]{0:T(256)S(1)} %copy-done.4, f32[256]{0:T(256)S(1)} %copy-done.5, f32[2,128]{1,0:T(2,128)S(1)} %add_convert_fusion.7), kind=kLoop, calls=%fused_computation.34 | loop fusion | flops 131072 | bytes 527360 | tf_op jit(solution)/shard_map/mul | solution.py:80
  47.8 4.3 %all-to-all-done.1 = f32[8,1,4096]{2,1,0:T(1,128)S(1)} async-done(((f32[8,1,4096]{2,1,0:T(1,128)}), f32[8,1,4096]{2,1,0:T(1,128)S(1)}, u32[]{:S(2)}, u32[]{:S(2)}) %all-to-all-start.1) | async-done | bytes 131104 | tf_op jit(solution)/shard_map/all_to_all | solution.py:251
  52.6 1.0 %reduce = f32[8,4096]{1,0:T(8,128)S(1)} reduce(f32[8,1,4096]{2,1,0:T(1,128)S(1)} %all-to-all-done.1, f32[]{:T(128)} %broadcast.506), dimensions={1}, to_apply=%all_to_all.10.reduce_sub_computation | reduce | bytes 262148 | tf_op jit(solution)/shard_map/all_to_all | solution.py:251
  53.9 3.0 %fusion.52 = f32[4,16,4096]{2,1,0:T(8,128)S(1)} fusion(bf16[4,16,512]{2,1,0:T(8,128)(2,1)S(1)} %bitcast.86, bf16[512,4096,1]{1,0,2:T(8,128)(2,1)} %bitcast.80), kind=kOutput, calls=%fused_computation.108 | convolution fusion | flops 268435456 | bytes 5308416 | tf_op jit(solution)/shard_map/dot_general | solution.py:262
  56.9 1.1 %copy.53 = f32[4,2,16,8,256]{4,3,1,0,2:T(8,128)} copy(f32[4,2,16,8,256]{4,3,2,1,0:T(8,128)S(1)} %bitcast.82) | data formatting | bytes 2097152 | tf_op jit(solution)/shard_map/reshape | solution.py:276
  58.0 6.3 %all-to-all-start.2 = ((f32[4,16,16,256]{3,1,0,2:T(8,128)}), f32[4,16,16,256]{3,1,0,2:T(8,128)S(1)}, u32[]{:S(2)}, u32[]{:S(2)}) async-start(f32[4,16,16,256]{3,1,0,2:T(8,128)} %bitcast.81), calls=%async_computation.2 | async-start | bytes 2097152 | tf_op jit(solution)/shard_map/all_to_all | solution.py:277
  64.3 18.9 %shard_map.131 = bf16[2,128,8,512]{3,2,1,0:T(8,128)(2,1)} custom-call(f32[8]{0:T(128)} %get-tuple-element.30.rates_ref, s32[2]{0:T(128)} %copy-done.6, bf16[2,128,8,256]{3,2,1,0:T(8,128)(2,1)} %q_ref, bf16[2,128,8,256]{3,2,1,0:T(8,128)(2,1)} %k_ref, bf16[2,128,8,512]{3,2,1,0:T(8,128)(2,1)} %v_ref, bf16[2,8,256,512]{3,2,1,0:T(8,128)(2,1)} %prior_ref, ...), custom_call_target="tpu_custom_call" | custom-call | tf_op jit(solution)/shard_map/pallas_call | solution.py:90
  83.3 4.3 %all-to-all-done.2 = f32[4,16,16,256]{3,1,0,2:T(8,128)S(1)} async-done(((f32[4,16,16,256]{3,1,0,2:T(8,128)}), f32[4,16,16,256]{3,1,0,2:T(8,128)S(1)}, u32[]{:S(2)}, u32[]{:S(2)}) %all-to-all-start.2) | async-done | bytes 1048608 | tf_op jit(solution)/shard_map/all_to_all | solution.py:277
  87.5 0.7 reduce_sum.29
  (64 shorter events, 8.9 us)
Async XLA Ops:
  0.6 1.6 %copy-start = (bf16[4096,1,1,256]{3,0,2,1:T(8,128)(2,1)S(1)}, bf16[4096,1,1,256]{3,0,2,1:T(8,128)(2,1)}, u32[]{:S(2)}) copy-start(bf16[4096,1,1,256]{3,0,2,1:T(8,128)(2,1)} %param.19) | copy-start | bytes 6291460
  0.6 3.3 %copy-start.2 = (bf16[4,16,4096]{2,1,0:T(8,128)(2,1)S(1)}, bf16[4,16,4096]{2,1,0:T(8,128)(2,1)}, u32[]{:S(2)}) copy-start(bf16[4,16,4096]{2,1,0:T(8,128)(2,1)} %param.18) | copy-start | bytes 1572868
  2.2 4.4 %copy-start.3 = (bf16[4096,1,8,1,64]{0,4,3,2,1:T(8,128)(2,1)S(1)}, bf16[4096,1,8,1,64]{0,4,3,2,1:T(8,128)(2,1)}, u32[]{:S(2)}) copy-start(bf16[4096,1,8,1,64]{0,4,3,2,1:T(8,128)(2,1)} %param.21) | copy-start | bytes 12582916
  6.6 8.6 %copy-start.7 = (s32[16]{0:T(128)S(1)}, s32[16]{0:T(128)}, u32[]{:S(2)}) copy-start(s32[16]{0:T(128)} %param.17) | copy-start | bytes 196
  8.9 20.8 %all-to-all-start = ((bf16[8,4,2,1024]{3,1,2,0:T(4,128)(2,1)}), bf16[8,4,2,1024]{3,1,2,0:T(4,128)(2,1)S(1)}, u32[]{:S(2)}, u32[]{:S(2)}) async-start(bf16[8,4,2,1024]{3,1,2,0:T(4,128)(2,1)} %bitcast.71), calls=%async_computation | async-start | bytes 262144 | tf_op jit(solution)/shard_map/all_to_all | solution.py:205
  15.4 5.9 %copy-start.6 = (s32[2]{0:T(128)}, s32[2]{0:T(128)S(1)}, u32[]{:S(2)}) copy-start(s32[2]{0:T(128)S(1)} %get-tuple-element.27.live_ref) | copy-start | bytes 28
  15.4 5.9 %copy-start.8 = (s32[2]{0:T(128)}, s32[2]{0:T(128)S(1)}, u32[]{:S(2)}) copy-start(s32[2]{0:T(128)S(1)} %get-tuple-element.14) | copy-start | bytes 28
  18.5 2.8 %copy-start.10 = (f32[16]{0:T(128)S(1)}, f32[16]{0:T(128)}, u32[]{:S(2)}) copy-start(f32[16]{0:T(128)} %param.16) | copy-start | bytes 196
  23.3 4.3 %copy-start.1 = (f32[2,128,8,128,2]{1,2,4,3,0:T(8,128)S(1)}, f32[2,128,8,128,2]{1,2,4,3,0:T(8,128)}, u32[]{:S(2)}) copy-start(f32[2,128,8,128,2]{1,2,4,3,0:T(8,128)} %convert.2) | copy-start | bytes 6291460
  38.8 7.1 %copy-start.9 = (s32[2]{0:T(128)S(1)}, s32[2]{0:T(128)}, u32[]{:S(2)}) copy-start(s32[2]{0:T(128)} %copy-done.8) | copy-start | bytes 28
  38.8 7.2 %copy-start.4 = (f32[256]{0:T(256)S(1)}, f32[256]{0:T(256)}, u32[]{:S(2)}) copy-start(f32[256]{0:T(256)} %get-tuple-element.44) | copy-start | bytes 3076
  38.8 7.2 %copy-start.5 = (f32[256]{0:T(256)S(1)}, f32[256]{0:T(256)}, u32[]{:S(2)}) copy-start(f32[256]{0:T(256)} %get-tuple-element.45) | copy-start | bytes 3076
  40.5 11.6 %all-to-all-start.1 = ((f32[8,1,4096]{2,1,0:T(1,128)}), f32[8,1,4096]{2,1,0:T(1,128)S(1)}, u32[]{:S(2)}, u32[]{:S(2)}) async-start(f32[8,1,4096]{2,1,0:T(1,128)} %reshape.396), calls=%async_computation.1 | async-start | bytes 262144 | tf_op jit(solution)/shard_map/all_to_all | solution.py:251
  58.0 29.5 %all-to-all-start.2 = ((f32[4,16,16,256]{3,1,0,2:T(8,128)}), f32[4,16,16,256]{3,1,0,2:T(8,128)S(1)}, u32[]{:S(2)}, u32[]{:S(2)}) async-start(f32[4,16,16,256]{3,1,0,2:T(8,128)} %bitcast.81), calls=%async_computation.2 | async-start | bytes 2097152 | tf_op jit(solution)/shard_map/all_to_all | solution.py:277

commit v12 on v10

--- a/solution.py
+++ b/solution.py
@@ -165,8 +165,11 @@
     tables = prefill_tables(key_width, span_len, local_rates, span_start, live_count)
     offsets = jnp.arange(span_len)
     positions = (span_start[:, None] + offsets[None, :]).astype(jnp.float32)
+    cosine, sine_part, swap = tables[:3]
+    key_partner = jnp.einsum("bihk,kl->bihl", key_span, swap, preferred_element_type=jnp.float32)
     keys = (
-        rotate(key_span.astype(jnp.float32), positions[:, :, None]) * key_width ** (-0.5)
+        (key_span.astype(jnp.float32) * cosine[:, :, None, :] + key_partner * sine_part[:, :, None, :])
+        * key_width ** (-0.5)
     ).astype(jnp.bfloat16)
     valid_rows = offsets[None, :] < live_count[:, None]
     remaining = (live_count[:, None] - 1 - offsets[None, :]).astype(jnp.float32)

time: 85.1 us -> 83.3 us (0.979)
  local copies, waits for them, and re-layouts: 9.85 us -> 5.49 us
  matrix products: 18.7 us -> 22.3 us
  other arithmetic: 12.7 us -> 9.19 us
  waiting for transfers between devices: 3.84 us -> 6.31 us
    dot_general x0 -> x1, matrix products: none -> 3.22 us  [per_device(): jnp.einsum('bihk,kl->bihl', key_span, swap, preferred_element_type=jnp.fl...]
    unnamed x15 -> x24, local copies, waits for them, and re-layouts: 4.55 us -> 1.63 us
    reshape x1 -> x0, other arithmetic: 2.72 us -> none  [rotate(): paired = values.reshape(values.shape[:-1] + (halfway, 2))]
    all_to_all x1, waiting for transfers between devices: 1.22 us -> 3.69 us  [per_device(): pieces = lax.all_to_all(pieces, ('heads', 'tp'), 2, 2, tiled=True)]
    sub x1 -> x0, other arithmetic: 1.8 us -> none  [rotate(): even_part * cosine - odd_part * sine_part]
    reshape x2 -> x0, local copies, waits for them, and re-layouts: 1.67 us -> none  [the longest x1 0.84 us: prefill_tables(): sine_part = jnp.stack([-sine_part, sine_part], -1).reshape(cosine.shape)]
    convert_element_type x4 -> x2, other arithmetic: 2.13 us -> 0.75 us  [the longest x1 0.68 us: prefill_tables(): swap = (lane[:, None] == lane[None, :] ^ 1).astype(jnp.bfloat16)]
  transfers between devices with their start and end apart: 3 -> 3, of which waited for: 2 -> 2; matrix products, arithmetic and copies ran while one was open for 21% -> 15% of each run, Pallas kernels for 23% -> 23%
where the time goes in v12:
time: 83.3 us; the launch traced here: 81.8 us
  matrix products  22.3 us (27%)
  Pallas kernels  18.9 us (23%)
  starting transfers between devices  18.6 us (22%)
  other arithmetic  9.19 us (11%)
  waiting for transfers between devices  6.31 us (8%)
  local copies, waits for them, and re-layouts  5.49 us (7%)
  between operations  0.99 us (1%)
    pallas_call x1, Pallas kernels, prefill_output(): pl.pallas_call(output_kernel, grid=(prompts_here,), in_specs=[whole, whol...  18.9 us
    all_to_all x1, starting transfers between devices, per_device(): pieces = lax.all_to_all(pieces, ('heads', 'tp'), 2, 2, tiled=True)  6.74 us
    all_to_all x1, starting transfers between devices, per_device(): arrived = lax.all_to_all(packed, 'heads', 0, 0, tiled=True)  6.39 us
    dot_general x1, matrix products, per_device(): jnp.einsum('tbhk,bhkv->tbhv', query_rot, state_new, preferred_element_typ...  6.24 us
    all_to_all x1, starting transfers between devices, per_device(): normed = lax.all_to_all(normed, 'heads', 0, 0, tiled=True)  5.44 us
    all_to_all x1, waiting for transfers between devices, per_device(): pieces = lax.all_to_all(pieces, ('heads', 'tp'), 2, 2, tiled=True)  3.69 us
    dot_general x1, matrix products, per_device(): jnp.dot(flat_inputs, w_gate.reshape(model_width, heads_here * value_slice...  3.57 us
    dot_general x1, matrix products, per_device(): jnp.einsum('bihk,kl->bihl', key_span, swap, preferred_element_type=jnp.fl...  3.22 us
  transfers between devices with their start and end apart: 3, of which 2 were waited for; matrix products, arithmetic and copies ran while one was open for 15% of the time, Pallas kernels for 23%

profile of v12, /device:TPU:1, one launch (start us, length us, event | category | flops | bytes accessed | tf_op | source)
XLA Modules:
  0.0 81.8 jit_solution(4260740840679648405)
XLA Ops:
  0.7 0.8 add_convert_fusion.6
  1.6 0.6 copy-done
  2.2 1.6 %fusion.28 = bf16[64,256]{1,0:T(8,128)(2,1)S(1)} fusion(bf16[64,4096]{1,0:T(8,128)(2,1)} %bitcast.86, bf16[4096,1,1,256]{3,0,2,1:T(8,128)(2,1)S(1)} %copy-done), kind=kOutput, calls=%fused_computation.27 | convolution fusion | flops 134234112 | bytes 2654208 | tf_op jit(solution)/shard_map/dot_general | solution.py:192
  3.9 2.1 %fusion.25 = bf16[64,256]{1,0:T(8,128)(2,1)S(1)} fusion(bf16[64,4096]{1,0:T(8,128)(2,1)S(1)} %bitcast.87, bf16[4096,1,1,256]{3,0,2,1:T(8,128)(2,1)} %param.19), kind=kOutput, calls=%fused_computation.26 | convolution fusion | flops 134234112 | bytes 2654208 | tf_op jit(solution)/shard_map/dot_general | solution.py:189
  6.7 1.4 %convolution_convert_fusion = bf16[64,512]{1,0:T(8,128)(2,1)S(1)} fusion(bf16[64,4096]{1,0:T(8,128)(2,1)S(1)} %bitcast.88, bf16[4096,512]{0,1:T(8,128)(2,1)S(1)} %bitcast.90), kind=kOutput, calls=%fused_computation.18 | convolution fusion | flops 268468224 | bytes 4784128 | tf_op jit(solution)/shard_map/dot_general | solution.py:195
  8.1 0.8 copy.77
  8.9 6.4 %all-to-all-start = ((bf16[8,4,2,1024]{3,1,2,0:T(4,128)(2,1)}), bf16[8,4,2,1024]{3,1,2,0:T(4,128)(2,1)S(1)}, u32[]{:S(2)}, u32[]{:S(2)}) async-start(bf16[8,4,2,1024]{3,1,2,0:T(4,128)(2,1)} %bitcast.85), calls=%async_computation | async-start | bytes 262144 | tf_op jit(solution)/shard_map/all_to_all | solution.py:230
  17.1 0.6 convert_maximum_fusion.1
  18.3 0.7 multiply_exponential_fusion.1
  19.6 0.8 %exponential_select_fusion = f32[2,128,8]{2,1,0:T(8,128)S(1)} fusion(f32[2,128]{1,0:T(2,128)} %convert_maximum_fusion.1, f32[8]{0:T(128)S(1)} %get-tuple-element.17, pred[2,128]{1,0:T(4,128)(4,1)} %iota_compare_fusion.3), kind=kLoop, calls=%fused_computation.42 | loop fusion | flops 4096 | bytes 9504 | tf_op jit(solution)/shard_map/jit(_where)/select_n | solution.py:176
  20.4 3.2 %multiply_convert_fusion = bf16[2,128,8,256]{3,2,1,0:T(8,128)(2,1)} fusion(bf16[2,128,8,256]{3,2,1,0:T(8,128)(2,1)} %k_ref, f32[2,128,8]{2,1,0:T(8,128)S(1)} %exponential_select_fusion, f32[2,128,256]{2,1,0:T(8,128)S(1)} %copy.39.sin_ref, f32[2,128,256]{2,1,0:T(8,128)S(1)} %copy.37.cos_ref, s32[256]{0:T(256)} %copy-done.7), kind=kOutput, calls=%fused_computation.13 | convolution fusion | flops 273219584 | bytes 2630656 | tf_op jit(solution)/shard_map/bihk,kl->bihl/dot_general | solution.py:169
  24.4 6.2 %fusion.17 = f32[4,2,8,512]{3,0,2,1:T(4,128)S(1)} fusion(bf16[2,8,256,512]{3,2,1,0:T(8,128)(2,1)} %prior_ref, f32[2,8]{1,0:T(2,128)S(1)} %copy-done.9, bf16[2,128,8,512]{3,2,1,0:T(8,128)(2,1)} %v_ref, bf16[2,128,8,256]{3,2,1,0:T(8,128)(2,1)} %multiply_convert_fusion, f32[4,8]{0,1:T(8,128)S(1)} %multiply_exponential_fusion, ...), kind=kOutput, calls=%fused_computation.17 | convolution fusion | flops 562069504 | bytes 7504064 | tf_op jit(solution)/shard_map/tbhk,bhkv->tbhv/dot_general | solution.py:247
  31.4 0.8 %reshape.333 = f32[8,1,4096]{2,1,0:T(1,128)} reshape(f32[8,4,2,8,64]{4,3,2,1,0:T(8,128)S(1)} %bitcast.97) | data formatting | bytes 262144
  32.2 5.4 %all-to-all-start.1 = ((f32[8,1,4096]{2,1,0:T(1,128)}), f32[8,1,4096]{2,1,0:T(1,128)S(1)}, u32[]{:S(2)}, u32[]{:S(2)}) async-start(f32[8,1,4096]{2,1,0:T(1,128)} %reshape.333), calls=%async_computation.1 | async-start | bytes 262144 | tf_op jit(solution)/shard_map/all_to_all | solution.py:272
  37.7 3.6 %fusion.49 = f32[64,512]{1,0:T(8,128)S(1)} fusion(bf16[64,4096]{1,0:T(8,128)(2,1)S(1)} %bitcast.89, bf16[4096,512]{0,1:T(8,128)(2,1)} %bitcast.91), kind=kOutput, calls=%fused_computation.94 | convolution fusion | flops 268435456 | bytes 4849664 | tf_op jit(solution)/shard_map/dot_general | solution.py:201
  41.2 2.6 %all-to-all-done.1 = f32[8,1,4096]{2,1,0:T(1,128)S(1)} async-done(((f32[8,1,4096]{2,1,0:T(1,128)}), f32[8,1,4096]{2,1,0:T(1,128)S(1)}, u32[]{:S(2)}, u32[]{:S(2)}) %all-to-all-start.1) | async-done | bytes 131104 | tf_op jit(solution)/shard_map/all_to_all | solution.py:272
  44.4 1.0 %reduce = f32[8,4096]{1,0:T(8,128)S(1)} reduce(f32[8,1,4096]{2,1,0:T(1,128)S(1)} %all-to-all-done.1, f32[]{:T(128)} %broadcast.414), dimensions={1}, to_apply=%all_to_all.10.reduce_sub_computation | reduce | bytes 262148 | tf_op jit(solution)/shard_map/all_to_all | solution.py:272
  45.6 3.0 %fusion.50 = f32[4,16,4096]{2,1,0:T(8,128)S(1)} fusion(bf16[4,16,512]{2,1,0:T(8,128)(2,1)S(1)} %bitcast.100, bf16[512,4096,1]{1,0,2:T(8,128)(2,1)} %bitcast.92), kind=kOutput, calls=%fused_computation.95 | convolution fusion | flops 268435456 | bytes 5308416 | tf_op jit(solution)/shard_map/dot_general | solution.py:282
  48.7 1.1 %copy.74 = f32[4,2,16,8,256]{4,3,1,0,2:T(8,128)} copy(f32[4,2,16,8,256]{4,3,2,1,0:T(8,128)S(1)} %bitcast.94) | data formatting | bytes 2097152 | tf_op jit(solution)/shard_map/reshape | solution.py:296
  49.8 6.7 %all-to-all-start.2 = ((f32[4,16,16,256]{3,1,0,2:T(8,128)}), f32[4,16,16,256]{3,1,0,2:T(8,128)}, u32[]{:S(2)}, u32[]{:S(2)}) async-start(f32[4,16,16,256]{3,1,0,2:T(8,128)} %bitcast.93), calls=%async_computation.2 | async-start | bytes 2097152 | tf_op jit(solution)/shard_map/all_to_all | solution.py:297
  56.6 0.7 fusion.33.swap_ref
  57.2 18.9 %shard_map.131 = bf16[2,128,8,512]{3,2,1,0:T(8,128)(2,1)} custom-call(f32[8]{0:T(128)} %get-tuple-element.18.rates_ref, s32[2]{0:T(128)} %copy-done.5, bf16[2,128,8,256]{3,2,1,0:T(8,128)(2,1)} %q_ref, bf16[2,128,8,256]{3,2,1,0:T(8,128)(2,1)} %k_ref, bf16[2,128,8,512]{3,2,1,0:T(8,128)(2,1)} %v_ref, bf16[2,8,256,512]{3,2,1,0:T(8,128)(2,1)} %prior_ref, ...), custom_call_target="tpu_custom_call" | custom-call | tf_op jit(solution)/shard_map/pallas_call | solution.py:111
  76.2 3.7 %all-to-all-done.2 = f32[4,16,16,256]{3,1,0,2:T(8,128)} async-done(((f32[4,16,16,256]{3,1,0,2:T(8,128)}), f32[4,16,16,256]{3,1,0,2:T(8,128)}, u32[]{:S(2)}, u32[]{:S(2)}) %all-to-all-start.2) | async-done | bytes 1048608 | tf_op jit(solution)/shard_map/all_to_all | solution.py:297
  79.8 1.9 %reduce_sum.29 = bf16[4,16,256]{2,1,0:T(8,128)(2,1)} reduce(f32[4,16,16,256]{3,1,0,2:T(8,128)} %all-to-all-done.2, f32[]{:T(128)} %constant.94.clone.1), dimensions={2}, to_apply=%region_2.3 | reduce | flops 245760 | bytes 1081348 | tf_op jit(solution)/shard_map/reduce_sum | solution.py:298
  (63 shorter events, 6.0 us)
Async XLA Ops:
  0.6 1.6 %copy-start = (bf16[4096,1,1,256]{3,0,2,1:T(8,128)(2,1)S(1)}, bf16[4096,1,1,256]{3,0,2,1:T(8,128)(2,1)}, u32[]{:S(2)}) copy-start(bf16[4096,1,1,256]{3,0,2,1:T(8,128)(2,1)} %param.20) | copy-start | bytes 6291460
  0.6 3.3 %copy-start.1 = (bf16[4,16,4096]{2,1,0:T(8,128)(2,1)S(1)}, bf16[4,16,4096]{2,1,0:T(8,128)(2,1)}, u32[]{:S(2)}) copy-start(bf16[4,16,4096]{2,1,0:T(8,128)(2,1)} %param.18) | copy-start | bytes 1572868
  0.7 5.6 %copy-start.7 = (s32[256]{0:T(256)}, s32[256]{0:T(256)S(1)}, u32[]{:S(2)}) copy-start(s32[256]{0:T(256)S(1)} %iota_xor_fusion) | copy-start | bytes 3076
  2.2 4.4 %copy-start.2 = (bf16[4096,1,8,1,64]{0,4,3,2,1:T(8,128)(2,1)S(1)}, bf16[4096,1,8,1,64]{0,4,3,2,1:T(8,128)(2,1)}, u32[]{:S(2)}) copy-start(bf16[4096,1,8,1,64]{0,4,3,2,1:T(8,128)(2,1)} %param.21) | copy-start | bytes 12582916
  6.6 8.7 %copy-start.6 = (s32[16]{0:T(128)S(1)}, s32[16]{0:T(128)}, u32[]{:S(2)}) copy-start(s32[16]{0:T(128)} %param.17) | copy-start | bytes 196
  6.7 11.1 %copy-start.10 = (f32[16]{0:T(128)S(1)}, f32[16]{0:T(128)}, u32[]{:S(2)}) copy-start(f32[16]{0:T(128)} %param.16) | copy-start | bytes 196
  8.9 14.9 %all-to-all-start = ((bf16[8,4,2,1024]{3,1,2,0:T(4,128)(2,1)}), bf16[8,4,2,1024]{3,1,2,0:T(4,128)(2,1)S(1)}, u32[]{:S(2)}, u32[]{:S(2)}) async-start(bf16[8,4,2,1024]{3,1,2,0:T(4,128)(2,1)} %bitcast.85), calls=%async_computation | async-start | bytes 262144 | tf_op jit(solution)/shard_map/all_to_all | solution.py:230
  15.4 8.3 %copy-start.5 = (s32[2]{0:T(128)}, s32[2]{0:T(128)S(1)}, u32[]{:S(2)}) copy-start(s32[2]{0:T(128)S(1)} %get-tuple-element.15.live_ref) | copy-start | bytes 28
  19.2 4.4 %copy-start.3 = (f32[2,128,256]{2,1,0:T(8,128)}, f32[2,128,256]{2,1,0:T(8,128)S(1)}, u32[]{:S(2)}) copy-start(f32[2,128,256]{2,1,0:T(8,128)S(1)} %copy.37.cos_ref) | copy-start | bytes 786436
  19.6 4.1 %copy-start.4 = (f32[2,128,256]{2,1,0:T(8,128)}, f32[2,128,256]{2,1,0:T(8,128)S(1)}, u32[]{:S(2)}) copy-start(f32[2,128,256]{2,1,0:T(8,128)S(1)} %copy.39.sin_ref) | copy-start | bytes 786436
  20.4 3.9 %copy-start.9 = (f32[2,8]{1,0:T(2,128)S(1)}, f32[2,8]{1,0:T(2,128)}, u32[]{:S(2)}) copy-start(f32[2,8]{1,0:T(2,128)} %multiply_exponential_fusion.1) | copy-start | bytes 196
  32.2 11.6 %all-to-all-start.1 = ((f32[8,1,4096]{2,1,0:T(1,128)}), f32[8,1,4096]{2,1,0:T(1,128)S(1)}, u32[]{:S(2)}, u32[]{:S(2)}) async-start(f32[8,1,4096]{2,1,0:T(1,128)} %reshape.333), calls=%async_computation.1 | async-start | bytes 262144 | tf_op jit(solution)/shard_map/all_to_all | solution.py:272
  48.7 7.9 %copy-start.8 = (s32[256]{0:T(256)S(1)}, s32[256]{0:T(256)}, u32[]{:S(2)}) copy-start(s32[256]{0:T(256)} %copy-done.7) | copy-start | bytes 3076
  49.8 30.0 %all-to-all-start.2 = ((f32[4,16,16,256]{3,1,0,2:T(8,128)}), f32[4,16,16,256]{3,1,0,2:T(8,128)}, u32[]{:S(2)}, u32[]{:S(2)}) async-start(f32[4,16,16,256]{3,1,0,2:T(8,128)} %bitcast.93), calls=%async_computation.2 | async-start | bytes 2097152 | tf_op jit(solution)/shard_map/all_to_all | solution.py:297

commit v13 on v12

--- a/solution.py
+++ b/solution.py
@@ -294,8 +294,8 @@
     out_slots = head_slots * lax.axis_size("tp")
     column_block = model_width // out_slots
     pieces = partial_out.reshape(step_total, total_prompts, out_slots, column_block)
-    pieces = lax.all_to_all(pieces, ("heads", "tp"), 2, 2, tiled=True)
-    decode_out = jnp.sum(pieces, 2).astype(jnp.bfloat16)
+    pieces = lax.all_to_all(pieces.astype(jnp.bfloat16), ("heads", "tp"), 2, 2, tiled=True)
+    decode_out = jnp.sum(pieces.astype(jnp.float32), 2).astype(jnp.bfloat16)
     return (prefill_out, decode_out)
 
 

time: 83.3 us -> 77 us (0.924)
  waiting for transfers between devices: 6.31 us -> 2.62 us
  other arithmetic: 9.19 us -> 8.08 us
    all_to_all x1, waiting for transfers between devices: 3.69 us -> 0.01 us  [per_device(): lax.all_to_all(pieces.astype(jnp.bfloat16), ('heads', 'tp'), 2, 2, tiled=...]
    reduce_sum x1, other arithmetic: 1.92 us -> 0.69 us  [per_device(): decode_out = jnp.sum(pieces.astype(jnp.float32), 2).astype(jnp.bfloat16)]
    reshape x1 -> x0, local copies, waits for them, and re-layouts: 1.13 us -> none  [per_device(): partial_out.reshape(step_total, total_prompts, out_slots, column_block)]
    convert_element_type x0 -> x1, local copies, waits for them, and re-layouts: none -> 0.86 us  [per_device(): pieces.astype(jnp.bfloat16)]
  transfers between devices with their start and end apart: 3 -> 3, of which waited for: 2 -> 1; matrix products, arithmetic and copies ran while one was open for 15% -> 17% of each run, Pallas kernels for 23% -> 25%
where the time goes in v13:
time: 77 us; the launch traced here: 76 us
  matrix products  22.3 us (29%)
  Pallas kernels  18.9 us (25%)
  starting transfers between devices  17.8 us (23%)
  other arithmetic  8.08 us (10%)
  local copies, waits for them, and re-layouts  5.22 us (7%)
  waiting for transfers between devices  2.62 us (3%)
  between operations  1 us (1%)
    pallas_call x1, Pallas kernels, prefill_output(): pl.pallas_call(output_kernel, grid=(prompts_here,), in_specs=[whole, whol...  18.9 us
    all_to_all x1, starting transfers between devices, per_device(): arrived = lax.all_to_all(packed, 'heads', 0, 0, tiled=True)  6.39 us
    dot_general x1, matrix products, per_device(): jnp.einsum('tbhk,bhkv->tbhv', query_rot, state_new, preferred_element_typ...  6.24 us
    all_to_all x1, starting transfers between devices, per_device(): lax.all_to_all(pieces.astype(jnp.bfloat16), ('heads', 'tp'), 2, 2, tiled=...  6.02 us
    all_to_all x1, starting transfers between devices, per_device(): normed = lax.all_to_all(normed, 'heads', 0, 0, tiled=True)  5.44 us
    dot_general x1, matrix products, per_device(): jnp.dot(flat_inputs, w_gate.reshape(model_width, heads_here * value_slice...  3.58 us
    dot_general x1, matrix products, per_device(): jnp.einsum('bihk,kl->bihl', key_span, swap, preferred_element_type=jnp.fl...  3.24 us
    dot_general x1, matrix products, per_device(): jnp.dot(activated, w_out.reshape(heads_here * value_slice, model_width),...  3.06 us
  transfers between devices with their start and end apart: 3, of which 1 were waited for; matrix products, arithmetic and copies ran while one was open for 17% of the time, Pallas kernels for 25%

profile of v13, /device:TPU:1, one launch (start us, length us, event | category | flops | bytes accessed | tf_op | source)
XLA Modules:
  0.0 76.0 jit_solution(3503343533579554425)
XLA Ops:
  0.7 0.8 %add_convert_fusion.6 = f32[4,16]{1,0:T(4,128)S(1)} fusion(s32[16]{0:T(128)} %param.17), kind=kLoop, calls=%fused_computation.65 | loop fusion | flops 128 | bytes 320 | tf_op jit(solution)/shard_map/convert_element_type | solution.py:212
  1.6 0.6 copy-done
  2.2 1.6 %fusion.28 = bf16[64,256]{1,0:T(8,128)(2,1)S(1)} fusion(bf16[64,4096]{1,0:T(8,128)(2,1)} %bitcast.86, bf16[4096,1,1,256]{3,0,2,1:T(8,128)(2,1)S(1)} %copy-done), kind=kOutput, calls=%fused_computation.27 | convolution fusion | flops 134234112 | bytes 2654208 | tf_op jit(solution)/shard_map/dot_general | solution.py:192
  3.9 2.1 %fusion.25 = bf16[64,256]{1,0:T(8,128)(2,1)S(1)} fusion(bf16[64,4096]{1,0:T(8,128)(2,1)S(1)} %bitcast.87, bf16[4096,1,1,256]{3,0,2,1:T(8,128)(2,1)} %param.19), kind=kOutput, calls=%fused_computation.26 | convolution fusion | flops 134234112 | bytes 2654208 | tf_op jit(solution)/shard_map/dot_general | solution.py:189
  6.7 1.4 %convolution_convert_fusion = bf16[64,512]{1,0:T(8,128)(2,1)S(1)} fusion(bf16[64,4096]{1,0:T(8,128)(2,1)S(1)} %bitcast.88, bf16[4096,512]{0,1:T(8,128)(2,1)S(1)} %bitcast.90), kind=kOutput, calls=%fused_computation.18 | convolution fusion | flops 268468224 | bytes 4784128 | tf_op jit(solution)/shard_map/dot_general | solution.py:195
  8.1 0.8 copy.77
  8.9 6.4 %all-to-all-start = ((bf16[8,4,2,1024]{3,1,2,0:T(4,128)(2,1)}), bf16[8,4,2,1024]{3,1,2,0:T(4,128)(2,1)S(1)}, u32[]{:S(2)}, u32[]{:S(2)}) async-start(bf16[8,4,2,1024]{3,1,2,0:T(4,128)(2,1)} %bitcast.85), calls=%async_computation | async-start | bytes 262144 | tf_op jit(solution)/shard_map/all_to_all | solution.py:230
  15.4 0.7 iota_compare_fusion.3
  17.2 0.6 convert_maximum_fusion.1
  18.3 0.7 multiply_exponential_fusion.1
  19.7 0.9 %exponential_select_fusion = f32[2,128,8]{2,1,0:T(8,128)S(1)} fusion(f32[2,128]{1,0:T(2,128)} %convert_maximum_fusion.1, f32[8]{0:T(128)S(1)} %get-tuple-element.17, pred[2,128]{1,0:T(4,128)(4,1)} %iota_compare_fusion.3), kind=kLoop, calls=%fused_computation.42 | loop fusion | flops 4096 | bytes 9504 | tf_op jit(solution)/shard_map/jit(_where)/select_n | solution.py:176
  20.6 3.2 %multiply_convert_fusion = bf16[2,128,8,256]{3,2,1,0:T(8,128)(2,1)} fusion(bf16[2,128,8,256]{3,2,1,0:T(8,128)(2,1)} %k_ref, f32[2,128,8]{2,1,0:T(8,128)S(1)} %exponential_select_fusion, f32[2,128,256]{2,1,0:T(8,128)S(1)} %copy.39.sin_ref, f32[2,128,256]{2,1,0:T(8,128)S(1)} %copy.37.cos_ref, s32[256]{0:T(256)} %copy-done.7), kind=kOutput, calls=%fused_computation.13 | convolution fusion | flops 273219584 | bytes 2630656 | tf_op jit(solution)/shard_map/bihk,kl->bihl/dot_general | solution.py:169
  24.5 6.2 %fusion.17 = f32[4,2,8,512]{3,0,2,1:T(4,128)S(1)} fusion(bf16[2,8,256,512]{3,2,1,0:T(8,128)(2,1)} %prior_ref, f32[2,8]{1,0:T(2,128)S(1)} %copy-done.9, bf16[2,128,8,512]{3,2,1,0:T(8,128)(2,1)} %v_ref, bf16[2,128,8,256]{3,2,1,0:T(8,128)(2,1)} %multiply_convert_fusion, f32[4,8]{0,1:T(8,128)S(1)} %multiply_exponential_fusion, ...), kind=kOutput, calls=%fused_computation.17 | convolution fusion | flops 562069504 | bytes 7504064 | tf_op jit(solution)/shard_map/tbhk,bhkv->tbhv/dot_general | solution.py:247
  31.5 0.8 %reshape.331 = f32[8,1,4096]{2,1,0:T(1,128)} reshape(f32[8,4,2,8,64]{4,3,2,1,0:T(8,128)S(1)} %bitcast.96) | data formatting | bytes 262144
  32.4 5.4 %all-to-all-start.1 = ((f32[8,1,4096]{2,1,0:T(1,128)}), f32[8,1,4096]{2,1,0:T(1,128)S(1)}, u32[]{:S(2)}, u32[]{:S(2)}) async-start(f32[8,1,4096]{2,1,0:T(1,128)} %reshape.331), calls=%async_computation.1 | async-start | bytes 262144 | tf_op jit(solution)/shard_map/all_to_all | solution.py:272
  37.8 3.6 %fusion.49 = f32[64,512]{1,0:T(8,128)S(1)} fusion(bf16[64,4096]{1,0:T(8,128)(2,1)S(1)} %bitcast.89, bf16[4096,512]{0,1:T(8,128)(2,1)} %bitcast.91), kind=kOutput, calls=%fused_computation.94 | convolution fusion | flops 268435456 | bytes 4849664 | tf_op jit(solution)/shard_map/dot_general | solution.py:201
  41.4 2.6 %all-to-all-done.1 = f32[8,1,4096]{2,1,0:T(1,128)S(1)} async-done(((f32[8,1,4096]{2,1,0:T(1,128)}), f32[8,1,4096]{2,1,0:T(1,128)S(1)}, u32[]{:S(2)}, u32[]{:S(2)}) %all-to-all-start.1) | async-done | bytes 131104 | tf_op jit(solution)/shard_map/all_to_all | solution.py:272
  44.5 1.0 %reduce.1 = f32[8,4096]{1,0:T(8,128)S(1)} reduce(f32[8,1,4096]{2,1,0:T(1,128)S(1)} %all-to-all-done.1, f32[]{:T(128)} %broadcast.414), dimensions={1}, to_apply=%all_to_all.10.reduce_sub_computation | reduce | bytes 262148 | tf_op jit(solution)/shard_map/all_to_all | solution.py:272
  45.8 3.1 %fusion.50 = bf16[4,16,4096]{2,1,0:T(8,128)(2,1)S(1)} fusion(bf16[4,16,512]{2,1,0:T(8,128)(2,1)S(1)} %bitcast.99, bf16[512,4096,1]{1,0,2:T(8,128)(2,1)} %bitcast.92), kind=kOutput, calls=%fused_computation.95 | convolution fusion | flops 268435456 | bytes 4784128 | tf_op jit(solution)/shard_map/dot_general | solution.py:282
  48.8 0.9 %copy.74 = bf16[4,2,16,8,256]{4,3,1,0,2:T(8,128)(2,1)} copy(bf16[4,2,16,8,256]{4,3,2,1,0:T(8,128)(2,1)S(1)} %bitcast.93) | data formatting | bytes 1048576 | tf_op jit(solution)/shard_map/convert_element_type | solution.py:297
  49.7 6.0 %all-to-all-start.2 = ((bf16[4,16,16,256]{3,1,0,2:T(8,128)(2,1)}), bf16[4,16,16,256]{3,1,0,2:T(8,128)(2,1)S(1)}, u32[]{:S(2)}, u32[]{:S(2)}) async-start(bf16[4,16,16,256]{3,1,0,2:T(8,128)(2,1)} %bitcast.82), calls=%async_computation.2 | async-start | bytes 1048576 | tf_op jit(solution)/shard_map/all_to_all | solution.py:297
  55.7 0.7 fusion.33.swap_ref
  56.4 18.9 %shard_map.131 = bf16[2,128,8,512]{3,2,1,0:T(8,128)(2,1)} custom-call(f32[8]{0:T(128)} %get-tuple-element.18.rates_ref, s32[2]{0:T(128)} %copy-done.5, bf16[2,128,8,256]{3,2,1,0:T(8,128)(2,1)} %q_ref, bf16[2,128,8,256]{3,2,1,0:T(8,128)(2,1)} %k_ref, bf16[2,128,8,512]{3,2,1,0:T(8,128)(2,1)} %v_ref, bf16[2,8,256,512]{3,2,1,0:T(8,128)(2,1)} %prior_ref, ...), custom_call_target="tpu_custom_call" | custom-call | tf_op jit(solution)/shard_map/pallas_call | solution.py:111
  75.3 0.7 reduce_sum.32
  (63 shorter events, 5.4 us)
Async XLA Ops:
  0.6 1.6 %copy-start = (bf16[4096,1,1,256]{3,0,2,1:T(8,128)(2,1)S(1)}, bf16[4096,1,1,256]{3,0,2,1:T(8,128)(2,1)}, u32[]{:S(2)}) copy-start(bf16[4096,1,1,256]{3,0,2,1:T(8,128)(2,1)} %param.20) | copy-start | bytes 6291460
  0.6 3.3 %copy-start.1 = (bf16[4,16,4096]{2,1,0:T(8,128)(2,1)S(1)}, bf16[4,16,4096]{2,1,0:T(8,128)(2,1)}, u32[]{:S(2)}) copy-start(bf16[4,16,4096]{2,1,0:T(8,128)(2,1)} %param.18) | copy-start | bytes 1572868
  0.7 5.6 %copy-start.7 = (s32[256]{0:T(256)}, s32[256]{0:T(256)S(1)}, u32[]{:S(2)}) copy-start(s32[256]{0:T(256)S(1)} %iota_xor_fusion) | copy-start | bytes 3076
  2.2 4.4 %copy-start.2 = (bf16[4096,1,8,1,64]{0,4,3,2,1:T(8,128)(2,1)S(1)}, bf16[4096,1,8,1,64]{0,4,3,2,1:T(8,128)(2,1)}, u32[]{:S(2)}) copy-start(bf16[4096,1,8,1,64]{0,4,3,2,1:T(8,128)(2,1)} %param.21) | copy-start | bytes 12582916
  6.6 8.7 %copy-start.6 = (s32[16]{0:T(128)S(1)}, s32[16]{0:T(128)}, u32[]{:S(2)}) copy-start(s32[16]{0:T(128)} %param.17) | copy-start | bytes 196
  6.7 11.1 %copy-start.10 = (f32[16]{0:T(128)S(1)}, f32[16]{0:T(128)}, u32[]{:S(2)}) copy-start(f32[16]{0:T(128)} %param.16) | copy-start | bytes 196
  8.9 15.0 %all-to-all-start = ((bf16[8,4,2,1024]{3,1,2,0:T(4,128)(2,1)}), bf16[8,4,2,1024]{3,1,2,0:T(4,128)(2,1)S(1)}, u32[]{:S(2)}, u32[]{:S(2)}) async-start(bf16[8,4,2,1024]{3,1,2,0:T(4,128)(2,1)} %bitcast.85), calls=%async_computation | async-start | bytes 262144 | tf_op jit(solution)/shard_map/all_to_all | solution.py:230
  15.4 8.4 %copy-start.5 = (s32[2]{0:T(128)}, s32[2]{0:T(128)S(1)}, u32[]{:S(2)}) copy-start(s32[2]{0:T(128)S(1)} %get-tuple-element.15.live_ref) | copy-start | bytes 28
  19.3 4.5 %copy-start.3 = (f32[2,128,256]{2,1,0:T(8,128)}, f32[2,128,256]{2,1,0:T(8,128)S(1)}, u32[]{:S(2)}) copy-start(f32[2,128,256]{2,1,0:T(8,128)S(1)} %copy.37.cos_ref) | copy-start | bytes 786436
  19.7 4.1 %copy-start.4 = (f32[2,128,256]{2,1,0:T(8,128)}, f32[2,128,256]{2,1,0:T(8,128)S(1)}, u32[]{:S(2)}) copy-start(f32[2,128,256]{2,1,0:T(8,128)S(1)} %copy.39.sin_ref) | copy-start | bytes 786436
  20.5 3.9 %copy-start.9 = (f32[2,8]{1,0:T(2,128)S(1)}, f32[2,8]{1,0:T(2,128)}, u32[]{:S(2)}) copy-start(f32[2,8]{1,0:T(2,128)} %multiply_exponential_fusion.1) | copy-start | bytes 196
  32.4 11.6 %all-to-all-start.1 = ((f32[8,1,4096]{2,1,0:T(1,128)}), f32[8,1,4096]{2,1,0:T(1,128)S(1)}, u32[]{:S(2)}, u32[]{:S(2)}) async-start(f32[8,1,4096]{2,1,0:T(1,128)} %reshape.331), calls=%async_computation.1 | async-start | bytes 262144 | tf_op jit(solution)/shard_map/all_to_all | solution.py:272
  48.8 6.9 %copy-start.8 = (s32[256]{0:T(256)S(1)}, s32[256]{0:T(256)}, u32[]{:S(2)}) copy-start(s32[256]{0:T(256)} %copy-done.7) | copy-start | bytes 3076
  49.7 25.6 %all-to-all-start.2 = ((bf16[4,16,16,256]{3,1,0,2:T(8,128)(2,1)}), bf16[4,16,16,256]{3,1,0,2:T(8,128)(2,1)S(1)}, u32[]{:S(2)}, u32[]{:S(2)}) async-start(bf16[4,16,16,256]{3,1,0,2:T(8,128)(2,1)} %bitcast.82), calls=%async_computation.2 | async-start | bytes 1048576 | tf_op jit(solution)/shard_map/all_to_all | solution.py:297

commit v14 on v13

--- a/solution.py
+++ b/solution.py
@@ -46,10 +46,13 @@
     keep = (row >= column) & (column < live)
     row_index = lax.broadcasted_iota(jnp.int32, (span_len, 1), 0)
     valid = row_index < live
+    q_all = q_ref[...]
+    k_all = k_ref[...]
+    v_all = v_ref[...]
     for head in range(q_ref.shape[1]):
         rate = rates_ref[head]
-        q_raw = q_ref[:, head, :]
-        k_raw = k_ref[:, head, :]
+        q_raw = q_all[:, head, :]
+        k_raw = k_all[:, head, :]
         queries = turn_lanes(q_raw, swap, cosine, sine_part).astype(jnp.bfloat16)
         keys = (turn_lanes(k_raw, swap, cosine, sine_part) * (k_raw.shape[-1] ** (-0.5))).astype(
             jnp.bfloat16
@@ -59,7 +62,7 @@
         )
         table = jnp.where(keep, jnp.exp(-rate * distance), 0.0)
         weights = (scores * table).astype(jnp.bfloat16)
-        inner = jnp.dot(weights, v_ref[:, head, :], preferred_element_type=jnp.float32)
+        inner = jnp.dot(weights, v_all[:, head, :], preferred_element_type=jnp.float32)
         carried = jnp.dot(queries, prior_ref[head], preferred_element_type=jnp.float32)
         lead = jnp.exp(-rate * (row_index + 1).astype(jnp.float32))
         mixed = inner + lead * carried

time: 77 us -> 74.5 us (0.968)
  Pallas kernels: 18.9 us -> 16.4 us
    pallas_call x1, Pallas kernels: 18.9 us -> 16.4 us  [prefill_output(): pl.pallas_call(output_kernel, grid=(prompts_here,), in_specs=[whole, whol...]
  transfers between devices with their start and end apart: 3 -> 3, of which waited for: 1 -> 1; matrix products, arithmetic and copies ran while one was open for 17% -> 17% of each run, Pallas kernels for 25% -> 22%
where the time goes in v14:
time: 74.5 us; the launch traced here: 73.5 us
  matrix products  22.3 us (30%)
  starting transfers between devices  17.8 us (24%)
  Pallas kernels  16.4 us (22%)
  other arithmetic  8.08 us (11%)
  local copies, waits for them, and re-layouts  5.22 us (7%)
  waiting for transfers between devices  2.62 us (4%)
  between operations  1 us (1%)
    pallas_call x1, Pallas kernels, prefill_output(): pl.pallas_call(output_kernel, grid=(prompts_here,), in_specs=[whole, whol...  16.4 us
    all_to_all x1, starting transfers between devices, per_device(): arrived = lax.all_to_all(packed, 'heads', 0, 0, tiled=True)  6.39 us
    dot_general x1, matrix products, per_device(): jnp.einsum('tbhk,bhkv->tbhv', query_rot, state_new, preferred_element_typ...  6.24 us
    all_to_all x1, starting transfers between devices, per_device(): lax.all_to_all(pieces.astype(jnp.bfloat16), ('heads', 'tp'), 2, 2, tiled=...  6.02 us
    all_to_all x1, starting transfers between devices, per_device(): normed = lax.all_to_all(normed, 'heads', 0, 0, tiled=True)  5.44 us
    dot_general x1, matrix products, per_device(): jnp.dot(flat_inputs, w_gate.reshape(model_width, heads_here * value_slice...  3.58 us
    dot_general x1, matrix products, per_device(): jnp.einsum('bihk,kl->bihl', key_span, swap, preferred_element_type=jnp.fl...  3.24 us
    dot_general x1, matrix products, per_device(): jnp.dot(activated, w_out.reshape(heads_here * value_slice, model_width),...  3.06 us
  transfers between devices with their start and end apart: 3, of which 1 were waited for; matrix products, arithmetic and copies ran while one was open for 17% of the time, Pallas kernels for 22%

profile of v14, /device:TPU:1, one launch (start us, length us, event | category | flops | bytes accessed | tf_op | source)
XLA Modules:
  0.0 73.5 jit_solution(1149279670844840066)
XLA Ops:
  0.7 0.8 %add_convert_fusion.6 = f32[4,16]{1,0:T(4,128)S(1)} fusion(s32[16]{0:T(128)} %param.17), kind=kLoop, calls=%fused_computation.65 | loop fusion | flops 128 | bytes 320 | tf_op jit(solution)/shard_map/convert_element_type | solution.py:215
  1.6 0.6 copy-done
  2.2 1.6 %fusion.28 = bf16[64,256]{1,0:T(8,128)(2,1)S(1)} fusion(bf16[64,4096]{1,0:T(8,128)(2,1)} %bitcast.86, bf16[4096,1,1,256]{3,0,2,1:T(8,128)(2,1)S(1)} %copy-done), kind=kOutput, calls=%fused_computation.27 | convolution fusion | flops 134234112 | bytes 2654208 | tf_op jit(solution)/shard_map/dot_general | solution.py:195
  3.9 2.1 %fusion.25 = bf16[64,256]{1,0:T(8,128)(2,1)S(1)} fusion(bf16[64,4096]{1,0:T(8,128)(2,1)S(1)} %bitcast.87, bf16[4096,1,1,256]{3,0,2,1:T(8,128)(2,1)} %param.19), kind=kOutput, calls=%fused_computation.26 | convolution fusion | flops 134234112 | bytes 2654208 | tf_op jit(solution)/shard_map/dot_general | solution.py:192
  6.7 1.4 %convolution_convert_fusion = bf16[64,512]{1,0:T(8,128)(2,1)S(1)} fusion(bf16[64,4096]{1,0:T(8,128)(2,1)S(1)} %bitcast.88, bf16[4096,512]{0,1:T(8,128)(2,1)S(1)} %bitcast.90), kind=kOutput, calls=%fused_computation.18 | convolution fusion | flops 268468224 | bytes 4784128 | tf_op jit(solution)/shard_map/dot_general | solution.py:198
  8.1 0.8 %copy.77 = bf16[4,8,2,1024]{3,0,2,1:T(4,128)(2,1)} copy(bf16[4,8,2,1024]{3,2,1,0:T(2,128)(2,1)S(1)} %reshape.323) | data formatting | bytes 262144 | tf_op jit(solution)/shard_map/reshape | solution.py:232
  8.9 6.4 %all-to-all-start = ((bf16[8,4,2,1024]{3,1,2,0:T(4,128)(2,1)}), bf16[8,4,2,1024]{3,1,2,0:T(4,128)(2,1)S(1)}, u32[]{:S(2)}, u32[]{:S(2)}) async-start(bf16[8,4,2,1024]{3,1,2,0:T(4,128)(2,1)} %bitcast.85), calls=%async_computation | async-start | bytes 262144 | tf_op jit(solution)/shard_map/all_to_all | solution.py:233
  15.4 0.7 iota_compare_fusion.3
  17.2 0.6 convert_maximum_fusion.1
  18.3 0.7 multiply_exponential_fusion.1
  19.7 0.9 %exponential_select_fusion = f32[2,128,8]{2,1,0:T(8,128)S(1)} fusion(f32[2,128]{1,0:T(2,128)} %convert_maximum_fusion.1, f32[8]{0:T(128)S(1)} %get-tuple-element.17, pred[2,128]{1,0:T(4,128)(4,1)} %iota_compare_fusion.3), kind=kLoop, calls=%fused_computation.42 | loop fusion | flops 4096 | bytes 9504 | tf_op jit(solution)/shard_map/jit(_where)/select_n | solution.py:179
  20.6 3.2 %multiply_convert_fusion = bf16[2,128,8,256]{3,2,1,0:T(8,128)(2,1)} fusion(bf16[2,128,8,256]{3,2,1,0:T(8,128)(2,1)} %k_ref, f32[2,128,8]{2,1,0:T(8,128)S(1)} %exponential_select_fusion, f32[2,128,256]{2,1,0:T(8,128)S(1)} %copy.39.sin_ref, f32[2,128,256]{2,1,0:T(8,128)S(1)} %copy.37.cos_ref, s32[256]{0:T(256)} %copy-done.7), kind=kOutput, calls=%fused_computation.13 | convolution fusion | flops 273219584 | bytes 2630656 | tf_op jit(solution)/shard_map/bihk,kl->bihl/dot_general | solution.py:172
  24.5 6.2 %fusion.17 = f32[4,2,8,512]{3,0,2,1:T(4,128)S(1)} fusion(bf16[2,8,256,512]{3,2,1,0:T(8,128)(2,1)} %prior_ref, f32[2,8]{1,0:T(2,128)S(1)} %copy-done.9, bf16[2,128,8,512]{3,2,1,0:T(8,128)(2,1)} %v_ref, bf16[2,128,8,256]{3,2,1,0:T(8,128)(2,1)} %multiply_convert_fusion, f32[4,8]{0,1:T(8,128)S(1)} %multiply_exponential_fusion, ...), kind=kOutput, calls=%fused_computation.17 | convolution fusion | flops 562069504 | bytes 7504064 | tf_op jit(solution)/shard_map/tbhk,bhkv->tbhv/dot_general | solution.py:250
  31.5 0.8 %reshape.331 = f32[8,1,4096]{2,1,0:T(1,128)} reshape(f32[8,4,2,8,64]{4,3,2,1,0:T(8,128)S(1)} %bitcast.96) | data formatting | bytes 262144
  32.4 5.4 %all-to-all-start.1 = ((f32[8,1,4096]{2,1,0:T(1,128)}), f32[8,1,4096]{2,1,0:T(1,128)S(1)}, u32[]{:S(2)}, u32[]{:S(2)}) async-start(f32[8,1,4096]{2,1,0:T(1,128)} %reshape.331), calls=%async_computation.1 | async-start | bytes 262144 | tf_op jit(solution)/shard_map/all_to_all | solution.py:275
  37.8 3.6 %fusion.49 = f32[64,512]{1,0:T(8,128)S(1)} fusion(bf16[64,4096]{1,0:T(8,128)(2,1)S(1)} %bitcast.89, bf16[4096,512]{0,1:T(8,128)(2,1)} %bitcast.91), kind=kOutput, calls=%fused_computation.94 | convolution fusion | flops 268435456 | bytes 4849664 | tf_op jit(solution)/shard_map/dot_general | solution.py:204
  41.4 2.6 %all-to-all-done.1 = f32[8,1,4096]{2,1,0:T(1,128)S(1)} async-done(((f32[8,1,4096]{2,1,0:T(1,128)}), f32[8,1,4096]{2,1,0:T(1,128)S(1)}, u32[]{:S(2)}, u32[]{:S(2)}) %all-to-all-start.1) | async-done | bytes 131104 | tf_op jit(solution)/shard_map/all_to_all | solution.py:275
  44.5 1.0 %reduce.1 = f32[8,4096]{1,0:T(8,128)S(1)} reduce(f32[8,1,4096]{2,1,0:T(1,128)S(1)} %all-to-all-done.1, f32[]{:T(128)} %broadcast.414), dimensions={1}, to_apply=%all_to_all.10.reduce_sub_computation | reduce | bytes 262148 | tf_op jit(solution)/shard_map/all_to_all | solution.py:275
  45.8 3.1 %fusion.50 = bf16[4,16,4096]{2,1,0:T(8,128)(2,1)S(1)} fusion(bf16[4,16,512]{2,1,0:T(8,128)(2,1)S(1)} %bitcast.99, bf16[512,4096,1]{1,0,2:T(8,128)(2,1)} %bitcast.92), kind=kOutput, calls=%fused_computation.95 | convolution fusion | flops 268435456 | bytes 4784128 | tf_op jit(solution)/shard_map/dot_general | solution.py:285
  48.8 0.9 %copy.74 = bf16[4,2,16,8,256]{4,3,1,0,2:T(8,128)(2,1)} copy(bf16[4,2,16,8,256]{4,3,2,1,0:T(8,128)(2,1)S(1)} %bitcast.93) | data formatting | bytes 1048576 | tf_op jit(solution)/shard_map/convert_element_type | solution.py:300
  49.7 6.0 %all-to-all-start.2 = ((bf16[4,16,16,256]{3,1,0,2:T(8,128)(2,1)}), bf16[4,16,16,256]{3,1,0,2:T(8,128)(2,1)S(1)}, u32[]{:S(2)}, u32[]{:S(2)}) async-start(bf16[4,16,16,256]{3,1,0,2:T(8,128)(2,1)} %bitcast.82), calls=%async_computation.2 | async-start | bytes 1048576 | tf_op jit(solution)/shard_map/all_to_all | solution.py:300
  55.7 0.7 fusion.33.swap_ref
  56.4 16.4 %shard_map.131 = bf16[2,128,8,512]{3,2,1,0:T(8,128)(2,1)} custom-call(f32[8]{0:T(128)} %get-tuple-element.18.rates_ref, s32[2]{0:T(128)} %copy-done.5, bf16[2,128,8,256]{3,2,1,0:T(8,128)(2,1)} %q_ref, bf16[2,128,8,256]{3,2,1,0:T(8,128)(2,1)} %k_ref, bf16[2,128,8,512]{3,2,1,0:T(8,128)(2,1)} %v_ref, bf16[2,8,256,512]{3,2,1,0:T(8,128)(2,1)} %prior_ref, ...), custom_call_target="tpu_custom_call" | custom-call | tf_op jit(solution)/shard_map/pallas_call | solution.py:114
  72.9 0.7 reduce_sum.32
  (63 shorter events, 5.4 us)
Async XLA Ops:
  0.6 1.6 %copy-start = (bf16[4096,1,1,256]{3,0,2,1:T(8,128)(2,1)S(1)}, bf16[4096,1,1,256]{3,0,2,1:T(8,128)(2,1)}, u32[]{:S(2)}) copy-start(bf16[4096,1,1,256]{3,0,2,1:T(8,128)(2,1)} %param.20) | copy-start | bytes 6291460
  0.6 3.3 %copy-start.1 = (bf16[4,16,4096]{2,1,0:T(8,128)(2,1)S(1)}, bf16[4,16,4096]{2,1,0:T(8,128)(2,1)}, u32[]{:S(2)}) copy-start(bf16[4,16,4096]{2,1,0:T(8,128)(2,1)} %param.18) | copy-start | bytes 1572868
  0.7 5.6 %copy-start.7 = (s32[256]{0:T(256)}, s32[256]{0:T(256)S(1)}, u32[]{:S(2)}) copy-start(s32[256]{0:T(256)S(1)} %iota_xor_fusion) | copy-start | bytes 3076
  2.2 4.4 %copy-start.2 = (bf16[4096,1,8,1,64]{0,4,3,2,1:T(8,128)(2,1)S(1)}, bf16[4096,1,8,1,64]{0,4,3,2,1:T(8,128)(2,1)}, u32[]{:S(2)}) copy-start(bf16[4096,1,8,1,64]{0,4,3,2,1:T(8,128)(2,1)} %param.21) | copy-start | bytes 12582916
  6.6 8.7 %copy-start.6 = (s32[16]{0:T(128)S(1)}, s32[16]{0:T(128)}, u32[]{:S(2)}) copy-start(s32[16]{0:T(128)} %param.17) | copy-start | bytes 196
  6.7 11.1 %copy-start.10 = (f32[16]{0:T(128)S(1)}, f32[16]{0:T(128)}, u32[]{:S(2)}) copy-start(f32[16]{0:T(128)} %param.16) | copy-start | bytes 196
  8.9 15.0 %all-to-all-start = ((bf16[8,4,2,1024]{3,1,2,0:T(4,128)(2,1)}), bf16[8,4,2,1024]{3,1,2,0:T(4,128)(2,1)S(1)}, u32[]{:S(2)}, u32[]{:S(2)}) async-start(bf16[8,4,2,1024]{3,1,2,0:T(4,128)(2,1)} %bitcast.85), calls=%async_computation | async-start | bytes 262144 | tf_op jit(solution)/shard_map/all_to_all | solution.py:233
  15.4 8.4 %copy-start.5 = (s32[2]{0:T(128)}, s32[2]{0:T(128)S(1)}, u32[]{:S(2)}) copy-start(s32[2]{0:T(128)S(1)} %get-tuple-element.15.live_ref) | copy-start | bytes 28
  19.3 4.5 %copy-start.3 = (f32[2,128,256]{2,1,0:T(8,128)}, f32[2,128,256]{2,1,0:T(8,128)S(1)}, u32[]{:S(2)}) copy-start(f32[2,128,256]{2,1,0:T(8,128)S(1)} %copy.37.cos_ref) | copy-start | bytes 786436
  19.7 4.1 %copy-start.4 = (f32[2,128,256]{2,1,0:T(8,128)}, f32[2,128,256]{2,1,0:T(8,128)S(1)}, u32[]{:S(2)}) copy-start(f32[2,128,256]{2,1,0:T(8,128)S(1)} %copy.39.sin_ref) | copy-start | bytes 786436
  20.5 3.9 %copy-start.9 = (f32[2,8]{1,0:T(2,128)S(1)}, f32[2,8]{1,0:T(2,128)}, u32[]{:S(2)}) copy-start(f32[2,8]{1,0:T(2,128)} %multiply_exponential_fusion.1) | copy-start | bytes 196
  32.4 11.6 %all-to-all-start.1 = ((f32[8,1,4096]{2,1,0:T(1,128)}), f32[8,1,4096]{2,1,0:T(1,128)S(1)}, u32[]{:S(2)}, u32[]{:S(2)}) async-start(f32[8,1,4096]{2,1,0:T(1,128)} %reshape.331), calls=%async_computation.1 | async-start | bytes 262144 | tf_op jit(solution)/shard_map/all_to_all | solution.py:275
  48.8 6.9 %copy-start.8 = (s32[256]{0:T(256)S(1)}, s32[256]{0:T(256)}, u32[]{:S(2)}) copy-start(s32[256]{0:T(256)} %copy-done.7) | copy-start | bytes 3076
  49.7 23.1 %all-to-all-start.2 = ((bf16[4,16,16,256]{3,1,0,2:T(8,128)(2,1)}), bf16[4,16,16,256]{3,1,0,2:T(8,128)(2,1)S(1)}, u32[]{:S(2)}, u32[]{:S(2)}) async-start(bf16[4,16,16,256]{3,1,0,2:T(8,128)(2,1)} %bitcast.82), calls=%async_computation.2 | async-start | bytes 1048576 | tf_op jit(solution)/shard_map/all_to_all | solution.py:300

commit v15 on v14

--- a/solution.py
+++ b/solution.py
@@ -272,10 +272,10 @@
     normed = norm_with(readout, read_mean, read_square)
     normed = normed.reshape(step_total, prompts_here, heads_here, slots, value_slice)
     normed = normed.transpose(3, 0, 1, 2, 4)
-    normed = lax.all_to_all(normed, "heads", 0, 0, tiled=True)
+    normed = lax.all_to_all(normed.astype(jnp.bfloat16), "heads", 0, 0, tiled=True)
     normed = normed.transpose(1, 0, 2, 3, 4).reshape(
         step_total, total_prompts, heads_here, value_slice
-    )
+    ).astype(jnp.float32)
     gates_steps = gate_values.reshape(step_total, total_prompts, heads_here, value_slice)
     activated = (
         (jax.nn.silu(gates_steps) * normed)

time: 74.5 us -> 72.5 us (0.973)
  other arithmetic: 8.08 us -> 7.16 us
    all_to_all x1 -> x0, other arithmetic: 0.95 us -> none  [per_device(): normed = lax.all_to_all(normed, 'heads', 0, 0, tiled=True)]
  transfers between devices with their start and end apart: 3 -> 3, of which waited for: 1 -> 1; matrix products, arithmetic and copies ran while one was open for 17% -> 18% of each run, Pallas kernels for 22% -> 23%
where the time goes in v15:
time: 72.5 us; the launch traced here: 71.6 us
  matrix products  22.3 us (31%)
  starting transfers between devices  17.8 us (25%)
  Pallas kernels  16.4 us (23%)
  other arithmetic  7.16 us (10%)
  local copies, waits for them, and re-layouts  4.57 us (6%)
  waiting for transfers between devices  2.19 us (3%)
  between operations  1.01 us (1%)
    pallas_call x1, Pallas kernels, prefill_output(): pl.pallas_call(output_kernel, grid=(prompts_here,), in_specs=[whole, whol...  16.4 us
    all_to_all x1, starting transfers between devices, per_device(): arrived = lax.all_to_all(packed, 'heads', 0, 0, tiled=True)  6.39 us
    dot_general x1, matrix products, per_device(): jnp.einsum('tbhk,bhkv->tbhv', query_rot, state_new, preferred_element_typ...  6.24 us
    all_to_all x1, starting transfers between devices, per_device(): lax.all_to_all(pieces.astype(jnp.bfloat16), ('heads', 'tp'), 2, 2, tiled=...  6.02 us
    all_to_all x1, starting transfers between devices, per_device(): lax.all_to_all(normed.astype(jnp.bfloat16), 'heads', 0, 0, tiled=True)  5.44 us
    dot_general x1, matrix products, per_device(): jnp.dot(flat_inputs, w_gate.reshape(model_width, heads_here * value_slice...  3.58 us
    dot_general x1, matrix products, per_device(): jnp.einsum('bihk,kl->bihl', key_span, swap, preferred_element_type=jnp.fl...  3.24 us
    dot_general x1, matrix products, per_device(): jnp.dot(activated, w_out.reshape(heads_here * value_slice, model_width),...  3.06 us
  transfers between devices with their start and end apart: 3, of which 1 were waited for; matrix products, arithmetic and copies ran while one was open for 18% of the time, Pallas kernels for 23%

profile of v15, /device:TPU:1, one launch (start us, length us, event | category | flops | bytes accessed | tf_op | source)
XLA Modules:
  0.0 71.6 jit_solution(6643020018143113597)
XLA Ops:
  0.7 0.8 %add_convert_fusion.6 = f32[4,16]{1,0:T(4,128)S(1)} fusion(s32[16]{0:T(128)} %param.17), kind=kLoop, calls=%fused_computation.66 | loop fusion | flops 128 | bytes 320 | tf_op jit(solution)/shard_map/convert_element_type | solution.py:215
  1.6 0.6 copy-done
  2.2 1.6 %fusion.28 = bf16[64,256]{1,0:T(8,128)(2,1)S(1)} fusion(bf16[64,4096]{1,0:T(8,128)(2,1)} %bitcast.87, bf16[4096,1,1,256]{3,0,2,1:T(8,128)(2,1)S(1)} %copy-done), kind=kOutput, calls=%fused_computation.27 | convolution fusion | flops 134234112 | bytes 2654208 | tf_op jit(solution)/shard_map/dot_general | solution.py:195
  3.9 2.1 %fusion.25 = bf16[64,256]{1,0:T(8,128)(2,1)S(1)} fusion(bf16[64,4096]{1,0:T(8,128)(2,1)S(1)} %bitcast.88, bf16[4096,1,1,256]{3,0,2,1:T(8,128)(2,1)} %param.19), kind=kOutput, calls=%fused_computation.26 | convolution fusion | flops 134234112 | bytes 2654208 | tf_op jit(solution)/shard_map/dot_general | solution.py:192
  6.7 1.4 %convolution_convert_fusion = bf16[64,512]{1,0:T(8,128)(2,1)S(1)} fusion(bf16[64,4096]{1,0:T(8,128)(2,1)S(1)} %bitcast.89, bf16[4096,512]{0,1:T(8,128)(2,1)S(1)} %bitcast.91), kind=kOutput, calls=%fused_computation.18 | convolution fusion | flops 268468224 | bytes 4784128 | tf_op jit(solution)/shard_map/dot_general | solution.py:198
  8.1 0.8 %copy.77 = bf16[4,8,2,1024]{3,0,2,1:T(4,128)(2,1)} copy(bf16[4,8,2,1024]{3,2,1,0:T(2,128)(2,1)S(1)} %reshape.322) | data formatting | bytes 262144 | tf_op jit(solution)/shard_map/reshape | solution.py:232
  8.9 6.4 %all-to-all-start = ((bf16[8,4,2,1024]{3,1,2,0:T(4,128)(2,1)}), bf16[8,4,2,1024]{3,1,2,0:T(4,128)(2,1)S(1)}, u32[]{:S(2)}, u32[]{:S(2)}) async-start(bf16[8,4,2,1024]{3,1,2,0:T(4,128)(2,1)} %bitcast.86), calls=%async_computation | async-start | bytes 262144 | tf_op jit(solution)/shard_map/all_to_all | solution.py:233
  15.4 0.6 iota_compare_fusion.3
  17.1 0.6 convert_maximum_fusion.1
  17.8 0.6 fusion.47
  18.4 0.6 multiply_exponential_fusion.1
  19.7 0.8 %exponential_select_fusion = f32[2,128,8]{2,1,0:T(8,128)S(1)} fusion(f32[2,128]{1,0:T(2,128)} %convert_maximum_fusion.1, f32[8]{0:T(128)S(1)} %get-tuple-element.17, pred[2,128]{1,0:T(4,128)(4,1)} %iota_compare_fusion.3), kind=kLoop, calls=%fused_computation.43 | loop fusion | flops 4096 | bytes 9504 | tf_op jit(solution)/shard_map/jit(_where)/select_n | solution.py:179
  20.6 3.2 %multiply_convert_fusion = bf16[2,128,8,256]{3,2,1,0:T(8,128)(2,1)} fusion(bf16[2,128,8,256]{3,2,1,0:T(8,128)(2,1)} %k_ref, f32[2,128,8]{2,1,0:T(8,128)S(1)} %exponential_select_fusion, f32[2,128,256]{2,1,0:T(8,128)S(1)} %copy.39.sin_ref, f32[2,128,256]{2,1,0:T(8,128)S(1)} %copy.37.cos_ref, s32[256]{0:T(256)} %copy-done.7), kind=kOutput, calls=%fused_computation.13 | convolution fusion | flops 273219584 | bytes 2630656 | tf_op jit(solution)/shard_map/bihk,kl->bihl/dot_general | solution.py:172
  24.5 6.2 %fusion.17 = f32[4,2,8,512]{3,0,2,1:T(4,128)S(1)} fusion(bf16[2,8,256,512]{3,2,1,0:T(8,128)(2,1)} %prior_ref, f32[2,8]{1,0:T(2,128)S(1)} %copy-done.9, bf16[2,128,8,512]{3,2,1,0:T(8,128)(2,1)} %v_ref, bf16[2,128,8,256]{3,2,1,0:T(8,128)(2,1)} %multiply_convert_fusion, f32[4,8]{0,1:T(8,128)S(1)} %multiply_exponential_fusion, ...), kind=kOutput, calls=%fused_computation.17 | convolution fusion | flops 562069504 | bytes 7504064 | tf_op jit(solution)/shard_map/tbhk,bhkv->tbhv/dot_general | solution.py:250
  31.4 0.8 %reshape.329 = bf16[8,2,2048]{2,1,0:T(2,128)(2,1)} reshape(bf16[8,4,2,8,64]{4,3,2,1,0:T(8,128)(2,1)S(1)} %bitcast.98) | data formatting | bytes 131072
  32.2 5.4 %all-to-all-start.1 = ((bf16[8,2,2048]{2,1,0:T(2,128)(2,1)}), bf16[8,2,2048]{2,1,0:T(2,128)(2,1)S(1)}, u32[]{:S(2)}, u32[]{:S(2)}) async-start(bf16[8,2,2048]{2,1,0:T(2,128)(2,1)} %reshape.329), calls=%async_computation.1 | async-start | bytes 131072 | tf_op jit(solution)/shard_map/all_to_all | solution.py:275
  37.7 3.6 %fusion.49 = f32[64,512]{1,0:T(8,128)S(1)} fusion(bf16[64,4096]{1,0:T(8,128)(2,1)S(1)} %bitcast.90, bf16[4096,512]{0,1:T(8,128)(2,1)} %bitcast.92), kind=kOutput, calls=%fused_computation.95 | convolution fusion | flops 268435456 | bytes 4849664 | tf_op jit(solution)/shard_map/dot_general | solution.py:204
  41.2 2.2 %all-to-all-done.1 = bf16[8,2,2048]{2,1,0:T(2,128)(2,1)S(1)} async-done(((bf16[8,2,2048]{2,1,0:T(2,128)(2,1)}), bf16[8,2,2048]{2,1,0:T(2,128)(2,1)S(1)}, u32[]{:S(2)}, u32[]{:S(2)}) %all-to-all-start.1) | async-done | bytes 65568 | tf_op jit(solution)/shard_map/all_to_all | solution.py:275
  43.8 3.1 %fusion.50 = bf16[4,16,4096]{2,1,0:T(8,128)(2,1)S(1)} fusion(bf16[4,16,512]{2,1,0:T(8,128)(2,1)S(1)} %bitcast.99, bf16[512,4096,1]{1,0,2:T(8,128)(2,1)} %bitcast.93), kind=kOutput, calls=%fused_computation.96 | convolution fusion | flops 268435456 | bytes 4784128 | tf_op jit(solution)/shard_map/dot_general | solution.py:285
  46.9 0.8 %copy.74 = bf16[4,2,16,8,256]{4,3,1,0,2:T(8,128)(2,1)} copy(bf16[4,2,16,8,256]{4,3,2,1,0:T(8,128)(2,1)S(1)} %bitcast.94) | data formatting | bytes 1048576 | tf_op jit(solution)/shard_map/convert_element_type | solution.py:300
  47.7 6.0 %all-to-all-start.2 = ((bf16[4,16,16,256]{3,1,0,2:T(8,128)(2,1)}), bf16[4,16,16,256]{3,1,0,2:T(8,128)(2,1)S(1)}, u32[]{:S(2)}, u32[]{:S(2)}) async-start(bf16[4,16,16,256]{3,1,0,2:T(8,128)(2,1)} %bitcast.83), calls=%async_computation.2 | async-start | bytes 1048576 | tf_op jit(solution)/shard_map/all_to_all | solution.py:300
  53.7 0.7 fusion.33.swap_ref
  54.4 16.4 %shard_map.131 = bf16[2,128,8,512]{3,2,1,0:T(8,128)(2,1)} custom-call(f32[8]{0:T(128)} %get-tuple-element.18.rates_ref, s32[2]{0:T(128)} %copy-done.5, bf16[2,128,8,256]{3,2,1,0:T(8,128)(2,1)} %q_ref, bf16[2,128,8,256]{3,2,1,0:T(8,128)(2,1)} %k_ref, bf16[2,128,8,512]{3,2,1,0:T(8,128)(2,1)} %v_ref, bf16[2,8,256,512]{3,2,1,0:T(8,128)(2,1)} %prior_ref, ...), custom_call_target="tpu_custom_call" | custom-call | tf_op jit(solution)/shard_map/pallas_call | solution.py:114
  70.9 0.7 reduce_sum.32
  (62 shorter events, 4.3 us)
Async XLA Ops:
  0.6 1.6 %copy-start = (bf16[4096,1,1,256]{3,0,2,1:T(8,128)(2,1)S(1)}, bf16[4096,1,1,256]{3,0,2,1:T(8,128)(2,1)}, u32[]{:S(2)}) copy-start(bf16[4096,1,1,256]{3,0,2,1:T(8,128)(2,1)} %param.20) | copy-start | bytes 6291460
  0.6 3.3 %copy-start.1 = (bf16[4,16,4096]{2,1,0:T(8,128)(2,1)S(1)}, bf16[4,16,4096]{2,1,0:T(8,128)(2,1)}, u32[]{:S(2)}) copy-start(bf16[4,16,4096]{2,1,0:T(8,128)(2,1)} %param.18) | copy-start | bytes 1572868
  0.7 5.6 %copy-start.7 = (s32[256]{0:T(256)}, s32[256]{0:T(256)S(1)}, u32[]{:S(2)}) copy-start(s32[256]{0:T(256)S(1)} %iota_xor_fusion) | copy-start | bytes 3076
  2.2 4.4 %copy-start.2 = (bf16[4096,1,8,1,64]{0,4,3,2,1:T(8,128)(2,1)S(1)}, bf16[4096,1,8,1,64]{0,4,3,2,1:T(8,128)(2,1)}, u32[]{:S(2)}) copy-start(bf16[4096,1,8,1,64]{0,4,3,2,1:T(8,128)(2,1)} %param.21) | copy-start | bytes 12582916
  6.6 8.7 %copy-start.6 = (s32[16]{0:T(128)S(1)}, s32[16]{0:T(128)}, u32[]{:S(2)}) copy-start(s32[16]{0:T(128)} %param.17) | copy-start | bytes 196
  6.7 11.1 %copy-start.10 = (f32[16]{0:T(128)S(1)}, f32[16]{0:T(128)}, u32[]{:S(2)}) copy-start(f32[16]{0:T(128)} %param.16) | copy-start | bytes 196
  8.9 15.0 %all-to-all-start = ((bf16[8,4,2,1024]{3,1,2,0:T(4,128)(2,1)}), bf16[8,4,2,1024]{3,1,2,0:T(4,128)(2,1)S(1)}, u32[]{:S(2)}, u32[]{:S(2)}) async-start(bf16[8,4,2,1024]{3,1,2,0:T(4,128)(2,1)} %bitcast.86), calls=%async_computation | async-start | bytes 262144 | tf_op jit(solution)/shard_map/all_to_all | solution.py:233
  15.4 8.4 %copy-start.5 = (s32[2]{0:T(128)}, s32[2]{0:T(128)S(1)}, u32[]{:S(2)}) copy-start(s32[2]{0:T(128)S(1)} %get-tuple-element.15.live_ref) | copy-start | bytes 28
  19.4 4.5 %copy-start.3 = (f32[2,128,256]{2,1,0:T(8,128)}, f32[2,128,256]{2,1,0:T(8,128)S(1)}, u32[]{:S(2)}) copy-start(f32[2,128,256]{2,1,0:T(8,128)S(1)} %copy.37.cos_ref) | copy-start | bytes 786436
  19.7 4.1 %copy-start.4 = (f32[2,128,256]{2,1,0:T(8,128)}, f32[2,128,256]{2,1,0:T(8,128)S(1)}, u32[]{:S(2)}) copy-start(f32[2,128,256]{2,1,0:T(8,128)S(1)} %copy.39.sin_ref) | copy-start | bytes 786436
  20.6 3.9 %copy-start.9 = (f32[2,8]{1,0:T(2,128)S(1)}, f32[2,8]{1,0:T(2,128)}, u32[]{:S(2)}) copy-start(f32[2,8]{1,0:T(2,128)} %multiply_exponential_fusion.1) | copy-start | bytes 196
  32.2 11.2 %all-to-all-start.1 = ((bf16[8,2,2048]{2,1,0:T(2,128)(2,1)}), bf16[8,2,2048]{2,1,0:T(2,128)(2,1)S(1)}, u32[]{:S(2)}, u32[]{:S(2)}) async-start(bf16[8,2,2048]{2,1,0:T(2,128)(2,1)} %reshape.329), calls=%async_computation.1 | async-start | bytes 131072 | tf_op jit(solution)/shard_map/all_to_all | solution.py:275
  46.9 6.9 %copy-start.8 = (s32[256]{0:T(256)S(1)}, s32[256]{0:T(256)}, u32[]{:S(2)}) copy-start(s32[256]{0:T(256)} %copy-done.7) | copy-start | bytes 3076
  47.7 23.1 %all-to-all-start.2 = ((bf16[4,16,16,256]{3,1,0,2:T(8,128)(2,1)}), bf16[4,16,16,256]{3,1,0,2:T(8,128)(2,1)S(1)}, u32[]{:S(2)}, u32[]{:S(2)}) async-start(bf16[4,16,16,256]{3,1,0,2:T(8,128)(2,1)} %bitcast.83), calls=%async_computation.2 | async-start | bytes 1048576 | tf_op jit(solution)/shard_map/all_to_all | solution.py:300

commit v16 on v15

--- a/solution.py
+++ b/solution.py
@@ -106,33 +106,49 @@
     return cosine, sine_part, swap, rows, valid_rows
 
 
-def prefill_output(query_span, key_span, value_span, prior_state, local_rates, tables, live_count):
+def prefill_output(
+    query_span, key_span, value_span, prior_state, local_rates, tables, live_count,
+    first, count, earlier,
+):
     prompts_here, span_len, heads_here, key_width = query_span.shape
     value_width = value_span.shape[3]
     cosine, sine_part, swap, rows, valid_rows = tables
     whole = pl.BlockSpec(memory_space=pltpu.SMEM)
+    in_specs = [
+        whole,
+        whole,
+        pl.BlockSpec((None, span_len, heads_here, key_width), lambda i: (first + i, 0, 0, 0)),
+        pl.BlockSpec((None, span_len, heads_here, key_width), lambda i: (first + i, 0, 0, 0)),
+        pl.BlockSpec((None, span_len, heads_here, value_width), lambda i: (first + i, 0, 0, 0)),
+        pl.BlockSpec((None, heads_here, key_width, value_width), lambda i: (first + i, 0, 0, 0)),
+        pl.BlockSpec((None, span_len, key_width), lambda i: (first + i, 0, 0)),
+        pl.BlockSpec((None, span_len, key_width), lambda i: (first + i, 0, 0)),
+        pl.BlockSpec((key_width, key_width), lambda i: (0, 0)),
+    ]
+    operands = [
+        local_rates, live_count[first : first + count].astype(jnp.int32), query_span, key_span,
+        value_span, prior_state, cosine, sine_part, swap,
+    ]
+    kernel = output_kernel
+    aliases = {}
+    if earlier is not None:
+        in_specs.append(pl.BlockSpec(memory_space=pl.ANY))
+        operands.append(earlier)
+        aliases = {len(operands) - 1: 0}
+
+        def kernel(*refs):
+            output_kernel(*refs[:9], refs[10])
+
     return pl.pallas_call(
-        output_kernel,
-        grid=(prompts_here,),
-        in_specs=[
-            whole,
-            whole,
-            pl.BlockSpec((None, span_len, heads_here, key_width), lambda b: (b, 0, 0, 0)),
-            pl.BlockSpec((None, span_len, heads_here, key_width), lambda b: (b, 0, 0, 0)),
-            pl.BlockSpec((None, span_len, heads_here, value_width), lambda b: (b, 0, 0, 0)),
-            pl.BlockSpec((None, heads_here, key_width, value_width), lambda b: (b, 0, 0, 0)),
-            pl.BlockSpec((None, span_len, key_width), lambda b: (b, 0, 0)),
-            pl.BlockSpec((None, span_len, key_width), lambda b: (b, 0, 0)),
-            pl.BlockSpec((key_width, key_width), lambda b: (0, 0)),
-        ],
+        kernel,
+        grid=(count,),
+        in_specs=in_specs,
         out_specs=pl.BlockSpec(
-            (None, span_len, heads_here, value_width), lambda b: (b, 0, 0, 0)
+            (None, span_len, heads_here, value_width), lambda i: (first + i, 0, 0, 0)
         ),
         out_shape=jax.ShapeDtypeStruct(value_span.shape, jnp.bfloat16),
-    )(
-        local_rates, live_count.astype(jnp.int32), query_span, key_span, value_span,
-        prior_state, cosine, sine_part, swap,
-    )
+        input_output_aliases=aliases,
+    )(*operands)
 
 
 def per_device(
@@ -272,7 +288,16 @@
     normed = norm_with(readout, read_mean, read_square)
     normed = normed.reshape(step_total, prompts_here, heads_here, slots, value_slice)
     normed = normed.transpose(3, 0, 1, 2, 4)
+    first_half = prompts_here // 2
+    q_early, k_early, v_early, prior_early, normed = lax.optimization_barrier(
+        (query_span, key_span, value_span, prior_state, normed)
+    )
+    prefill_early = prefill_output(
+        q_early, k_early, v_early, prior_early, local_rates, tables, live_count,
+        0, first_half, None,
+    )
     normed = lax.all_to_all(normed.astype(jnp.bfloat16), "heads", 0, 0, tiled=True)
+    normed, prefill_early = lax.optimization_barrier((normed, prefill_early))
     normed = normed.transpose(1, 0, 2, 3, 4).reshape(
         step_total, total_prompts, heads_here, value_slice
     ).astype(jnp.float32)
@@ -292,7 +317,8 @@
         (query_span, key_span, value_span, prior_state, partial_out)
     )
     prefill_out = prefill_output(
-        query_span, key_span, value_span, prior_state, local_rates, tables, live_count
+        query_span, key_span, value_span, prior_state, local_rates, tables, live_count,
+        first_half, prompts_here - first_half, prefill_early,
     )
     out_slots = head_slots * lax.axis_size("tp")
     column_block = model_width // out_slots

time: 72.5 us -> 80.2 us (1.11)
  Pallas kernels: 16.4 us -> 19.9 us
  waiting for transfers between devices: 2.19 us -> 4.13 us
  starting transfers between devices: 17.8 us -> 19.4 us
    all_to_all x1, waiting for transfers between devices: 0.01 us -> 4.12 us  [per_device(): lax.all_to_all(pieces.astype(jnp.bfloat16), ('heads', 'tp'), 2, 2, tiled=...]
    pallas_call x1 -> x2, Pallas kernels: 16.4 us -> 19.9 us  [prefill_output(): pl.pallas_call(kernel, grid=(count,), in_specs=in_specs, out_specs=pl.Blo...]
    all_to_all x1, waiting for transfers between devices: 2.18 us -> 0.01 us  [per_device(): lax.all_to_all(normed.astype(jnp.bfloat16), 'heads', 0, 0, tiled=True)]
    all_to_all x1, starting transfers between devices: 6.02 us -> 7.53 us  [per_device(): lax.all_to_all(pieces.astype(jnp.bfloat16), ('heads', 'tp'), 2, 2, tiled=...]
    unnamed x24 -> x21, local copies, waits for them, and re-layouts: 1.62 us -> 1.46 us
  transfers between devices with their start and end apart: 3 -> 3, of which waited for: 1 -> 1; matrix products, arithmetic and copies ran while one was open for 18% -> 17% of each run, Pallas kernels for 23% -> 25%
where the time goes in v16:
time: 80.2 us; the launch traced here: 79.1 us
  matrix products  22.4 us (28%)
  Pallas kernels  19.9 us (25%)
  starting transfers between devices  19.4 us (24%)
  other arithmetic  7.11 us (9%)
  local copies, waits for them, and re-layouts  5.2 us (6%)
  waiting for transfers between devices  4.13 us (5%)
  between operations  1 us (1%)
    pallas_call x2, Pallas kernels, prefill_output(): pl.pallas_call(kernel, grid=(count,), in_specs=in_specs, out_specs=pl.Blo...  19.9 us
    all_to_all x1, starting transfers between devices, per_device(): lax.all_to_all(pieces.astype(jnp.bfloat16), ('heads', 'tp'), 2, 2, tiled=...  7.53 us
    all_to_all x1, starting transfers between devices, per_device(): arrived = lax.all_to_all(packed, 'heads', 0, 0, tiled=True)  6.39 us
    dot_general x1, matrix products, per_device(): jnp.einsum('tbhk,bhkv->tbhv', query_rot, state_new, preferred_element_typ...  6.24 us
    all_to_all x1, starting transfers between devices, per_device(): lax.all_to_all(normed.astype(jnp.bfloat16), 'heads', 0, 0, tiled=True)  5.44 us
    all_to_all x1, waiting for transfers between devices, per_device(): lax.all_to_all(pieces.astype(jnp.bfloat16), ('heads', 'tp'), 2, 2, tiled=...  4.12 us
    dot_general x1, matrix products, per_device(): jnp.dot(flat_inputs, w_gate.reshape(model_width, heads_here * value_slice...  3.68 us
    dot_general x1, matrix products, per_device(): jnp.einsum('bihk,kl->bihl', key_span, swap, preferred_element_type=jnp.fl...  3.23 us
  transfers between devices with their start and end apart: 3, of which 1 were waited for; matrix products, arithmetic and copies ran while one was open for 17% of the time, Pallas kernels for 25%

profile of v16, /device:TPU:1, one launch (start us, length us, event | category | flops | bytes accessed | tf_op | source)
XLA Modules:
  0.0 79.1 jit_solution(11948397537819917081)
XLA Ops:
  0.7 0.8 %add_convert_fusion.6 = f32[4,16]{1,0:T(4,128)S(1)} fusion(s32[16]{0:T(128)} %param.17), kind=kLoop, calls=%fused_computation.66 | loop fusion | flops 128 | bytes 320 | tf_op jit(solution)/shard_map/convert_element_type | solution.py:231
  1.6 0.6 copy-done
  2.2 1.6 %fusion.28 = bf16[64,256]{1,0:T(8,128)(2,1)S(1)} fusion(bf16[64,4096]{1,0:T(8,128)(2,1)} %bitcast.87, bf16[4096,1,1,256]{3,0,2,1:T(8,128)(2,1)S(1)} %copy-done), kind=kOutput, calls=%fused_computation.27 | convolution fusion | flops 134234112 | bytes 2654208 | tf_op jit(solution)/shard_map/dot_general | solution.py:211
  3.9 2.1 %fusion.25 = bf16[64,256]{1,0:T(8,128)(2,1)S(1)} fusion(bf16[64,4096]{1,0:T(8,128)(2,1)S(1)} %bitcast.88, bf16[4096,1,1,256]{3,0,2,1:T(8,128)(2,1)} %param.19), kind=kOutput, calls=%fused_computation.26 | convolution fusion | flops 134234112 | bytes 2654208 | tf_op jit(solution)/shard_map/dot_general | solution.py:208
  6.7 1.4 %convolution_convert_fusion = bf16[64,512]{1,0:T(8,128)(2,1)S(1)} fusion(bf16[64,4096]{1,0:T(8,128)(2,1)S(1)} %bitcast.89, bf16[4096,512]{0,1:T(8,128)(2,1)S(1)} %bitcast.91), kind=kOutput, calls=%fused_computation.18 | convolution fusion | flops 268468224 | bytes 4784128 | tf_op jit(solution)/shard_map/dot_general | solution.py:214
  8.1 0.8 copy.84
  8.9 6.4 %all-to-all-start = ((bf16[8,4,2,1024]{3,1,2,0:T(4,128)(2,1)}), bf16[8,4,2,1024]{3,1,2,0:T(4,128)(2,1)S(1)}, u32[]{:S(2)}, u32[]{:S(2)}) async-start(bf16[8,4,2,1024]{3,1,2,0:T(4,128)(2,1)} %bitcast.86), calls=%async_computation | async-start | bytes 262144 | tf_op jit(solution)/shard_map/all_to_all | solution.py:249
  17.1 0.6 convert_maximum_fusion.1
  18.4 0.6 multiply_exponential_fusion.1
  19.3 3.7 %fusion.50 = f32[64,512]{1,0:T(8,128)S(1)} fusion(bf16[64,4096]{1,0:T(8,128)(2,1)S(1)} %bitcast.90, bf16[4096,512]{0,1:T(8,128)(2,1)} %bitcast.92), kind=kOutput, calls=%fused_computation.96 | convolution fusion | flops 268435456 | bytes 4849664 | tf_op jit(solution)/shard_map/dot_general | solution.py:220
  23.3 0.8 %exponential_select_fusion = f32[2,128,8]{2,1,0:T(8,128)S(1)} fusion(f32[2,128]{1,0:T(2,128)} %convert_maximum_fusion.1, f32[8]{0:T(128)S(1)} %get-tuple-element.31, pred[2,128]{1,0:T(4,128)(4,1)} %iota_compare_fusion.3), kind=kLoop, calls=%fused_computation.43 | loop fusion | flops 4096 | bytes 9504 | tf_op jit(solution)/shard_map/jit(_where)/select_n | solution.py:195
  24.2 3.2 %multiply_convert_fusion = bf16[2,128,8,256]{3,2,1,0:T(8,128)(2,1)} fusion(bf16[2,128,8,256]{3,2,1,0:T(8,128)(2,1)} %refs_3_, f32[2,128,8]{2,1,0:T(8,128)S(1)} %exponential_select_fusion, f32[2,128,256]{2,1,0:T(8,128)S(1)} %copy.44.sin_ref.refs_7_, f32[2,128,256]{2,1,0:T(8,128)S(1)} %copy.42.cos_ref.refs_6_, s32[256]{0:T(256)} %copy-done.6), kind=kOutput, calls=%fused_computation.13 | convolution fusion | flops 273219584 | bytes 2630656 | tf_op jit(solution)/shard_map/bihk,kl->bihl/dot_general | solution.py:188
  28.1 6.2 %fusion.17 = f32[4,2,8,512]{3,0,2,1:T(4,128)S(1)} fusion(bf16[2,8,256,512]{3,2,1,0:T(8,128)(2,1)} %refs_5_, f32[2,8]{1,0:T(2,128)S(1)} %copy-done.8, bf16[2,128,8,512]{3,2,1,0:T(8,128)(2,1)} %refs_4_, bf16[2,128,8,256]{3,2,1,0:T(8,128)(2,1)} %multiply_convert_fusion, f32[4,8]{0,1:T(8,128)S(1)} %multiply_exponential_fusion, ...), kind=kOutput, calls=%fused_computation.17 | convolution fusion | flops 562069504 | bytes 7504064 | tf_op jit(solution)/shard_map/tbhk,bhkv->tbhv/dot_general | solution.py:266
  35.1 0.8 reshape.331
  35.8 5.4 %all-to-all-start.1 = ((bf16[8,2,2048]{2,1,0:T(2,128)(2,1)}), bf16[8,2,2048]{2,1,0:T(2,128)(2,1)S(1)}, u32[]{:S(2)}, u32[]{:S(2)}) async-start(bf16[8,2,2048]{2,1,0:T(2,128)(2,1)} %reshape.331), calls=%async_computation.1 | async-start | bytes 131072 | tf_op jit(solution)/shard_map/all_to_all | solution.py:299
  41.3 0.7 fusion.33.swap_ref.refs_8_
  42.0 0.6 fusion.49
  42.6 10.0 %shard_map.131.refs_9_ = bf16[2,128,8,512]{3,2,1,0:T(8,128)(2,1)} custom-call(f32[8]{0:T(128)} %get-tuple-element.32.rates_ref.refs_0_, s32[1]{0:T(128)} %get-tuple-element.39.live_ref, bf16[2,128,8,256]{3,2,1,0:T(8,128)(2,1)} %refs_2_, bf16[2,128,8,256]{3,2,1,0:T(8,128)(2,1)} %refs_3_, bf16[2,128,8,512]{3,2,1,0:T(8,128)(2,1)} %refs_4_, ...), custom_call_target="tpu_custom_call" | custom-call | tf_op jit(solution)/shard_map/pallas_call | solution.py:142
  52.9 3.0 %fusion.51 = bf16[4,16,4096]{2,1,0:T(8,128)(2,1)S(1)} fusion(bf16[4,16,512]{2,1,0:T(8,128)(2,1)S(1)} %bitcast.99, bf16[512,4096,1]{1,0,2:T(8,128)(2,1)} %bitcast.93), kind=kOutput, calls=%fused_computation.97 | convolution fusion | flops 268435456 | bytes 4784128 | tf_op jit(solution)/shard_map/dot_general | solution.py:310
  56.0 0.8 %copy.81 = bf16[4,2,16,8,256]{4,3,1,0,2:T(8,128)(2,1)} copy(bf16[4,2,16,8,256]{4,3,2,1,0:T(8,128)(2,1)S(1)} %bitcast.94) | data formatting | bytes 1048576 | tf_op jit(solution)/shard_map/convert_element_type | solution.py:326
  56.8 7.5 %all-to-all-start.2 = ((bf16[4,16,16,256]{3,1,0,2:T(8,128)(2,1)}), bf16[4,16,16,256]{3,1,0,2:T(8,128)(2,1)S(1)}, u32[]{:S(2)}, u32[]{:S(2)}) async-start(bf16[4,16,16,256]{3,1,0,2:T(8,128)(2,1)} %bitcast.83), calls=%async_computation.2 | async-start | bytes 1048576 | tf_op jit(solution)/shard_map/all_to_all | solution.py:326
  64.3 10.0 %shard_map.132 = bf16[2,128,8,512]{3,2,1,0:T(8,128)(2,1)} custom-call(f32[8]{0:T(128)} %get-tuple-element.32.rates_ref.refs_0_, s32[1]{0:T(128)} %get-tuple-element.40.refs_1_, bf16[2,128,8,256]{3,2,1,0:T(8,128)(2,1)} %refs_2_, bf16[2,128,8,256]{3,2,1,0:T(8,128)(2,1)} %refs_3_, bf16[2,128,8,512]{3,2,1,0:T(8,128)(2,1)} %refs_4_, ...), custom_call_target="tpu_custom_call", output_to_operand_aliasing={{}: (9, {})} | custom-call | tf_op jit(solution)/shard_map/pallas_call | solution.py:142
  74.3 4.1 %all-to-all-done.2 = bf16[4,16,16,256]{3,1,0,2:T(8,128)(2,1)S(1)} async-done(((bf16[4,16,16,256]{3,1,0,2:T(8,128)(2,1)}), bf16[4,16,16,256]{3,1,0,2:T(8,128)(2,1)S(1)}, u32[]{:S(2)}, u32[]{:S(2)}) %all-to-all-start.2) | async-done | bytes 524320 | tf_op jit(solution)/shard_map/all_to_all | solution.py:326
  78.4 0.7 reduce_sum.32
  (62 shorter events, 5.5 us)
Async XLA Ops:
  0.6 1.6 %copy-start = (bf16[4096,1,1,256]{3,0,2,1:T(8,128)(2,1)S(1)}, bf16[4096,1,1,256]{3,0,2,1:T(8,128)(2,1)}, u32[]{:S(2)}) copy-start(bf16[4096,1,1,256]{3,0,2,1:T(8,128)(2,1)} %param.20) | copy-start | bytes 6291460
  0.6 3.3 %copy-start.1 = (bf16[4,16,4096]{2,1,0:T(8,128)(2,1)S(1)}, bf16[4,16,4096]{2,1,0:T(8,128)(2,1)}, u32[]{:S(2)}) copy-start(bf16[4,16,4096]{2,1,0:T(8,128)(2,1)} %param.18) | copy-start | bytes 1572868
  0.7 5.6 %copy-start.6 = (s32[256]{0:T(256)}, s32[256]{0:T(256)S(1)}, u32[]{:S(2)}) copy-start(s32[256]{0:T(256)S(1)} %iota_xor_fusion) | copy-start | bytes 3076
  2.2 4.4 %copy-start.2 = (bf16[4096,1,8,1,64]{0,4,3,2,1:T(8,128)(2,1)S(1)}, bf16[4096,1,8,1,64]{0,4,3,2,1:T(8,128)(2,1)}, u32[]{:S(2)}) copy-start(bf16[4096,1,8,1,64]{0,4,3,2,1:T(8,128)(2,1)} %param.21) | copy-start | bytes 12582916
  6.6 8.7 %copy-start.5 = (s32[16]{0:T(128)S(1)}, s32[16]{0:T(128)}, u32[]{:S(2)}) copy-start(s32[16]{0:T(128)} %param.17) | copy-start | bytes 196
  6.7 11.1 %copy-start.9 = (f32[16]{0:T(128)S(1)}, f32[16]{0:T(128)}, u32[]{:S(2)}) copy-start(f32[16]{0:T(128)} %param.16) | copy-start | bytes 196
  8.9 18.6 %all-to-all-start = ((bf16[8,4,2,1024]{3,1,2,0:T(4,128)(2,1)}), bf16[8,4,2,1024]{3,1,2,0:T(4,128)(2,1)S(1)}, u32[]{:S(2)}, u32[]{:S(2)}) async-start(bf16[8,4,2,1024]{3,1,2,0:T(4,128)(2,1)} %bitcast.86), calls=%async_computation | async-start | bytes 262144 | tf_op jit(solution)/shard_map/all_to_all | solution.py:249
  19.3 4.9 %copy-start.3 = (f32[2,128,256]{2,1,0:T(8,128)}, f32[2,128,256]{2,1,0:T(8,128)S(1)}, u32[]{:S(2)}) copy-start(f32[2,128,256]{2,1,0:T(8,128)S(1)} %copy.42.cos_ref.refs_6_) | copy-start | bytes 786436
  23.3 4.1 %copy-start.4 = (f32[2,128,256]{2,1,0:T(8,128)}, f32[2,128,256]{2,1,0:T(8,128)S(1)}, u32[]{:S(2)}) copy-start(f32[2,128,256]{2,1,0:T(8,128)S(1)} %copy.44.sin_ref.refs_7_) | copy-start | bytes 786436
  24.2 3.9 %copy-start.8 = (f32[2,8]{1,0:T(2,128)S(1)}, f32[2,8]{1,0:T(2,128)}, u32[]{:S(2)}) copy-start(f32[2,8]{1,0:T(2,128)} %multiply_exponential_fusion.1) | copy-start | bytes 196
  28.1 13.2 %copy-start.7 = (s32[256]{0:T(256)S(1)}, s32[256]{0:T(256)}, u32[]{:S(2)}) copy-start(s32[256]{0:T(256)} %copy-done.6) | copy-start | bytes 3076
  35.8 16.7 %all-to-all-start.1 = ((bf16[8,2,2048]{2,1,0:T(2,128)(2,1)}), bf16[8,2,2048]{2,1,0:T(2,128)(2,1)S(1)}, u32[]{:S(2)}, u32[]{:S(2)}) async-start(bf16[8,2,2048]{2,1,0:T(2,128)(2,1)} %reshape.331), calls=%async_computation.1 | async-start | bytes 131072 | tf_op jit(solution)/shard_map/all_to_all | solution.py:299
  56.8 21.6 %all-to-all-start.2 = ((bf16[4,16,16,256]{3,1,0,2:T(8,128)(2,1)}), bf16[4,16,16,256]{3,1,0,2:T(8,128)(2,1)S(1)}, u32[]{:S(2)}, u32[]{:S(2)}) async-start(bf16[4,16,16,256]{3,1,0,2:T(8,128)(2,1)} %bitcast.83), calls=%async_computation.2 | async-start | bytes 1048576 | tf_op jit(solution)/shard_map/all_to_all | solution.py:326

commit v17 on v15

--- a/solution.py
+++ b/solution.py
@@ -53,10 +53,15 @@
         rate = rates_ref[head]
         q_raw = q_all[:, head, :]
         k_raw = k_all[:, head, :]
-        queries = turn_lanes(q_raw, swap, cosine, sine_part).astype(jnp.bfloat16)
-        keys = (turn_lanes(k_raw, swap, cosine, sine_part) * (k_raw.shape[-1] ** (-0.5))).astype(
-            jnp.bfloat16
-        )
+        both = jnp.concatenate([q_raw, k_raw], 0)
+        partner = jnp.dot(both, swap, preferred_element_type=jnp.float32)
+        queries = (
+            q_raw.astype(jnp.float32) * cosine + partner[:span_len] * sine_part
+        ).astype(jnp.bfloat16)
+        keys = (
+            (k_raw.astype(jnp.float32) * cosine + partner[span_len:] * sine_part)
+            * (k_raw.shape[-1] ** (-0.5))
+        ).astype(jnp.bfloat16)
         scores = lax.dot_general(
             queries, keys, (((1,), (1,)), ((), ())), preferred_element_type=jnp.float32
         )

time: 72.5 us -> 72.6 us (level)
  no operation moved by 1% of the time
where the time goes in v17:
time: 72.6 us; the launch traced here: 71.6 us
  matrix products  22.3 us (31%)
  starting transfers between devices  17.8 us (25%)
  Pallas kernels  16.5 us (23%)
  other arithmetic  7.16 us (10%)
  local copies, waits for them, and re-layouts  4.57 us (6%)
  waiting for transfers between devices  2.19 us (3%)
  between operations  1.01 us (1%)
    pallas_call x1, Pallas kernels, prefill_output(): pl.pallas_call(output_kernel, grid=(prompts_here,), in_specs=[whole, whol...  16.5 us
    all_to_all x1, starting transfers between devices, per_device(): arrived = lax.all_to_all(packed, 'heads', 0, 0, tiled=True)  6.39 us
    dot_general x1, matrix products, per_device(): jnp.einsum('tbhk,bhkv->tbhv', query_rot, state_new, preferred_element_typ...  6.24 us
    all_to_all x1, starting transfers between devices, per_device(): lax.all_to_all(pieces.astype(jnp.bfloat16), ('heads', 'tp'), 2, 2, tiled=...  6.02 us
    all_to_all x1, starting transfers between devices, per_device(): lax.all_to_all(normed.astype(jnp.bfloat16), 'heads', 0, 0, tiled=True)  5.44 us
    dot_general x1, matrix products, per_device(): jnp.dot(flat_inputs, w_gate.reshape(model_width, heads_here * value_slice...  3.58 us
    dot_general x1, matrix products, per_device(): jnp.einsum('bihk,kl->bihl', key_span, swap, preferred_element_type=jnp.fl...  3.24 us
    dot_general x1, matrix products, per_device(): jnp.dot(activated, w_out.reshape(heads_here * value_slice, model_width),...  3.06 us
  transfers between devices with their start and end apart: 3, of which 1 were waited for; matrix products, arithmetic and copies ran while one was open for 18% of the time, Pallas kernels for 23%

profile of v17, /device:TPU:1, one launch (start us, length us, event | category | flops | bytes accessed | tf_op | source)
XLA Modules:
  0.0 71.6 jit_solution(18319586099319888707)
XLA Ops:
  0.7 0.8 %add_convert_fusion.6 = f32[4,16]{1,0:T(4,128)S(1)} fusion(s32[16]{0:T(128)} %param.17), kind=kLoop, calls=%fused_computation.66 | loop fusion | flops 128 | bytes 320 | tf_op jit(solution)/shard_map/convert_element_type | solution.py:220
  1.6 0.6 copy-done
  2.2 1.6 %fusion.28 = bf16[64,256]{1,0:T(8,128)(2,1)S(1)} fusion(bf16[64,4096]{1,0:T(8,128)(2,1)} %bitcast.87, bf16[4096,1,1,256]{3,0,2,1:T(8,128)(2,1)S(1)} %copy-done), kind=kOutput, calls=%fused_computation.27 | convolution fusion | flops 134234112 | bytes 2654208 | tf_op jit(solution)/shard_map/dot_general | solution.py:200
  3.9 2.1 %fusion.25 = bf16[64,256]{1,0:T(8,128)(2,1)S(1)} fusion(bf16[64,4096]{1,0:T(8,128)(2,1)S(1)} %bitcast.88, bf16[4096,1,1,256]{3,0,2,1:T(8,128)(2,1)} %param.19), kind=kOutput, calls=%fused_computation.26 | convolution fusion | flops 134234112 | bytes 2654208 | tf_op jit(solution)/shard_map/dot_general | solution.py:197
  6.7 1.4 %convolution_convert_fusion = bf16[64,512]{1,0:T(8,128)(2,1)S(1)} fusion(bf16[64,4096]{1,0:T(8,128)(2,1)S(1)} %bitcast.89, bf16[4096,512]{0,1:T(8,128)(2,1)S(1)} %bitcast.91), kind=kOutput, calls=%fused_computation.18 | convolution fusion | flops 268468224 | bytes 4784128 | tf_op jit(solution)/shard_map/dot_general | solution.py:203
  8.1 0.8 %copy.77 = bf16[4,8,2,1024]{3,0,2,1:T(4,128)(2,1)} copy(bf16[4,8,2,1024]{3,2,1,0:T(2,128)(2,1)S(1)} %reshape.322) | data formatting | bytes 262144 | tf_op jit(solution)/shard_map/reshape | solution.py:237
  8.9 6.4 %all-to-all-start = ((bf16[8,4,2,1024]{3,1,2,0:T(4,128)(2,1)}), bf16[8,4,2,1024]{3,1,2,0:T(4,128)(2,1)S(1)}, u32[]{:S(2)}, u32[]{:S(2)}) async-start(bf16[8,4,2,1024]{3,1,2,0:T(4,128)(2,1)} %bitcast.86), calls=%async_computation | async-start | bytes 262144 | tf_op jit(solution)/shard_map/all_to_all | solution.py:238
  15.4 0.6 iota_compare_fusion.3
  17.1 0.6 convert_maximum_fusion.1
  17.8 0.6 fusion.47
  18.4 0.6 multiply_exponential_fusion.1
  19.7 0.8 %exponential_select_fusion = f32[2,128,8]{2,1,0:T(8,128)S(1)} fusion(f32[2,128]{1,0:T(2,128)} %convert_maximum_fusion.1, f32[8]{0:T(128)S(1)} %get-tuple-element.17, pred[2,128]{1,0:T(4,128)(4,1)} %iota_compare_fusion.3), kind=kLoop, calls=%fused_computation.43 | loop fusion | flops 4096 | bytes 9504 | tf_op jit(solution)/shard_map/jit(_where)/select_n | solution.py:184
  20.6 3.2 %multiply_convert_fusion = bf16[2,128,8,256]{3,2,1,0:T(8,128)(2,1)} fusion(bf16[2,128,8,256]{3,2,1,0:T(8,128)(2,1)} %k_ref, f32[2,128,8]{2,1,0:T(8,128)S(1)} %exponential_select_fusion, f32[2,128,256]{2,1,0:T(8,128)S(1)} %copy.39.sin_ref, f32[2,128,256]{2,1,0:T(8,128)S(1)} %copy.37.cos_ref, s32[256]{0:T(256)} %copy-done.7), kind=kOutput, calls=%fused_computation.13 | convolution fusion | flops 273219584 | bytes 2630656 | tf_op jit(solution)/shard_map/bihk,kl->bihl/dot_general | solution.py:177
  24.5 6.2 %fusion.17 = f32[4,2,8,512]{3,0,2,1:T(4,128)S(1)} fusion(bf16[2,8,256,512]{3,2,1,0:T(8,128)(2,1)} %prior_ref, f32[2,8]{1,0:T(2,128)S(1)} %copy-done.9, bf16[2,128,8,512]{3,2,1,0:T(8,128)(2,1)} %v_ref, bf16[2,128,8,256]{3,2,1,0:T(8,128)(2,1)} %multiply_convert_fusion, f32[4,8]{0,1:T(8,128)S(1)} %multiply_exponential_fusion, ...), kind=kOutput, calls=%fused_computation.17 | convolution fusion | flops 562069504 | bytes 7504064 | tf_op jit(solution)/shard_map/tbhk,bhkv->tbhv/dot_general | solution.py:255
  31.4 0.8 %reshape.329 = bf16[8,2,2048]{2,1,0:T(2,128)(2,1)} reshape(bf16[8,4,2,8,64]{4,3,2,1,0:T(8,128)(2,1)S(1)} %bitcast.98) | data formatting | bytes 131072
  32.2 5.4 %all-to-all-start.1 = ((bf16[8,2,2048]{2,1,0:T(2,128)(2,1)}), bf16[8,2,2048]{2,1,0:T(2,128)(2,1)S(1)}, u32[]{:S(2)}, u32[]{:S(2)}) async-start(bf16[8,2,2048]{2,1,0:T(2,128)(2,1)} %reshape.329), calls=%async_computation.1 | async-start | bytes 131072 | tf_op jit(solution)/shard_map/all_to_all | solution.py:280
  37.7 3.6 %fusion.49 = f32[64,512]{1,0:T(8,128)S(1)} fusion(bf16[64,4096]{1,0:T(8,128)(2,1)S(1)} %bitcast.90, bf16[4096,512]{0,1:T(8,128)(2,1)} %bitcast.92), kind=kOutput, calls=%fused_computation.95 | convolution fusion | flops 268435456 | bytes 4849664 | tf_op jit(solution)/shard_map/dot_general | solution.py:209
  41.2 2.2 %all-to-all-done.1 = bf16[8,2,2048]{2,1,0:T(2,128)(2,1)S(1)} async-done(((bf16[8,2,2048]{2,1,0:T(2,128)(2,1)}), bf16[8,2,2048]{2,1,0:T(2,128)(2,1)S(1)}, u32[]{:S(2)}, u32[]{:S(2)}) %all-to-all-start.1) | async-done | bytes 65568 | tf_op jit(solution)/shard_map/all_to_all | solution.py:280
  43.8 3.1 %fusion.50 = bf16[4,16,4096]{2,1,0:T(8,128)(2,1)S(1)} fusion(bf16[4,16,512]{2,1,0:T(8,128)(2,1)S(1)} %bitcast.99, bf16[512,4096,1]{1,0,2:T(8,128)(2,1)} %bitcast.93), kind=kOutput, calls=%fused_computation.96 | convolution fusion | flops 268435456 | bytes 4784128 | tf_op jit(solution)/shard_map/dot_general | solution.py:290
  46.9 0.8 %copy.74 = bf16[4,2,16,8,256]{4,3,1,0,2:T(8,128)(2,1)} copy(bf16[4,2,16,8,256]{4,3,2,1,0:T(8,128)(2,1)S(1)} %bitcast.94) | data formatting | bytes 1048576 | tf_op jit(solution)/shard_map/convert_element_type | solution.py:305
  47.7 6.0 %all-to-all-start.2 = ((bf16[4,16,16,256]{3,1,0,2:T(8,128)(2,1)}), bf16[4,16,16,256]{3,1,0,2:T(8,128)(2,1)S(1)}, u32[]{:S(2)}, u32[]{:S(2)}) async-start(bf16[4,16,16,256]{3,1,0,2:T(8,128)(2,1)} %bitcast.83), calls=%async_computation.2 | async-start | bytes 1048576 | tf_op jit(solution)/shard_map/all_to_all | solution.py:305
  53.7 0.7 fusion.33.swap_ref
  54.4 16.5 %shard_map.131 = bf16[2,128,8,512]{3,2,1,0:T(8,128)(2,1)} custom-call(f32[8]{0:T(128)} %get-tuple-element.18.rates_ref, s32[2]{0:T(128)} %copy-done.5, bf16[2,128,8,256]{3,2,1,0:T(8,128)(2,1)} %q_ref, bf16[2,128,8,256]{3,2,1,0:T(8,128)(2,1)} %k_ref, bf16[2,128,8,512]{3,2,1,0:T(8,128)(2,1)} %v_ref, bf16[2,8,256,512]{3,2,1,0:T(8,128)(2,1)} %prior_ref, ...), custom_call_target="tpu_custom_call" | custom-call | tf_op jit(solution)/shard_map/pallas_call | solution.py:119
  70.9 0.7 reduce_sum.32
  (62 shorter events, 4.3 us)
Async XLA Ops:
  0.6 1.6 %copy-start = (bf16[4096,1,1,256]{3,0,2,1:T(8,128)(2,1)S(1)}, bf16[4096,1,1,256]{3,0,2,1:T(8,128)(2,1)}, u32[]{:S(2)}) copy-start(bf16[4096,1,1,256]{3,0,2,1:T(8,128)(2,1)} %param.20) | copy-start | bytes 6291460
  0.6 3.3 %copy-start.1 = (bf16[4,16,4096]{2,1,0:T(8,128)(2,1)S(1)}, bf16[4,16,4096]{2,1,0:T(8,128)(2,1)}, u32[]{:S(2)}) copy-start(bf16[4,16,4096]{2,1,0:T(8,128)(2,1)} %param.18) | copy-start | bytes 1572868
  0.7 5.6 %copy-start.7 = (s32[256]{0:T(256)}, s32[256]{0:T(256)S(1)}, u32[]{:S(2)}) copy-start(s32[256]{0:T(256)S(1)} %iota_xor_fusion) | copy-start | bytes 3076
  2.2 4.4 %copy-start.2 = (bf16[4096,1,8,1,64]{0,4,3,2,1:T(8,128)(2,1)S(1)}, bf16[4096,1,8,1,64]{0,4,3,2,1:T(8,128)(2,1)}, u32[]{:S(2)}) copy-start(bf16[4096,1,8,1,64]{0,4,3,2,1:T(8,128)(2,1)} %param.21) | copy-start | bytes 12582916
  6.6 8.7 %copy-start.6 = (s32[16]{0:T(128)S(1)}, s32[16]{0:T(128)}, u32[]{:S(2)}) copy-start(s32[16]{0:T(128)} %param.17) | copy-start | bytes 196
  6.7 11.1 %copy-start.10 = (f32[16]{0:T(128)S(1)}, f32[16]{0:T(128)}, u32[]{:S(2)}) copy-start(f32[16]{0:T(128)} %param.16) | copy-start | bytes 196
  8.9 15.0 %all-to-all-start = ((bf16[8,4,2,1024]{3,1,2,0:T(4,128)(2,1)}), bf16[8,4,2,1024]{3,1,2,0:T(4,128)(2,1)S(1)}, u32[]{:S(2)}, u32[]{:S(2)}) async-start(bf16[8,4,2,1024]{3,1,2,0:T(4,128)(2,1)} %bitcast.86), calls=%async_computation | async-start | bytes 262144 | tf_op jit(solution)/shard_map/all_to_all | solution.py:238
  15.4 8.4 %copy-start.5 = (s32[2]{0:T(128)}, s32[2]{0:T(128)S(1)}, u32[]{:S(2)}) copy-start(s32[2]{0:T(128)S(1)} %get-tuple-element.15.live_ref) | copy-start | bytes 28
  19.4 4.5 %copy-start.3 = (f32[2,128,256]{2,1,0:T(8,128)}, f32[2,128,256]{2,1,0:T(8,128)S(1)}, u32[]{:S(2)}) copy-start(f32[2,128,256]{2,1,0:T(8,128)S(1)} %copy.37.cos_ref) | copy-start | bytes 786436
  19.7 4.1 %copy-start.4 = (f32[2,128,256]{2,1,0:T(8,128)}, f32[2,128,256]{2,1,0:T(8,128)S(1)}, u32[]{:S(2)}) copy-start(f32[2,128,256]{2,1,0:T(8,128)S(1)} %copy.39.sin_ref) | copy-start | bytes 786436
  20.6 3.9 %copy-start.9 = (f32[2,8]{1,0:T(2,128)S(1)}, f32[2,8]{1,0:T(2,128)}, u32[]{:S(2)}) copy-start(f32[2,8]{1,0:T(2,128)} %multiply_exponential_fusion.1) | copy-start | bytes 196
  32.2 11.2 %all-to-all-start.1 = ((bf16[8,2,2048]{2,1,0:T(2,128)(2,1)}), bf16[8,2,2048]{2,1,0:T(2,128)(2,1)S(1)}, u32[]{:S(2)}, u32[]{:S(2)}) async-start(bf16[8,2,2048]{2,1,0:T(2,128)(2,1)} %reshape.329), calls=%async_computation.1 | async-start | bytes 131072 | tf_op jit(solution)/shard_map/all_to_all | solution.py:280
  46.9 6.9 %copy-start.8 = (s32[256]{0:T(256)S(1)}, s32[256]{0:T(256)}, u32[]{:S(2)}) copy-start(s32[256]{0:T(256)} %copy-done.7) | copy-start | bytes 3076
  47.7 23.2 %all-to-all-start.2 = ((bf16[4,16,16,256]{3,1,0,2:T(8,128)(2,1)}), bf16[4,16,16,256]{3,1,0,2:T(8,128)(2,1)S(1)}, u32[]{:S(2)}, u32[]{:S(2)}) async-start(bf16[4,16,16,256]{3,1,0,2:T(8,128)(2,1)} %bitcast.83), calls=%async_computation.2 | async-start | bytes 1048576 | tf_op jit(solution)/shard_map/all_to_all | solution.py:305

commit v18 on v15

--- a/solution.py
+++ b/solution.py
@@ -189,12 +189,14 @@
     )
     slots = head_slots
     flat_inputs = decode_inputs.reshape(step_total * total_prompts, model_width)
-    query_part = jnp.dot(
-        flat_inputs, w_query.reshape(model_width, key_piece), preferred_element_type=jnp.float32
-    ).astype(jnp.bfloat16)
-    key_part = jnp.dot(
-        flat_inputs, w_key.reshape(model_width, key_piece), preferred_element_type=jnp.float32
-    ).astype(jnp.bfloat16)
+    query_part = lax.dot_general(
+        w_query.reshape(model_width, key_piece), flat_inputs, (((0,), (1,)), ((), ())),
+        preferred_element_type=jnp.float32,
+    ).T.astype(jnp.bfloat16)
+    key_part = lax.dot_general(
+        w_key.reshape(model_width, key_piece), flat_inputs, (((0,), (1,)), ((), ())),
+        preferred_element_type=jnp.float32,
+    ).T.astype(jnp.bfloat16)
     value_dec = jnp.dot(
         flat_inputs,
         w_value.reshape(model_width, heads_here * value_slice),

time: 72.5 us -> 72.5 us (level)
  no operation moved by 1% of the time
where the time goes in v18:
time: 72.5 us; the launch traced here: 71.6 us
  matrix products  22.3 us (31%)
  starting transfers between devices  17.8 us (25%)
  Pallas kernels  16.4 us (23%)
  other arithmetic  7.16 us (10%)
  local copies, waits for them, and re-layouts  4.57 us (6%)
  waiting for transfers between devices  2.19 us (3%)
  between operations  1.01 us (1%)
    pallas_call x1, Pallas kernels, prefill_output(): pl.pallas_call(output_kernel, grid=(prompts_here,), in_specs=[whole, whol...  16.4 us
    all_to_all x1, starting transfers between devices, per_device(): arrived = lax.all_to_all(packed, 'heads', 0, 0, tiled=True)  6.39 us
    dot_general x1, matrix products, per_device(): jnp.einsum('tbhk,bhkv->tbhv', query_rot, state_new, preferred_element_typ...  6.24 us
    all_to_all x1, starting transfers between devices, per_device(): lax.all_to_all(pieces.astype(jnp.bfloat16), ('heads', 'tp'), 2, 2, tiled=...  6.02 us
    all_to_all x1, starting transfers between devices, per_device(): lax.all_to_all(normed.astype(jnp.bfloat16), 'heads', 0, 0, tiled=True)  5.44 us
    dot_general x1, matrix products, per_device(): jnp.dot(flat_inputs, w_gate.reshape(model_width, heads_here * value_slice...  3.58 us
    dot_general x1, matrix products, per_device(): jnp.einsum('bihk,kl->bihl', key_span, swap, preferred_element_type=jnp.fl...  3.24 us
    dot_general x1, matrix products, per_device(): jnp.dot(activated, w_out.reshape(heads_here * value_slice, model_width),...  3.06 us
  transfers between devices with their start and end apart: 3, of which 1 were waited for; matrix products, arithmetic and copies ran while one was open for 18% of the time, Pallas kernels for 23%

profile of v18, /device:TPU:1, one launch (start us, length us, event | category | flops | bytes accessed | tf_op | source)
XLA Modules:
  0.0 71.6 jit_solution(6643020018143113597)
XLA Ops:
  0.7 0.8 %add_convert_fusion.6 = f32[4,16]{1,0:T(4,128)S(1)} fusion(s32[16]{0:T(128)} %param.17), kind=kLoop, calls=%fused_computation.66 | loop fusion | flops 128 | bytes 320 | tf_op jit(solution)/shard_map/convert_element_type | solution.py:217
  1.6 0.6 copy-done
  2.2 1.6 %fusion.28 = bf16[64,256]{1,0:T(8,128)(2,1)S(1)} fusion(bf16[64,4096]{1,0:T(8,128)(2,1)} %bitcast.87, bf16[4096,1,1,256]{3,0,2,1:T(8,128)(2,1)S(1)} %copy-done), kind=kOutput, calls=%fused_computation.27 | convolution fusion | flops 134234112 | bytes 2654208 | tf_op jit(solution)/shard_map/dot_general | solution.py:196
  3.9 2.1 %fusion.25 = bf16[64,256]{1,0:T(8,128)(2,1)S(1)} fusion(bf16[64,4096]{1,0:T(8,128)(2,1)S(1)} %bitcast.88, bf16[4096,1,1,256]{3,0,2,1:T(8,128)(2,1)} %param.19), kind=kOutput, calls=%fused_computation.26 | convolution fusion | flops 134234112 | bytes 2654208 | tf_op jit(solution)/shard_map/dot_general | solution.py:192
  6.7 1.4 %convolution_convert_fusion = bf16[64,512]{1,0:T(8,128)(2,1)S(1)} fusion(bf16[64,4096]{1,0:T(8,128)(2,1)S(1)} %bitcast.89, bf16[4096,512]{0,1:T(8,128)(2,1)S(1)} %bitcast.91), kind=kOutput, calls=%fused_computation.18 | convolution fusion | flops 268468224 | bytes 4784128 | tf_op jit(solution)/shard_map/dot_general | solution.py:200
  8.1 0.8 %copy.77 = bf16[4,8,2,1024]{3,0,2,1:T(4,128)(2,1)} copy(bf16[4,8,2,1024]{3,2,1,0:T(2,128)(2,1)S(1)} %reshape.322) | data formatting | bytes 262144 | tf_op jit(solution)/shard_map/reshape | solution.py:234
  8.9 6.4 %all-to-all-start = ((bf16[8,4,2,1024]{3,1,2,0:T(4,128)(2,1)}), bf16[8,4,2,1024]{3,1,2,0:T(4,128)(2,1)S(1)}, u32[]{:S(2)}, u32[]{:S(2)}) async-start(bf16[8,4,2,1024]{3,1,2,0:T(4,128)(2,1)} %bitcast.86), calls=%async_computation | async-start | bytes 262144 | tf_op jit(solution)/shard_map/all_to_all | solution.py:235
  15.4 0.6 iota_compare_fusion.3
  17.1 0.6 convert_maximum_fusion.1
  17.8 0.6 fusion.47
  18.4 0.6 multiply_exponential_fusion.1
  19.7 0.8 %exponential_select_fusion = f32[2,128,8]{2,1,0:T(8,128)S(1)} fusion(f32[2,128]{1,0:T(2,128)} %convert_maximum_fusion.1, f32[8]{0:T(128)S(1)} %get-tuple-element.17, pred[2,128]{1,0:T(4,128)(4,1)} %iota_compare_fusion.3), kind=kLoop, calls=%fused_computation.43 | loop fusion | flops 4096 | bytes 9504 | tf_op jit(solution)/shard_map/jit(_where)/select_n | solution.py:179
  20.6 3.2 %multiply_convert_fusion = bf16[2,128,8,256]{3,2,1,0:T(8,128)(2,1)} fusion(bf16[2,128,8,256]{3,2,1,0:T(8,128)(2,1)} %k_ref, f32[2,128,8]{2,1,0:T(8,128)S(1)} %exponential_select_fusion, f32[2,128,256]{2,1,0:T(8,128)S(1)} %copy.39.sin_ref, f32[2,128,256]{2,1,0:T(8,128)S(1)} %copy.37.cos_ref, s32[256]{0:T(256)} %copy-done.7), kind=kOutput, calls=%fused_computation.13 | convolution fusion | flops 273219584 | bytes 2630656 | tf_op jit(solution)/shard_map/bihk,kl->bihl/dot_general | solution.py:172
  24.5 6.2 %fusion.17 = f32[4,2,8,512]{3,0,2,1:T(4,128)S(1)} fusion(bf16[2,8,256,512]{3,2,1,0:T(8,128)(2,1)} %prior_ref, f32[2,8]{1,0:T(2,128)S(1)} %copy-done.9, bf16[2,128,8,512]{3,2,1,0:T(8,128)(2,1)} %v_ref, bf16[2,128,8,256]{3,2,1,0:T(8,128)(2,1)} %multiply_convert_fusion, f32[4,8]{0,1:T(8,128)S(1)} %multiply_exponential_fusion, ...), kind=kOutput, calls=%fused_computation.17 | convolution fusion | flops 562069504 | bytes 7504064 | tf_op jit(solution)/shard_map/tbhk,bhkv->tbhv/dot_general | solution.py:252
  31.4 0.8 %reshape.329 = bf16[8,2,2048]{2,1,0:T(2,128)(2,1)} reshape(bf16[8,4,2,8,64]{4,3,2,1,0:T(8,128)(2,1)S(1)} %bitcast.98) | data formatting | bytes 131072
  32.2 5.4 %all-to-all-start.1 = ((bf16[8,2,2048]{2,1,0:T(2,128)(2,1)}), bf16[8,2,2048]{2,1,0:T(2,128)(2,1)S(1)}, u32[]{:S(2)}, u32[]{:S(2)}) async-start(bf16[8,2,2048]{2,1,0:T(2,128)(2,1)} %reshape.329), calls=%async_computation.1 | async-start | bytes 131072 | tf_op jit(solution)/shard_map/all_to_all | solution.py:277
  37.7 3.6 %fusion.49 = f32[64,512]{1,0:T(8,128)S(1)} fusion(bf16[64,4096]{1,0:T(8,128)(2,1)S(1)} %bitcast.90, bf16[4096,512]{0,1:T(8,128)(2,1)} %bitcast.92), kind=kOutput, calls=%fused_computation.95 | convolution fusion | flops 268435456 | bytes 4849664 | tf_op jit(solution)/shard_map/dot_general | solution.py:206
  41.2 2.2 %all-to-all-done.1 = bf16[8,2,2048]{2,1,0:T(2,128)(2,1)S(1)} async-done(((bf16[8,2,2048]{2,1,0:T(2,128)(2,1)}), bf16[8,2,2048]{2,1,0:T(2,128)(2,1)S(1)}, u32[]{:S(2)}, u32[]{:S(2)}) %all-to-all-start.1) | async-done | bytes 65568 | tf_op jit(solution)/shard_map/all_to_all | solution.py:277
  43.8 3.1 %fusion.50 = bf16[4,16,4096]{2,1,0:T(8,128)(2,1)S(1)} fusion(bf16[4,16,512]{2,1,0:T(8,128)(2,1)S(1)} %bitcast.99, bf16[512,4096,1]{1,0,2:T(8,128)(2,1)} %bitcast.93), kind=kOutput, calls=%fused_computation.96 | convolution fusion | flops 268435456 | bytes 4784128 | tf_op jit(solution)/shard_map/dot_general | solution.py:287
  46.9 0.8 %copy.74 = bf16[4,2,16,8,256]{4,3,1,0,2:T(8,128)(2,1)} copy(bf16[4,2,16,8,256]{4,3,2,1,0:T(8,128)(2,1)S(1)} %bitcast.94) | data formatting | bytes 1048576 | tf_op jit(solution)/shard_map/convert_element_type | solution.py:302
  47.7 6.0 %all-to-all-start.2 = ((bf16[4,16,16,256]{3,1,0,2:T(8,128)(2,1)}), bf16[4,16,16,256]{3,1,0,2:T(8,128)(2,1)S(1)}, u32[]{:S(2)}, u32[]{:S(2)}) async-start(bf16[4,16,16,256]{3,1,0,2:T(8,128)(2,1)} %bitcast.83), calls=%async_computation.2 | async-start | bytes 1048576 | tf_op jit(solution)/shard_map/all_to_all | solution.py:302
  53.7 0.7 fusion.33.swap_ref
  54.4 16.4 %shard_map.131 = bf16[2,128,8,512]{3,2,1,0:T(8,128)(2,1)} custom-call(f32[8]{0:T(128)} %get-tuple-element.18.rates_ref, s32[2]{0:T(128)} %copy-done.5, bf16[2,128,8,256]{3,2,1,0:T(8,128)(2,1)} %q_ref, bf16[2,128,8,256]{3,2,1,0:T(8,128)(2,1)} %k_ref, bf16[2,128,8,512]{3,2,1,0:T(8,128)(2,1)} %v_ref, bf16[2,8,256,512]{3,2,1,0:T(8,128)(2,1)} %prior_ref, ...), custom_call_target="tpu_custom_call" | custom-call | tf_op jit(solution)/shard_map/pallas_call | solution.py:114
  70.9 0.7 reduce_sum.32
  (62 shorter events, 4.3 us)
Async XLA Ops:
  0.6 1.6 %copy-start = (bf16[4096,1,1,256]{3,0,2,1:T(8,128)(2,1)S(1)}, bf16[4096,1,1,256]{3,0,2,1:T(8,128)(2,1)}, u32[]{:S(2)}) copy-start(bf16[4096,1,1,256]{3,0,2,1:T(8,128)(2,1)} %param.20) | copy-start | bytes 6291460
  0.6 3.3 %copy-start.1 = (bf16[4,16,4096]{2,1,0:T(8,128)(2,1)S(1)}, bf16[4,16,4096]{2,1,0:T(8,128)(2,1)}, u32[]{:S(2)}) copy-start(bf16[4,16,4096]{2,1,0:T(8,128)(2,1)} %param.18) | copy-start | bytes 1572868
  0.7 5.6 %copy-start.7 = (s32[256]{0:T(256)}, s32[256]{0:T(256)S(1)}, u32[]{:S(2)}) copy-start(s32[256]{0:T(256)S(1)} %iota_xor_fusion) | copy-start | bytes 3076
  2.2 4.4 %copy-start.2 = (bf16[4096,1,8,1,64]{0,4,3,2,1:T(8,128)(2,1)S(1)}, bf16[4096,1,8,1,64]{0,4,3,2,1:T(8,128)(2,1)}, u32[]{:S(2)}) copy-start(bf16[4096,1,8,1,64]{0,4,3,2,1:T(8,128)(2,1)} %param.21) | copy-start | bytes 12582916
  6.6 8.7 %copy-start.6 = (s32[16]{0:T(128)S(1)}, s32[16]{0:T(128)}, u32[]{:S(2)}) copy-start(s32[16]{0:T(128)} %param.17) | copy-start | bytes 196
  6.7 11.1 %copy-start.10 = (f32[16]{0:T(128)S(1)}, f32[16]{0:T(128)}, u32[]{:S(2)}) copy-start(f32[16]{0:T(128)} %param.16) | copy-start | bytes 196
  8.9 15.0 %all-to-all-start = ((bf16[8,4,2,1024]{3,1,2,0:T(4,128)(2,1)}), bf16[8,4,2,1024]{3,1,2,0:T(4,128)(2,1)S(1)}, u32[]{:S(2)}, u32[]{:S(2)}) async-start(bf16[8,4,2,1024]{3,1,2,0:T(4,128)(2,1)} %bitcast.86), calls=%async_computation | async-start | bytes 262144 | tf_op jit(solution)/shard_map/all_to_all | solution.py:235
  15.4 8.4 %copy-start.5 = (s32[2]{0:T(128)}, s32[2]{0:T(128)S(1)}, u32[]{:S(2)}) copy-start(s32[2]{0:T(128)S(1)} %get-tuple-element.15.live_ref) | copy-start | bytes 28
  19.4 4.5 %copy-start.3 = (f32[2,128,256]{2,1,0:T(8,128)}, f32[2,128,256]{2,1,0:T(8,128)S(1)}, u32[]{:S(2)}) copy-start(f32[2,128,256]{2,1,0:T(8,128)S(1)} %copy.37.cos_ref) | copy-start | bytes 786436
  19.7 4.1 %copy-start.4 = (f32[2,128,256]{2,1,0:T(8,128)}, f32[2,128,256]{2,1,0:T(8,128)S(1)}, u32[]{:S(2)}) copy-start(f32[2,128,256]{2,1,0:T(8,128)S(1)} %copy.39.sin_ref) | copy-start | bytes 786436
  20.6 3.9 %copy-start.9 = (f32[2,8]{1,0:T(2,128)S(1)}, f32[2,8]{1,0:T(2,128)}, u32[]{:S(2)}) copy-start(f32[2,8]{1,0:T(2,128)} %multiply_exponential_fusion.1) | copy-start | bytes 196
  32.2 11.2 %all-to-all-start.1 = ((bf16[8,2,2048]{2,1,0:T(2,128)(2,1)}), bf16[8,2,2048]{2,1,0:T(2,128)(2,1)S(1)}, u32[]{:S(2)}, u32[]{:S(2)}) async-start(bf16[8,2,2048]{2,1,0:T(2,128)(2,1)} %reshape.329), calls=%async_computation.1 | async-start | bytes 131072 | tf_op jit(solution)/shard_map/all_to_all | solution.py:277
  46.9 6.9 %copy-start.8 = (s32[256]{0:T(256)S(1)}, s32[256]{0:T(256)}, u32[]{:S(2)}) copy-start(s32[256]{0:T(256)} %copy-done.7) | copy-start | bytes 3076
  47.7 23.1 %all-to-all-start.2 = ((bf16[4,16,16,256]{3,1,0,2:T(8,128)(2,1)}), bf16[4,16,16,256]{3,1,0,2:T(8,128)(2,1)S(1)}, u32[]{:S(2)}, u32[]{:S(2)}) async-start(bf16[4,16,16,256]{3,1,0,2:T(8,128)(2,1)} %bitcast.83), calls=%async_computation.2 | async-start | bytes 1048576 | tf_op jit(solution)/shard_map/all_to_all | solution.py:302

commit v19 on v15

--- a/solution.py
+++ b/solution.py
@@ -1,4 +1,5 @@
 import jax
+import numpy as np
 import jax.numpy as jnp
 from jax import lax
 from jax.experimental import pallas as pl
@@ -81,8 +82,8 @@
     cosine = jnp.repeat(jnp.cos(angles), 2, axis=-1)
     sine_part = jnp.sin(angles)
     sine_part = jnp.stack([-sine_part, sine_part], -1).reshape(cosine.shape)
-    lane = jnp.arange(key_width)
-    swap = (lane[:, None] == (lane[None, :] ^ 1)).astype(jnp.bfloat16)
+    pairs = np.arange(key_width)
+    swap = jnp.asarray((pairs[:, None] == (pairs[None, :] ^ 1)).astype(np.float32), jnp.bfloat16)
     valid_rows = offsets[None, :] < live_count[:, None]
     lead_decay = jnp.exp(-local_rates[:, None] * (offsets[None, :] + 1).astype(jnp.float32))
     remaining = (live_count[:, None] - 1 - offsets[None, :]).astype(jnp.float32)

time: 72.5 us -> 71.8 us (level)
    unnamed x24 -> x20, local copies, waits for them, and re-layouts: 1.62 us -> 1.62 us
  transfers between devices with their start and end apart: 3 -> 3, of which waited for: 1 -> 1; matrix products, arithmetic and copies ran while one was open for 18% -> 17% of each run, Pallas kernels for 23% -> 23%
where the time goes in v19:
time: 71.8 us; the launch traced here: 70.8 us
  matrix products  22.3 us (31%)
  starting transfers between devices  17.8 us (25%)
  Pallas kernels  16.5 us (23%)
  other arithmetic  6.47 us (9%)
  local copies, waits for them, and re-layouts  4.57 us (6%)
  waiting for transfers between devices  2.2 us (3%)
  between operations  0.98 us (1%)
    pallas_call x1, Pallas kernels, prefill_output(): pl.pallas_call(output_kernel, grid=(prompts_here,), in_specs=[whole, whol...  16.5 us
    all_to_all x1, starting transfers between devices, per_device(): arrived = lax.all_to_all(packed, 'heads', 0, 0, tiled=True)  6.38 us
    dot_general x1, matrix products, per_device(): jnp.einsum('tbhk,bhkv->tbhv', query_rot, state_new, preferred_element_typ...  6.24 us
    all_to_all x1, starting transfers between devices, per_device(): lax.all_to_all(pieces.astype(jnp.bfloat16), ('heads', 'tp'), 2, 2, tiled=...  6 us
    all_to_all x1, starting transfers between devices, per_device(): lax.all_to_all(normed.astype(jnp.bfloat16), 'heads', 0, 0, tiled=True)  5.44 us
    dot_general x1, matrix products, per_device(): jnp.dot(flat_inputs, w_gate.reshape(model_width, heads_here * value_slice...  3.58 us
    dot_general x1, matrix products, per_device(): jnp.einsum('bihk,kl->bihl', key_span, swap, preferred_element_type=jnp.fl...  3.24 us
    dot_general x1, matrix products, per_device(): jnp.dot(activated, w_out.reshape(heads_here * value_slice, model_width),...  3.06 us
  transfers between devices with their start and end apart: 3, of which 1 were waited for; matrix products, arithmetic and copies ran while one was open for 17% of the time, Pallas kernels for 23%

profile of v19, /device:TPU:1, one launch (start us, length us, event | category | flops | bytes accessed | tf_op | source)
XLA Modules:
  0.0 70.8 jit_solution(6415014841895357314)
XLA Ops:
  0.7 0.8 %add_convert_fusion.6 = f32[4,16]{1,0:T(4,128)S(1)} fusion(s32[16]{0:T(128)} %param.18), kind=kLoop, calls=%fused_computation.63 | loop fusion | flops 128 | bytes 320 | tf_op jit(solution)/shard_map/convert_element_type | solution.py:216
  1.6 0.6 copy-done
  2.2 1.6 %fusion.28 = bf16[64,256]{1,0:T(8,128)(2,1)S(1)} fusion(bf16[64,4096]{1,0:T(8,128)(2,1)} %bitcast.86, bf16[4096,1,1,256]{3,0,2,1:T(8,128)(2,1)S(1)} %copy-done), kind=kOutput, calls=%fused_computation.27 | convolution fusion | flops 134234112 | bytes 2654208 | tf_op jit(solution)/shard_map/dot_general | solution.py:196
  3.9 2.1 %fusion.25 = bf16[64,256]{1,0:T(8,128)(2,1)S(1)} fusion(bf16[64,4096]{1,0:T(8,128)(2,1)S(1)} %bitcast.87, bf16[4096,1,1,256]{3,0,2,1:T(8,128)(2,1)} %param.20), kind=kOutput, calls=%fused_computation.26 | convolution fusion | flops 134234112 | bytes 2654208 | tf_op jit(solution)/shard_map/dot_general | solution.py:193
  6.7 1.4 %convolution_convert_fusion = bf16[64,512]{1,0:T(8,128)(2,1)S(1)} fusion(bf16[64,4096]{1,0:T(8,128)(2,1)S(1)} %bitcast.88, bf16[4096,512]{0,1:T(8,128)(2,1)S(1)} %bitcast.90), kind=kOutput, calls=%fused_computation.18 | convolution fusion | flops 268468224 | bytes 4784128 | tf_op jit(solution)/shard_map/dot_general | solution.py:199
  8.1 0.8 %copy.78 = bf16[4,8,2,1024]{3,0,2,1:T(4,128)(2,1)} copy(bf16[4,8,2,1024]{3,2,1,0:T(2,128)(2,1)S(1)} %reshape.322) | data formatting | bytes 262144 | tf_op jit(solution)/shard_map/reshape | solution.py:233
  8.9 6.4 %all-to-all-start = ((bf16[8,4,2,1024]{3,1,2,0:T(4,128)(2,1)}), bf16[8,4,2,1024]{3,1,2,0:T(4,128)(2,1)S(1)}, u32[]{:S(2)}, u32[]{:S(2)}) async-start(bf16[8,4,2,1024]{3,1,2,0:T(4,128)(2,1)} %bitcast.85), calls=%async_computation | async-start | bytes 262144 | tf_op jit(solution)/shard_map/all_to_all | solution.py:234
  15.4 0.6 iota_compare_fusion.3
  16.6 0.5 fusion.38
  17.1 0.6 convert_maximum_fusion.1
  17.7 0.7 fusion.43
  18.4 0.6 multiply_exponential_fusion.1
  19.7 0.8 %exponential_select_fusion = f32[2,128,8]{2,1,0:T(8,128)S(1)} fusion(f32[2,128]{1,0:T(2,128)} %convert_maximum_fusion.1, f32[8]{0:T(128)S(1)} %get-tuple-element.17, pred[2,128]{1,0:T(4,128)(4,1)} %iota_compare_fusion.3), kind=kLoop, calls=%fused_computation.43 | loop fusion | flops 4096 | bytes 9504 | tf_op jit(solution)/shard_map/jit(_where)/select_n | solution.py:180
  20.5 3.2 %multiply_convert_fusion = bf16[2,128,8,256]{3,2,1,0:T(8,128)(2,1)} fusion(bf16[256,256,1,1]{1,0,3,2:T(8,128)(2,1)} %constant.114, bf16[2,128,8,256]{3,2,1,0:T(8,128)(2,1)} %k_ref, f32[2,128,8]{2,1,0:T(8,128)S(1)} %exponential_select_fusion, f32[2,128,256]{2,1,0:T(8,128)S(1)} %copy.40.sin_ref, f32[2,128,256]{2,1,0:T(8,128)S(1)} %copy.38.cos_ref), kind=kOutput, calls=%fused_computation.13 | convolution fusion | flops 273154048 | bytes 2760704 | tf_op jit(solution)/shard_map/bihk,kl->bihl/dot_general | solution.py:173
  24.5 6.2 %fusion.17 = f32[4,2,8,512]{3,0,2,1:T(4,128)S(1)} fusion(bf16[2,8,256,512]{3,2,1,0:T(8,128)(2,1)} %prior_ref, f32[2,8]{1,0:T(2,128)S(1)} %copy-done.7, bf16[2,128,8,512]{3,2,1,0:T(8,128)(2,1)} %v_ref, bf16[2,128,8,256]{3,2,1,0:T(8,128)(2,1)} %multiply_convert_fusion, f32[4,8]{0,1:T(8,128)S(1)} %multiply_exponential_fusion, ...), kind=kOutput, calls=%fused_computation.17 | convolution fusion | flops 562069504 | bytes 7504064 | tf_op jit(solution)/shard_map/tbhk,bhkv->tbhv/dot_general | solution.py:251
  31.4 0.8 %reshape.329 = bf16[8,2,2048]{2,1,0:T(2,128)(2,1)} reshape(bf16[8,4,2,8,64]{4,3,2,1,0:T(8,128)(2,1)S(1)} %bitcast.97) | data formatting | bytes 131072
  32.2 5.4 %all-to-all-start.1 = ((bf16[8,2,2048]{2,1,0:T(2,128)(2,1)}), bf16[8,2,2048]{2,1,0:T(2,128)(2,1)S(1)}, u32[]{:S(2)}, u32[]{:S(2)}) async-start(bf16[8,2,2048]{2,1,0:T(2,128)(2,1)} %reshape.329), calls=%async_computation.1 | async-start | bytes 131072 | tf_op jit(solution)/shard_map/all_to_all | solution.py:276
  37.6 3.6 %fusion.45 = f32[64,512]{1,0:T(8,128)S(1)} fusion(bf16[64,4096]{1,0:T(8,128)(2,1)S(1)} %bitcast.89, bf16[4096,512]{0,1:T(8,128)(2,1)} %bitcast.91), kind=kOutput, calls=%fused_computation.92 | convolution fusion | flops 268435456 | bytes 4849664 | tf_op jit(solution)/shard_map/dot_general | solution.py:205
  41.2 2.2 %all-to-all-done.1 = bf16[8,2,2048]{2,1,0:T(2,128)(2,1)S(1)} async-done(((bf16[8,2,2048]{2,1,0:T(2,128)(2,1)}), bf16[8,2,2048]{2,1,0:T(2,128)(2,1)S(1)}, u32[]{:S(2)}, u32[]{:S(2)}) %all-to-all-start.1) | async-done | bytes 65568 | tf_op jit(solution)/shard_map/all_to_all | solution.py:276
  43.8 3.1 %fusion.46 = bf16[4,16,4096]{2,1,0:T(8,128)(2,1)S(1)} fusion(bf16[4,16,512]{2,1,0:T(8,128)(2,1)S(1)} %bitcast.98, bf16[512,4096,1]{1,0,2:T(8,128)(2,1)} %bitcast.92), kind=kOutput, calls=%fused_computation.93 | convolution fusion | flops 268435456 | bytes 4784128 | tf_op jit(solution)/shard_map/dot_general | solution.py:286
  46.8 0.8 %copy.75 = bf16[4,2,16,8,256]{4,3,1,0,2:T(8,128)(2,1)} copy(bf16[4,2,16,8,256]{4,3,2,1,0:T(8,128)(2,1)S(1)} %bitcast.93) | data formatting | bytes 1048576 | tf_op jit(solution)/shard_map/convert_element_type | solution.py:301
  47.7 6.0 %all-to-all-start.2 = ((bf16[4,16,16,256]{3,1,0,2:T(8,128)(2,1)}), bf16[4,16,16,256]{3,1,0,2:T(8,128)(2,1)S(1)}, u32[]{:S(2)}, u32[]{:S(2)}) async-start(bf16[4,16,16,256]{3,1,0,2:T(8,128)(2,1)} %bitcast.82), calls=%async_computation.2 | async-start | bytes 1048576 | tf_op jit(solution)/shard_map/all_to_all | solution.py:301
  53.7 16.5 %shard_map.140 = bf16[2,128,8,512]{3,2,1,0:T(8,128)(2,1)} custom-call(f32[8]{0:T(128)} %get-tuple-element.18.rates_ref, s32[2]{0:T(128)} %copy-done.5, bf16[2,128,8,256]{3,2,1,0:T(8,128)(2,1)} %q_ref, bf16[2,128,8,256]{3,2,1,0:T(8,128)(2,1)} %k_ref, bf16[2,128,8,512]{3,2,1,0:T(8,128)(2,1)} %v_ref, bf16[2,8,256,512]{3,2,1,0:T(8,128)(2,1)} %prior_ref, ...), custom_call_target="tpu_custom_call" | custom-call | tf_op jit(solution)/shard_map/pallas_call | solution.py:115
  70.1 0.7 reduce_sum.32
  (57 shorter events, 3.8 us)
Async XLA Ops:
  0.6 1.6 %copy-start = (bf16[4096,1,1,256]{3,0,2,1:T(8,128)(2,1)S(1)}, bf16[4096,1,1,256]{3,0,2,1:T(8,128)(2,1)}, u32[]{:S(2)}) copy-start(bf16[4096,1,1,256]{3,0,2,1:T(8,128)(2,1)} %param.21) | copy-start | bytes 6291460
  0.6 3.3 %copy-start.1 = (bf16[4,16,4096]{2,1,0:T(8,128)(2,1)S(1)}, bf16[4,16,4096]{2,1,0:T(8,128)(2,1)}, u32[]{:S(2)}) copy-start(bf16[4,16,4096]{2,1,0:T(8,128)(2,1)} %param.19) | copy-start | bytes 1572868
  2.2 4.4 %copy-start.2 = (bf16[4096,1,8,1,64]{0,4,3,2,1:T(8,128)(2,1)S(1)}, bf16[4096,1,8,1,64]{0,4,3,2,1:T(8,128)(2,1)}, u32[]{:S(2)}) copy-start(bf16[4096,1,8,1,64]{0,4,3,2,1:T(8,128)(2,1)} %param.22) | copy-start | bytes 12582916
  6.6 8.7 %copy-start.6 = (s32[16]{0:T(128)S(1)}, s32[16]{0:T(128)}, u32[]{:S(2)}) copy-start(s32[16]{0:T(128)} %param.18) | copy-start | bytes 196
  6.6 11.1 %copy-start.8 = (f32[16]{0:T(128)S(1)}, f32[16]{0:T(128)}, u32[]{:S(2)}) copy-start(f32[16]{0:T(128)} %param.17) | copy-start | bytes 196
  8.9 15.0 %all-to-all-start = ((bf16[8,4,2,1024]{3,1,2,0:T(4,128)(2,1)}), bf16[8,4,2,1024]{3,1,2,0:T(4,128)(2,1)S(1)}, u32[]{:S(2)}, u32[]{:S(2)}) async-start(bf16[8,4,2,1024]{3,1,2,0:T(4,128)(2,1)} %bitcast.85), calls=%async_computation | async-start | bytes 262144 | tf_op jit(solution)/shard_map/all_to_all | solution.py:234
  15.4 8.4 %copy-start.5 = (s32[2]{0:T(128)}, s32[2]{0:T(128)S(1)}, u32[]{:S(2)}) copy-start(s32[2]{0:T(128)S(1)} %get-tuple-element.15.live_ref) | copy-start | bytes 28
  19.3 4.5 %copy-start.3 = (f32[2,128,256]{2,1,0:T(8,128)}, f32[2,128,256]{2,1,0:T(8,128)S(1)}, u32[]{:S(2)}) copy-start(f32[2,128,256]{2,1,0:T(8,128)S(1)} %copy.38.cos_ref) | copy-start | bytes 786436
  19.7 4.1 %copy-start.4 = (f32[2,128,256]{2,1,0:T(8,128)}, f32[2,128,256]{2,1,0:T(8,128)S(1)}, u32[]{:S(2)}) copy-start(f32[2,128,256]{2,1,0:T(8,128)S(1)} %copy.40.sin_ref) | copy-start | bytes 786436
  20.5 3.9 %copy-start.7 = (f32[2,8]{1,0:T(2,128)S(1)}, f32[2,8]{1,0:T(2,128)}, u32[]{:S(2)}) copy-start(f32[2,8]{1,0:T(2,128)} %multiply_exponential_fusion.1) | copy-start | bytes 196
  32.2 11.2 %all-to-all-start.1 = ((bf16[8,2,2048]{2,1,0:T(2,128)(2,1)}), bf16[8,2,2048]{2,1,0:T(2,128)(2,1)S(1)}, u32[]{:S(2)}, u32[]{:S(2)}) async-start(bf16[8,2,2048]{2,1,0:T(2,128)(2,1)} %reshape.329), calls=%async_computation.1 | async-start | bytes 131072 | tf_op jit(solution)/shard_map/all_to_all | solution.py:276
  47.7 22.5 %all-to-all-start.2 = ((bf16[4,16,16,256]{3,1,0,2:T(8,128)(2,1)}), bf16[4,16,16,256]{3,1,0,2:T(8,128)(2,1)S(1)}, u32[]{:S(2)}, u32[]{:S(2)}) async-start(bf16[4,16,16,256]{3,1,0,2:T(8,128)(2,1)} %bitcast.82), calls=%async_computation.2 | async-start | bytes 1048576 | tf_op jit(solution)/shard_map/all_to_all | solution.py:301

commit v20 on v19

--- a/solution.py
+++ b/solution.py
@@ -77,11 +77,11 @@
     halfway = key_width // 2
     offsets = jnp.arange(span_len)
     positions = (span_start[:, None] + offsets[None, :]).astype(jnp.float32)
-    frequency = 10000.0 ** (-jnp.arange(halfway).astype(jnp.float32) / halfway)
+    lane = np.arange(key_width)
+    frequency = 10000.0 ** (-jnp.asarray(lane // 2).astype(jnp.float32) / halfway)
     angles = positions[..., None] * frequency
-    cosine = jnp.repeat(jnp.cos(angles), 2, axis=-1)
-    sine_part = jnp.sin(angles)
-    sine_part = jnp.stack([-sine_part, sine_part], -1).reshape(cosine.shape)
+    cosine = jnp.cos(angles)
+    sine_part = jnp.asarray(np.where(lane % 2 == 0, -1.0, 1.0), jnp.float32) * jnp.sin(angles)
     pairs = np.arange(key_width)
     swap = jnp.asarray((pairs[:, None] == (pairs[None, :] ^ 1)).astype(np.float32), jnp.bfloat16)
     valid_rows = offsets[None, :] < live_count[:, None]

time: 71.8 us -> 68.9 us (0.960)
  other arithmetic: 6.47 us -> 4.01 us
    unnamed x20 -> x24, local copies, waits for them, and re-layouts: 1.62 us -> 1.63 us
  transfers between devices with their start and end apart: 3 -> 3, of which waited for: 1 -> 2; matrix products, arithmetic and copies ran while one was open for 17% -> 14% of each run, Pallas kernels for 23% -> 24%
where the time goes in v20:
time: 68.9 us; the launch traced here: 68 us
  matrix products  22.4 us (33%)
  starting transfers between devices  17.4 us (25%)
  Pallas kernels  16.5 us (24%)
  local copies, waits for them, and re-layouts  4.08 us (6%)
  other arithmetic  4.01 us (6%)
  waiting for transfers between devices  2.66 us (4%)
  between operations  0.95 us (1%)
    pallas_call x1, Pallas kernels, prefill_output(): pl.pallas_call(output_kernel, grid=(prompts_here,), in_specs=[whole, whol...  16.5 us
    all_to_all x1, starting transfers between devices, per_device(): arrived = lax.all_to_all(packed, 'heads', 0, 0, tiled=True)  6.38 us
    dot_general x1, matrix products, per_device(): jnp.einsum('tbhk,bhkv->tbhv', query_rot, state_new, preferred_element_typ...  6.24 us
    all_to_all x1, starting transfers between devices, per_device(): lax.all_to_all(pieces.astype(jnp.bfloat16), ('heads', 'tp'), 2, 2, tiled=...  6 us
    all_to_all x1, starting transfers between devices, per_device(): lax.all_to_all(normed.astype(jnp.bfloat16), 'heads', 0, 0, tiled=True)  4.98 us
    dot_general x1, matrix products, per_device(): jnp.dot(flat_inputs, w_gate.reshape(model_width, heads_here * value_slice...  3.58 us
    dot_general x1, matrix products, per_device(): jnp.einsum('bihk,kl->bihl', key_span, swap, preferred_element_type=jnp.fl...  3.37 us
    dot_general x1, matrix products, per_device(): jnp.dot(activated, w_out.reshape(heads_here * value_slice, model_width),...  3.03 us
  transfers between devices with their start and end apart: 3, of which 2 were waited for; matrix products, arithmetic and copies ran while one was open for 14% of the time, Pallas kernels for 24%

profile of v20, /device:TPU:1, one launch (start us, length us, event | category | flops | bytes accessed | tf_op | source)
XLA Modules:
  0.0 68.0 jit_solution(14355416109139677117)
XLA Ops:
  0.7 0.8 %add_convert_fusion.6 = f32[4,16]{1,0:T(4,128)S(1)} fusion(s32[16]{0:T(128)} %param.20), kind=kLoop, calls=%fused_computation.63 | loop fusion | flops 128 | bytes 320 | tf_op jit(solution)/shard_map/convert_element_type | solution.py:216
  1.6 0.6 copy-done
  2.2 1.6 %fusion.28 = bf16[64,256]{1,0:T(8,128)(2,1)S(1)} fusion(bf16[64,4096]{1,0:T(8,128)(2,1)} %bitcast.83, bf16[4096,1,1,256]{3,0,2,1:T(8,128)(2,1)S(1)} %copy-done), kind=kOutput, calls=%fused_computation.27 | convolution fusion | flops 134234112 | bytes 2654208 | tf_op jit(solution)/shard_map/dot_general | solution.py:196
  3.9 2.1 %fusion.25 = bf16[64,256]{1,0:T(8,128)(2,1)S(1)} fusion(bf16[64,4096]{1,0:T(8,128)(2,1)S(1)} %bitcast.84, bf16[4096,1,1,256]{3,0,2,1:T(8,128)(2,1)} %param.22), kind=kOutput, calls=%fused_computation.26 | convolution fusion | flops 134234112 | bytes 2654208 | tf_op jit(solution)/shard_map/dot_general | solution.py:193
  6.0 0.3 fusion.24
  6.3 0.3 fusion.23
  6.7 1.4 %convolution_convert_fusion = bf16[64,512]{1,0:T(8,128)(2,1)S(1)} fusion(bf16[64,4096]{1,0:T(8,128)(2,1)S(1)} %bitcast.85, bf16[4096,512]{0,1:T(8,128)(2,1)S(1)} %bitcast.87), kind=kOutput, calls=%fused_computation.18 | convolution fusion | flops 268468224 | bytes 4784128 | tf_op jit(solution)/shard_map/dot_general | solution.py:199
  8.2 0.8 %copy.54 = bf16[4,8,2,1024]{3,0,2,1:T(4,128)(2,1)} copy(bf16[4,8,2,1024]{3,2,1,0:T(2,128)(2,1)S(1)} %reshape.308) | data formatting | bytes 262144 | tf_op jit(solution)/shard_map/reshape | solution.py:233
  8.9 6.4 %all-to-all-start = ((bf16[8,4,2,1024]{3,1,2,0:T(4,128)(2,1)}), bf16[8,4,2,1024]{3,1,2,0:T(4,128)(2,1)S(1)}, u32[]{:S(2)}, u32[]{:S(2)}) async-start(bf16[8,4,2,1024]{3,1,2,0:T(4,128)(2,1)} %bitcast.82), calls=%async_computation | async-start | bytes 262144 | tf_op jit(solution)/shard_map/all_to_all | solution.py:234
  15.7 0.6 fusion.44
  16.6 1.0 %multiply_cosine_fusion = (f32[2,128,256]{2,1,0:T(8,128)S(1)}, f32[2,128,256]{2,1,0:T(8,128)S(1)}) fusion(f32[256]{0:T(256)S(1)} %copy-done.7, f32[2,128]{1,0:T(2,128)S(1)} %add_convert_fusion.7, f32[256]{0:T(256)S(1)} %copy-done.8), kind=kLoop, calls=%fused_computation.32 | loop fusion | flops 131072 | bytes 527360 | tf_op jit(solution)/shard_map/cos | solution.py:83
  17.6 3.4 %multiply_convert_fusion = bf16[2,128,8,256]{3,2,1,0:T(8,128)(2,1)} fusion(bf16[256,256,1,1]{1,0,3,2:T(8,128)(2,1)S(1)} %copy-done.10, bf16[2,128,8,256]{3,2,1,0:T(8,128)(2,1)} %k_ref, f32[2,128,8]{2,1,0:T(8,128)S(1)} %exponential_select_fusion, f32[2,128,256]{2,1,0:T(8,128)S(1)} %get-tuple-element.24.sin_ref, f32[2,128,256]{2,1,0:T(8,128)S(1)} %get-tuple-element.23.cos_ref), kind=kOutput, calls=%fused_computation.13 | convolution fusion | flops 273154048 | bytes 2760704 | tf_op jit(solution)/shard_map/bihk,kl->bihl/dot_general | solution.py:173
  21.1 0.5 all-to-all-done
  22.1 6.2 %fusion.17 = f32[4,2,8,512]{3,0,2,1:T(4,128)S(1)} fusion(bf16[2,8,256,512]{3,2,1,0:T(8,128)(2,1)} %prior_ref, f32[2,8]{1,0:T(2,128)S(1)} %multiply_exponential_fusion.1, bf16[2,128,8,512]{3,2,1,0:T(8,128)(2,1)} %v_ref, bf16[2,128,8,256]{3,2,1,0:T(8,128)(2,1)} %multiply_convert_fusion, f32[4,8]{0,1:T(8,128)S(1)} %multiply_exponential_fusion, ...), kind=kOutput, calls=%fused_computation.17 | convolution fusion | flops 562069504 | bytes 7504064 | tf_op jit(solution)/shard_map/tbhk,bhkv->tbhv/dot_general | solution.py:251
  28.3 0.4 fusion.42
  29.0 0.8 %reshape.315 = bf16[8,2,2048]{2,1,0:T(2,128)(2,1)} reshape(bf16[8,4,2,8,64]{4,3,2,1,0:T(8,128)(2,1)S(1)} %bitcast.92) | data formatting | bytes 131072
  29.8 5.0 %all-to-all-start.1 = ((bf16[8,2,2048]{2,1,0:T(2,128)(2,1)}), bf16[8,2,2048]{2,1,0:T(2,128)(2,1)S(1)}, u32[]{:S(2)}, u32[]{:S(2)}) async-start(bf16[8,2,2048]{2,1,0:T(2,128)(2,1)} %reshape.315), calls=%async_computation.1 | async-start | bytes 131072 | tf_op jit(solution)/shard_map/all_to_all | solution.py:276
  34.8 3.6 %fusion.45 = f32[64,512]{1,0:T(8,128)S(1)} fusion(bf16[64,4096]{1,0:T(8,128)(2,1)S(1)} %bitcast.86, bf16[4096,512]{0,1:T(8,128)(2,1)} %bitcast.88), kind=kOutput, calls=%fused_computation.90 | convolution fusion | flops 268435456 | bytes 4849664 | tf_op jit(solution)/shard_map/dot_general | solution.py:205
  38.4 2.2 %all-to-all-done.1 = bf16[8,2,2048]{2,1,0:T(2,128)(2,1)S(1)} async-done(((bf16[8,2,2048]{2,1,0:T(2,128)(2,1)}), bf16[8,2,2048]{2,1,0:T(2,128)(2,1)S(1)}, u32[]{:S(2)}, u32[]{:S(2)}) %all-to-all-start.1) | async-done | bytes 65568 | tf_op jit(solution)/shard_map/all_to_all | solution.py:276
  40.9 3.0 %fusion.46 = bf16[4,16,4096]{2,1,0:T(8,128)(2,1)S(1)} fusion(bf16[4,16,512]{2,1,0:T(8,128)(2,1)S(1)} %bitcast.93, bf16[512,4096,1]{1,0,2:T(8,128)(2,1)} %bitcast.89), kind=kOutput, calls=%fused_computation.91 | convolution fusion | flops 268435456 | bytes 4784128 | tf_op jit(solution)/shard_map/dot_general | solution.py:286
  44.0 0.8 %copy.51 = bf16[4,2,16,8,256]{4,3,1,0,2:T(8,128)(2,1)} copy(bf16[4,2,16,8,256]{4,3,2,1,0:T(8,128)(2,1)S(1)} %bitcast.90) | data formatting | bytes 1048576 | tf_op jit(solution)/shard_map/convert_element_type | solution.py:301
  44.8 6.0 %all-to-all-start.2 = ((bf16[4,16,16,256]{3,1,0,2:T(8,128)(2,1)}), bf16[4,16,16,256]{3,1,0,2:T(8,128)(2,1)S(1)}, u32[]{:S(2)}, u32[]{:S(2)}) async-start(bf16[4,16,16,256]{3,1,0,2:T(8,128)(2,1)} %bitcast.79), calls=%async_computation.2 | async-start | bytes 1048576 | tf_op jit(solution)/shard_map/all_to_all | solution.py:301
  50.8 16.5 %shard_map.158 = bf16[2,128,8,512]{3,2,1,0:T(8,128)(2,1)} custom-call(f32[8]{0:T(128)} %get-tuple-element.18.rates_ref, s32[2]{0:T(128)} %copy-done.5, bf16[2,128,8,256]{3,2,1,0:T(8,128)(2,1)} %q_ref, bf16[2,128,8,256]{3,2,1,0:T(8,128)(2,1)} %k_ref, bf16[2,128,8,512]{3,2,1,0:T(8,128)(2,1)} %v_ref, bf16[2,8,256,512]{3,2,1,0:T(8,128)(2,1)} %prior_ref, ...), custom_call_target="tpu_custom_call" | custom-call | tf_op jit(solution)/shard_map/pallas_call | solution.py:115
  67.3 0.7 %reduce_sum.32 = bf16[4,16,256]{2,1,0:T(8,128)(2,1)} reduce(bf16[4,16,16,256]{3,1,0,2:T(8,128)(2,1)S(1)} %all-to-all-done.2, bf16[]{:T(256)} %constant.105.clone.1), dimensions={2}, to_apply=%region_2.3 | reduce | flops 245760 | bytes 557058 | tf_op jit(solution)/shard_map/reduce_sum | solution.py:302
  (54 shorter events, 2.1 us)
Async XLA Ops:
  0.6 1.6 %copy-start = (bf16[4096,1,1,256]{3,0,2,1:T(8,128)(2,1)S(1)}, bf16[4096,1,1,256]{3,0,2,1:T(8,128)(2,1)}, u32[]{:S(2)}) copy-start(bf16[4096,1,1,256]{3,0,2,1:T(8,128)(2,1)} %param.23) | copy-start | bytes 6291460
  0.6 3.3 %copy-start.1 = (bf16[4,16,4096]{2,1,0:T(8,128)(2,1)S(1)}, bf16[4,16,4096]{2,1,0:T(8,128)(2,1)}, u32[]{:S(2)}) copy-start(bf16[4,16,4096]{2,1,0:T(8,128)(2,1)} %param.21) | copy-start | bytes 1572868
  2.2 4.4 %copy-start.2 = (bf16[4096,1,8,1,64]{0,4,3,2,1:T(8,128)(2,1)S(1)}, bf16[4096,1,8,1,64]{0,4,3,2,1:T(8,128)(2,1)}, u32[]{:S(2)}) copy-start(bf16[4096,1,8,1,64]{0,4,3,2,1:T(8,128)(2,1)} %param.24) | copy-start | bytes 12582916
  6.6 8.7 %copy-start.6 = (s32[16]{0:T(128)S(1)}, s32[16]{0:T(128)}, u32[]{:S(2)}) copy-start(s32[16]{0:T(128)} %param.20) | copy-start | bytes 196
  6.6 9.0 %copy-start.9 = (f32[16]{0:T(128)S(1)}, f32[16]{0:T(128)}, u32[]{:S(2)}) copy-start(f32[16]{0:T(128)} %param.19) | copy-start | bytes 196
  6.7 9.9 %copy-start.7 = (f32[256]{0:T(256)S(1)}, f32[256]{0:T(256)}, u32[]{:S(2)}) copy-start(f32[256]{0:T(256)} %constant.121) | copy-start | bytes 3076
  6.7 9.9 %copy-start.8 = (f32[256]{0:T(256)S(1)}, f32[256]{0:T(256)}, u32[]{:S(2)}) copy-start(f32[256]{0:T(256)} %constant.107.clone) | copy-start | bytes 3076
  6.7 10.9 %copy-start.10 = (bf16[256,256,1,1]{1,0,3,2:T(8,128)(2,1)S(1)}, bf16[256,256,1,1]{1,0,3,2:T(8,128)(2,1)}, u32[]{:S(2)}) copy-start(bf16[256,256,1,1]{1,0,3,2:T(8,128)(2,1)} %constant.122) | copy-start | bytes 393220
  8.9 12.6 %all-to-all-start = ((bf16[8,4,2,1024]{3,1,2,0:T(4,128)(2,1)}), bf16[8,4,2,1024]{3,1,2,0:T(4,128)(2,1)S(1)}, u32[]{:S(2)}, u32[]{:S(2)}) async-start(bf16[8,4,2,1024]{3,1,2,0:T(4,128)(2,1)} %bitcast.82), calls=%async_computation | async-start | bytes 262144 | tf_op jit(solution)/shard_map/all_to_all | solution.py:234
  15.4 5.5 %copy-start.5 = (s32[2]{0:T(128)}, s32[2]{0:T(128)S(1)}, u32[]{:S(2)}) copy-start(s32[2]{0:T(128)S(1)} %get-tuple-element.15.live_ref) | copy-start | bytes 28
  17.6 3.4 %copy-start.3 = (f32[2,128,256]{2,1,0:T(8,128)}, f32[2,128,256]{2,1,0:T(8,128)S(1)}, u32[]{:S(2)}) copy-start(f32[2,128,256]{2,1,0:T(8,128)S(1)} %get-tuple-element.23.cos_ref) | copy-start | bytes 786436
  17.6 3.4 %copy-start.4 = (f32[2,128,256]{2,1,0:T(8,128)}, f32[2,128,256]{2,1,0:T(8,128)S(1)}, u32[]{:S(2)}) copy-start(f32[2,128,256]{2,1,0:T(8,128)S(1)} %get-tuple-element.24.sin_ref) | copy-start | bytes 786436
  29.8 10.8 %all-to-all-start.1 = ((bf16[8,2,2048]{2,1,0:T(2,128)(2,1)}), bf16[8,2,2048]{2,1,0:T(2,128)(2,1)S(1)}, u32[]{:S(2)}, u32[]{:S(2)}) async-start(bf16[8,2,2048]{2,1,0:T(2,128)(2,1)} %reshape.315), calls=%async_computation.1 | async-start | bytes 131072 | tf_op jit(solution)/shard_map/all_to_all | solution.py:276
  44.8 22.5 %all-to-all-start.2 = ((bf16[4,16,16,256]{3,1,0,2:T(8,128)(2,1)}), bf16[4,16,16,256]{3,1,0,2:T(8,128)(2,1)S(1)}, u32[]{:S(2)}, u32[]{:S(2)}) async-start(bf16[4,16,16,256]{3,1,0,2:T(8,128)(2,1)} %bitcast.79), calls=%async_computation.2 | async-start | bytes 1048576 | tf_op jit(solution)/shard_map/all_to_all | solution.py:301
